TPU v7x, 256 devices: a whole 4x4x8 slice. The times are simulated.
256 devices in a mesh: sec: 16 (over x, y), vel: 16 (over z, core).
Axes of the slice: x: 4, y: 4, z: 8, core: 2. Of those that a mesh axis runs over, the one named last changes fastest.
Arguments:
- distribution: float32 [13824, 4096], P('vel', 'sec'), may hold values from -6 to 6
- collision: float32 [4096], P('sec'), may hold values from 0.05 to 2
- lower_blocks: float32 [25, 4096], P(None, 'sec'), may hold values from -0.6 to 0.6
- upper_blocks: float32 [25, 4096], P(None, 'sec'), may hold values from -0.6 to 0.6
- diag_inverse: float32 [25, 4096], P(None, 'sec'), may hold values from -0.2 to 1.4
Outputs:
- new_distribution: float32 [13824, 4096], P('vel', 'sec')
- macro: float32 [5, 4096], P(None, 'sec')
All inputs are finite; a program needn't handle non-finite values.
Results may differ from a plain program's by a relative error of at most 0.0003.
Values sent between devices are 32-bit elements; how exact they have to be, the bound alone decides.
No kernel may reach another device: no remote copies, remote signals or barrier semaphores. Data moves between devices by JAX's collectives and lax.ppermute only.
A program may use at most 64 MiB of HBM per device.

v0:
```python
import math

import jax
import jax.numpy as jnp
import numpy as np
from jax import lax
from jax.sharding import PartitionSpec as P

NXI = 24
TUBES = 128
JACOBI = 4
NEWTON = 2


HIGH = lax.Precision.HIGHEST
pseudo_rate = 1.0


def passed_along(block, axis, distance):
    devices = range(lax.axis_size(axis))
    route = [(i - distance, i) for i in devices if i - distance in devices]
    return lax.ppermute(block, axis, route)


def extended(array, sides, width):
    for axis, dim in sides:
        count, length = (lax.axis_size(axis), array.shape[dim])
        up = [(i, (i + 1) % count) for i in range(count - 1)]
        down = [(j, i) for i, j in up]
        last = lax.slice_in_dim(array, length - width, length, axis=dim)
        first = lax.slice_in_dim(array, 0, width, axis=dim)
        before = lax.ppermute(last, axis, up)
        after = lax.ppermute(first, axis, down)
        array = jnp.concatenate([before, array, after], axis=dim)
    return array


def hermite_rule(count):
    quarter = math.pi ** (-0.25)
    found = []
    last_slope = 1.0
    for index in range(count // 2):
        if index == 0:
            guess = math.sqrt(2.0 * count + 1.0) - 1.85575 * (2.0 * count + 1.0) ** (-0.16667)
        elif index == 1:
            guess = guess - 1.14 * count**0.426 / guess
        elif index == 2:
            guess = 1.86 * guess - 0.86 * found[0][0]
        elif index == 3:
            guess = 1.91 * guess - 0.91 * found[1][0]
        else:
            guess = 2.0 * guess - found[index - 2][0]
        for repeat in range(60):
            current = quarter
            previous = 0.0
            for order in range(count):
                older = previous
                previous = current
                current = (
                    guess * math.sqrt(2.0 / (order + 1)) * previous
                    - math.sqrt(order / (order + 1.0)) * older
                )
            last_slope = math.sqrt(2.0 * count) * previous
            guess = guess - current / last_slope
        found.append((guess, 2.0 / (last_slope * last_slope)))
    positive = found[::-1]
    points = [-pair[0] for pair in found] + [pair[0] for pair in positive]
    weights = [pair[1] for pair in found] + [pair[1] for pair in positive]
    return (np.array(points), np.array(weights))


def node_tables(axis_points):
    points, weights = hermite_rule(axis_points)
    node_index = np.arange(axis_points**3)
    idx_x = node_index % axis_points
    idx_z = node_index // axis_points % axis_points
    idx_y = node_index // (axis_points * axis_points)
    along_x = points[idx_x]
    along_y = points[idx_y]
    along_z = points[idx_z]
    node_weight = weights[idx_x] * weights[idx_y] * weights[idx_z] / math.pi**1.5
    energy = along_x**2 + along_y**2 + along_z**2 - 1.5
    moment_basis = np.stack([along_x * 0.0 + 1.0, along_x, along_y, along_z, energy])
    norm_scale = np.array([1.0, 0.5, 0.5, 0.5, 1.5])
    return (
        along_x,
        node_weight,
        moment_basis * node_weight[None, :],
        moment_basis / norm_scale[:, None],
    )


def apply_block(matrices, vector):
    shaped = matrices.reshape((5, 5) + vector.shape[1:])
    return jnp.sum(shaped * vector[None], axis=1)


def affine_combine(earlier_map, later_map):
    return (later_map[0] * earlier_map[0], later_map[0] * earlier_map[1] + later_map[1])


def newton_sums(loaded, signed, shift_mass, shift_flow):
    growth = jnp.exp(shift_mass + shift_flow * signed)
    scaled = loaded * growth
    excess = loaded * (growth - 1.0)
    return jnp.stack(
        [
            jnp.sum(scaled),
            jnp.sum(scaled * signed),
            jnp.sum(scaled * signed * signed),
            jnp.sum(excess),
            jnp.sum(excess * signed),
        ]
    )


def newton_update(shift_mass, shift_flow, sums, goal_mass, goal_flow):
    resid_mass = sums[3] - goal_mass
    resid_flow = sums[4] - goal_flow
    determinant = sums[0] * sums[2] - sums[1] * sums[1]
    new_mass = shift_mass - (sums[2] * resid_mass - sums[1] * resid_flow) / determinant
    new_flow = shift_flow - (sums[0] * resid_flow - sums[1] * resid_mass) / determinant
    return (new_mass, new_flow)


def body(distribution, collision, lower_blocks, upper_blocks, diag_inverse):
    node_count = distribution.shape[0]
    cell_count = distribution.shape[1]
    length = cell_count // TUBES
    node_rows = node_count // NXI
    half_nodes = NXI // 2
    along_x, node_weight, weighted_np, rebuild_np = node_tables(NXI)
    all_signed = jnp.asarray(along_x, jnp.float32)
    all_mass = jnp.asarray(node_weight, jnp.float32)
    offset = lax.axis_index("vel") * node_count
    weighted = lax.dynamic_slice_in_dim(
        jnp.asarray(weighted_np, jnp.float32), offset, node_count, 1
    )
    rebuild = lax.dynamic_slice_in_dim(jnp.asarray(rebuild_np, jnp.float32), offset, node_count, 1)
    signed = lax.dynamic_slice_in_dim(all_signed, offset, node_count, 0)
    node_mass = lax.dynamic_slice_in_dim(all_mass, offset, node_count, 0)
    old_moments = lax.psum(jnp.dot(weighted, distribution, precision=HIGH), "vel")
    target = jnp.dot(rebuild.T, old_moments, precision=HIGH)
    total_length = length * lax.axis_size("sec")
    thickness = collision.reshape(1, 1, length, TUBES)
    node_speed = jnp.abs(signed).reshape(node_rows, NXI, 1, 1)
    denominator = node_speed * total_length + thickness + pseudo_rate
    carry_rate = node_speed * total_length / denominator
    drive_term = (
        thickness * target.reshape(node_rows, NXI, length, TUBES)
        + pseudo_rate * distribution.reshape(node_rows, NXI, length, TUBES)
    ) / denominator
    prod_neg, local_neg = lax.associative_scan(
        affine_combine,
        (carry_rate[:, :half_nodes], drive_term[:, :half_nodes]),
        reverse=True,
        axis=2,
    )
    prod_pos, local_pos = lax.associative_scan(
        affine_combine, (carry_rate[:, half_nodes:], drive_term[:, half_nodes:]), axis=2
    )
    summary_pos = (prod_pos[:, :, -1], local_pos[:, :, -1])
    summary_neg = (prod_neg[:, :, 0], local_neg[:, :, 0])

    def relay(turn_index, inflows):
        out_pos = summary_pos[0] * inflows[0] + summary_pos[1]
        out_neg = summary_neg[0] * inflows[1] + summary_neg[1]
        return (passed_along(out_pos, "sec", 1), passed_along(out_neg, "sec", -1))

    start_flows = (jnp.zeros_like(summary_pos[1]), jnp.zeros_like(summary_neg[1]))
    inflow_pos, inflow_neg = lax.fori_loop(0, lax.axis_size("sec") - 1, relay, start_flows)
    field_neg = local_neg + prod_neg * inflow_neg[:, :, None, :]
    field_pos = local_pos + prod_pos * inflow_pos[:, :, None, :]
    half_field = jnp.concatenate([field_neg, field_pos], axis=1).reshape(node_count, cell_count)
    half_moments = lax.psum(jnp.dot(weighted, half_field, precision=HIGH), "vel")
    residual = (half_moments - old_moments).reshape(5, length, TUBES)
    lower_r = lower_blocks.reshape(25, length, TUBES)
    upper_r = upper_blocks.reshape(25, length, TUBES)
    inverse_r = diag_inverse.reshape(25, length, TUBES)
    correction = apply_block(inverse_r, residual)
    for sweep_index in range(JACOBI):
        padded = extended(correction, (("sec", 1),), 1)
        correction = apply_block(
            inverse_r,
            residual - apply_block(lower_r, padded[:, :-2]) - apply_block(upper_r, padded[:, 2:]),
        )
    correction = correction.reshape(5, cell_count)
    macro = half_moments + correction
    synthetic = half_field + jnp.dot(rebuild.T, correction, precision=HIGH)
    local_totals = jnp.sum(old_moments - macro, axis=1)[0:2]
    magnitude = jnp.sum(jnp.abs(synthetic), axis=1)
    shift_mass = jnp.zeros((), jnp.float32)
    shift_flow = jnp.zeros((), jnp.float32)
    goals = lax.psum(local_totals, "sec")
    loaded = node_mass * magnitude
    for newton_turn in range(NEWTON):
        sums = lax.psum(newton_sums(loaded, signed, shift_mass, shift_flow), ("sec", "vel"))
        shift_mass, shift_flow = newton_update(shift_mass, shift_flow, sums, goals[0], goals[1])
    growth = jnp.exp(shift_mass + shift_flow * signed)
    new_distribution = synthetic + jnp.abs(synthetic) * (growth[:, None] - 1.0)
    return (new_distribution, macro)


def solution(mesh):
    in_specs = (P("vel", "sec"), P("sec"), P(None, "sec"), P(None, "sec"), P(None, "sec"))
    out_specs = (P("vel", "sec"), P(None, "sec"))
    return jax.shard_map(body, mesh=mesh, in_specs=in_specs, out_specs=out_specs, check_vma=False)
```

profile of v0, /device:TPU:32, one launch (start us, length us, event | category | flops | bytes accessed | tf_op | source)
XLA Modules:
  0.0 528.3 jit_solution(13319355678150819827)
XLA Ops:
  3.6 25.9 %psum.35 = f32[5,256]{1,0:T(8,128)S(1)} all-reduce(f32[5,256]{1,0:T(8,128)S(1)} %fusion.12), channel_id=1, replica_groups=mesh['sec'=16,'vel'=16] {'vel'}, use_global_device_ids=true, to_apply=%region_0.0 | all-reduce | flops 1280 | bytes 10240 | tf_op jit(solution)/shard_map/psum | solution.py:142
  42.4 201.4 %while.12 = (s32[]{:T(128)}, f32[36,12,128]{2,1,0:T(8,128)S(1)}, f32[36,12,128]{2,1,0:T(8,128)S(1)}, f32[36,12,128]{2,1,0:T(8,128)S(1)}, f32[36,12,128]{2,1,0:T(...) while((s32[]{:T(128)}, f32[36,12,128]{2,1,0:T(8,128)S(1)}, ...), condition=%wide.region_2.0_spmd, body=%wide.region_1.0_spmd.sunk | while | flops 221186 | bytes 3539109 | solution.py:171
  42.5 3.5 collective-permute-start
  50.2 4.5 collective-permute-done.1
  62.5 4.5 collective-permute-done.1
  67.0 4.4 collective-permute-start
  75.7 4.5 collective-permute-done.1
  80.2 4.0 collective-permute-start
  88.4 4.5 collective-permute-done.1
  93.0 4.0 collective-permute-start
  101.2 4.5 collective-permute-done.1
  105.8 4.0 collective-permute-start
  111.2 3.7 collective-permute-done
  114.9 4.7 collective-permute-done.1
  119.6 3.8 collective-permute-start
  124.8 4.9 collective-permute-done
  129.7 5.1 collective-permute-done.1
  134.8 3.8 collective-permute-start
  140.0 5.8 %collective-permute-done = f32[36,12,128]{2,1,0:T(8,128)S(1)} collective-permute-done((f32[36,12,128]{2,1,0:T(8,128)S(1)}, f32[36,12,128]{2,1,0:T(8,128)S(1)}, u32[]{:S(2)}, u32[]{:S(2)}) %collective-permute-start) | collective-permute-done | bytes 221216 | tf_op jit(solution)/shard_map/while/body/eval_jaxpr/ppermute | solution.py:22
  145.8 4.3 collective-permute-done.1
  150.1 4.0 collective-permute-start
  155.6 4.9 collective-permute-done
  160.5 4.2 collective-permute-done.1
  164.7 4.5 collective-permute-start
  170.6 4.3 collective-permute-done
  174.9 4.2 collective-permute-done.1
  179.2 4.3 collective-permute-start
  188.3 4.2 collective-permute-done.1
  192.5 4.3 collective-permute-start
  201.0 4.5 collective-permute-done.1
  205.6 4.0 collective-permute-start
  213.8 4.5 collective-permute-done.1
  218.4 4.0 collective-permute-start
  226.6 4.5 collective-permute-done.1
  231.1 4.0 collective-permute-start
  239.4 4.5 collective-permute-done.1
  247.0 25.8 %psum.36 = f32[5,256]{1,0:T(8,128)S(1)} all-reduce(f32[5,256]{1,0:T(8,128)S(1)} %fusion), channel_id=1, replica_groups=mesh['sec'=16,'vel'=16] {'vel'}, use_global_device_ids=true, to_apply=%region_3.0 | all-reduce | flops 1280 | bytes 10240 | tf_op jit(solution)/shard_map/psum | solution.py:175
  272.9 4.0 collective-permute-start.2
  278.3 4.1 collective-permute-done.3
  282.5 4.0 collective-permute-start.4
  287.9 4.2 collective-permute-done.5
  292.2 4.0 collective-permute-start.6
  297.5 4.2 collective-permute-done.7
  301.8 4.0 collective-permute-start.8
  307.2 4.2 collective-permute-done.9
  314.1 37.6 %psum.38 = f32[2]{0:T(128)S(1)} all-reduce(f32[2]{0:T(128)S(1)} %bitcast.57), channel_id=1, replica_groups=mesh['sec'=16,'vel'=16] {'sec'}, use_global_device_ids=true, to_apply=%region_25.0 | all-reduce | flops 2 | bytes 16 | tf_op jit(solution)/shard_map/psum | solution.py:194
  357.0 74.8 %psum.37 = f32[5]{0:T(128)S(1)} all-reduce(f32[5]{0:T(128)S(1)} %stack.41), channel_id=1, replica_groups=mesh['sec'=16,'vel'=16] {'sec','vel'}, use_global_device_ids=true, to_apply=%region_23.0 | all-reduce | flops 5 | bytes 40 | tf_op jit(solution)/shard_map/psum | solution.py:197
  444.7 73.5 %psum.39 = f32[5]{0:T(128)S(1)} all-reduce(f32[5]{0:T(128)S(1)} %stack.47), channel_id=1, replica_groups=mesh['sec'=16,'vel'=16] {'sec','vel'}, use_global_device_ids=true, to_apply=%region_31.0 | all-reduce | flops 5 | bytes 40 | tf_op jit(solution)/shard_map/psum | solution.py:197
  (142 shorter events, 93.8 us)
Async XLA Ops:
  0.6 1.7 copy-start
  32.7 0.7 copy-start.6
  42.5 7.7 %collective-permute-start = (f32[36,12,128]{2,1,0:T(8,128)S(1)}, f32[36,12,128]{2,1,0:T(8,128)S(1)}, u32[]{:S(2)}, u32[]{:S(2)}) collective-permute-start(f32[36,12,128]{2,1,0:T(8,128)S(1)} %multiply_add_fusion.6), channel_id=1, source_target_pairs={{0,16},{16,32},{32,48},{48,64},{64,80},{80,96},{96,112},{112,128},... | collective-permute-start | bytes 663560 | tf_op jit(solution)/shard_map/while/body/eval_jaxpr/ppermute | solution.py:22
  46.1 8.6 %collective-permute-start.1 = (f32[36,12,128]{2,1,0:T(8,128)S(1)}, f32[36,12,128]{2,1,0:T(8,128)S(1)}, u32[]{:S(2)}, u32[]{:S(2)}) collective-permute-start(f32[36,12,128]{2,1,0:T(8,128)S(1)} %multiply_add_fusion.7), channel_id=1, source_target_pairs={{16,0},{32,16},{48,32},{64,48},{80,64},{96,80},{112,96},{128,112},... | collective-permute-start | bytes 663560 | tf_op jit(solution)/shard_map/while/body/eval_jaxpr/ppermute | solution.py:22
  54.8 7.7 %collective-permute-start = (f32[36,12,128]{2,1,0:T(8,128)S(1)}, f32[36,12,128]{2,1,0:T(8,128)S(1)}, u32[]{:S(2)}, u32[]{:S(2)}) collective-permute-start(f32[36,12,128]{2,1,0:T(8,128)S(1)} %multiply_add_fusion.6), channel_id=1, source_target_pairs={{0,16},{16,32},{32,48},{48,64},{64,80},{80,96},{96,112},{112,128},... | collective-permute-start | bytes 663560 | tf_op jit(solution)/shard_map/while/body/eval_jaxpr/ppermute | solution.py:22
  58.3 8.6 %collective-permute-start.1 = (f32[36,12,128]{2,1,0:T(8,128)S(1)}, f32[36,12,128]{2,1,0:T(8,128)S(1)}, u32[]{:S(2)}, u32[]{:S(2)}) collective-permute-start(f32[36,12,128]{2,1,0:T(8,128)S(1)} %multiply_add_fusion.7), channel_id=1, source_target_pairs={{16,0},{32,16},{48,32},{64,48},{80,64},{96,80},{112,96},{128,112},... | collective-permute-start | bytes 663560 | tf_op jit(solution)/shard_map/while/body/eval_jaxpr/ppermute | solution.py:22
  67.0 8.6 %collective-permute-start = (f32[36,12,128]{2,1,0:T(8,128)S(1)}, f32[36,12,128]{2,1,0:T(8,128)S(1)}, u32[]{:S(2)}, u32[]{:S(2)}) collective-permute-start(f32[36,12,128]{2,1,0:T(8,128)S(1)} %multiply_add_fusion.6), channel_id=1, source_target_pairs={{0,16},{16,32},{32,48},{48,64},{64,80},{80,96},{96,112},{112,128},... | collective-permute-start | bytes 663560 | tf_op jit(solution)/shard_map/while/body/eval_jaxpr/ppermute | solution.py:22
  71.5 8.6 %collective-permute-start.1 = (f32[36,12,128]{2,1,0:T(8,128)S(1)}, f32[36,12,128]{2,1,0:T(8,128)S(1)}, u32[]{:S(2)}, u32[]{:S(2)}) collective-permute-start(f32[36,12,128]{2,1,0:T(8,128)S(1)} %multiply_add_fusion.7), channel_id=1, source_target_pairs={{16,0},{32,16},{48,32},{64,48},{80,64},{96,80},{112,96},{128,112},... | collective-permute-start | bytes 663560 | tf_op jit(solution)/shard_map/while/body/eval_jaxpr/ppermute | solution.py:22
  80.2 8.2 %collective-permute-start = (f32[36,12,128]{2,1,0:T(8,128)S(1)}, f32[36,12,128]{2,1,0:T(8,128)S(1)}, u32[]{:S(2)}, u32[]{:S(2)}) collective-permute-start(f32[36,12,128]{2,1,0:T(8,128)S(1)} %multiply_add_fusion.6), channel_id=1, source_target_pairs={{0,16},{16,32},{32,48},{48,64},{64,80},{80,96},{96,112},{112,128},... | collective-permute-start | bytes 663560 | tf_op jit(solution)/shard_map/while/body/eval_jaxpr/ppermute | solution.py:22
  84.3 8.6 %collective-permute-start.1 = (f32[36,12,128]{2,1,0:T(8,128)S(1)}, f32[36,12,128]{2,1,0:T(8,128)S(1)}, u32[]{:S(2)}, u32[]{:S(2)}) collective-permute-start(f32[36,12,128]{2,1,0:T(8,128)S(1)} %multiply_add_fusion.7), channel_id=1, source_target_pairs={{16,0},{32,16},{48,32},{64,48},{80,64},{96,80},{112,96},{128,112},... | collective-permute-start | bytes 663560 | tf_op jit(solution)/shard_map/while/body/eval_jaxpr/ppermute | solution.py:22
  93.0 8.2 %collective-permute-start = (f32[36,12,128]{2,1,0:T(8,128)S(1)}, f32[36,12,128]{2,1,0:T(8,128)S(1)}, u32[]{:S(2)}, u32[]{:S(2)}) collective-permute-start(f32[36,12,128]{2,1,0:T(8,128)S(1)} %multiply_add_fusion.6), channel_id=1, source_target_pairs={{0,16},{16,32},{32,48},{48,64},{64,80},{80,96},{96,112},{112,128},... | collective-permute-start | bytes 663560 | tf_op jit(solution)/shard_map/while/body/eval_jaxpr/ppermute | solution.py:22
  97.1 8.6 %collective-permute-start.1 = (f32[36,12,128]{2,1,0:T(8,128)S(1)}, f32[36,12,128]{2,1,0:T(8,128)S(1)}, u32[]{:S(2)}, u32[]{:S(2)}) collective-permute-start(f32[36,12,128]{2,1,0:T(8,128)S(1)} %multiply_add_fusion.7), channel_id=1, source_target_pairs={{16,0},{32,16},{48,32},{64,48},{80,64},{96,80},{112,96},{128,112},... | collective-permute-start | bytes 663560 | tf_op jit(solution)/shard_map/while/body/eval_jaxpr/ppermute | solution.py:22
  105.8 9.1 %collective-permute-start = (f32[36,12,128]{2,1,0:T(8,128)S(1)}, f32[36,12,128]{2,1,0:T(8,128)S(1)}, u32[]{:S(2)}, u32[]{:S(2)}) collective-permute-start(f32[36,12,128]{2,1,0:T(8,128)S(1)} %multiply_add_fusion.6), channel_id=1, source_target_pairs={{0,16},{16,32},{32,48},{48,64},{64,80},{80,96},{96,112},{112,128},... | collective-permute-start | bytes 663560 | tf_op jit(solution)/shard_map/while/body/eval_jaxpr/ppermute | solution.py:22
  109.9 9.7 %collective-permute-start.1 = (f32[36,12,128]{2,1,0:T(8,128)S(1)}, f32[36,12,128]{2,1,0:T(8,128)S(1)}, u32[]{:S(2)}, u32[]{:S(2)}) collective-permute-start(f32[36,12,128]{2,1,0:T(8,128)S(1)} %multiply_add_fusion.7), channel_id=1, source_target_pairs={{16,0},{32,16},{48,32},{64,48},{80,64},{96,80},{112,96},{128,112},... | collective-permute-start | bytes 663560 | tf_op jit(solution)/shard_map/while/body/eval_jaxpr/ppermute | solution.py:22
  119.6 10.1 %collective-permute-start = (f32[36,12,128]{2,1,0:T(8,128)S(1)}, f32[36,12,128]{2,1,0:T(8,128)S(1)}, u32[]{:S(2)}, u32[]{:S(2)}) collective-permute-start(f32[36,12,128]{2,1,0:T(8,128)S(1)} %multiply_add_fusion.6), channel_id=1, source_target_pairs={{0,16},{16,32},{32,48},{48,64},{64,80},{80,96},{96,112},{112,128},... | collective-permute-start | bytes 663560 | tf_op jit(solution)/shard_map/while/body/eval_jaxpr/ppermute | solution.py:22
  123.5 11.2 %collective-permute-start.1 = (f32[36,12,128]{2,1,0:T(8,128)S(1)}, f32[36,12,128]{2,1,0:T(8,128)S(1)}, u32[]{:S(2)}, u32[]{:S(2)}) collective-permute-start(f32[36,12,128]{2,1,0:T(8,128)S(1)} %multiply_add_fusion.7), channel_id=1, source_target_pairs={{16,0},{32,16},{48,32},{64,48},{80,64},{96,80},{112,96},{128,112},... | collective-permute-start | bytes 663560 | tf_op jit(solution)/shard_map/while/body/eval_jaxpr/ppermute | solution.py:22
  134.8 11.0 %collective-permute-start = (f32[36,12,128]{2,1,0:T(8,128)S(1)}, f32[36,12,128]{2,1,0:T(8,128)S(1)}, u32[]{:S(2)}, u32[]{:S(2)}) collective-permute-start(f32[36,12,128]{2,1,0:T(8,128)S(1)} %multiply_add_fusion.6), channel_id=1, source_target_pairs={{0,16},{16,32},{32,48},{48,64},{64,80},{80,96},{96,112},{112,128},... | collective-permute-start | bytes 663560 | tf_op jit(solution)/shard_map/while/body/eval_jaxpr/ppermute | solution.py:22
  138.7 11.4 %collective-permute-start.1 = (f32[36,12,128]{2,1,0:T(8,128)S(1)}, f32[36,12,128]{2,1,0:T(8,128)S(1)}, u32[]{:S(2)}, u32[]{:S(2)}) collective-permute-start(f32[36,12,128]{2,1,0:T(8,128)S(1)} %multiply_add_fusion.7), channel_id=1, source_target_pairs={{16,0},{32,16},{48,32},{64,48},{80,64},{96,80},{112,96},{128,112},... | collective-permute-start | bytes 663560 | tf_op jit(solution)/shard_map/while/body/eval_jaxpr/ppermute | solution.py:22
  150.1 10.3 %collective-permute-start = (f32[36,12,128]{2,1,0:T(8,128)S(1)}, f32[36,12,128]{2,1,0:T(8,128)S(1)}, u32[]{:S(2)}, u32[]{:S(2)}) collective-permute-start(f32[36,12,128]{2,1,0:T(8,128)S(1)} %multiply_add_fusion.6), channel_id=1, source_target_pairs={{0,16},{16,32},{32,48},{48,64},{64,80},{80,96},{96,112},{112,128},... | collective-permute-start | bytes 663560 | tf_op jit(solution)/shard_map/while/body/eval_jaxpr/ppermute | solution.py:22
  154.3 10.4 %collective-permute-start.1 = (f32[36,12,128]{2,1,0:T(8,128)S(1)}, f32[36,12,128]{2,1,0:T(8,128)S(1)}, u32[]{:S(2)}, u32[]{:S(2)}) collective-permute-start(f32[36,12,128]{2,1,0:T(8,128)S(1)} %multiply_add_fusion.7), channel_id=1, source_target_pairs={{16,0},{32,16},{48,32},{64,48},{80,64},{96,80},{112,96},{128,112},... | collective-permute-start | bytes 663560 | tf_op jit(solution)/shard_map/while/body/eval_jaxpr/ppermute | solution.py:22
  164.7 10.2 %collective-permute-start = (f32[36,12,128]{2,1,0:T(8,128)S(1)}, f32[36,12,128]{2,1,0:T(8,128)S(1)}, u32[]{:S(2)}, u32[]{:S(2)}) collective-permute-start(f32[36,12,128]{2,1,0:T(8,128)S(1)} %multiply_add_fusion.6), channel_id=1, source_target_pairs={{0,16},{16,32},{32,48},{48,64},{64,80},{80,96},{96,112},{112,128},... | collective-permute-start | bytes 663560 | tf_op jit(solution)/shard_map/while/body/eval_jaxpr/ppermute | solution.py:22
  169.3 9.8 %collective-permute-start.1 = (f32[36,12,128]{2,1,0:T(8,128)S(1)}, f32[36,12,128]{2,1,0:T(8,128)S(1)}, u32[]{:S(2)}, u32[]{:S(2)}) collective-permute-start(f32[36,12,128]{2,1,0:T(8,128)S(1)} %multiply_add_fusion.7), channel_id=1, source_target_pairs={{16,0},{32,16},{48,32},{64,48},{80,64},{96,80},{112,96},{128,112},... | collective-permute-start | bytes 663560 | tf_op jit(solution)/shard_map/while/body/eval_jaxpr/ppermute | solution.py:22
  179.2 9.1 %collective-permute-start = (f32[36,12,128]{2,1,0:T(8,128)S(1)}, f32[36,12,128]{2,1,0:T(8,128)S(1)}, u32[]{:S(2)}, u32[]{:S(2)}) collective-permute-start(f32[36,12,128]{2,1,0:T(8,128)S(1)} %multiply_add_fusion.6), channel_id=1, source_target_pairs={{0,16},{16,32},{32,48},{48,64},{64,80},{80,96},{96,112},{112,128},... | collective-permute-start | bytes 663560 | tf_op jit(solution)/shard_map/while/body/eval_jaxpr/ppermute | solution.py:22
  183.6 8.9 %collective-permute-start.1 = (f32[36,12,128]{2,1,0:T(8,128)S(1)}, f32[36,12,128]{2,1,0:T(8,128)S(1)}, u32[]{:S(2)}, u32[]{:S(2)}) collective-permute-start(f32[36,12,128]{2,1,0:T(8,128)S(1)} %multiply_add_fusion.7), channel_id=1, source_target_pairs={{16,0},{32,16},{48,32},{64,48},{80,64},{96,80},{112,96},{128,112},... | collective-permute-start | bytes 663560 | tf_op jit(solution)/shard_map/while/body/eval_jaxpr/ppermute | solution.py:22
  192.5 8.5 %collective-permute-start = (f32[36,12,128]{2,1,0:T(8,128)S(1)}, f32[36,12,128]{2,1,0:T(8,128)S(1)}, u32[]{:S(2)}, u32[]{:S(2)}) collective-permute-start(f32[36,12,128]{2,1,0:T(8,128)S(1)} %multiply_add_fusion.6), channel_id=1, source_target_pairs={{0,16},{16,32},{32,48},{48,64},{64,80},{80,96},{96,112},{112,128},... | collective-permute-start | bytes 663560 | tf_op jit(solution)/shard_map/while/body/eval_jaxpr/ppermute | solution.py:22
  196.9 8.6 %collective-permute-start.1 = (f32[36,12,128]{2,1,0:T(8,128)S(1)}, f32[36,12,128]{2,1,0:T(8,128)S(1)}, u32[]{:S(2)}, u32[]{:S(2)}) collective-permute-start(f32[36,12,128]{2,1,0:T(8,128)S(1)} %multiply_add_fusion.7), channel_id=1, source_target_pairs={{16,0},{32,16},{48,32},{64,48},{80,64},{96,80},{112,96},{128,112},... | collective-permute-start | bytes 663560 | tf_op jit(solution)/shard_map/while/body/eval_jaxpr/ppermute | solution.py:22
  205.6 8.2 %collective-permute-start = (f32[36,12,128]{2,1,0:T(8,128)S(1)}, f32[36,12,128]{2,1,0:T(8,128)S(1)}, u32[]{:S(2)}, u32[]{:S(2)}) collective-permute-start(f32[36,12,128]{2,1,0:T(8,128)S(1)} %multiply_add_fusion.6), channel_id=1, source_target_pairs={{0,16},{16,32},{32,48},{48,64},{64,80},{80,96},{96,112},{112,128},... | collective-permute-start | bytes 663560 | tf_op jit(solution)/shard_map/while/body/eval_jaxpr/ppermute | solution.py:22
  209.7 8.6 %collective-permute-start.1 = (f32[36,12,128]{2,1,0:T(8,128)S(1)}, f32[36,12,128]{2,1,0:T(8,128)S(1)}, u32[]{:S(2)}, u32[]{:S(2)}) collective-permute-start(f32[36,12,128]{2,1,0:T(8,128)S(1)} %multiply_add_fusion.7), channel_id=1, source_target_pairs={{16,0},{32,16},{48,32},{64,48},{80,64},{96,80},{112,96},{128,112},... | collective-permute-start | bytes 663560 | tf_op jit(solution)/shard_map/while/body/eval_jaxpr/ppermute | solution.py:22
  218.4 8.2 %collective-permute-start = (f32[36,12,128]{2,1,0:T(8,128)S(1)}, f32[36,12,128]{2,1,0:T(8,128)S(1)}, u32[]{:S(2)}, u32[]{:S(2)}) collective-permute-start(f32[36,12,128]{2,1,0:T(8,128)S(1)} %multiply_add_fusion.6), channel_id=1, source_target_pairs={{0,16},{16,32},{32,48},{48,64},{64,80},{80,96},{96,112},{112,128},... | collective-permute-start | bytes 663560 | tf_op jit(solution)/shard_map/while/body/eval_jaxpr/ppermute | solution.py:22
  222.5 8.6 %collective-permute-start.1 = (f32[36,12,128]{2,1,0:T(8,128)S(1)}, f32[36,12,128]{2,1,0:T(8,128)S(1)}, u32[]{:S(2)}, u32[]{:S(2)}) collective-permute-start(f32[36,12,128]{2,1,0:T(8,128)S(1)} %multiply_add_fusion.7), channel_id=1, source_target_pairs={{16,0},{32,16},{48,32},{64,48},{80,64},{96,80},{112,96},{128,112},... | collective-permute-start | bytes 663560 | tf_op jit(solution)/shard_map/while/body/eval_jaxpr/ppermute | solution.py:22
  231.1 8.2 %collective-permute-start = (f32[36,12,128]{2,1,0:T(8,128)S(1)}, f32[36,12,128]{2,1,0:T(8,128)S(1)}, u32[]{:S(2)}, u32[]{:S(2)}) collective-permute-start(f32[36,12,128]{2,1,0:T(8,128)S(1)} %multiply_add_fusion.6), channel_id=1, source_target_pairs={{0,16},{16,32},{32,48},{48,64},{64,80},{80,96},{96,112},{112,128},... | collective-permute-start | bytes 663560 | tf_op jit(solution)/shard_map/while/body/eval_jaxpr/ppermute | solution.py:22
  235.2 8.6 %collective-permute-start.1 = (f32[36,12,128]{2,1,0:T(8,128)S(1)}, f32[36,12,128]{2,1,0:T(8,128)S(1)}, u32[]{:S(2)}, u32[]{:S(2)}) collective-permute-start(f32[36,12,128]{2,1,0:T(8,128)S(1)} %multiply_add_fusion.7), channel_id=1, source_target_pairs={{16,0},{32,16},{48,32},{64,48},{80,64},{96,80},{112,96},{128,112},... | collective-permute-start | bytes 663560 | tf_op jit(solution)/shard_map/while/body/eval_jaxpr/ppermute | solution.py:22
  243.9 1.0 copy-start.1
  243.9 1.1 copy-start.2
  247.0 25.8 %copy-start.3 = (f32[25,256]{1,0:T(8,128)S(1)}, f32[25,256]{1,0:T(8,128)}, u32[]{:S(2)}) copy-start(f32[25,256]{1,0:T(8,128)} %param.15) | copy-start | bytes 76804
  272.8 5.4 %copy-start.4 = (f32[25,256]{1,0:T(8,128)S(1)}, f32[25,256]{1,0:T(8,128)}, u32[]{:S(2)}) copy-start(f32[25,256]{1,0:T(8,128)} %param.13) | copy-start | bytes 76804
  272.9 5.4 %copy-start.5 = (f32[25,256]{1,0:T(8,128)S(1)}, f32[25,256]{1,0:T(8,128)}, u32[]{:S(2)}) copy-start(f32[25,256]{1,0:T(8,128)} %param.14) | copy-start | bytes 76804
  272.9 5.4 %collective-permute-start.2 = (f32[5,1,128]{2,1,0:T(1,128)S(1)}, f32[5,1,128]{2,1,0:T(1,128)S(1)}, u32[]{:S(2)}, u32[]{:S(2)}) collective-permute-start(f32[5,1,128]{2,1,0:T(1,128)S(1)} %get-tuple-element.99), channel_id=1, source_target_pairs={{0,16},{16,32},{32,48},{48,64},{64,80},{80,96},{96,112},{112,128},... | collective-permute-start | bytes 7688 | tf_op jit(solution)/shard_map/ppermute | solution.py:32
  276.9 5.5 %collective-permute-start.3 = (f32[5,1,128]{2,1,0:T(1,128)S(1)}, f32[5,1,128]{2,1,0:T(1,128)S(1)}, u32[]{:S(2)}, u32[]{:S(2)}) collective-permute-start(f32[5,1,128]{2,1,0:T(1,128)S(1)} %get-tuple-element.100), channel_id=1, source_target_pairs={{16,0},{32,16},{48,32},{64,48},{80,64},{96,80},{112,96},{128,112},... | collective-permute-start | bytes 7688 | tf_op jit(solution)/shard_map/ppermute | solution.py:33
  282.5 5.3 %collective-permute-start.4 = (f32[5,1,128]{2,1,0:T(1,128)S(1)}, f32[5,1,128]{2,1,0:T(1,128)S(1)}, u32[]{:S(2)}, u32[]{:S(2)}) collective-permute-start(f32[5,1,128]{2,1,0:T(1,128)S(1)} %get-tuple-element.95), channel_id=1, source_target_pairs={{0,16},{16,32},{32,48},{48,64},{64,80},{80,96},{96,112},{112,128},... | collective-permute-start | bytes 7688 | tf_op jit(solution)/shard_map/ppermute | solution.py:32
  286.6 5.5 %collective-permute-start.5 = (f32[5,1,128]{2,1,0:T(1,128)S(1)}, f32[5,1,128]{2,1,0:T(1,128)S(1)}, u32[]{:S(2)}, u32[]{:S(2)}) collective-permute-start(f32[5,1,128]{2,1,0:T(1,128)S(1)} %get-tuple-element.96), channel_id=1, source_target_pairs={{16,0},{32,16},{48,32},{64,48},{80,64},{96,80},{112,96},{128,112},... | collective-permute-start | bytes 7688 | tf_op jit(solution)/shard_map/ppermute | solution.py:33
  292.2 5.3 %collective-permute-start.6 = (f32[5,1,128]{2,1,0:T(1,128)S(1)}, f32[5,1,128]{2,1,0:T(1,128)S(1)}, u32[]{:S(2)}, u32[]{:S(2)}) collective-permute-start(f32[5,1,128]{2,1,0:T(1,128)S(1)} %get-tuple-element.91), channel_id=1, source_target_pairs={{0,16},{16,32},{32,48},{48,64},{64,80},{80,96},{96,112},{112,128},... | collective-permute-start | bytes 7688 | tf_op jit(solution)/shard_map/ppermute | solution.py:32
  296.2 5.5 %collective-permute-start.7 = (f32[5,1,128]{2,1,0:T(1,128)S(1)}, f32[5,1,128]{2,1,0:T(1,128)S(1)}, u32[]{:S(2)}, u32[]{:S(2)}) collective-permute-start(f32[5,1,128]{2,1,0:T(1,128)S(1)} %get-tuple-element.92), channel_id=1, source_target_pairs={{16,0},{32,16},{48,32},{64,48},{80,64},{96,80},{112,96},{128,112},... | collective-permute-start | bytes 7688 | tf_op jit(solution)/shard_map/ppermute | solution.py:33
  301.8 5.3 %collective-permute-start.8 = (f32[5,1,128]{2,1,0:T(1,128)S(1)}, f32[5,1,128]{2,1,0:T(1,128)S(1)}, u32[]{:S(2)}, u32[]{:S(2)}) collective-permute-start(f32[5,1,128]{2,1,0:T(1,128)S(1)} %get-tuple-element.87), channel_id=1, source_target_pairs={{0,16},{16,32},{32,48},{48,64},{64,80},{80,96},{96,112},{112,128},... | collective-permute-start | bytes 7688 | tf_op jit(solution)/shard_map/ppermute | solution.py:32
  305.9 5.5 %collective-permute-start.9 = (f32[5,1,128]{2,1,0:T(1,128)S(1)}, f32[5,1,128]{2,1,0:T(1,128)S(1)}, u32[]{:S(2)}, u32[]{:S(2)}) collective-permute-start(f32[5,1,128]{2,1,0:T(1,128)S(1)} %get-tuple-element.88), channel_id=1, source_target_pairs={{16,0},{32,16},{48,32},{64,48},{80,64},{96,80},{112,96},{128,112},... | collective-permute-start | bytes 7688 | tf_op jit(solution)/shard_map/ppermute | solution.py:33
where the time goes:
time: 532 us; the launch traced here: 528 us
  blocking collectives  238 us (45%)
  waiting for transfers between devices  136 us (26%)
  starting transfers between devices  101 us (19%)
  between operations  16.2 us (3%)
  local copies, waits for them, and re-layouts  15.9 us (3%)
  other arithmetic  14.6 us (3%)
  matrix products  6.31 us (1%)
    psum x2, blocking collectives, body(): lax.psum(newton_sums(loaded, signed, shift_mass, shift_flow), ('sec', 've...  148 us
    ppermute x30, waiting for transfers between devices, passed_along(): return lax.ppermute(block, axis, route)  119 us
    ppermute x30, starting transfers between devices, passed_along(): return lax.ppermute(block, axis, route)  79.8 us
    psum x1, blocking collectives, body(): goals = lax.psum(local_totals, 'sec')  37.6 us
    psum x1, blocking collectives, body(): lax.psum(jnp.dot(weighted, distribution, precision=HIGH), 'vel')  25.9 us
    psum x1, blocking collectives, body(): lax.psum(jnp.dot(weighted, half_field, precision=HIGH), 'vel')  25.8 us
    ppermute x4, waiting for transfers between devices, extended(): after = lax.ppermute(first, axis, down)  16.6 us
    ppermute x4, starting transfers between devices, extended(): before = lax.ppermute(last, axis, up)  16.1 us
  transfers between devices with their start and end apart: 38, of which 34 were waited for; matrix products, arithmetic and copies ran while one was open for 0% of the time, Pallas kernels for 0%

commit v1 on v0

--- a/solution.py
+++ b/solution.py
@@ -123,6 +123,40 @@
     return (new_mass, new_flow)
 
 
+def received(block, distance):
+    count = lax.axis_size("sec")
+    if abs(distance) >= count:
+        return jnp.zeros_like(block)
+    return passed_along(block, "sec", distance)
+
+
+def exclusive_inflow(rate, drive, sign):
+    count = lax.axis_size("sec")
+
+    def fetch(a, b, distance):
+        got = received(jnp.concatenate([a, b], axis=0), sign * distance)
+        return got[:1], got[1:]
+
+    near_a, near_b = fetch(rate, drive, 1)
+    span = 1
+    if count > 2:
+        far_a, far_b = fetch(rate, drive, 2)
+        near_a, near_b = near_a * far_a, near_a * far_b + near_b
+        span = 2
+    while span < count - 1:
+        got_a, got_b = fetch(near_a, near_b, span)
+        near_a, near_b = near_a * got_a, near_a * got_b + near_b
+        span *= 2
+    return near_b
+
+
+def with_halo(array, width):
+    parts = [received(array, d) for d in range(width, 0, -1)]
+    parts.append(array)
+    parts.extend(received(array, -d) for d in range(1, width + 1))
+    return jnp.concatenate(parts, axis=1)
+
+
 def body(distribution, collision, lower_blocks, upper_blocks, diag_inverse):
     node_count = distribution.shape[0]
     cell_count = distribution.shape[1]
@@ -130,20 +164,19 @@
     node_rows = node_count // NXI
     half_nodes = NXI // 2
     along_x, node_weight, weighted_np, rebuild_np = node_tables(NXI)
-    all_signed = jnp.asarray(along_x, jnp.float32)
     all_mass = jnp.asarray(node_weight, jnp.float32)
     offset = lax.axis_index("vel") * node_count
     weighted = lax.dynamic_slice_in_dim(
         jnp.asarray(weighted_np, jnp.float32), offset, node_count, 1
     )
     rebuild = lax.dynamic_slice_in_dim(jnp.asarray(rebuild_np, jnp.float32), offset, node_count, 1)
-    signed = lax.dynamic_slice_in_dim(all_signed, offset, node_count, 0)
     node_mass = lax.dynamic_slice_in_dim(all_mass, offset, node_count, 0)
+    line_signed = jnp.asarray(along_x[:NXI], jnp.float32)
     old_moments = lax.psum(jnp.dot(weighted, distribution, precision=HIGH), "vel")
     target = jnp.dot(rebuild.T, old_moments, precision=HIGH)
     total_length = length * lax.axis_size("sec")
     thickness = collision.reshape(1, 1, length, TUBES)
-    node_speed = jnp.abs(signed).reshape(node_rows, NXI, 1, 1)
+    node_speed = jnp.abs(line_signed).reshape(1, NXI, 1, 1)
     denominator = node_speed * total_length + thickness + pseudo_rate
     carry_rate = node_speed * total_length / denominator
     drive_term = (
@@ -152,53 +185,61 @@
     ) / denominator
     prod_neg, local_neg = lax.associative_scan(
         affine_combine,
-        (carry_rate[:, :half_nodes], drive_term[:, :half_nodes]),
+        (jnp.broadcast_to(carry_rate[:, :half_nodes], (1, half_nodes, length, TUBES)),
+         drive_term[:, :half_nodes]),
         reverse=True,
         axis=2,
     )
     prod_pos, local_pos = lax.associative_scan(
-        affine_combine, (carry_rate[:, half_nodes:], drive_term[:, half_nodes:]), axis=2
-    )
-    summary_pos = (prod_pos[:, :, -1], local_pos[:, :, -1])
-    summary_neg = (prod_neg[:, :, 0], local_neg[:, :, 0])
-
-    def relay(turn_index, inflows):
-        out_pos = summary_pos[0] * inflows[0] + summary_pos[1]
-        out_neg = summary_neg[0] * inflows[1] + summary_neg[1]
-        return (passed_along(out_pos, "sec", 1), passed_along(out_neg, "sec", -1))
-
-    start_flows = (jnp.zeros_like(summary_pos[1]), jnp.zeros_like(summary_neg[1]))
-    inflow_pos, inflow_neg = lax.fori_loop(0, lax.axis_size("sec") - 1, relay, start_flows)
+        affine_combine,
+        (jnp.broadcast_to(carry_rate[:, half_nodes:], (1, NXI - half_nodes, length, TUBES)),
+         drive_term[:, half_nodes:]),
+        axis=2,
+    )
+    inflow_pos = exclusive_inflow(prod_pos[:, :, -1], local_pos[:, :, -1], 1)
+    inflow_neg = exclusive_inflow(prod_neg[:, :, 0], local_neg[:, :, 0], -1)
     field_neg = local_neg + prod_neg * inflow_neg[:, :, None, :]
     field_pos = local_pos + prod_pos * inflow_pos[:, :, None, :]
     half_field = jnp.concatenate([field_neg, field_pos], axis=1).reshape(node_count, cell_count)
     half_moments = lax.psum(jnp.dot(weighted, half_field, precision=HIGH), "vel")
     residual = (half_moments - old_moments).reshape(5, length, TUBES)
-    lower_r = lower_blocks.reshape(25, length, TUBES)
-    upper_r = upper_blocks.reshape(25, length, TUBES)
-    inverse_r = diag_inverse.reshape(25, length, TUBES)
-    correction = apply_block(inverse_r, residual)
+    width = min(-(-JACOBI // length), lax.axis_size("sec") - 1)
+    blocks = jnp.concatenate([lower_blocks, upper_blocks, diag_inverse], axis=0)
+    blocks_wide = with_halo(blocks.reshape(75, length, TUBES), width)
+    lower_r = blocks_wide[:25]
+    upper_r = blocks_wide[25:50]
+    inverse_r = blocks_wide[50:]
+    residual_wide = with_halo(residual, width)
+    correction = apply_block(inverse_r, residual_wide)
+    edge_zero = jnp.zeros((5, 1, TUBES), jnp.float32)
     for sweep_index in range(JACOBI):
-        padded = extended(correction, (("sec", 1),), 1)
+        from_left = jnp.concatenate([edge_zero, correction[:, :-1]], axis=1)
+        from_right = jnp.concatenate([correction[:, 1:], edge_zero], axis=1)
         correction = apply_block(
             inverse_r,
-            residual - apply_block(lower_r, padded[:, :-2]) - apply_block(upper_r, padded[:, 2:]),
+            residual_wide - apply_block(lower_r, from_left) - apply_block(upper_r, from_right),
         )
-    correction = correction.reshape(5, cell_count)
+    correction = correction[:, width * length : (width + 1) * length].reshape(5, cell_count)
     macro = half_moments + correction
     synthetic = half_field + jnp.dot(rebuild.T, correction, precision=HIGH)
     local_totals = jnp.sum(old_moments - macro, axis=1)[0:2]
     magnitude = jnp.sum(jnp.abs(synthetic), axis=1)
+    line_loaded = jnp.sum((node_mass * magnitude).reshape(node_rows, NXI), axis=0)
+    first_copy = (lax.axis_index("vel") == 0).astype(jnp.float32)
+    gathered = lax.psum(
+        jnp.concatenate([line_loaded, local_totals * first_copy]), ("sec", "vel")
+    )
+    loaded = gathered[:NXI]
+    goals = gathered[NXI:]
     shift_mass = jnp.zeros((), jnp.float32)
     shift_flow = jnp.zeros((), jnp.float32)
-    goals = lax.psum(local_totals, "sec")
-    loaded = node_mass * magnitude
     for newton_turn in range(NEWTON):
-        sums = lax.psum(newton_sums(loaded, signed, shift_mass, shift_flow), ("sec", "vel"))
+        sums = newton_sums(loaded, line_signed, shift_mass, shift_flow)
         shift_mass, shift_flow = newton_update(shift_mass, shift_flow, sums, goals[0], goals[1])
-    growth = jnp.exp(shift_mass + shift_flow * signed)
-    new_distribution = synthetic + jnp.abs(synthetic) * (growth[:, None] - 1.0)
-    return (new_distribution, macro)
+    growth = jnp.exp(shift_mass + shift_flow * line_signed)
+    synthetic_rows = synthetic.reshape(node_rows, NXI, cell_count)
+    new_distribution = synthetic_rows + jnp.abs(synthetic_rows) * (growth[None, :, None] - 1.0)
+    return (new_distribution.reshape(node_count, cell_count), macro)
 
 
 def solution(mesh):

time: 532 us -> 255 us (0.48)
  waiting for transfers between devices: 136 us -> 16.4 us
  blocking collectives: 238 us -> 131 us
  starting transfers between devices: 101 us -> 67.3 us
  local copies, waits for them, and re-layouts: 15.9 us -> 7.31 us
  other arithmetic: 14.6 us -> 8.25 us
    psum x3 -> x1, blocking collectives: 186 us -> 81.2 us  [body(): lax.psum(jnp.concatenate([line_loaded, local_totals * first_copy]), ('sec...]
    ppermute x30 -> x18, waiting for transfers between devices: 119 us -> 16.4 us  [passed_along(): return lax.ppermute(block, axis, route)]
    ppermute x8 -> x0, starting transfers between devices: 21.3 us -> none  [the longest x4 16.1 us: extended(): before = lax.ppermute(last, axis, up)]
    ppermute x8 -> x0, waiting for transfers between devices: 16.7 us -> none  [the longest x4 16.6 us: extended(): after = lax.ppermute(first, axis, down)]
    ppermute x30 -> x18, starting transfers between devices: 79.8 us -> 67.3 us  [passed_along(): return lax.ppermute(block, axis, route)]
    another operation x7 -> x0, local copies, waits for them, and re-layouts: 6.52 us -> none  [the longest x2 6.42 us: newton_sums(): jnp.stack([jnp.sum(scaled), jnp.sum(scaled * signed), jnp.sum(scaled * si...]
  transfers between devices with their start and end apart: 38 -> 18, of which waited for: 34 -> 8; matrix products, arithmetic and copies ran while one was open for 0% -> 2% of each run, Pallas kernels for 0% -> 0%
where the time goes in v1:
time: 255 us; the launch traced here: 253 us
  blocking collectives  131 us (51%)
  starting transfers between devices  67.3 us (26%)
  between operations  16.8 us (7%)
  waiting for transfers between devices  16.4 us (6%)
  other arithmetic  8.25 us (3%)
  local copies, waits for them, and re-layouts  7.31 us (3%)
  matrix products  6.31 us (2%)
    psum x1, blocking collectives, body(): lax.psum(jnp.concatenate([line_loaded, local_totals * first_copy]), ('sec...  81.2 us
    ppermute x18, starting transfers between devices, passed_along(): return lax.ppermute(block, axis, route)  67.3 us
    psum x1, blocking collectives, body(): lax.psum(jnp.dot(weighted, distribution, precision=HIGH), 'vel')  25.9 us
    psum x1, blocking collectives, body(): lax.psum(jnp.dot(weighted, half_field, precision=HIGH), 'vel')  24.1 us
    ppermute x18, waiting for transfers between devices, passed_along(): return lax.ppermute(block, axis, route)  16.4 us
  transfers between devices with their start and end apart: 18, of which 8 were waited for; matrix products, arithmetic and copies ran while one was open for 2% of the time, Pallas kernels for 0%

profile of v1, /device:TPU:32, one launch (start us, length us, event | category | flops | bytes accessed | tf_op | source)
XLA Modules:
  0.0 253.5 jit_solution(769121284347335400)
XLA Ops:
  0.7 0.7 copy-done.4
  1.5 1.7 reshape.255
  3.2 1.3 fusion.13
  4.5 25.9 %psum.21 = f32[5,256]{1,0:T(8,128)S(1)} all-reduce(f32[5,256]{1,0:T(8,128)S(1)} %fusion.13), channel_id=1, replica_groups=mesh['sec'=16,'vel'=16] {'vel'}, use_global_device_ids=true, to_apply=%region_0.0 | all-reduce | flops 1280 | bytes 10240 | tf_op jit(solution)/shard_map/psum | solution.py:175
  30.4 1.8 fusion.16
  32.3 0.5 reshape.254
  32.9 0.7 fusion.29
  33.6 0.4 fusion.10
  34.1 1.3 collective-permute-start
  35.4 1.3 collective-permute-start.1
  36.8 6.8 %collective-permute-start.10 = (f32[75,2,128]{2,1,0:T(2,128)S(1)}, f32[75,2,128]{2,1,0:T(2,128)S(1)}, u32[]{:S(2)}, u32[]{:S(2)}) collective-permute-start(f32[75,2,128]{2,1,0:T(2,128)S(1)} %reshape.257), channel_id=1, source_target_pairs={{0,32},{16,48},{32,64},{48,80},{64,96},{80,112},{96,128},{112,144}... | collective-permute-start | bytes 230408 | tf_op jit(solution)/shard_map/ppermute | solution.py:22
  43.6 3.8 %collective-permute-start.11 = (f32[75,2,128]{2,1,0:T(2,128)S(1)}, f32[75,2,128]{2,1,0:T(2,128)S(1)}, u32[]{:S(2)}, u32[]{:S(2)}) collective-permute-start(f32[75,2,128]{2,1,0:T(2,128)S(1)} %reshape.257), channel_id=1, source_target_pairs={{0,16},{16,32},{32,48},{48,64},{64,80},{80,96},{96,112},{112,128},... | collective-permute-start | bytes 230408 | tf_op jit(solution)/shard_map/ppermute | solution.py:22
  47.4 1.3 collective-permute-start.12
  49.1 1.1 rev.8
  50.2 0.4 fusion.11
  50.7 1.3 collective-permute-start.13
  52.0 5.0 %collective-permute-start.5 = (f32[37,12,128]{2,0,1:T(8,128)S(1)}, f32[37,12,128]{2,0,1:T(8,128)S(1)}, u32[]{:S(2)}, u32[]{:S(2)}) collective-permute-start(f32[37,12,128]{2,0,1:T(8,128)S(1)} %pad_maximum_fusion.5), channel_id=1, source_target_pairs={{0,16},{16,32},{32,48},{48,64},{64,80},{80,96},{96,112},{112,128},... | collective-permute-start | bytes 681992 | tf_op jit(solution)/shard_map/ppermute | solution.py:22
  57.1 6.7 %collective-permute-start.6 = (f32[37,12,128]{2,0,1:T(8,128)S(1)}, f32[37,12,128]{2,0,1:T(8,128)S(1)}, u32[]{:S(2)}, u32[]{:S(2)}) collective-permute-start(f32[37,12,128]{2,0,1:T(8,128)S(1)} %pad_maximum_fusion.5), channel_id=1, source_target_pairs={{0,32},{16,48},{32,64},{48,80},{64,96},{80,112},{96,128},{112,144}... | collective-permute-start | bytes 681992 | tf_op jit(solution)/shard_map/ppermute | solution.py:22
  63.8 2.1 concatenate.91
  66.0 1.3 collective-permute-start.2
  67.6 6.5 %collective-permute-start.7 = (f32[37,12,128]{2,0,1:T(8,128)S(1)}, f32[37,12,128]{2,0,1:T(8,128)S(1)}, u32[]{:S(2)}, u32[]{:S(2)}) collective-permute-start(f32[37,12,128]{2,0,1:T(8,128)S(1)} %pad_maximum_fusion.6), channel_id=1, source_target_pairs={{0,32},{16,48},{32,64},{48,80},{64,96},{80,112},{96,128},{112,144}... | collective-permute-start | bytes 681992 | tf_op jit(solution)/shard_map/ppermute | solution.py:22
  74.1 1.8 collective-permute-done.2
  76.0 1.3 collective-permute-start.3
  77.3 2.0 collective-permute-done.7
  79.4 12.0 %collective-permute-start.8 = (f32[37,12,128]{2,0,1:T(8,128)S(1)}, f32[37,12,128]{2,0,1:T(8,128)S(1)}, u32[]{:S(2)}, u32[]{:S(2)}) collective-permute-start(f32[37,12,128]{2,0,1:T(8,128)S(1)} %pad_maximum_fusion.7), channel_id=1, source_target_pairs={{0,64},{16,80},{32,96},{48,112},{64,128},{80,144},{96,160},{112,17... | collective-permute-start | bytes 681992 | tf_op jit(solution)/shard_map/ppermute | solution.py:22
  91.4 0.4 collective-permute-done.3
  92.0 1.3 collective-permute-start.4
  93.3 2.4 collective-permute-done.8
  95.8 10.6 %collective-permute-start.9 = (f32[37,12,128]{2,0,1:T(8,128)S(1)}, f32[37,12,128]{2,0,1:T(8,128)S(1)}, u32[]{:S(2)}, u32[]{:S(2)}) collective-permute-start(f32[37,12,128]{2,0,1:T(8,128)S(1)} %pad_maximum_fusion.8), channel_id=1, source_target_pairs={{0,128},{16,144},{32,160},{48,176},{64,192},{80,208},{96,224},{112... | collective-permute-start | bytes 681992 | tf_op jit(solution)/shard_map/ppermute | solution.py:22
  106.5 3.6 %collective-permute-done.9 = f32[37,12,128]{2,0,1:T(8,128)S(1)} collective-permute-done((f32[37,12,128]{2,0,1:T(8,128)S(1)}, f32[37,12,128]{2,0,1:T(8,128)S(1)}, u32[]{:S(2)}, u32[]{:S(2)}) %collective-permute-start.9) | collective-permute-done | bytes 227360 | tf_op jit(solution)/shard_map/ppermute | solution.py:22
  110.1 0.5 fusion.3
  110.8 0.4 pad_maximum_fusion
  111.2 1.3 fusion
  112.5 24.1 %psum.22 = f32[5,256]{1,0:T(8,128)S(1)} all-reduce(f32[5,256]{1,0:T(8,128)S(1)} %fusion), channel_id=1, replica_groups=mesh['sec'=16,'vel'=16] {'vel'}, use_global_device_ids=true, to_apply=%region_1.0 | all-reduce | flops 1280 | bytes 10240 | tf_op jit(solution)/shard_map/psum | solution.py:204
  136.6 3.0 %collective-permute-start.14 = (f32[5,2,128]{2,1,0:T(2,128)S(1)}, f32[5,2,128]{2,1,0:T(2,128)S(1)}, u32[]{:S(2)}, u32[]{:S(2)}) collective-permute-start(f32[5,2,128]{2,1,0:T(2,128)S(1)} %reshape.259), channel_id=1, source_target_pairs={{0,32},{16,48},{32,64},{48,80},{64,96},{80,112},{96,128},{112,144}... | collective-permute-start | bytes 15368 | tf_op jit(solution)/shard_map/ppermute | solution.py:22
  139.6 1.3 collective-permute-start.15
  140.9 1.3 collective-permute-start.16
  142.2 1.3 collective-permute-start.17
  143.6 2.8 %collective-permute-done.16 = f32[5,2,128]{2,1,0:T(2,128)S(1)} collective-permute-done((f32[5,2,128]{2,1,0:T(2,128)S(1)}, f32[5,2,128]{2,1,0:T(2,128)S(1)}, u32[]{:S(2)}, u32[]{:S(2)}) %collective-permute-start.16) | collective-permute-done | bytes 5152 | tf_op jit(solution)/shard_map/ppermute | solution.py:22
  146.4 3.2 %collective-permute-done.17 = f32[5,2,128]{2,1,0:T(2,128)S(1)} collective-permute-done((f32[5,2,128]{2,1,0:T(2,128)S(1)}, f32[5,2,128]{2,1,0:T(2,128)S(1)}, u32[]{:S(2)}, u32[]{:S(2)}) %collective-permute-start.17) | collective-permute-done | bytes 5152 | tf_op jit(solution)/shard_map/ppermute | solution.py:22
  150.3 1.9 abs_reduce_fusion
  152.2 0.7 subtract_reduce_fusion
  153.0 0.8 dynamic-slice_multiply_fusion
  153.9 81.2 %psum.23 = f32[26]{0:T(128)S(1)} all-reduce(f32[26]{0:T(128)S(1)} %pad_maximum_fusion.10), channel_id=1, replica_groups=mesh['sec'=16,'vel'=16] {'sec','vel'}, use_global_device_ids=true, to_apply=%region_18.0 | all-reduce | flops 26 | bytes 208 | tf_op jit(solution)/shard_map/psum | solution.py:229
  235.1 0.7 fusion.36
  235.8 0.7 multiply_reduce_fusion.14
  244.0 0.7 multiply_reduce_fusion.13
  252.4 1.1 multiply_add_fusion
  (116 shorter events, 2.9 us)
Async XLA Ops:
  0.6 0.7 copy-start.4
  0.6 0.7 copy-start.6
  1.5 1.7 copy-start
  34.0 2.7 %copy-start.1 = (f32[25,256]{1,0:T(8,128)S(1)}, f32[25,256]{1,0:T(8,128)}, u32[]{:S(2)}) copy-start(f32[25,256]{1,0:T(8,128)} %param.13) | copy-start | bytes 76804
  34.0 2.7 %copy-start.2 = (f32[25,256]{1,0:T(8,128)S(1)}, f32[25,256]{1,0:T(8,128)}, u32[]{:S(2)}) copy-start(f32[25,256]{1,0:T(8,128)} %param.12) | copy-start | bytes 76804
  34.0 2.7 %copy-start.3 = (f32[25,256]{1,0:T(8,128)S(1)}, f32[25,256]{1,0:T(8,128)}, u32[]{:S(2)}) copy-start(f32[25,256]{1,0:T(8,128)} %param.11) | copy-start | bytes 76804
  34.1 31.8 %collective-permute-start = (f32[37,12,128]{2,0,1:T(8,128)S(1)}, f32[37,12,128]{2,0,1:T(8,128)S(1)}, u32[]{:S(2)}, u32[]{:S(2)}) collective-permute-start(f32[37,12,128]{2,0,1:T(8,128)S(1)} %pad_maximum_fusion.1), channel_id=1, source_target_pairs={{16,0},{32,16},{48,32},{64,48},{80,64},{96,80},{112,96},{128,112},... | collective-permute-start | bytes 681992 | tf_op jit(solution)/shard_map/ppermute | solution.py:22
  35.4 30.5 %collective-permute-start.1 = (f32[37,12,128]{2,0,1:T(8,128)S(1)}, f32[37,12,128]{2,0,1:T(8,128)S(1)}, u32[]{:S(2)}, u32[]{:S(2)}) collective-permute-start(f32[37,12,128]{2,0,1:T(8,128)S(1)} %pad_maximum_fusion.1), channel_id=1, source_target_pairs={{32,0},{48,16},{64,32},{80,48},{96,64},{112,80},{128,96},{144,112}... | collective-permute-start | bytes 681992 | tf_op jit(solution)/shard_map/ppermute | solution.py:22
  36.8 13.9 %collective-permute-start.10 = (f32[75,2,128]{2,1,0:T(2,128)S(1)}, f32[75,2,128]{2,1,0:T(2,128)S(1)}, u32[]{:S(2)}, u32[]{:S(2)}) collective-permute-start(f32[75,2,128]{2,1,0:T(2,128)S(1)} %reshape.257), channel_id=1, source_target_pairs={{0,32},{16,48},{32,64},{48,80},{64,96},{80,112},{96,128},{112,144}... | collective-permute-start | bytes 230408 | tf_op jit(solution)/shard_map/ppermute | solution.py:22
  43.6 8.4 %collective-permute-start.11 = (f32[75,2,128]{2,1,0:T(2,128)S(1)}, f32[75,2,128]{2,1,0:T(2,128)S(1)}, u32[]{:S(2)}, u32[]{:S(2)}) collective-permute-start(f32[75,2,128]{2,1,0:T(2,128)S(1)} %reshape.257), channel_id=1, source_target_pairs={{0,16},{16,32},{32,48},{48,64},{64,80},{80,96},{96,112},{112,128},... | collective-permute-start | bytes 230408 | tf_op jit(solution)/shard_map/ppermute | solution.py:22
  47.4 9.7 %collective-permute-start.12 = (f32[75,2,128]{2,1,0:T(2,128)S(1)}, f32[75,2,128]{2,1,0:T(2,128)S(1)}, u32[]{:S(2)}, u32[]{:S(2)}) collective-permute-start(f32[75,2,128]{2,1,0:T(2,128)S(1)} %reshape.257), channel_id=1, source_target_pairs={{16,0},{32,16},{48,32},{64,48},{80,64},{96,80},{112,96},{128,112},... | collective-permute-start | bytes 230408 | tf_op jit(solution)/shard_map/ppermute | solution.py:22
  50.7 13.0 %collective-permute-start.13 = (f32[75,2,128]{2,1,0:T(2,128)S(1)}, f32[75,2,128]{2,1,0:T(2,128)S(1)}, u32[]{:S(2)}, u32[]{:S(2)}) collective-permute-start(f32[75,2,128]{2,1,0:T(2,128)S(1)} %reshape.257), channel_id=1, source_target_pairs={{32,0},{48,16},{64,32},{80,48},{96,64},{112,80},{128,96},{144,112}... | collective-permute-start | bytes 230408 | tf_op jit(solution)/shard_map/ppermute | solution.py:22
  52.0 15.3 %collective-permute-start.5 = (f32[37,12,128]{2,0,1:T(8,128)S(1)}, f32[37,12,128]{2,0,1:T(8,128)S(1)}, u32[]{:S(2)}, u32[]{:S(2)}) collective-permute-start(f32[37,12,128]{2,0,1:T(8,128)S(1)} %pad_maximum_fusion.5), channel_id=1, source_target_pairs={{0,16},{16,32},{32,48},{48,64},{64,80},{80,96},{96,112},{112,128},... | collective-permute-start | bytes 681992 | tf_op jit(solution)/shard_map/ppermute | solution.py:22
  57.1 10.4 %collective-permute-start.6 = (f32[37,12,128]{2,0,1:T(8,128)S(1)}, f32[37,12,128]{2,0,1:T(8,128)S(1)}, u32[]{:S(2)}, u32[]{:S(2)}) collective-permute-start(f32[37,12,128]{2,0,1:T(8,128)S(1)} %pad_maximum_fusion.5), channel_id=1, source_target_pairs={{0,32},{16,48},{32,64},{48,80},{64,96},{80,112},{96,128},{112,144}... | collective-permute-start | bytes 681992 | tf_op jit(solution)/shard_map/ppermute | solution.py:22
  66.0 9.9 %collective-permute-start.2 = (f32[37,12,128]{2,0,1:T(8,128)S(1)}, f32[37,12,128]{2,0,1:T(8,128)S(1)}, u32[]{:S(2)}, u32[]{:S(2)}) collective-permute-start(f32[37,12,128]{2,0,1:T(8,128)S(1)} %pad_maximum_fusion.2), channel_id=1, source_target_pairs={{32,0},{48,16},{64,32},{80,48},{96,64},{112,80},{128,96},{144,112}... | collective-permute-start | bytes 681992 | tf_op jit(solution)/shard_map/ppermute | solution.py:22
  67.6 11.6 %collective-permute-start.7 = (f32[37,12,128]{2,0,1:T(8,128)S(1)}, f32[37,12,128]{2,0,1:T(8,128)S(1)}, u32[]{:S(2)}, u32[]{:S(2)}) collective-permute-start(f32[37,12,128]{2,0,1:T(8,128)S(1)} %pad_maximum_fusion.6), channel_id=1, source_target_pairs={{0,32},{16,48},{32,64},{48,80},{64,96},{80,112},{96,128},{112,144}... | collective-permute-start | bytes 681992 | tf_op jit(solution)/shard_map/ppermute | solution.py:22
  76.0 15.9 %collective-permute-start.3 = (f32[37,12,128]{2,0,1:T(8,128)S(1)}, f32[37,12,128]{2,0,1:T(8,128)S(1)}, u32[]{:S(2)}, u32[]{:S(2)}) collective-permute-start(f32[37,12,128]{2,0,1:T(8,128)S(1)} %pad_maximum_fusion.3), channel_id=1, source_target_pairs={{64,0},{80,16},{96,32},{112,48},{128,64},{144,80},{160,96},{176,11... | collective-permute-start | bytes 681992 | tf_op jit(solution)/shard_map/ppermute | solution.py:22
  79.4 16.3 %collective-permute-start.8 = (f32[37,12,128]{2,0,1:T(8,128)S(1)}, f32[37,12,128]{2,0,1:T(8,128)S(1)}, u32[]{:S(2)}, u32[]{:S(2)}) collective-permute-start(f32[37,12,128]{2,0,1:T(8,128)S(1)} %pad_maximum_fusion.7), channel_id=1, source_target_pairs={{0,64},{16,80},{32,96},{48,112},{64,128},{80,144},{96,160},{112,17... | collective-permute-start | bytes 681992 | tf_op jit(solution)/shard_map/ppermute | solution.py:22
  92.0 14.4 %collective-permute-start.4 = (f32[37,12,128]{2,0,1:T(8,128)S(1)}, f32[37,12,128]{2,0,1:T(8,128)S(1)}, u32[]{:S(2)}, u32[]{:S(2)}) collective-permute-start(f32[37,12,128]{2,0,1:T(8,128)S(1)} %pad_maximum_fusion.4), channel_id=1, source_target_pairs={{128,0},{144,16},{160,32},{176,48},{192,64},{208,80},{224,96},{240... | collective-permute-start | bytes 681992 | tf_op jit(solution)/shard_map/ppermute | solution.py:22
  95.8 14.3 %collective-permute-start.9 = (f32[37,12,128]{2,0,1:T(8,128)S(1)}, f32[37,12,128]{2,0,1:T(8,128)S(1)}, u32[]{:S(2)}, u32[]{:S(2)}) collective-permute-start(f32[37,12,128]{2,0,1:T(8,128)S(1)} %pad_maximum_fusion.8), channel_id=1, source_target_pairs={{0,128},{16,144},{32,160},{48,176},{64,192},{80,208},{96,224},{112... | collective-permute-start | bytes 681992 | tf_op jit(solution)/shard_map/ppermute | solution.py:22
  136.6 7.0 %collective-permute-start.14 = (f32[5,2,128]{2,1,0:T(2,128)S(1)}, f32[5,2,128]{2,1,0:T(2,128)S(1)}, u32[]{:S(2)}, u32[]{:S(2)}) collective-permute-start(f32[5,2,128]{2,1,0:T(2,128)S(1)} %reshape.259), channel_id=1, source_target_pairs={{0,32},{16,48},{32,64},{48,80},{64,96},{80,112},{96,128},{112,144}... | collective-permute-start | bytes 15368 | tf_op jit(solution)/shard_map/ppermute | solution.py:22
  139.6 4.0 %collective-permute-start.15 = (f32[5,2,128]{2,1,0:T(2,128)S(1)}, f32[5,2,128]{2,1,0:T(2,128)S(1)}, u32[]{:S(2)}, u32[]{:S(2)}) collective-permute-start(f32[5,2,128]{2,1,0:T(2,128)S(1)} %reshape.259), channel_id=1, source_target_pairs={{0,16},{16,32},{32,48},{48,64},{64,80},{80,96},{96,112},{112,128},... | collective-permute-start | bytes 15368 | tf_op jit(solution)/shard_map/ppermute | solution.py:22
  140.9 5.5 %collective-permute-start.16 = (f32[5,2,128]{2,1,0:T(2,128)S(1)}, f32[5,2,128]{2,1,0:T(2,128)S(1)}, u32[]{:S(2)}, u32[]{:S(2)}) collective-permute-start(f32[5,2,128]{2,1,0:T(2,128)S(1)} %reshape.259), channel_id=1, source_target_pairs={{16,0},{32,16},{48,32},{64,48},{80,64},{96,80},{112,96},{128,112},... | collective-permute-start | bytes 15368 | tf_op jit(solution)/shard_map/ppermute | solution.py:22
  142.2 7.4 %collective-permute-start.17 = (f32[5,2,128]{2,1,0:T(2,128)S(1)}, f32[5,2,128]{2,1,0:T(2,128)S(1)}, u32[]{:S(2)}, u32[]{:S(2)}) collective-permute-start(f32[5,2,128]{2,1,0:T(2,128)S(1)} %reshape.259), channel_id=1, source_target_pairs={{32,0},{48,16},{64,32},{80,48},{96,64},{112,80},{128,96},{144,112}... | collective-permute-start | bytes 15368 | tf_op jit(solution)/shard_map/ppermute | solution.py:22
  235.1 0.7 copy-start.5
  235.1 0.7 copy-start.7

commit v2 on v1

--- a/solution.py
+++ b/solution.py
@@ -157,6 +157,19 @@
     return jnp.concatenate(parts, axis=1)
 
 
+def tree_sum(block, axes):
+    for axis in axes:
+        count = lax.axis_size(axis)
+        if count & (count - 1):
+            block = lax.psum(block, axis)
+            continue
+        bit = 1
+        while bit < count:
+            block = block + lax.ppermute(block, axis, [(i, i ^ bit) for i in range(count)])
+            bit *= 2
+    return block
+
+
 def body(distribution, collision, lower_blocks, upper_blocks, diag_inverse):
     node_count = distribution.shape[0]
     cell_count = distribution.shape[1]
@@ -172,7 +185,7 @@
     rebuild = lax.dynamic_slice_in_dim(jnp.asarray(rebuild_np, jnp.float32), offset, node_count, 1)
     node_mass = lax.dynamic_slice_in_dim(all_mass, offset, node_count, 0)
     line_signed = jnp.asarray(along_x[:NXI], jnp.float32)
-    old_moments = lax.psum(jnp.dot(weighted, distribution, precision=HIGH), "vel")
+    old_moments = tree_sum(jnp.dot(weighted, distribution, precision=HIGH), ("vel",))
     target = jnp.dot(rebuild.T, old_moments, precision=HIGH)
     total_length = length * lax.axis_size("sec")
     thickness = collision.reshape(1, 1, length, TUBES)
@@ -201,7 +214,7 @@
     field_neg = local_neg + prod_neg * inflow_neg[:, :, None, :]
     field_pos = local_pos + prod_pos * inflow_pos[:, :, None, :]
     half_field = jnp.concatenate([field_neg, field_pos], axis=1).reshape(node_count, cell_count)
-    half_moments = lax.psum(jnp.dot(weighted, half_field, precision=HIGH), "vel")
+    half_moments = tree_sum(jnp.dot(weighted, half_field, precision=HIGH), ("vel",))
     residual = (half_moments - old_moments).reshape(5, length, TUBES)
     width = min(-(-JACOBI // length), lax.axis_size("sec") - 1)
     blocks = jnp.concatenate([lower_blocks, upper_blocks, diag_inverse], axis=0)
@@ -226,8 +239,8 @@
     magnitude = jnp.sum(jnp.abs(synthetic), axis=1)
     line_loaded = jnp.sum((node_mass * magnitude).reshape(node_rows, NXI), axis=0)
     first_copy = (lax.axis_index("vel") == 0).astype(jnp.float32)
-    gathered = lax.psum(
-        jnp.concatenate([line_loaded, local_totals * first_copy]), ("sec", "vel")
+    gathered = tree_sum(
+        jnp.concatenate([line_loaded, local_totals * first_copy]), ("vel", "sec")
     )
     loaded = gathered[:NXI]
     goals = gathered[NXI:]

time: 255 us -> 220 us (0.86)
  blocking collectives: 131 us -> 0 us
  waiting for transfers between devices: 16.4 us -> 91.1 us
  starting transfers between devices: 67.3 us -> 87.6 us
    psum x3 -> x0, blocking collectives: 131 us -> none  [the longest x1 81.2 us: body(): lax.psum(jnp.concatenate([line_loaded, local_totals * first_copy]), ('sec...]
    ppermute x18, waiting for transfers between devices: 16.4 us -> 64.4 us  [passed_along(): return lax.ppermute(block, axis, route)]
    ppermute x0 -> x16, starting transfers between devices: none -> 40.4 us  [tree_sum(): lax.ppermute(block, axis, [(i, i ^ bit) for i in range(count)])]
    ppermute x0 -> x16, waiting for transfers between devices: none -> 26.7 us  [tree_sum(): lax.ppermute(block, axis, [(i, i ^ bit) for i in range(count)])]
    ppermute x18, starting transfers between devices: 67.3 us -> 47.1 us  [passed_along(): return lax.ppermute(block, axis, route)]
  transfers between devices with their start and end apart: 18 -> 34, of which waited for: 8 -> 25; matrix products, arithmetic and copies ran while one was open for 2% -> 6% of each run, Pallas kernels for 0% -> 0%
where the time goes in v2:
time: 220 us; the launch traced here: 217 us
  waiting for transfers between devices  91.1 us (41%)
  starting transfers between devices  87.6 us (40%)
  between operations  16.7 us (8%)
  other arithmetic  9.26 us (4%)
  matrix products  6.73 us (3%)
  local copies, waits for them, and re-layouts  5.99 us (3%)
    ppermute x18, waiting for transfers between devices, passed_along(): return lax.ppermute(block, axis, route)  64.4 us
    ppermute x18, starting transfers between devices, passed_along(): return lax.ppermute(block, axis, route)  47.1 us
    ppermute x16, starting transfers between devices, tree_sum(): lax.ppermute(block, axis, [(i, i ^ bit) for i in range(count)])  40.4 us
    ppermute x16, waiting for transfers between devices, tree_sum(): lax.ppermute(block, axis, [(i, i ^ bit) for i in range(count)])  26.7 us
  transfers between devices with their start and end apart: 34, of which 25 were waited for; matrix products, arithmetic and copies ran while one was open for 6% of the time, Pallas kernels for 0%

profile of v2, /device:TPU:32, one launch (start us, length us, event | category | flops | bytes accessed | tf_op | source)
XLA Modules:
  0.0 217.3 jit_solution(16637700108931783879)
XLA Ops:
  1.6 5.1 %collective-permute-start.14 = (f32[75,2,128]{2,1,0:T(2,128)S(1)}, f32[75,2,128]{2,1,0:T(2,128)S(1)}, u32[]{:S(2)}, u32[]{:S(2)}) collective-permute-start(f32[75,2,128]{2,1,0:T(2,128)S(1)} %reshape.257), channel_id=1, source_target_pairs={{0,32},{16,48},{32,64},{48,80},{64,96},{80,112},{96,128},{112,144}... | collective-permute-start | bytes 230408 | tf_op jit(solution)/shard_map/ppermute | solution.py:22
  6.7 2.6 %collective-permute-start.15 = (f32[75,2,128]{2,1,0:T(2,128)S(1)}, f32[75,2,128]{2,1,0:T(2,128)S(1)}, u32[]{:S(2)}, u32[]{:S(2)}) collective-permute-start(f32[75,2,128]{2,1,0:T(2,128)S(1)} %reshape.257), channel_id=1, source_target_pairs={{0,16},{16,32},{32,48},{48,64},{64,80},{80,96},{96,112},{112,128},... | collective-permute-start | bytes 230408 | tf_op jit(solution)/shard_map/ppermute | solution.py:22
  9.3 1.3 collective-permute-start.16
  10.6 1.7 fusion.13
  13.7 3.5 %collective-permute-done.1 = f32[5,256]{1,0:T(8,128)S(1)} collective-permute-done((f32[5,256]{1,0:T(8,128)S(1)}, f32[5,256]{1,0:T(8,128)S(1)}, u32[]{:S(2)}, u32[]{:S(2)}) %collective-permute-start.1) | collective-permute-done | bytes 5152 | tf_op jit(solution)/shard_map/ppermute | solution.py:168
  17.2 3.3 %collective-permute-start.2 = (f32[5,256]{1,0:T(8,128)S(1)}, f32[5,256]{1,0:T(8,128)S(1)}, u32[]{:S(2)}, u32[]{:S(2)}) collective-permute-start(f32[5,256]{1,0:T(8,128)S(1)} %add.215), channel_id=1, source_target_pairs={{0,4},{1,5},{2,6},{3,7},{4,0},{5,1},{6,2},{7,3},{8,12},{9,13},{10,... | collective-permute-start | bytes 15368 | tf_op jit(solution)/shard_map/ppermute | solution.py:168
  20.5 1.6 collective-permute-done.2
  22.1 5.9 %collective-permute-start.3 = (f32[5,256]{1,0:T(8,128)S(1)}, f32[5,256]{1,0:T(8,128)S(1)}, u32[]{:S(2)}, u32[]{:S(2)}) collective-permute-start(f32[5,256]{1,0:T(8,128)S(1)} %add.216), channel_id=1, source_target_pairs={{0,8},{1,9},{2,10},{3,11},{4,12},{5,13},{6,14},{7,15},{8,0},{9,1},... | collective-permute-start | bytes 15368 | tf_op jit(solution)/shard_map/ppermute | solution.py:168
  29.7 1.8 fusion.16
  33.2 1.3 collective-permute-start.4
  34.5 1.3 collective-permute-start.5
  37.8 6.2 %collective-permute-done.4 = f32[37,12,128]{2,0,1:T(8,128)S(1)} collective-permute-done((f32[37,12,128]{2,0,1:T(8,128)S(1)}, f32[37,12,128]{2,0,1:T(8,128)S(1)}, u32[]{:S(2)}, u32[]{:S(2)}) %collective-permute-start.4) | collective-permute-done | bytes 227360 | tf_op jit(solution)/shard_map/ppermute | solution.py:22
  44.0 4.7 %collective-permute-start.10 = (f32[37,12,128]{2,0,1:T(8,128)S(1)}, f32[37,12,128]{2,0,1:T(8,128)S(1)}, u32[]{:S(2)}, u32[]{:S(2)}) collective-permute-start(f32[37,12,128]{2,0,1:T(8,128)S(1)} %pad_maximum_fusion.5), channel_id=1, source_target_pairs={{0,32},{16,48},{32,64},{48,80},{64,96},{80,112},{96,128},{112,144}... | collective-permute-start | bytes 681992 | tf_op jit(solution)/shard_map/ppermute | solution.py:22
  48.7 6.7 %collective-permute-start.9 = (f32[37,12,128]{2,0,1:T(8,128)S(1)}, f32[37,12,128]{2,0,1:T(8,128)S(1)}, u32[]{:S(2)}, u32[]{:S(2)}) collective-permute-start(f32[37,12,128]{2,0,1:T(8,128)S(1)} %pad_maximum_fusion.5), channel_id=1, source_target_pairs={{0,16},{16,32},{32,48},{48,64},{64,80},{80,96},{96,112},{112,128},... | collective-permute-start | bytes 681992 | tf_op jit(solution)/shard_map/ppermute | solution.py:22
  55.5 1.3 collective-permute-start.17
  56.8 2.5 %collective-permute-done.9 = f32[37,12,128]{2,0,1:T(8,128)S(1)} collective-permute-done((f32[37,12,128]{2,0,1:T(8,128)S(1)}, f32[37,12,128]{2,0,1:T(8,128)S(1)}, u32[]{:S(2)}, u32[]{:S(2)}) %collective-permute-start.9) | collective-permute-done | bytes 227360 | tf_op jit(solution)/shard_map/ppermute | solution.py:22
  60.7 13.2 %collective-permute-done.6 = f32[37,12,128]{2,0,1:T(8,128)S(1)} collective-permute-done((f32[37,12,128]{2,0,1:T(8,128)S(1)}, f32[37,12,128]{2,0,1:T(8,128)S(1)}, u32[]{:S(2)}, u32[]{:S(2)}) %collective-permute-start.6) | collective-permute-done | bytes 227360 | tf_op jit(solution)/shard_map/ppermute | solution.py:22
  74.0 6.4 %collective-permute-start.11 = (f32[37,12,128]{2,0,1:T(8,128)S(1)}, f32[37,12,128]{2,0,1:T(8,128)S(1)}, u32[]{:S(2)}, u32[]{:S(2)}) collective-permute-start(f32[37,12,128]{2,0,1:T(8,128)S(1)} %pad_maximum_fusion.6), channel_id=1, source_target_pairs={{0,32},{16,48},{32,64},{48,80},{64,96},{80,112},{96,128},{112,144}... | collective-permute-start | bytes 681992 | tf_op jit(solution)/shard_map/ppermute | solution.py:22
  80.5 3.6 %collective-permute-done.11 = f32[37,12,128]{2,0,1:T(8,128)S(1)} collective-permute-done((f32[37,12,128]{2,0,1:T(8,128)S(1)}, f32[37,12,128]{2,0,1:T(8,128)S(1)}, u32[]{:S(2)}, u32[]{:S(2)}) %collective-permute-start.11) | collective-permute-done | bytes 227360 | tf_op jit(solution)/shard_map/ppermute | solution.py:22
  85.5 12.1 %collective-permute-done.7 = f32[37,12,128]{2,0,1:T(8,128)S(1)} collective-permute-done((f32[37,12,128]{2,0,1:T(8,128)S(1)}, f32[37,12,128]{2,0,1:T(8,128)S(1)}, u32[]{:S(2)}, u32[]{:S(2)}) %collective-permute-start.7) | collective-permute-done | bytes 227360 | tf_op jit(solution)/shard_map/ppermute | solution.py:22
  97.5 6.1 %collective-permute-start.12 = (f32[37,12,128]{2,0,1:T(8,128)S(1)}, f32[37,12,128]{2,0,1:T(8,128)S(1)}, u32[]{:S(2)}, u32[]{:S(2)}) collective-permute-start(f32[37,12,128]{2,0,1:T(8,128)S(1)} %pad_maximum_fusion.7), channel_id=1, source_target_pairs={{0,64},{16,80},{32,96},{48,112},{64,128},{80,144},{96,160},{112,17... | collective-permute-start | bytes 681992 | tf_op jit(solution)/shard_map/ppermute | solution.py:22
  103.7 3.6 %collective-permute-done.12 = f32[37,12,128]{2,0,1:T(8,128)S(1)} collective-permute-done((f32[37,12,128]{2,0,1:T(8,128)S(1)}, f32[37,12,128]{2,0,1:T(8,128)S(1)}, u32[]{:S(2)}, u32[]{:S(2)}) %collective-permute-start.12) | collective-permute-done | bytes 227360 | tf_op jit(solution)/shard_map/ppermute | solution.py:22
  108.7 8.2 %collective-permute-done.8 = f32[37,12,128]{2,0,1:T(8,128)S(1)} collective-permute-done((f32[37,12,128]{2,0,1:T(8,128)S(1)}, f32[37,12,128]{2,0,1:T(8,128)S(1)}, u32[]{:S(2)}, u32[]{:S(2)}) %collective-permute-start.8) | collective-permute-done | bytes 227360 | tf_op jit(solution)/shard_map/ppermute | solution.py:22
  116.9 1.5 collective-permute-start.13
  118.5 3.6 %collective-permute-done.13 = f32[37,12,128]{2,0,1:T(8,128)S(1)} collective-permute-done((f32[37,12,128]{2,0,1:T(8,128)S(1)}, f32[37,12,128]{2,0,1:T(8,128)S(1)}, u32[]{:S(2)}, u32[]{:S(2)}) %collective-permute-start.13) | collective-permute-done | bytes 227360 | tf_op jit(solution)/shard_map/ppermute | solution.py:22
  126.7 2.6 %collective-permute-done.19 = f32[5,256]{1,0:T(8,128)S(1)} collective-permute-done((f32[5,256]{1,0:T(8,128)S(1)}, f32[5,256]{1,0:T(8,128)S(1)}, u32[]{:S(2)}, u32[]{:S(2)}) %collective-permute-start.19) | collective-permute-done | bytes 5152 | tf_op jit(solution)/shard_map/ppermute | solution.py:168
  129.4 2.9 %collective-permute-start.20 = (f32[5,256]{1,0:T(8,128)S(1)}, f32[5,256]{1,0:T(8,128)S(1)}, u32[]{:S(2)}, u32[]{:S(2)}) collective-permute-start(f32[5,256]{1,0:T(8,128)S(1)} %add.246), channel_id=1, source_target_pairs={{0,4},{1,5},{2,6},{3,7},{4,0},{5,1},{6,2},{7,3},{8,12},{9,13},{10,... | collective-permute-start | bytes 15368 | tf_op jit(solution)/shard_map/ppermute | solution.py:168
  132.3 1.6 collective-permute-done.20
  133.9 5.9 %collective-permute-start.21 = (f32[5,256]{1,0:T(8,128)S(1)}, f32[5,256]{1,0:T(8,128)S(1)}, u32[]{:S(2)}, u32[]{:S(2)}) collective-permute-start(f32[5,256]{1,0:T(8,128)S(1)} %add.247), channel_id=1, source_target_pairs={{0,8},{1,9},{2,10},{3,11},{4,12},{5,13},{6,14},{7,15},{8,0},{9,1},... | collective-permute-start | bytes 15368 | tf_op jit(solution)/shard_map/ppermute | solution.py:168
  139.9 2.1 concatenate.91
  144.6 1.3 collective-permute-start.24
  145.9 1.3 collective-permute-start.25
  147.3 7.5 %collective-permute-done.24 = f32[5,2,128]{2,1,0:T(2,128)S(1)} collective-permute-done((f32[5,2,128]{2,1,0:T(2,128)S(1)}, f32[5,2,128]{2,1,0:T(2,128)S(1)}, u32[]{:S(2)}, u32[]{:S(2)}) %collective-permute-start.24) | collective-permute-done | bytes 5152 | tf_op jit(solution)/shard_map/ppermute | solution.py:22
  154.8 4.0 %collective-permute-done.25 = f32[5,2,128]{2,1,0:T(2,128)S(1)} collective-permute-done((f32[5,2,128]{2,1,0:T(2,128)S(1)}, f32[5,2,128]{2,1,0:T(2,128)S(1)}, u32[]{:S(2)}, u32[]{:S(2)}) %collective-permute-start.25) | collective-permute-done | bytes 5152 | tf_op jit(solution)/shard_map/ppermute | solution.py:22
  159.4 1.9 abs_reduce_fusion
  165.3 2.5 %collective-permute-done.27 = f32[26]{0:T(128)S(1)} collective-permute-done((f32[26]{0:T(128)S(1)}, f32[26]{0:T(128)S(1)}, u32[]{:S(2)}, u32[]{:S(2)}) %collective-permute-start.27) | collective-permute-done | bytes 136 | tf_op jit(solution)/shard_map/ppermute | solution.py:168
  167.9 2.4 %collective-permute-start.28 = (f32[26]{0:T(128)S(1)}, f32[26]{0:T(128)S(1)}, u32[]{:S(2)}, u32[]{:S(2)}) collective-permute-start(f32[26]{0:T(128)S(1)} %add.252), channel_id=1, source_target_pairs={{0,4},{1,5},{2,6},{3,7},{4,0},{5,1},{6,2},{7,3},{8,12},{9,13},{10,... | collective-permute-start | bytes 320 | tf_op jit(solution)/shard_map/ppermute | solution.py:168
  170.3 2.1 collective-permute-done.28
  172.3 5.4 %collective-permute-start.29 = (f32[26]{0:T(128)S(1)}, f32[26]{0:T(128)S(1)}, u32[]{:S(2)}, u32[]{:S(2)}) collective-permute-start(f32[26]{0:T(128)S(1)} %add.253), channel_id=1, source_target_pairs={{0,8},{1,9},{2,10},{3,11},{4,12},{5,13},{6,14},{7,15},{8,0},{9,1},... | collective-permute-start | bytes 320 | tf_op jit(solution)/shard_map/ppermute | solution.py:168
  177.7 2.0 collective-permute-done.29
  179.8 1.5 collective-permute-start.30
  181.2 2.1 collective-permute-done.30
  183.3 4.4 %collective-permute-start.31 = (f32[26]{0:T(128)S(1)}, f32[26]{0:T(128)S(1)}, u32[]{:S(2)}, u32[]{:S(2)}) collective-permute-start(f32[26]{0:T(128)S(1)} %add.255), channel_id=1, source_target_pairs={{0,32},{16,48},{32,0},{48,16},{64,96},{80,112},{96,64},{112,80},{1... | collective-permute-start | bytes 320 | tf_op jit(solution)/shard_map/ppermute | solution.py:168
  187.7 1.5 collective-permute-done.31
  189.3 1.8 collective-permute-start.32
  191.0 1.8 collective-permute-done.32
  192.8 4.6 %collective-permute-start.33 = (f32[26]{0:T(128)S(1)}, f32[26]{0:T(128)S(1)}, u32[]{:S(2)}, u32[]{:S(2)}) collective-permute-start(f32[26]{0:T(128)S(1)} %add.257), channel_id=1, source_target_pairs={{0,128},{16,144},{32,160},{48,176},{64,192},{80,208},{96,224},{112... | collective-permute-start | bytes 320 | tf_op jit(solution)/shard_map/ppermute | solution.py:168
  197.4 1.5 collective-permute-done.33
  (154 shorter events, 26.9 us)
Async XLA Ops:
  0.6 27.5 %copy-start = (f32[864,256]{1,0:T(8,128)S(1)}, f32[864,256]{1,0:T(8,128)}, u32[]{:S(2)}) copy-start(f32[864,256]{1,0:T(8,128)} %param.9) | copy-start | bytes 2654212
  1.6 138.3 %collective-permute-start.14 = (f32[75,2,128]{2,1,0:T(2,128)S(1)}, f32[75,2,128]{2,1,0:T(2,128)S(1)}, u32[]{:S(2)}, u32[]{:S(2)}) collective-permute-start(f32[75,2,128]{2,1,0:T(2,128)S(1)} %reshape.257), channel_id=1, source_target_pairs={{0,32},{16,48},{32,64},{48,80},{64,96},{80,112},{96,128},{112,144}... | collective-permute-start | bytes 230408 | tf_op jit(solution)/shard_map/ppermute | solution.py:22
  6.7 133.2 %collective-permute-start.15 = (f32[75,2,128]{2,1,0:T(2,128)S(1)}, f32[75,2,128]{2,1,0:T(2,128)S(1)}, u32[]{:S(2)}, u32[]{:S(2)}) collective-permute-start(f32[75,2,128]{2,1,0:T(2,128)S(1)} %reshape.257), channel_id=1, source_target_pairs={{0,16},{16,32},{32,48},{48,64},{64,80},{80,96},{96,112},{112,128},... | collective-permute-start | bytes 230408 | tf_op jit(solution)/shard_map/ppermute | solution.py:22
  9.3 130.6 %collective-permute-start.16 = (f32[75,2,128]{2,1,0:T(2,128)S(1)}, f32[75,2,128]{2,1,0:T(2,128)S(1)}, u32[]{:S(2)}, u32[]{:S(2)}) collective-permute-start(f32[75,2,128]{2,1,0:T(2,128)S(1)} %reshape.257), channel_id=1, source_target_pairs={{16,0},{32,16},{48,32},{64,48},{80,64},{96,80},{112,96},{128,112},... | collective-permute-start | bytes 230408 | tf_op jit(solution)/shard_map/ppermute | solution.py:22
  12.3 0.7 copy-start.1
  12.3 0.7 copy-start.3
  12.3 1.3 collective-permute-start
  13.6 3.7 %collective-permute-start.1 = (f32[5,256]{1,0:T(8,128)S(1)}, f32[5,256]{1,0:T(8,128)S(1)}, u32[]{:S(2)}, u32[]{:S(2)}) collective-permute-start(f32[5,256]{1,0:T(8,128)S(1)} %add.214), channel_id=1, source_target_pairs={{0,2},{1,3},{2,0},{3,1},{4,6},{5,7},{6,4},{7,5},{8,10},{9,11},{10,... | collective-permute-start | bytes 15368 | tf_op jit(solution)/shard_map/ppermute | solution.py:168
  17.2 4.9 %collective-permute-start.2 = (f32[5,256]{1,0:T(8,128)S(1)}, f32[5,256]{1,0:T(8,128)S(1)}, u32[]{:S(2)}, u32[]{:S(2)}) collective-permute-start(f32[5,256]{1,0:T(8,128)S(1)} %add.215), channel_id=1, source_target_pairs={{0,4},{1,5},{2,6},{3,7},{4,0},{5,1},{6,2},{7,3},{8,12},{9,13},{10,... | collective-permute-start | bytes 15368 | tf_op jit(solution)/shard_map/ppermute | solution.py:168
  22.1 7.6 %collective-permute-start.3 = (f32[5,256]{1,0:T(8,128)S(1)}, f32[5,256]{1,0:T(8,128)S(1)}, u32[]{:S(2)}, u32[]{:S(2)}) collective-permute-start(f32[5,256]{1,0:T(8,128)S(1)} %add.216), channel_id=1, source_target_pairs={{0,8},{1,9},{2,10},{3,11},{4,12},{5,13},{6,14},{7,15},{8,0},{9,1},... | collective-permute-start | bytes 15368 | tf_op jit(solution)/shard_map/ppermute | solution.py:168
  33.2 10.8 %collective-permute-start.4 = (f32[37,12,128]{2,0,1:T(8,128)S(1)}, f32[37,12,128]{2,0,1:T(8,128)S(1)}, u32[]{:S(2)}, u32[]{:S(2)}) collective-permute-start(f32[37,12,128]{2,0,1:T(8,128)S(1)} %pad_maximum_fusion.1), channel_id=1, source_target_pairs={{16,0},{32,16},{48,32},{64,48},{80,64},{96,80},{112,96},{128,112},... | collective-permute-start | bytes 681992 | tf_op jit(solution)/shard_map/ppermute | solution.py:22
  34.5 14.1 %collective-permute-start.5 = (f32[37,12,128]{2,0,1:T(8,128)S(1)}, f32[37,12,128]{2,0,1:T(8,128)S(1)}, u32[]{:S(2)}, u32[]{:S(2)}) collective-permute-start(f32[37,12,128]{2,0,1:T(8,128)S(1)} %pad_maximum_fusion.1), channel_id=1, source_target_pairs={{32,0},{48,16},{64,32},{80,48},{96,64},{112,80},{128,96},{144,112}... | collective-permute-start | bytes 681992 | tf_op jit(solution)/shard_map/ppermute | solution.py:22
  44.0 11.5 %collective-permute-start.10 = (f32[37,12,128]{2,0,1:T(8,128)S(1)}, f32[37,12,128]{2,0,1:T(8,128)S(1)}, u32[]{:S(2)}, u32[]{:S(2)}) collective-permute-start(f32[37,12,128]{2,0,1:T(8,128)S(1)} %pad_maximum_fusion.5), channel_id=1, source_target_pairs={{0,32},{16,48},{32,64},{48,80},{64,96},{80,112},{96,128},{112,144}... | collective-permute-start | bytes 681992 | tf_op jit(solution)/shard_map/ppermute | solution.py:22
  48.7 10.6 %collective-permute-start.9 = (f32[37,12,128]{2,0,1:T(8,128)S(1)}, f32[37,12,128]{2,0,1:T(8,128)S(1)}, u32[]{:S(2)}, u32[]{:S(2)}) collective-permute-start(f32[37,12,128]{2,0,1:T(8,128)S(1)} %pad_maximum_fusion.5), channel_id=1, source_target_pairs={{0,16},{16,32},{32,48},{48,64},{64,80},{80,96},{96,112},{112,128},... | collective-permute-start | bytes 681992 | tf_op jit(solution)/shard_map/ppermute | solution.py:22
  55.5 84.3 %collective-permute-start.17 = (f32[75,2,128]{2,1,0:T(2,128)S(1)}, f32[75,2,128]{2,1,0:T(2,128)S(1)}, u32[]{:S(2)}, u32[]{:S(2)}) collective-permute-start(f32[75,2,128]{2,1,0:T(2,128)S(1)} %reshape.257), channel_id=1, source_target_pairs={{32,0},{48,16},{64,32},{80,48},{96,64},{112,80},{128,96},{144,112}... | collective-permute-start | bytes 230408 | tf_op jit(solution)/shard_map/ppermute | solution.py:22
  59.3 14.7 %collective-permute-start.6 = (f32[37,12,128]{2,0,1:T(8,128)S(1)}, f32[37,12,128]{2,0,1:T(8,128)S(1)}, u32[]{:S(2)}, u32[]{:S(2)}) collective-permute-start(f32[37,12,128]{2,0,1:T(8,128)S(1)} %pad_maximum_fusion.2), channel_id=1, source_target_pairs={{32,0},{48,16},{64,32},{80,48},{96,64},{112,80},{128,96},{144,112}... | collective-permute-start | bytes 681992 | tf_op jit(solution)/shard_map/ppermute | solution.py:22
  74.0 10.1 %collective-permute-start.11 = (f32[37,12,128]{2,0,1:T(8,128)S(1)}, f32[37,12,128]{2,0,1:T(8,128)S(1)}, u32[]{:S(2)}, u32[]{:S(2)}) collective-permute-start(f32[37,12,128]{2,0,1:T(8,128)S(1)} %pad_maximum_fusion.6), channel_id=1, source_target_pairs={{0,32},{16,48},{32,64},{48,80},{64,96},{80,112},{96,128},{112,144}... | collective-permute-start | bytes 681992 | tf_op jit(solution)/shard_map/ppermute | solution.py:22
  84.1 13.5 %collective-permute-start.7 = (f32[37,12,128]{2,0,1:T(8,128)S(1)}, f32[37,12,128]{2,0,1:T(8,128)S(1)}, u32[]{:S(2)}, u32[]{:S(2)}) collective-permute-start(f32[37,12,128]{2,0,1:T(8,128)S(1)} %pad_maximum_fusion.3), channel_id=1, source_target_pairs={{64,0},{80,16},{96,32},{112,48},{128,64},{144,80},{160,96},{176,11... | collective-permute-start | bytes 681992 | tf_op jit(solution)/shard_map/ppermute | solution.py:22
  97.5 9.8 %collective-permute-start.12 = (f32[37,12,128]{2,0,1:T(8,128)S(1)}, f32[37,12,128]{2,0,1:T(8,128)S(1)}, u32[]{:S(2)}, u32[]{:S(2)}) collective-permute-start(f32[37,12,128]{2,0,1:T(8,128)S(1)} %pad_maximum_fusion.7), channel_id=1, source_target_pairs={{0,64},{16,80},{32,96},{48,112},{64,128},{80,144},{96,160},{112,17... | collective-permute-start | bytes 681992 | tf_op jit(solution)/shard_map/ppermute | solution.py:22
  107.3 9.6 %collective-permute-start.8 = (f32[37,12,128]{2,0,1:T(8,128)S(1)}, f32[37,12,128]{2,0,1:T(8,128)S(1)}, u32[]{:S(2)}, u32[]{:S(2)}) collective-permute-start(f32[37,12,128]{2,0,1:T(8,128)S(1)} %pad_maximum_fusion.4), channel_id=1, source_target_pairs={{128,0},{144,16},{160,32},{176,48},{192,64},{208,80},{224,96},{240... | collective-permute-start | bytes 681992 | tf_op jit(solution)/shard_map/ppermute | solution.py:22
  116.9 5.1 %collective-permute-start.13 = (f32[37,12,128]{2,0,1:T(8,128)S(1)}, f32[37,12,128]{2,0,1:T(8,128)S(1)}, u32[]{:S(2)}, u32[]{:S(2)}) collective-permute-start(f32[37,12,128]{2,0,1:T(8,128)S(1)} %pad_maximum_fusion.8), channel_id=1, source_target_pairs={{0,128},{16,144},{32,160},{48,176},{64,192},{80,208},{96,224},{112... | collective-permute-start | bytes 681992 | tf_op jit(solution)/shard_map/ppermute | solution.py:22
  124.5 1.2 collective-permute-start.18
  125.7 3.7 %collective-permute-start.19 = (f32[5,256]{1,0:T(8,128)S(1)}, f32[5,256]{1,0:T(8,128)S(1)}, u32[]{:S(2)}, u32[]{:S(2)}) collective-permute-start(f32[5,256]{1,0:T(8,128)S(1)} %add.245), channel_id=1, source_target_pairs={{0,2},{1,3},{2,0},{3,1},{4,6},{5,7},{6,4},{7,5},{8,10},{9,11},{10,... | collective-permute-start | bytes 15368 | tf_op jit(solution)/shard_map/ppermute | solution.py:168
  129.4 4.6 %collective-permute-start.20 = (f32[5,256]{1,0:T(8,128)S(1)}, f32[5,256]{1,0:T(8,128)S(1)}, u32[]{:S(2)}, u32[]{:S(2)}) collective-permute-start(f32[5,256]{1,0:T(8,128)S(1)} %add.246), channel_id=1, source_target_pairs={{0,4},{1,5},{2,6},{3,7},{4,0},{5,1},{6,2},{7,3},{8,12},{9,13},{10,... | collective-permute-start | bytes 15368 | tf_op jit(solution)/shard_map/ppermute | solution.py:168
  133.9 8.1 %collective-permute-start.21 = (f32[5,256]{1,0:T(8,128)S(1)}, f32[5,256]{1,0:T(8,128)S(1)}, u32[]{:S(2)}, u32[]{:S(2)}) collective-permute-start(f32[5,256]{1,0:T(8,128)S(1)} %add.247), channel_id=1, source_target_pairs={{0,8},{1,9},{2,10},{3,11},{4,12},{5,13},{6,14},{7,15},{8,0},{9,1},... | collective-permute-start | bytes 15368 | tf_op jit(solution)/shard_map/ppermute | solution.py:168
  142.0 5.2 %collective-permute-start.22 = (f32[5,2,128]{2,1,0:T(2,128)S(1)}, f32[5,2,128]{2,1,0:T(2,128)S(1)}, u32[]{:S(2)}, u32[]{:S(2)}) collective-permute-start(f32[5,2,128]{2,1,0:T(2,128)S(1)} %reshape.259), channel_id=1, source_target_pairs={{0,32},{16,48},{32,64},{48,80},{64,96},{80,112},{96,128},{112,144}... | collective-permute-start | bytes 15368 | tf_op jit(solution)/shard_map/ppermute | solution.py:22
  143.3 4.0 %collective-permute-start.23 = (f32[5,2,128]{2,1,0:T(2,128)S(1)}, f32[5,2,128]{2,1,0:T(2,128)S(1)}, u32[]{:S(2)}, u32[]{:S(2)}) collective-permute-start(f32[5,2,128]{2,1,0:T(2,128)S(1)} %reshape.259), channel_id=1, source_target_pairs={{0,16},{16,32},{32,48},{48,64},{64,80},{80,96},{96,112},{112,128},... | collective-permute-start | bytes 15368 | tf_op jit(solution)/shard_map/ppermute | solution.py:22
  144.6 10.1 %collective-permute-start.24 = (f32[5,2,128]{2,1,0:T(2,128)S(1)}, f32[5,2,128]{2,1,0:T(2,128)S(1)}, u32[]{:S(2)}, u32[]{:S(2)}) collective-permute-start(f32[5,2,128]{2,1,0:T(2,128)S(1)} %reshape.259), channel_id=1, source_target_pairs={{16,0},{32,16},{48,32},{64,48},{80,64},{96,80},{112,96},{128,112},... | collective-permute-start | bytes 15368 | tf_op jit(solution)/shard_map/ppermute | solution.py:22
  145.9 12.8 %collective-permute-start.25 = (f32[5,2,128]{2,1,0:T(2,128)S(1)}, f32[5,2,128]{2,1,0:T(2,128)S(1)}, u32[]{:S(2)}, u32[]{:S(2)}) collective-permute-start(f32[5,2,128]{2,1,0:T(2,128)S(1)} %reshape.259), channel_id=1, source_target_pairs={{32,0},{48,16},{64,32},{80,48},{96,64},{112,80},{128,96},{144,112}... | collective-permute-start | bytes 15368 | tf_op jit(solution)/shard_map/ppermute | solution.py:22
  163.1 1.1 collective-permute-start.26
  164.3 3.6 %collective-permute-start.27 = (f32[26]{0:T(128)S(1)}, f32[26]{0:T(128)S(1)}, u32[]{:S(2)}, u32[]{:S(2)}) collective-permute-start(f32[26]{0:T(128)S(1)} %fusion.40), channel_id=1, source_target_pairs={{0,2},{1,3},{2,0},{3,1},{4,6},{5,7},{6,4},{7,5},{8,10},{9,11},{10,... | collective-permute-start | bytes 320 | tf_op jit(solution)/shard_map/ppermute | solution.py:168
  167.9 4.4 %collective-permute-start.28 = (f32[26]{0:T(128)S(1)}, f32[26]{0:T(128)S(1)}, u32[]{:S(2)}, u32[]{:S(2)}) collective-permute-start(f32[26]{0:T(128)S(1)} %add.252), channel_id=1, source_target_pairs={{0,4},{1,5},{2,6},{3,7},{4,0},{5,1},{6,2},{7,3},{8,12},{9,13},{10,... | collective-permute-start | bytes 320 | tf_op jit(solution)/shard_map/ppermute | solution.py:168
  172.3 7.4 %collective-permute-start.29 = (f32[26]{0:T(128)S(1)}, f32[26]{0:T(128)S(1)}, u32[]{:S(2)}, u32[]{:S(2)}) collective-permute-start(f32[26]{0:T(128)S(1)} %add.253), channel_id=1, source_target_pairs={{0,8},{1,9},{2,10},{3,11},{4,12},{5,13},{6,14},{7,15},{8,0},{9,1},... | collective-permute-start | bytes 320 | tf_op jit(solution)/shard_map/ppermute | solution.py:168
  179.8 3.5 %collective-permute-start.30 = (f32[26]{0:T(128)S(1)}, f32[26]{0:T(128)S(1)}, u32[]{:S(2)}, u32[]{:S(2)}) collective-permute-start(f32[26]{0:T(128)S(1)} %add.254), channel_id=1, source_target_pairs={{0,16},{16,0},{32,48},{48,32},{64,80},{80,64},{96,112},{112,96},{1... | collective-permute-start | bytes 320 | tf_op jit(solution)/shard_map/ppermute | solution.py:168
  183.3 5.9 %collective-permute-start.31 = (f32[26]{0:T(128)S(1)}, f32[26]{0:T(128)S(1)}, u32[]{:S(2)}, u32[]{:S(2)}) collective-permute-start(f32[26]{0:T(128)S(1)} %add.255), channel_id=1, source_target_pairs={{0,32},{16,48},{32,0},{48,16},{64,96},{80,112},{96,64},{112,80},{1... | collective-permute-start | bytes 320 | tf_op jit(solution)/shard_map/ppermute | solution.py:168
  189.3 3.5 %collective-permute-start.32 = (f32[26]{0:T(128)S(1)}, f32[26]{0:T(128)S(1)}, u32[]{:S(2)}, u32[]{:S(2)}) collective-permute-start(f32[26]{0:T(128)S(1)} %add.256), channel_id=1, source_target_pairs={{0,64},{16,80},{32,96},{48,112},{64,0},{80,16},{96,32},{112,48},{1... | collective-permute-start | bytes 320 | tf_op jit(solution)/shard_map/ppermute | solution.py:168
  192.8 6.1 %collective-permute-start.33 = (f32[26]{0:T(128)S(1)}, f32[26]{0:T(128)S(1)}, u32[]{:S(2)}, u32[]{:S(2)}) collective-permute-start(f32[26]{0:T(128)S(1)} %add.257), channel_id=1, source_target_pairs={{0,128},{16,144},{32,160},{48,176},{64,192},{80,208},{96,224},{112... | collective-permute-start | bytes 320 | tf_op jit(solution)/shard_map/ppermute | solution.py:168
  198.9 0.7 copy-start.2
  198.9 0.7 copy-start.4

commit v3 on v2

--- a/solution.py
+++ b/solution.py
@@ -243,12 +243,20 @@
         jnp.concatenate([line_loaded, local_totals * first_copy]), ("vel", "sec")
     )
     loaded = gathered[:NXI]
-    goals = gathered[NXI:]
-    shift_mass = jnp.zeros((), jnp.float32)
-    shift_flow = jnp.zeros((), jnp.float32)
+    goal_mass = jnp.broadcast_to(gathered[NXI], (NXI,))
+    goal_flow = jnp.broadcast_to(gathered[NXI + 1], (NXI,))
+    spread = jnp.ones((NXI, NXI), jnp.float32)
+    shift_mass = jnp.zeros((NXI,), jnp.float32)
+    shift_flow = jnp.zeros((NXI,), jnp.float32)
     for newton_turn in range(NEWTON):
-        sums = newton_sums(loaded, line_signed, shift_mass, shift_flow)
-        shift_mass, shift_flow = newton_update(shift_mass, shift_flow, sums, goals[0], goals[1])
+        growth = jnp.exp(shift_mass + shift_flow * line_signed)
+        scaled = loaded * growth
+        excess = loaded * (growth - 1.0)
+        terms = jnp.stack(
+            [scaled, scaled * line_signed, scaled * line_signed * line_signed, excess, excess * line_signed]
+        )
+        sums = jnp.dot(terms, spread, precision=HIGH)
+        shift_mass, shift_flow = newton_update(shift_mass, shift_flow, sums, goal_mass, goal_flow)
     growth = jnp.exp(shift_mass + shift_flow * line_signed)
     synthetic_rows = synthetic.reshape(node_rows, NXI, cell_count)
     new_distribution = synthetic_rows + jnp.abs(synthetic_rows) * (growth[None, :, None] - 1.0)

time: 220 us -> 207 us (0.941)
  between operations: 16.7 us -> 1.57 us
where the time goes in v3:
time: 207 us; the launch traced here: 204 us
  waiting for transfers between devices  91.1 us (44%)
  starting transfers between devices  87.6 us (42%)
  other arithmetic  10.5 us (5%)
  matrix products  6.97 us (3%)
  local copies, waits for them, and re-layouts  6.7 us (3%)
    ppermute x18, waiting for transfers between devices, passed_along(): return lax.ppermute(block, axis, route)  64.4 us
    ppermute x18, starting transfers between devices, passed_along(): return lax.ppermute(block, axis, route)  47.1 us
    ppermute x16, starting transfers between devices, tree_sum(): lax.ppermute(block, axis, [(i, i ^ bit) for i in range(count)])  40.4 us
    ppermute x16, waiting for transfers between devices, tree_sum(): lax.ppermute(block, axis, [(i, i ^ bit) for i in range(count)])  26.7 us
  transfers between devices with their start and end apart: 34, of which 25 were waited for; matrix products, arithmetic and copies ran while one was open for 6% of the time, Pallas kernels for 0%

profile of v3, /device:TPU:32, one launch (start us, length us, event | category | flops | bytes accessed | tf_op | source)
XLA Modules:
  0.0 204.4 jit_solution(12317371855780912302)
XLA Ops:
  1.6 5.1 %collective-permute-start.14 = (f32[75,2,128]{2,1,0:T(2,128)S(1)}, f32[75,2,128]{2,1,0:T(2,128)S(1)}, u32[]{:S(2)}, u32[]{:S(2)}) collective-permute-start(f32[75,2,128]{2,1,0:T(2,128)S(1)} %reshape.287), channel_id=1, source_target_pairs={{0,32},{16,48},{32,64},{48,80},{64,96},{80,112},{96,128},{112,144}... | collective-permute-start | bytes 230408 | tf_op jit(solution)/shard_map/ppermute | solution.py:22
  6.7 2.6 %collective-permute-start.15 = (f32[75,2,128]{2,1,0:T(2,128)S(1)}, f32[75,2,128]{2,1,0:T(2,128)S(1)}, u32[]{:S(2)}, u32[]{:S(2)}) collective-permute-start(f32[75,2,128]{2,1,0:T(2,128)S(1)} %reshape.287), channel_id=1, source_target_pairs={{0,16},{16,32},{32,48},{48,64},{64,80},{80,96},{96,112},{112,128},... | collective-permute-start | bytes 230408 | tf_op jit(solution)/shard_map/ppermute | solution.py:22
  9.3 1.3 collective-permute-start.16
  10.6 1.7 fusion.13
  13.7 3.5 %collective-permute-done.1 = f32[5,256]{1,0:T(8,128)S(1)} collective-permute-done((f32[5,256]{1,0:T(8,128)S(1)}, f32[5,256]{1,0:T(8,128)S(1)}, u32[]{:S(2)}, u32[]{:S(2)}) %collective-permute-start.1) | collective-permute-done | bytes 5152 | tf_op jit(solution)/shard_map/ppermute | solution.py:168
  17.2 3.3 %collective-permute-start.2 = (f32[5,256]{1,0:T(8,128)S(1)}, f32[5,256]{1,0:T(8,128)S(1)}, u32[]{:S(2)}, u32[]{:S(2)}) collective-permute-start(f32[5,256]{1,0:T(8,128)S(1)} %add.209), channel_id=1, source_target_pairs={{0,4},{1,5},{2,6},{3,7},{4,0},{5,1},{6,2},{7,3},{8,12},{9,13},{10,... | collective-permute-start | bytes 15368 | tf_op jit(solution)/shard_map/ppermute | solution.py:168
  20.5 1.6 collective-permute-done.2
  22.1 5.9 %collective-permute-start.3 = (f32[5,256]{1,0:T(8,128)S(1)}, f32[5,256]{1,0:T(8,128)S(1)}, u32[]{:S(2)}, u32[]{:S(2)}) collective-permute-start(f32[5,256]{1,0:T(8,128)S(1)} %add.210), channel_id=1, source_target_pairs={{0,8},{1,9},{2,10},{3,11},{4,12},{5,13},{6,14},{7,15},{8,0},{9,1},... | collective-permute-start | bytes 15368 | tf_op jit(solution)/shard_map/ppermute | solution.py:168
  29.7 1.8 fusion.16
  33.2 1.3 collective-permute-start.4
  34.5 1.3 collective-permute-start.5
  37.8 6.2 %collective-permute-done.4 = f32[37,12,128]{2,0,1:T(8,128)S(1)} collective-permute-done((f32[37,12,128]{2,0,1:T(8,128)S(1)}, f32[37,12,128]{2,0,1:T(8,128)S(1)}, u32[]{:S(2)}, u32[]{:S(2)}) %collective-permute-start.4) | collective-permute-done | bytes 227360 | tf_op jit(solution)/shard_map/ppermute | solution.py:22
  44.0 4.7 %collective-permute-start.10 = (f32[37,12,128]{2,0,1:T(8,128)S(1)}, f32[37,12,128]{2,0,1:T(8,128)S(1)}, u32[]{:S(2)}, u32[]{:S(2)}) collective-permute-start(f32[37,12,128]{2,0,1:T(8,128)S(1)} %pad_maximum_fusion.5), channel_id=1, source_target_pairs={{0,32},{16,48},{32,64},{48,80},{64,96},{80,112},{96,128},{112,144}... | collective-permute-start | bytes 681992 | tf_op jit(solution)/shard_map/ppermute | solution.py:22
  48.7 6.7 %collective-permute-start.9 = (f32[37,12,128]{2,0,1:T(8,128)S(1)}, f32[37,12,128]{2,0,1:T(8,128)S(1)}, u32[]{:S(2)}, u32[]{:S(2)}) collective-permute-start(f32[37,12,128]{2,0,1:T(8,128)S(1)} %pad_maximum_fusion.5), channel_id=1, source_target_pairs={{0,16},{16,32},{32,48},{48,64},{64,80},{80,96},{96,112},{112,128},... | collective-permute-start | bytes 681992 | tf_op jit(solution)/shard_map/ppermute | solution.py:22
  56.8 2.5 %collective-permute-done.9 = f32[37,12,128]{2,0,1:T(8,128)S(1)} collective-permute-done((f32[37,12,128]{2,0,1:T(8,128)S(1)}, f32[37,12,128]{2,0,1:T(8,128)S(1)}, u32[]{:S(2)}, u32[]{:S(2)}) %collective-permute-start.9) | collective-permute-done | bytes 227360 | tf_op jit(solution)/shard_map/ppermute | solution.py:22
  60.7 13.2 %collective-permute-done.6 = f32[37,12,128]{2,0,1:T(8,128)S(1)} collective-permute-done((f32[37,12,128]{2,0,1:T(8,128)S(1)}, f32[37,12,128]{2,0,1:T(8,128)S(1)}, u32[]{:S(2)}, u32[]{:S(2)}) %collective-permute-start.6) | collective-permute-done | bytes 227360 | tf_op jit(solution)/shard_map/ppermute | solution.py:22
  74.0 6.4 %collective-permute-start.11 = (f32[37,12,128]{2,0,1:T(8,128)S(1)}, f32[37,12,128]{2,0,1:T(8,128)S(1)}, u32[]{:S(2)}, u32[]{:S(2)}) collective-permute-start(f32[37,12,128]{2,0,1:T(8,128)S(1)} %pad_maximum_fusion.6), channel_id=1, source_target_pairs={{0,32},{16,48},{32,64},{48,80},{64,96},{80,112},{96,128},{112,144}... | collective-permute-start | bytes 681992 | tf_op jit(solution)/shard_map/ppermute | solution.py:22
  80.5 3.6 %collective-permute-done.11 = f32[37,12,128]{2,0,1:T(8,128)S(1)} collective-permute-done((f32[37,12,128]{2,0,1:T(8,128)S(1)}, f32[37,12,128]{2,0,1:T(8,128)S(1)}, u32[]{:S(2)}, u32[]{:S(2)}) %collective-permute-start.11) | collective-permute-done | bytes 227360 | tf_op jit(solution)/shard_map/ppermute | solution.py:22
  85.5 12.1 %collective-permute-done.7 = f32[37,12,128]{2,0,1:T(8,128)S(1)} collective-permute-done((f32[37,12,128]{2,0,1:T(8,128)S(1)}, f32[37,12,128]{2,0,1:T(8,128)S(1)}, u32[]{:S(2)}, u32[]{:S(2)}) %collective-permute-start.7) | collective-permute-done | bytes 227360 | tf_op jit(solution)/shard_map/ppermute | solution.py:22
  97.5 6.1 %collective-permute-start.12 = (f32[37,12,128]{2,0,1:T(8,128)S(1)}, f32[37,12,128]{2,0,1:T(8,128)S(1)}, u32[]{:S(2)}, u32[]{:S(2)}) collective-permute-start(f32[37,12,128]{2,0,1:T(8,128)S(1)} %pad_maximum_fusion.7), channel_id=1, source_target_pairs={{0,64},{16,80},{32,96},{48,112},{64,128},{80,144},{96,160},{112,17... | collective-permute-start | bytes 681992 | tf_op jit(solution)/shard_map/ppermute | solution.py:22
  103.7 3.6 %collective-permute-done.12 = f32[37,12,128]{2,0,1:T(8,128)S(1)} collective-permute-done((f32[37,12,128]{2,0,1:T(8,128)S(1)}, f32[37,12,128]{2,0,1:T(8,128)S(1)}, u32[]{:S(2)}, u32[]{:S(2)}) %collective-permute-start.12) | collective-permute-done | bytes 227360 | tf_op jit(solution)/shard_map/ppermute | solution.py:22
  108.7 8.2 %collective-permute-done.8 = f32[37,12,128]{2,0,1:T(8,128)S(1)} collective-permute-done((f32[37,12,128]{2,0,1:T(8,128)S(1)}, f32[37,12,128]{2,0,1:T(8,128)S(1)}, u32[]{:S(2)}, u32[]{:S(2)}) %collective-permute-start.8) | collective-permute-done | bytes 227360 | tf_op jit(solution)/shard_map/ppermute | solution.py:22
  116.9 1.5 collective-permute-start.13
  118.5 3.6 %collective-permute-done.13 = f32[37,12,128]{2,0,1:T(8,128)S(1)} collective-permute-done((f32[37,12,128]{2,0,1:T(8,128)S(1)}, f32[37,12,128]{2,0,1:T(8,128)S(1)}, u32[]{:S(2)}, u32[]{:S(2)}) %collective-permute-start.13) | collective-permute-done | bytes 227360 | tf_op jit(solution)/shard_map/ppermute | solution.py:22
  126.7 2.6 %collective-permute-done.19 = f32[5,256]{1,0:T(8,128)S(1)} collective-permute-done((f32[5,256]{1,0:T(8,128)S(1)}, f32[5,256]{1,0:T(8,128)S(1)}, u32[]{:S(2)}, u32[]{:S(2)}) %collective-permute-start.19) | collective-permute-done | bytes 5152 | tf_op jit(solution)/shard_map/ppermute | solution.py:168
  129.4 2.9 %collective-permute-start.20 = (f32[5,256]{1,0:T(8,128)S(1)}, f32[5,256]{1,0:T(8,128)S(1)}, u32[]{:S(2)}, u32[]{:S(2)}) collective-permute-start(f32[5,256]{1,0:T(8,128)S(1)} %add.240), channel_id=1, source_target_pairs={{0,4},{1,5},{2,6},{3,7},{4,0},{5,1},{6,2},{7,3},{8,12},{9,13},{10,... | collective-permute-start | bytes 15368 | tf_op jit(solution)/shard_map/ppermute | solution.py:168
  132.3 1.6 collective-permute-done.20
  133.9 5.9 %collective-permute-start.21 = (f32[5,256]{1,0:T(8,128)S(1)}, f32[5,256]{1,0:T(8,128)S(1)}, u32[]{:S(2)}, u32[]{:S(2)}) collective-permute-start(f32[5,256]{1,0:T(8,128)S(1)} %add.241), channel_id=1, source_target_pairs={{0,8},{1,9},{2,10},{3,11},{4,12},{5,13},{6,14},{7,15},{8,0},{9,1},... | collective-permute-start | bytes 15368 | tf_op jit(solution)/shard_map/ppermute | solution.py:168
  139.9 2.1 %concatenate.91 = f32[75,10,128]{2,1,0:T(8,128)S(1)} concatenate(f32[75,2,128]{2,1,0:T(2,128)S(1)} %collective-permute-done.14, f32[75,2,128]{2,1,0:T(2,128)S(1)} %collective-permute-done.15, f32[75,2,128]{2,1,0:T(2,128)S(1)} %reshape.287, f32[75,2,128]{2,1,0:T(2,128)S(1)} %collective-permute-done.16, f32[75,2,128]{2,1,0:T(2,128)S(1)} %collective-permute-done.17), dimensions={1} | concatenate | bytes 768000 | tf_op jit(solution)/shard_map/concatenate | solution.py:157
  144.6 1.3 collective-permute-start.24
  145.9 1.3 collective-permute-start.25
  147.3 7.5 %collective-permute-done.24 = f32[5,2,128]{2,1,0:T(2,128)S(1)} collective-permute-done((f32[5,2,128]{2,1,0:T(2,128)S(1)}, f32[5,2,128]{2,1,0:T(2,128)S(1)}, u32[]{:S(2)}, u32[]{:S(2)}) %collective-permute-start.24) | collective-permute-done | bytes 5152 | tf_op jit(solution)/shard_map/ppermute | solution.py:22
  154.8 4.0 %collective-permute-done.25 = f32[5,2,128]{2,1,0:T(2,128)S(1)} collective-permute-done((f32[5,2,128]{2,1,0:T(2,128)S(1)}, f32[5,2,128]{2,1,0:T(2,128)S(1)}, u32[]{:S(2)}, u32[]{:S(2)}) %collective-permute-start.25) | collective-permute-done | bytes 5152 | tf_op jit(solution)/shard_map/ppermute | solution.py:22
  159.4 1.9 abs_reduce_fusion
  165.3 2.5 %collective-permute-done.27 = f32[26]{0:T(128)S(1)} collective-permute-done((f32[26]{0:T(128)S(1)}, f32[26]{0:T(128)S(1)}, u32[]{:S(2)}, u32[]{:S(2)}) %collective-permute-start.27) | collective-permute-done | bytes 136 | tf_op jit(solution)/shard_map/ppermute | solution.py:168
  167.9 2.4 %collective-permute-start.28 = (f32[26]{0:T(128)S(1)}, f32[26]{0:T(128)S(1)}, u32[]{:S(2)}, u32[]{:S(2)}) collective-permute-start(f32[26]{0:T(128)S(1)} %add.246), channel_id=1, source_target_pairs={{0,4},{1,5},{2,6},{3,7},{4,0},{5,1},{6,2},{7,3},{8,12},{9,13},{10,... | collective-permute-start | bytes 320 | tf_op jit(solution)/shard_map/ppermute | solution.py:168
  170.3 2.1 %collective-permute-done.28 = f32[26]{0:T(128)S(1)} collective-permute-done((f32[26]{0:T(128)S(1)}, f32[26]{0:T(128)S(1)}, u32[]{:S(2)}, u32[]{:S(2)}) %collective-permute-start.28) | collective-permute-done | bytes 136 | tf_op jit(solution)/shard_map/ppermute | solution.py:168
  172.3 5.4 %collective-permute-start.29 = (f32[26]{0:T(128)S(1)}, f32[26]{0:T(128)S(1)}, u32[]{:S(2)}, u32[]{:S(2)}) collective-permute-start(f32[26]{0:T(128)S(1)} %add.247), channel_id=1, source_target_pairs={{0,8},{1,9},{2,10},{3,11},{4,12},{5,13},{6,14},{7,15},{8,0},{9,1},... | collective-permute-start | bytes 320 | tf_op jit(solution)/shard_map/ppermute | solution.py:168
  177.7 2.0 %collective-permute-done.29 = f32[26]{0:T(128)S(1)} collective-permute-done((f32[26]{0:T(128)S(1)}, f32[26]{0:T(128)S(1)}, u32[]{:S(2)}, u32[]{:S(2)}) %collective-permute-start.29) | collective-permute-done | bytes 136 | tf_op jit(solution)/shard_map/ppermute | solution.py:168
  179.8 1.5 collective-permute-start.30
  181.2 2.1 %collective-permute-done.30 = f32[26]{0:T(128)S(1)} collective-permute-done((f32[26]{0:T(128)S(1)}, f32[26]{0:T(128)S(1)}, u32[]{:S(2)}, u32[]{:S(2)}) %collective-permute-start.30) | collective-permute-done | bytes 136 | tf_op jit(solution)/shard_map/ppermute | solution.py:168
  183.3 4.4 %collective-permute-start.31 = (f32[26]{0:T(128)S(1)}, f32[26]{0:T(128)S(1)}, u32[]{:S(2)}, u32[]{:S(2)}) collective-permute-start(f32[26]{0:T(128)S(1)} %add.249), channel_id=1, source_target_pairs={{0,32},{16,48},{32,0},{48,16},{64,96},{80,112},{96,64},{112,80},{1... | collective-permute-start | bytes 320 | tf_op jit(solution)/shard_map/ppermute | solution.py:168
  187.7 1.5 collective-permute-done.31
  189.3 1.8 collective-permute-start.32
  191.0 1.8 collective-permute-done.32
  192.8 4.6 %collective-permute-start.33 = (f32[26]{0:T(128)S(1)}, f32[26]{0:T(128)S(1)}, u32[]{:S(2)}, u32[]{:S(2)}) collective-permute-start(f32[26]{0:T(128)S(1)} %add.251), channel_id=1, source_target_pairs={{0,128},{16,144},{32,160},{48,176},{64,192},{80,208},{96,224},{112... | collective-permute-start | bytes 320 | tf_op jit(solution)/shard_map/ppermute | solution.py:168
  197.4 1.5 collective-permute-done.33
  201.9 1.3 add_bitcast_fusion
  (161 shorter events, 29.1 us)
Async XLA Ops:
  0.6 27.5 %copy-start = (f32[864,256]{1,0:T(8,128)S(1)}, f32[864,256]{1,0:T(8,128)}, u32[]{:S(2)}) copy-start(f32[864,256]{1,0:T(8,128)} %param.9) | copy-start | bytes 2654212
  1.6 138.3 %collective-permute-start.14 = (f32[75,2,128]{2,1,0:T(2,128)S(1)}, f32[75,2,128]{2,1,0:T(2,128)S(1)}, u32[]{:S(2)}, u32[]{:S(2)}) collective-permute-start(f32[75,2,128]{2,1,0:T(2,128)S(1)} %reshape.287), channel_id=1, source_target_pairs={{0,32},{16,48},{32,64},{48,80},{64,96},{80,112},{96,128},{112,144}... | collective-permute-start | bytes 230408 | tf_op jit(solution)/shard_map/ppermute | solution.py:22
  6.7 133.2 %collective-permute-start.15 = (f32[75,2,128]{2,1,0:T(2,128)S(1)}, f32[75,2,128]{2,1,0:T(2,128)S(1)}, u32[]{:S(2)}, u32[]{:S(2)}) collective-permute-start(f32[75,2,128]{2,1,0:T(2,128)S(1)} %reshape.287), channel_id=1, source_target_pairs={{0,16},{16,32},{32,48},{48,64},{64,80},{80,96},{96,112},{112,128},... | collective-permute-start | bytes 230408 | tf_op jit(solution)/shard_map/ppermute | solution.py:22
  9.3 130.6 %collective-permute-start.16 = (f32[75,2,128]{2,1,0:T(2,128)S(1)}, f32[75,2,128]{2,1,0:T(2,128)S(1)}, u32[]{:S(2)}, u32[]{:S(2)}) collective-permute-start(f32[75,2,128]{2,1,0:T(2,128)S(1)} %reshape.287), channel_id=1, source_target_pairs={{16,0},{32,16},{48,32},{64,48},{80,64},{96,80},{112,96},{128,112},... | collective-permute-start | bytes 230408 | tf_op jit(solution)/shard_map/ppermute | solution.py:22
  12.3 0.7 copy-start.1
  12.3 0.7 copy-start.4
  12.3 1.3 collective-permute-start
  13.6 3.7 %collective-permute-start.1 = (f32[5,256]{1,0:T(8,128)S(1)}, f32[5,256]{1,0:T(8,128)S(1)}, u32[]{:S(2)}, u32[]{:S(2)}) collective-permute-start(f32[5,256]{1,0:T(8,128)S(1)} %add.208), channel_id=1, source_target_pairs={{0,2},{1,3},{2,0},{3,1},{4,6},{5,7},{6,4},{7,5},{8,10},{9,11},{10,... | collective-permute-start | bytes 15368 | tf_op jit(solution)/shard_map/ppermute | solution.py:168
  17.2 4.9 %collective-permute-start.2 = (f32[5,256]{1,0:T(8,128)S(1)}, f32[5,256]{1,0:T(8,128)S(1)}, u32[]{:S(2)}, u32[]{:S(2)}) collective-permute-start(f32[5,256]{1,0:T(8,128)S(1)} %add.209), channel_id=1, source_target_pairs={{0,4},{1,5},{2,6},{3,7},{4,0},{5,1},{6,2},{7,3},{8,12},{9,13},{10,... | collective-permute-start | bytes 15368 | tf_op jit(solution)/shard_map/ppermute | solution.py:168
  22.1 7.6 %collective-permute-start.3 = (f32[5,256]{1,0:T(8,128)S(1)}, f32[5,256]{1,0:T(8,128)S(1)}, u32[]{:S(2)}, u32[]{:S(2)}) collective-permute-start(f32[5,256]{1,0:T(8,128)S(1)} %add.210), channel_id=1, source_target_pairs={{0,8},{1,9},{2,10},{3,11},{4,12},{5,13},{6,14},{7,15},{8,0},{9,1},... | collective-permute-start | bytes 15368 | tf_op jit(solution)/shard_map/ppermute | solution.py:168
  33.2 10.8 %collective-permute-start.4 = (f32[37,12,128]{2,0,1:T(8,128)S(1)}, f32[37,12,128]{2,0,1:T(8,128)S(1)}, u32[]{:S(2)}, u32[]{:S(2)}) collective-permute-start(f32[37,12,128]{2,0,1:T(8,128)S(1)} %pad_maximum_fusion.1), channel_id=1, source_target_pairs={{16,0},{32,16},{48,32},{64,48},{80,64},{96,80},{112,96},{128,112},... | collective-permute-start | bytes 681992 | tf_op jit(solution)/shard_map/ppermute | solution.py:22
  34.5 14.1 %collective-permute-start.5 = (f32[37,12,128]{2,0,1:T(8,128)S(1)}, f32[37,12,128]{2,0,1:T(8,128)S(1)}, u32[]{:S(2)}, u32[]{:S(2)}) collective-permute-start(f32[37,12,128]{2,0,1:T(8,128)S(1)} %pad_maximum_fusion.1), channel_id=1, source_target_pairs={{32,0},{48,16},{64,32},{80,48},{96,64},{112,80},{128,96},{144,112}... | collective-permute-start | bytes 681992 | tf_op jit(solution)/shard_map/ppermute | solution.py:22
  44.0 11.5 %collective-permute-start.10 = (f32[37,12,128]{2,0,1:T(8,128)S(1)}, f32[37,12,128]{2,0,1:T(8,128)S(1)}, u32[]{:S(2)}, u32[]{:S(2)}) collective-permute-start(f32[37,12,128]{2,0,1:T(8,128)S(1)} %pad_maximum_fusion.5), channel_id=1, source_target_pairs={{0,32},{16,48},{32,64},{48,80},{64,96},{80,112},{96,128},{112,144}... | collective-permute-start | bytes 681992 | tf_op jit(solution)/shard_map/ppermute | solution.py:22
  48.7 10.6 %collective-permute-start.9 = (f32[37,12,128]{2,0,1:T(8,128)S(1)}, f32[37,12,128]{2,0,1:T(8,128)S(1)}, u32[]{:S(2)}, u32[]{:S(2)}) collective-permute-start(f32[37,12,128]{2,0,1:T(8,128)S(1)} %pad_maximum_fusion.5), channel_id=1, source_target_pairs={{0,16},{16,32},{32,48},{48,64},{64,80},{80,96},{96,112},{112,128},... | collective-permute-start | bytes 681992 | tf_op jit(solution)/shard_map/ppermute | solution.py:22
  55.5 84.3 %collective-permute-start.17 = (f32[75,2,128]{2,1,0:T(2,128)S(1)}, f32[75,2,128]{2,1,0:T(2,128)S(1)}, u32[]{:S(2)}, u32[]{:S(2)}) collective-permute-start(f32[75,2,128]{2,1,0:T(2,128)S(1)} %reshape.287), channel_id=1, source_target_pairs={{32,0},{48,16},{64,32},{80,48},{96,64},{112,80},{128,96},{144,112}... | collective-permute-start | bytes 230408 | tf_op jit(solution)/shard_map/ppermute | solution.py:22
  59.3 14.7 %collective-permute-start.6 = (f32[37,12,128]{2,0,1:T(8,128)S(1)}, f32[37,12,128]{2,0,1:T(8,128)S(1)}, u32[]{:S(2)}, u32[]{:S(2)}) collective-permute-start(f32[37,12,128]{2,0,1:T(8,128)S(1)} %pad_maximum_fusion.2), channel_id=1, source_target_pairs={{32,0},{48,16},{64,32},{80,48},{96,64},{112,80},{128,96},{144,112}... | collective-permute-start | bytes 681992 | tf_op jit(solution)/shard_map/ppermute | solution.py:22
  74.0 10.1 %collective-permute-start.11 = (f32[37,12,128]{2,0,1:T(8,128)S(1)}, f32[37,12,128]{2,0,1:T(8,128)S(1)}, u32[]{:S(2)}, u32[]{:S(2)}) collective-permute-start(f32[37,12,128]{2,0,1:T(8,128)S(1)} %pad_maximum_fusion.6), channel_id=1, source_target_pairs={{0,32},{16,48},{32,64},{48,80},{64,96},{80,112},{96,128},{112,144}... | collective-permute-start | bytes 681992 | tf_op jit(solution)/shard_map/ppermute | solution.py:22
  84.1 13.5 %collective-permute-start.7 = (f32[37,12,128]{2,0,1:T(8,128)S(1)}, f32[37,12,128]{2,0,1:T(8,128)S(1)}, u32[]{:S(2)}, u32[]{:S(2)}) collective-permute-start(f32[37,12,128]{2,0,1:T(8,128)S(1)} %pad_maximum_fusion.3), channel_id=1, source_target_pairs={{64,0},{80,16},{96,32},{112,48},{128,64},{144,80},{160,96},{176,11... | collective-permute-start | bytes 681992 | tf_op jit(solution)/shard_map/ppermute | solution.py:22
  97.5 9.8 %collective-permute-start.12 = (f32[37,12,128]{2,0,1:T(8,128)S(1)}, f32[37,12,128]{2,0,1:T(8,128)S(1)}, u32[]{:S(2)}, u32[]{:S(2)}) collective-permute-start(f32[37,12,128]{2,0,1:T(8,128)S(1)} %pad_maximum_fusion.7), channel_id=1, source_target_pairs={{0,64},{16,80},{32,96},{48,112},{64,128},{80,144},{96,160},{112,17... | collective-permute-start | bytes 681992 | tf_op jit(solution)/shard_map/ppermute | solution.py:22
  107.3 9.6 %collective-permute-start.8 = (f32[37,12,128]{2,0,1:T(8,128)S(1)}, f32[37,12,128]{2,0,1:T(8,128)S(1)}, u32[]{:S(2)}, u32[]{:S(2)}) collective-permute-start(f32[37,12,128]{2,0,1:T(8,128)S(1)} %pad_maximum_fusion.4), channel_id=1, source_target_pairs={{128,0},{144,16},{160,32},{176,48},{192,64},{208,80},{224,96},{240... | collective-permute-start | bytes 681992 | tf_op jit(solution)/shard_map/ppermute | solution.py:22
  116.9 5.1 %collective-permute-start.13 = (f32[37,12,128]{2,0,1:T(8,128)S(1)}, f32[37,12,128]{2,0,1:T(8,128)S(1)}, u32[]{:S(2)}, u32[]{:S(2)}) collective-permute-start(f32[37,12,128]{2,0,1:T(8,128)S(1)} %pad_maximum_fusion.8), channel_id=1, source_target_pairs={{0,128},{16,144},{32,160},{48,176},{64,192},{80,208},{96,224},{112... | collective-permute-start | bytes 681992 | tf_op jit(solution)/shard_map/ppermute | solution.py:22
  124.5 1.2 collective-permute-start.18
  125.7 3.7 %collective-permute-start.19 = (f32[5,256]{1,0:T(8,128)S(1)}, f32[5,256]{1,0:T(8,128)S(1)}, u32[]{:S(2)}, u32[]{:S(2)}) collective-permute-start(f32[5,256]{1,0:T(8,128)S(1)} %add.239), channel_id=1, source_target_pairs={{0,2},{1,3},{2,0},{3,1},{4,6},{5,7},{6,4},{7,5},{8,10},{9,11},{10,... | collective-permute-start | bytes 15368 | tf_op jit(solution)/shard_map/ppermute | solution.py:168
  129.4 4.6 %collective-permute-start.20 = (f32[5,256]{1,0:T(8,128)S(1)}, f32[5,256]{1,0:T(8,128)S(1)}, u32[]{:S(2)}, u32[]{:S(2)}) collective-permute-start(f32[5,256]{1,0:T(8,128)S(1)} %add.240), channel_id=1, source_target_pairs={{0,4},{1,5},{2,6},{3,7},{4,0},{5,1},{6,2},{7,3},{8,12},{9,13},{10,... | collective-permute-start | bytes 15368 | tf_op jit(solution)/shard_map/ppermute | solution.py:168
  133.9 8.1 %collective-permute-start.21 = (f32[5,256]{1,0:T(8,128)S(1)}, f32[5,256]{1,0:T(8,128)S(1)}, u32[]{:S(2)}, u32[]{:S(2)}) collective-permute-start(f32[5,256]{1,0:T(8,128)S(1)} %add.241), channel_id=1, source_target_pairs={{0,8},{1,9},{2,10},{3,11},{4,12},{5,13},{6,14},{7,15},{8,0},{9,1},... | collective-permute-start | bytes 15368 | tf_op jit(solution)/shard_map/ppermute | solution.py:168
  142.0 5.2 %collective-permute-start.22 = (f32[5,2,128]{2,1,0:T(2,128)S(1)}, f32[5,2,128]{2,1,0:T(2,128)S(1)}, u32[]{:S(2)}, u32[]{:S(2)}) collective-permute-start(f32[5,2,128]{2,1,0:T(2,128)S(1)} %reshape.289), channel_id=1, source_target_pairs={{0,32},{16,48},{32,64},{48,80},{64,96},{80,112},{96,128},{112,144}... | collective-permute-start | bytes 15368 | tf_op jit(solution)/shard_map/ppermute | solution.py:22
  143.3 4.0 %collective-permute-start.23 = (f32[5,2,128]{2,1,0:T(2,128)S(1)}, f32[5,2,128]{2,1,0:T(2,128)S(1)}, u32[]{:S(2)}, u32[]{:S(2)}) collective-permute-start(f32[5,2,128]{2,1,0:T(2,128)S(1)} %reshape.289), channel_id=1, source_target_pairs={{0,16},{16,32},{32,48},{48,64},{64,80},{80,96},{96,112},{112,128},... | collective-permute-start | bytes 15368 | tf_op jit(solution)/shard_map/ppermute | solution.py:22
  144.6 10.1 %collective-permute-start.24 = (f32[5,2,128]{2,1,0:T(2,128)S(1)}, f32[5,2,128]{2,1,0:T(2,128)S(1)}, u32[]{:S(2)}, u32[]{:S(2)}) collective-permute-start(f32[5,2,128]{2,1,0:T(2,128)S(1)} %reshape.289), channel_id=1, source_target_pairs={{16,0},{32,16},{48,32},{64,48},{80,64},{96,80},{112,96},{128,112},... | collective-permute-start | bytes 15368 | tf_op jit(solution)/shard_map/ppermute | solution.py:22
  145.9 12.8 %collective-permute-start.25 = (f32[5,2,128]{2,1,0:T(2,128)S(1)}, f32[5,2,128]{2,1,0:T(2,128)S(1)}, u32[]{:S(2)}, u32[]{:S(2)}) collective-permute-start(f32[5,2,128]{2,1,0:T(2,128)S(1)} %reshape.289), channel_id=1, source_target_pairs={{32,0},{48,16},{64,32},{80,48},{96,64},{112,80},{128,96},{144,112}... | collective-permute-start | bytes 15368 | tf_op jit(solution)/shard_map/ppermute | solution.py:22
  163.1 1.1 collective-permute-start.26
  164.3 3.6 %collective-permute-start.27 = (f32[26]{0:T(128)S(1)}, f32[26]{0:T(128)S(1)}, u32[]{:S(2)}, u32[]{:S(2)}) collective-permute-start(f32[26]{0:T(128)S(1)} %fusion.54), channel_id=1, source_target_pairs={{0,2},{1,3},{2,0},{3,1},{4,6},{5,7},{6,4},{7,5},{8,10},{9,11},{10,... | collective-permute-start | bytes 320 | tf_op jit(solution)/shard_map/ppermute | solution.py:168
  167.9 4.4 %collective-permute-start.28 = (f32[26]{0:T(128)S(1)}, f32[26]{0:T(128)S(1)}, u32[]{:S(2)}, u32[]{:S(2)}) collective-permute-start(f32[26]{0:T(128)S(1)} %add.246), channel_id=1, source_target_pairs={{0,4},{1,5},{2,6},{3,7},{4,0},{5,1},{6,2},{7,3},{8,12},{9,13},{10,... | collective-permute-start | bytes 320 | tf_op jit(solution)/shard_map/ppermute | solution.py:168
  172.3 7.4 %collective-permute-start.29 = (f32[26]{0:T(128)S(1)}, f32[26]{0:T(128)S(1)}, u32[]{:S(2)}, u32[]{:S(2)}) collective-permute-start(f32[26]{0:T(128)S(1)} %add.247), channel_id=1, source_target_pairs={{0,8},{1,9},{2,10},{3,11},{4,12},{5,13},{6,14},{7,15},{8,0},{9,1},... | collective-permute-start | bytes 320 | tf_op jit(solution)/shard_map/ppermute | solution.py:168
  179.8 3.5 %collective-permute-start.30 = (f32[26]{0:T(128)S(1)}, f32[26]{0:T(128)S(1)}, u32[]{:S(2)}, u32[]{:S(2)}) collective-permute-start(f32[26]{0:T(128)S(1)} %add.248), channel_id=1, source_target_pairs={{0,16},{16,0},{32,48},{48,32},{64,80},{80,64},{96,112},{112,96},{1... | collective-permute-start | bytes 320 | tf_op jit(solution)/shard_map/ppermute | solution.py:168
  183.3 5.9 %collective-permute-start.31 = (f32[26]{0:T(128)S(1)}, f32[26]{0:T(128)S(1)}, u32[]{:S(2)}, u32[]{:S(2)}) collective-permute-start(f32[26]{0:T(128)S(1)} %add.249), channel_id=1, source_target_pairs={{0,32},{16,48},{32,0},{48,16},{64,96},{80,112},{96,64},{112,80},{1... | collective-permute-start | bytes 320 | tf_op jit(solution)/shard_map/ppermute | solution.py:168
  189.3 3.5 %collective-permute-start.32 = (f32[26]{0:T(128)S(1)}, f32[26]{0:T(128)S(1)}, u32[]{:S(2)}, u32[]{:S(2)}) collective-permute-start(f32[26]{0:T(128)S(1)} %add.250), channel_id=1, source_target_pairs={{0,64},{16,80},{32,96},{48,112},{64,0},{80,16},{96,32},{112,48},{1... | collective-permute-start | bytes 320 | tf_op jit(solution)/shard_map/ppermute | solution.py:168
  192.8 6.1 %collective-permute-start.33 = (f32[26]{0:T(128)S(1)}, f32[26]{0:T(128)S(1)}, u32[]{:S(2)}, u32[]{:S(2)}) collective-permute-start(f32[26]{0:T(128)S(1)} %add.251), channel_id=1, source_target_pairs={{0,128},{16,144},{32,160},{48,176},{64,192},{80,208},{96,224},{112... | collective-permute-start | bytes 320 | tf_op jit(solution)/shard_map/ppermute | solution.py:168
  198.9 0.7 copy-start.2
  198.9 0.7 copy-start.5
  199.7 0.7 copy-start.3

commit v4 on v3

--- a/solution.py
+++ b/solution.py
@@ -130,24 +130,30 @@
     return passed_along(block, "sec", distance)
 
 
+def fetched(state, distance, sign):
+    rate, drive = state
+    got = received(jnp.concatenate([rate, drive], axis=0), sign * distance)
+    return got[:1], got[1:]
+
+
+def scan_first(rate, drive, sign):
+    near_a, near_b = fetched((rate, drive), 1, sign)
+    if lax.axis_size("sec") <= 2:
+        return (near_a, near_b), 1
+    far_a, far_b = fetched((rate, drive), 2, sign)
+    return (near_a * far_a, near_a * far_b + near_b), 2
+
+
+def scan_next(state, span, sign):
+    got_a, got_b = fetched(state, span, sign)
+    return (state[0] * got_a, state[0] * got_b + state[1]), span * 2
+
+
 def exclusive_inflow(rate, drive, sign):
-    count = lax.axis_size("sec")
-
-    def fetch(a, b, distance):
-        got = received(jnp.concatenate([a, b], axis=0), sign * distance)
-        return got[:1], got[1:]
-
-    near_a, near_b = fetch(rate, drive, 1)
-    span = 1
-    if count > 2:
-        far_a, far_b = fetch(rate, drive, 2)
-        near_a, near_b = near_a * far_a, near_a * far_b + near_b
-        span = 2
-    while span < count - 1:
-        got_a, got_b = fetch(near_a, near_b, span)
-        near_a, near_b = near_a * got_a, near_a * got_b + near_b
-        span *= 2
-    return near_b
+    state, span = scan_first(rate, drive, sign)
+    while span < lax.axis_size("sec") - 1:
+        state, span = scan_next(state, span, sign)
+    return state[1]
 
 
 def with_halo(array, width):
@@ -170,6 +176,62 @@
     return block
 
 
+def local_sweep(carry_rate, drive):
+    half_nodes = NXI // 2
+    shape = (1, half_nodes) + drive.shape[2:]
+    prod_neg, local_neg = lax.associative_scan(
+        affine_combine,
+        (jnp.broadcast_to(carry_rate[:, :half_nodes], shape), drive[:, :half_nodes]),
+        reverse=True,
+        axis=2,
+    )
+    prod_pos, local_pos = lax.associative_scan(
+        affine_combine,
+        (jnp.broadcast_to(carry_rate[:, half_nodes:], shape), drive[:, half_nodes:]),
+        axis=2,
+    )
+    return prod_neg, local_neg, prod_pos, local_pos
+
+
+def joined_field(sweep, inflow_neg, inflow_pos):
+    prod_neg, local_neg, prod_pos, local_pos = sweep
+    field_neg = local_neg + prod_neg * inflow_neg[:, :, None, :]
+    field_pos = local_pos + prod_pos * inflow_pos[:, :, None, :]
+    return jnp.concatenate([field_neg, field_pos], axis=1)
+
+
+def swept_field(carry_rate, drive):
+    sweep = local_sweep(carry_rate, drive)
+    inflow_pos = exclusive_inflow(sweep[2][:, :, -1], sweep[3][:, :, -1], 1)
+    inflow_neg = exclusive_inflow(sweep[0][:, :, 0], sweep[1][:, :, 0], -1)
+    return joined_field(sweep, inflow_neg, inflow_pos)
+
+
+def scan_beside_sum(sweep, block, axis):
+    count = lax.axis_size("sec")
+    pos, span = scan_first(sweep[2][:, :, -1], sweep[3][:, :, -1], 1)
+    neg, _ = scan_first(sweep[0][:, :, 0], sweep[1][:, :, 0], -1)
+    members = lax.axis_size(axis)
+    bit = 1
+    if members & (members - 1):
+        block = lax.psum(block, axis)
+        bit = members
+    elif bit < members:
+        block = block + lax.ppermute(block, axis, [(i, i ^ bit) for i in range(members)])
+        bit *= 2
+    pos, neg, block = lax.optimization_barrier((pos, neg, block))
+    while span < count - 1 or bit < members:
+        if span < count - 1:
+            pos, next_span = scan_next(pos, span, 1)
+            neg, _ = scan_next(neg, span, -1)
+            span = next_span
+        if bit < members:
+            block = block + lax.ppermute(block, axis, [(i, i ^ bit) for i in range(members)])
+            bit *= 2
+        pos, neg, block = lax.optimization_barrier((pos, neg, block))
+    return joined_field(sweep, neg[1], pos[1]), block
+
+
 def body(distribution, collision, lower_blocks, upper_blocks, diag_inverse):
     node_count = distribution.shape[0]
     cell_count = distribution.shape[1]
@@ -185,35 +247,22 @@
     rebuild = lax.dynamic_slice_in_dim(jnp.asarray(rebuild_np, jnp.float32), offset, node_count, 1)
     node_mass = lax.dynamic_slice_in_dim(all_mass, offset, node_count, 0)
     line_signed = jnp.asarray(along_x[:NXI], jnp.float32)
-    old_moments = tree_sum(jnp.dot(weighted, distribution, precision=HIGH), ("vel",))
-    target = jnp.dot(rebuild.T, old_moments, precision=HIGH)
     total_length = length * lax.axis_size("sec")
     thickness = collision.reshape(1, 1, length, TUBES)
     node_speed = jnp.abs(line_signed).reshape(1, NXI, 1, 1)
     denominator = node_speed * total_length + thickness + pseudo_rate
     carry_rate = node_speed * total_length / denominator
-    drive_term = (
-        thickness * target.reshape(node_rows, NXI, length, TUBES)
-        + pseudo_rate * distribution.reshape(node_rows, NXI, length, TUBES)
-    ) / denominator
-    prod_neg, local_neg = lax.associative_scan(
-        affine_combine,
-        (jnp.broadcast_to(carry_rate[:, :half_nodes], (1, half_nodes, length, TUBES)),
-         drive_term[:, :half_nodes]),
-        reverse=True,
-        axis=2,
-    )
-    prod_pos, local_pos = lax.associative_scan(
-        affine_combine,
-        (jnp.broadcast_to(carry_rate[:, half_nodes:], (1, NXI - half_nodes, length, TUBES)),
-         drive_term[:, half_nodes:]),
-        axis=2,
-    )
-    inflow_pos = exclusive_inflow(prod_pos[:, :, -1], local_pos[:, :, -1], 1)
-    inflow_neg = exclusive_inflow(prod_neg[:, :, 0], local_neg[:, :, 0], -1)
-    field_neg = local_neg + prod_neg * inflow_neg[:, :, None, :]
-    field_pos = local_pos + prod_pos * inflow_pos[:, :, None, :]
-    half_field = jnp.concatenate([field_neg, field_pos], axis=1).reshape(node_count, cell_count)
+    own_drive = pseudo_rate * distribution.reshape(node_rows, NXI, length, TUBES) / denominator
+    own_field, old_moments = scan_beside_sum(
+        local_sweep(carry_rate, own_drive),
+        jnp.dot(weighted, distribution, precision=HIGH),
+        "vel",
+    )
+    moment_drive = thickness * old_moments.reshape(5, 1, length, TUBES) / denominator
+    moment_field = swept_field(carry_rate, moment_drive)
+    basis = rebuild.reshape(5, node_rows, NXI, 1, 1)
+    half_field = own_field + jnp.sum(basis * moment_field[:, None], axis=0)
+    half_field = half_field.reshape(node_count, cell_count)
     half_moments = tree_sum(jnp.dot(weighted, half_field, precision=HIGH), ("vel",))
     residual = (half_moments - old_moments).reshape(5, length, TUBES)
     width = min(-(-JACOBI // length), lax.axis_size("sec") - 1)

time: 207 us -> 232 us (1.12)
  starting transfers between devices: 87.6 us -> 131 us
  waiting for transfers between devices: 91.1 us -> 75.3 us
    ppermute x18 -> x28, starting transfers between devices: 47.1 us -> 93.1 us  [passed_along(): return lax.ppermute(block, axis, route)]
    ppermute x18 -> x28, waiting for transfers between devices: 64.4 us -> 46.3 us  [passed_along(): return lax.ppermute(block, axis, route)]
    ppermute x16 -> x12, starting transfers between devices: 40.4 us -> 28.2 us  [tree_sum(): lax.ppermute(block, axis, [(i, i ^ bit) for i in range(count)])]
    ppermute x0 -> x4, starting transfers between devices: none -> 9.61 us  [scan_beside_sum(): lax.ppermute(block, axis, [(i, i ^ bit) for i in range(members)])]
    ppermute x0 -> x4, waiting for transfers between devices: none -> 7.68 us  [scan_beside_sum(): lax.ppermute(block, axis, [(i, i ^ bit) for i in range(members)])]
    ppermute x16 -> x12, waiting for transfers between devices: 26.7 us -> 21.3 us  [tree_sum(): lax.ppermute(block, axis, [(i, i ^ bit) for i in range(count)])]
  transfers between devices with their start and end apart: 34 -> 44, of which waited for: 25 -> 29; matrix products, arithmetic and copies ran while one was open for 6% -> 4% of each run, Pallas kernels for 0% -> 0%
where the time goes in v4:
time: 232 us; the launch traced here: 230 us
  starting transfers between devices  131 us (56%)
  waiting for transfers between devices  75.3 us (32%)
  other arithmetic  10.4 us (4%)
  local copies, waits for them, and re-layouts  6.31 us (3%)
  matrix products  4.73 us (2%)
    ppermute x28, starting transfers between devices, passed_along(): return lax.ppermute(block, axis, route)  93.1 us
    ppermute x28, waiting for transfers between devices, passed_along(): return lax.ppermute(block, axis, route)  46.3 us
    ppermute x12, starting transfers between devices, tree_sum(): lax.ppermute(block, axis, [(i, i ^ bit) for i in range(count)])  28.2 us
    ppermute x12, waiting for transfers between devices, tree_sum(): lax.ppermute(block, axis, [(i, i ^ bit) for i in range(count)])  21.3 us
    ppermute x4, starting transfers between devices, scan_beside_sum(): lax.ppermute(block, axis, [(i, i ^ bit) for i in range(members)])  9.61 us
    ppermute x4, waiting for transfers between devices, scan_beside_sum(): lax.ppermute(block, axis, [(i, i ^ bit) for i in range(members)])  7.68 us
  transfers between devices with their start and end apart: 44, of which 29 were waited for; matrix products, arithmetic and copies ran while one was open for 4% of the time, Pallas kernels for 0%

profile of v4, /device:TPU:32, one launch (start us, length us, event | category | flops | bytes accessed | tf_op | source)
XLA Modules:
  0.0 229.6 jit_solution(17472708950247997909)
XLA Ops:
  2.2 1.6 reshape.302
  7.7 4.5 %collective-permute-start = (f32[37,12,128]{2,0,1:T(8,128)}, f32[37,12,128]{2,0,1:T(8,128)S(1)}, u32[]{:S(2)}, u32[]{:S(2)}) collective-permute-start(f32[37,12,128]{2,0,1:T(8,128)} %pad_maximum_fusion), channel_id=1, source_target_pairs={{0,16},{16,32},{32,48},{48,64},{64,80},{80,96},{96,112},{112,128},... | collective-permute-start | bytes 681992 | tf_op jit(solution)/shard_map/ppermute | solution.py:22
  12.2 6.7 %collective-permute-start.1 = (f32[37,12,128]{2,0,1:T(8,128)}, f32[37,12,128]{2,0,1:T(8,128)S(1)}, u32[]{:S(2)}, u32[]{:S(2)}) collective-permute-start(f32[37,12,128]{2,0,1:T(8,128)} %pad_maximum_fusion), channel_id=1, source_target_pairs={{0,32},{16,48},{32,64},{48,80},{64,96},{80,112},{96,128},{112,144}... | collective-permute-start | bytes 681992 | tf_op jit(solution)/shard_map/ppermute | solution.py:22
  21.4 5.4 %collective-permute-start.24 = (f32[75,2,128]{2,1,0:T(2,128)S(1)}, f32[75,2,128]{2,1,0:T(2,128)}, u32[]{:S(2)}, u32[]{:S(2)}) collective-permute-start(f32[75,2,128]{2,1,0:T(2,128)S(1)} %reshape.304), channel_id=1, source_target_pairs={{0,32},{16,48},{32,64},{48,80},{64,96},{80,112},{96,128},{112,144}... | collective-permute-start | bytes 230408 | tf_op jit(solution)/shard_map/ppermute | solution.py:22
  26.8 4.4 %collective-permute-start.25 = (f32[75,2,128]{2,1,0:T(2,128)S(1)}, f32[75,2,128]{2,1,0:T(2,128)}, u32[]{:S(2)}, u32[]{:S(2)}) collective-permute-start(f32[75,2,128]{2,1,0:T(2,128)S(1)} %reshape.304), channel_id=1, source_target_pairs={{0,16},{16,32},{32,48},{48,64},{64,80},{80,96},{96,112},{112,128},... | collective-permute-start | bytes 230408 | tf_op jit(solution)/shard_map/ppermute | solution.py:22
  34.3 3.5 %collective-permute-done.7 = f32[5,256]{1,0:T(8,128)S(1)} collective-permute-done((f32[5,256]{1,0:T(8,128)S(1)}, f32[5,256]{1,0:T(8,128)S(1)}, u32[]{:S(2)}, u32[]{:S(2)}) %collective-permute-start.7) | collective-permute-done | bytes 5152 | tf_op jit(solution)/shard_map/ppermute | solution.py:229
  37.8 6.1 %collective-permute-start.5 = (f32[37,12,128]{2,0,1:T(8,128)S(1)}, f32[37,12,128]{2,0,1:T(8,128)S(1)}, u32[]{:S(2)}, u32[]{:S(2)}) collective-permute-start(f32[37,12,128]{2,0,1:T(8,128)S(1)} %pad_maximum_fusion.2), channel_id=1, source_target_pairs={{0,32},{16,48},{32,64},{48,80},{64,96},{80,112},{96,128},{112,144}... | collective-permute-start | bytes 681992 | tf_op jit(solution)/shard_map/ppermute | solution.py:22
  44.0 4.0 %collective-permute-done.5 = f32[37,12,128]{2,0,1:T(8,128)S(1)} collective-permute-done((f32[37,12,128]{2,0,1:T(8,128)S(1)}, f32[37,12,128]{2,0,1:T(8,128)S(1)}, u32[]{:S(2)}, u32[]{:S(2)}) %collective-permute-start.5) | collective-permute-done | bytes 227360 | tf_op jit(solution)/shard_map/ppermute | solution.py:22
  50.3 3.4 %collective-permute-start.10 = (f32[5,256]{1,0:T(8,128)S(1)}, f32[5,256]{1,0:T(8,128)S(1)}, u32[]{:S(2)}, u32[]{:S(2)}) collective-permute-start(f32[5,256]{1,0:T(8,128)S(1)} %add.288), channel_id=1, source_target_pairs={{0,4},{1,5},{2,6},{3,7},{4,0},{5,1},{6,2},{7,3},{8,12},{9,13},{10,... | collective-permute-start | bytes 15368 | tf_op jit(solution)/shard_map/ppermute | solution.py:229
  55.3 7.3 %collective-permute-start.8 = (f32[37,12,128]{2,0,1:T(8,128)S(1)}, f32[37,12,128]{2,0,1:T(8,128)S(1)}, u32[]{:S(2)}, u32[]{:S(2)}) collective-permute-start(f32[37,12,128]{2,0,1:T(8,128)S(1)} %pad_maximum_fusion.4), channel_id=1, source_target_pairs={{0,64},{16,80},{32,96},{48,112},{64,128},{80,144},{96,160},{112,17... | collective-permute-start | bytes 681992 | tf_op jit(solution)/shard_map/ppermute | solution.py:22
  62.7 3.6 %collective-permute-done.8 = f32[37,12,128]{2,0,1:T(8,128)S(1)} collective-permute-done((f32[37,12,128]{2,0,1:T(8,128)S(1)}, f32[37,12,128]{2,0,1:T(8,128)S(1)}, u32[]{:S(2)}, u32[]{:S(2)}) %collective-permute-start.8) | collective-permute-done | bytes 227360 | tf_op jit(solution)/shard_map/ppermute | solution.py:22
  67.7 6.0 %collective-permute-start.13 = (f32[5,256]{1,0:T(8,128)S(1)}, f32[5,256]{1,0:T(8,128)S(1)}, u32[]{:S(2)}, u32[]{:S(2)}) collective-permute-start(f32[5,256]{1,0:T(8,128)S(1)} %add.291), channel_id=1, source_target_pairs={{0,8},{1,9},{2,10},{3,11},{4,12},{5,13},{6,14},{7,15},{8,0},{9,1},... | collective-permute-start | bytes 15368 | tf_op jit(solution)/shard_map/ppermute | solution.py:229
  75.4 8.1 %collective-permute-start.11 = (f32[37,12,128]{2,0,1:T(8,128)S(1)}, f32[37,12,128]{2,0,1:T(8,128)S(1)}, u32[]{:S(2)}, u32[]{:S(2)}) collective-permute-start(f32[37,12,128]{2,0,1:T(8,128)S(1)} %pad_maximum_fusion.6), channel_id=1, source_target_pairs={{0,128},{16,144},{32,160},{48,176},{64,192},{80,208},{96,224},{112... | collective-permute-start | bytes 681992 | tf_op jit(solution)/shard_map/ppermute | solution.py:22
  83.5 3.6 %collective-permute-done.11 = f32[37,12,128]{2,0,1:T(8,128)S(1)} collective-permute-done((f32[37,12,128]{2,0,1:T(8,128)S(1)}, f32[37,12,128]{2,0,1:T(8,128)S(1)}, u32[]{:S(2)}, u32[]{:S(2)}) %collective-permute-start.11) | collective-permute-done | bytes 227360 | tf_op jit(solution)/shard_map/ppermute | solution.py:22
  87.3 3.0 %collective-permute-start.19 = (f32[6,12,128]{2,1,0:T(8,128)S(1)}, f32[6,12,128]{2,1,0:T(8,128)S(1)}, u32[]{:S(2)}, u32[]{:S(2)}) collective-permute-start(f32[6,12,128]{2,1,0:T(8,128)S(1)} %pad_maximum_fusion.14), channel_id=1, source_target_pairs={{0,16},{16,32},{32,48},{48,64},{64,80},{80,96},{96,112},{112,128},... | collective-permute-start | bytes 110600 | tf_op jit(solution)/shard_map/ppermute | solution.py:22
  90.4 3.5 %collective-permute-start.20 = (f32[6,12,128]{2,1,0:T(8,128)S(1)}, f32[6,12,128]{2,1,0:T(8,128)S(1)}, u32[]{:S(2)}, u32[]{:S(2)}) collective-permute-start(f32[6,12,128]{2,1,0:T(8,128)S(1)} %pad_maximum_fusion.14), channel_id=1, source_target_pairs={{0,32},{16,48},{32,64},{48,80},{64,96},{80,112},{96,128},{112,144}... | collective-permute-start | bytes 110600 | tf_op jit(solution)/shard_map/ppermute | solution.py:22
  97.0 3.9 %collective-permute-done.14 = f32[6,12,128]{2,1,0:T(8,128)S(1)} collective-permute-done((f32[6,12,128]{2,1,0:T(8,128)S(1)}, f32[6,12,128]{2,1,0:T(8,128)S(1)}, u32[]{:S(2)}, u32[]{:S(2)}) %collective-permute-start.14) | collective-permute-done | bytes 36896 | tf_op jit(solution)/shard_map/ppermute | solution.py:22
  102.2 2.7 %collective-permute-done.15 = f32[6,12,128]{2,1,0:T(8,128)S(1)} collective-permute-done((f32[6,12,128]{2,1,0:T(8,128)S(1)}, f32[6,12,128]{2,1,0:T(8,128)S(1)}, u32[]{:S(2)}, u32[]{:S(2)}) %collective-permute-start.15) | collective-permute-done | bytes 36896 | tf_op jit(solution)/shard_map/ppermute | solution.py:22
  104.9 6.3 %collective-permute-start.21 = (f32[6,12,128]{2,1,0:T(8,128)S(1)}, f32[6,12,128]{2,1,0:T(8,128)S(1)}, u32[]{:S(2)}, u32[]{:S(2)}) collective-permute-start(f32[6,12,128]{2,1,0:T(8,128)S(1)} %pad_maximum_fusion.15), channel_id=1, source_target_pairs={{0,32},{16,48},{32,64},{48,80},{64,96},{80,112},{96,128},{112,144}... | collective-permute-start | bytes 110600 | tf_op jit(solution)/shard_map/ppermute | solution.py:22
  111.2 1.7 collective-permute-done.21
  114.2 6.5 %collective-permute-done.16 = f32[6,12,128]{2,1,0:T(8,128)S(1)} collective-permute-done((f32[6,12,128]{2,1,0:T(8,128)S(1)}, f32[6,12,128]{2,1,0:T(8,128)S(1)}, u32[]{:S(2)}, u32[]{:S(2)}) %collective-permute-start.16) | collective-permute-done | bytes 36896 | tf_op jit(solution)/shard_map/ppermute | solution.py:22
  120.7 5.2 %collective-permute-start.22 = (f32[6,12,128]{2,1,0:T(8,128)S(1)}, f32[6,12,128]{2,1,0:T(8,128)S(1)}, u32[]{:S(2)}, u32[]{:S(2)}) collective-permute-start(f32[6,12,128]{2,1,0:T(8,128)S(1)} %pad_maximum_fusion.16), channel_id=1, source_target_pairs={{0,64},{16,80},{32,96},{48,112},{64,128},{80,144},{96,160},{112,17... | collective-permute-start | bytes 110600 | tf_op jit(solution)/shard_map/ppermute | solution.py:22
  126.0 1.7 collective-permute-done.22
  129.0 5.2 %collective-permute-done.17 = f32[6,12,128]{2,1,0:T(8,128)S(1)} collective-permute-done((f32[6,12,128]{2,1,0:T(8,128)S(1)}, f32[6,12,128]{2,1,0:T(8,128)S(1)}, u32[]{:S(2)}, u32[]{:S(2)}) %collective-permute-start.17) | collective-permute-done | bytes 36896 | tf_op jit(solution)/shard_map/ppermute | solution.py:22
  134.2 6.7 %collective-permute-start.23 = (f32[6,12,128]{2,1,0:T(8,128)S(1)}, f32[6,12,128]{2,1,0:T(8,128)S(1)}, u32[]{:S(2)}, u32[]{:S(2)}) collective-permute-start(f32[6,12,128]{2,1,0:T(8,128)S(1)} %pad_maximum_fusion.17), channel_id=1, source_target_pairs={{0,128},{16,144},{32,160},{48,176},{64,192},{80,208},{96,224},{112... | collective-permute-start | bytes 110600 | tf_op jit(solution)/shard_map/ppermute | solution.py:22
  140.9 1.7 collective-permute-done.23
  144.0 6.1 %collective-permute-done.18 = f32[6,12,128]{2,1,0:T(8,128)S(1)} collective-permute-done((f32[6,12,128]{2,1,0:T(8,128)S(1)}, f32[6,12,128]{2,1,0:T(8,128)S(1)}, u32[]{:S(2)}, u32[]{:S(2)}) %collective-permute-start.18) | collective-permute-done | bytes 36896 | tf_op jit(solution)/shard_map/ppermute | solution.py:22
  154.4 3.3 %collective-permute-done.29 = f32[5,256]{1,0:T(8,128)S(1)} collective-permute-done((f32[5,256]{1,0:T(8,128)S(1)}, f32[5,256]{1,0:T(8,128)S(1)}, u32[]{:S(2)}, u32[]{:S(2)}) %collective-permute-start.29) | collective-permute-done | bytes 5152 | tf_op jit(solution)/shard_map/ppermute | solution.py:174
  157.7 2.7 %collective-permute-start.30 = (f32[5,256]{1,0:T(8,128)S(1)}, f32[5,256]{1,0:T(8,128)S(1)}, u32[]{:S(2)}, u32[]{:S(2)}) collective-permute-start(f32[5,256]{1,0:T(8,128)S(1)} %add.314), channel_id=1, source_target_pairs={{0,4},{1,5},{2,6},{3,7},{4,0},{5,1},{6,2},{7,3},{8,12},{9,13},{10,... | collective-permute-start | bytes 15368 | tf_op jit(solution)/shard_map/ppermute | solution.py:174
  160.4 1.9 collective-permute-done.30
  162.3 5.7 %collective-permute-start.31 = (f32[5,256]{1,0:T(8,128)S(1)}, f32[5,256]{1,0:T(8,128)S(1)}, u32[]{:S(2)}, u32[]{:S(2)}) collective-permute-start(f32[5,256]{1,0:T(8,128)S(1)} %add.315), channel_id=1, source_target_pairs={{0,8},{1,9},{2,10},{3,11},{4,12},{5,13},{6,14},{7,15},{8,0},{9,1},... | collective-permute-start | bytes 15368 | tf_op jit(solution)/shard_map/ppermute | solution.py:174
  168.0 1.9 concatenate.129
  169.9 4.5 %collective-permute-start.32 = (f32[5,2,128]{2,1,0:T(2,128)S(1)}, f32[5,2,128]{2,1,0:T(2,128)S(1)}, u32[]{:S(2)}, u32[]{:S(2)}) collective-permute-start(f32[5,2,128]{2,1,0:T(2,128)S(1)} %reshape.306), channel_id=1, source_target_pairs={{0,32},{16,48},{32,64},{48,80},{64,96},{80,112},{96,128},{112,144}... | collective-permute-start | bytes 15368 | tf_op jit(solution)/shard_map/ppermute | solution.py:22
  174.5 3.2 %collective-permute-start.33 = (f32[5,2,128]{2,1,0:T(2,128)S(1)}, f32[5,2,128]{2,1,0:T(2,128)S(1)}, u32[]{:S(2)}, u32[]{:S(2)}) collective-permute-start(f32[5,2,128]{2,1,0:T(2,128)S(1)} %reshape.306), channel_id=1, source_target_pairs={{0,16},{16,32},{32,48},{48,64},{64,80},{80,96},{96,112},{112,128},... | collective-permute-start | bytes 15368 | tf_op jit(solution)/shard_map/ppermute | solution.py:22
  180.5 2.7 %collective-permute-done.34 = f32[5,2,128]{2,1,0:T(2,128)S(1)} collective-permute-done((f32[5,2,128]{2,1,0:T(2,128)S(1)}, f32[5,2,128]{2,1,0:T(2,128)S(1)}, u32[]{:S(2)}, u32[]{:S(2)}) %collective-permute-start.34) | collective-permute-done | bytes 5152 | tf_op jit(solution)/shard_map/ppermute | solution.py:22
  183.1 2.8 %collective-permute-done.35 = f32[5,2,128]{2,1,0:T(2,128)S(1)} collective-permute-done((f32[5,2,128]{2,1,0:T(2,128)S(1)}, f32[5,2,128]{2,1,0:T(2,128)S(1)}, u32[]{:S(2)}, u32[]{:S(2)}) %collective-permute-start.35) | collective-permute-done | bytes 5152 | tf_op jit(solution)/shard_map/ppermute | solution.py:22
  186.7 1.9 abs_reduce_fusion
  192.6 2.5 %collective-permute-done.37 = f32[26]{0:T(128)S(1)} collective-permute-done((f32[26]{0:T(128)S(1)}, f32[26]{0:T(128)S(1)}, u32[]{:S(2)}, u32[]{:S(2)}) %collective-permute-start.37) | collective-permute-done | bytes 136 | tf_op jit(solution)/shard_map/ppermute | solution.py:174
  195.1 2.6 %collective-permute-start.38 = (f32[26]{0:T(128)S(1)}, f32[26]{0:T(128)S(1)}, u32[]{:S(2)}, u32[]{:S(2)}) collective-permute-start(f32[26]{0:T(128)S(1)} %add.320), channel_id=1, source_target_pairs={{0,4},{1,5},{2,6},{3,7},{4,0},{5,1},{6,2},{7,3},{8,12},{9,13},{10,... | collective-permute-start | bytes 320 | tf_op jit(solution)/shard_map/ppermute | solution.py:174
  197.7 1.8 collective-permute-done.38
  199.5 5.6 %collective-permute-start.39 = (f32[26]{0:T(128)S(1)}, f32[26]{0:T(128)S(1)}, u32[]{:S(2)}, u32[]{:S(2)}) collective-permute-start(f32[26]{0:T(128)S(1)} %add.321), channel_id=1, source_target_pairs={{0,8},{1,9},{2,10},{3,11},{4,12},{5,13},{6,14},{7,15},{8,0},{9,1},... | collective-permute-start | bytes 320 | tf_op jit(solution)/shard_map/ppermute | solution.py:174
  205.2 1.8 collective-permute-done.39
  207.0 2.6 %collective-permute-start.40 = (f32[26]{0:T(128)S(1)}, f32[26]{0:T(128)S(1)}, u32[]{:S(2)}, u32[]{:S(2)}) collective-permute-start(f32[26]{0:T(128)S(1)} %add.322), channel_id=1, source_target_pairs={{0,16},{16,0},{32,48},{48,32},{64,80},{80,64},{96,112},{112,96},{1... | collective-permute-start | bytes 320 | tf_op jit(solution)/shard_map/ppermute | solution.py:174
  211.2 3.0 %collective-permute-start.41 = (f32[26]{0:T(128)S(1)}, f32[26]{0:T(128)S(1)}, u32[]{:S(2)}, u32[]{:S(2)}) collective-permute-start(f32[26]{0:T(128)S(1)} %add.323), channel_id=1, source_target_pairs={{0,32},{16,48},{32,0},{48,16},{64,96},{80,112},{96,64},{112,80},{1... | collective-permute-start | bytes 320 | tf_op jit(solution)/shard_map/ppermute | solution.py:174
  214.1 2.1 collective-permute-done.41
  216.2 2.0 collective-permute-start.42
  219.7 2.6 %collective-permute-start.43 = (f32[26]{0:T(128)S(1)}, f32[26]{0:T(128)S(1)}, u32[]{:S(2)}, u32[]{:S(2)}) collective-permute-start(f32[26]{0:T(128)S(1)} %add.325), channel_id=1, source_target_pairs={{0,128},{16,144},{32,160},{48,176},{64,192},{80,208},{96,224},{112... | collective-permute-start | bytes 320 | tf_op jit(solution)/shard_map/ppermute | solution.py:174
  222.3 2.5 %collective-permute-done.43 = f32[26]{0:T(128)S(1)} collective-permute-done((f32[26]{0:T(128)S(1)}, f32[26]{0:T(128)S(1)}, u32[]{:S(2)}, u32[]{:S(2)}) %collective-permute-start.43) | collective-permute-done | bytes 136 | tf_op jit(solution)/shard_map/ppermute | solution.py:174
  (220 shorter events, 45.5 us)
Async XLA Ops:
  4.2 22.6 %collective-permute-start.2 = (f32[37,12,128]{2,0,1:T(8,128)S(1)}, f32[37,12,128]{2,0,1:T(8,128)S(1)}, u32[]{:S(2)}, u32[]{:S(2)}) collective-permute-start(f32[37,12,128]{2,0,1:T(8,128)S(1)} %pad_maximum_fusion.1), channel_id=1, source_target_pairs={{16,0},{32,16},{48,32},{64,48},{80,64},{96,80},{112,96},{128,112},... | collective-permute-start | bytes 681992 | tf_op jit(solution)/shard_map/ppermute | solution.py:22
  5.5 25.7 %collective-permute-start.3 = (f32[37,12,128]{2,0,1:T(8,128)S(1)}, f32[37,12,128]{2,0,1:T(8,128)S(1)}, u32[]{:S(2)}, u32[]{:S(2)}) collective-permute-start(f32[37,12,128]{2,0,1:T(8,128)S(1)} %pad_maximum_fusion.1), channel_id=1, source_target_pairs={{32,0},{48,16},{64,32},{80,48},{96,64},{112,80},{128,96},{144,112}... | collective-permute-start | bytes 681992 | tf_op jit(solution)/shard_map/ppermute | solution.py:22
  7.7 24.8 %collective-permute-start = (f32[37,12,128]{2,0,1:T(8,128)}, f32[37,12,128]{2,0,1:T(8,128)S(1)}, u32[]{:S(2)}, u32[]{:S(2)}) collective-permute-start(f32[37,12,128]{2,0,1:T(8,128)} %pad_maximum_fusion), channel_id=1, source_target_pairs={{0,16},{16,32},{32,48},{48,64},{64,80},{80,96},{96,112},{112,128},... | collective-permute-start | bytes 681992 | tf_op jit(solution)/shard_map/ppermute | solution.py:22
  12.2 20.3 %collective-permute-start.1 = (f32[37,12,128]{2,0,1:T(8,128)}, f32[37,12,128]{2,0,1:T(8,128)S(1)}, u32[]{:S(2)}, u32[]{:S(2)}) collective-permute-start(f32[37,12,128]{2,0,1:T(8,128)} %pad_maximum_fusion), channel_id=1, source_target_pairs={{0,32},{16,48},{32,64},{48,80},{64,96},{80,112},{96,128},{112,144}... | collective-permute-start | bytes 681992 | tf_op jit(solution)/shard_map/ppermute | solution.py:22
  20.2 1.2 collective-permute-start.4
  21.4 146.6 %collective-permute-start.24 = (f32[75,2,128]{2,1,0:T(2,128)S(1)}, f32[75,2,128]{2,1,0:T(2,128)}, u32[]{:S(2)}, u32[]{:S(2)}) collective-permute-start(f32[75,2,128]{2,1,0:T(2,128)S(1)} %reshape.304), channel_id=1, source_target_pairs={{0,32},{16,48},{32,64},{48,80},{64,96},{80,112},{96,128},{112,144}... | collective-permute-start | bytes 230408 | tf_op jit(solution)/shard_map/ppermute | solution.py:22
  26.8 141.2 %collective-permute-start.25 = (f32[75,2,128]{2,1,0:T(2,128)S(1)}, f32[75,2,128]{2,1,0:T(2,128)}, u32[]{:S(2)}, u32[]{:S(2)}) collective-permute-start(f32[75,2,128]{2,1,0:T(2,128)S(1)} %reshape.304), channel_id=1, source_target_pairs={{0,16},{16,32},{32,48},{48,64},{64,80},{80,96},{96,112},{112,128},... | collective-permute-start | bytes 230408 | tf_op jit(solution)/shard_map/ppermute | solution.py:22
  31.2 136.8 %collective-permute-start.26 = (f32[75,2,128]{2,1,0:T(2,128)S(1)}, f32[75,2,128]{2,1,0:T(2,128)S(1)}, u32[]{:S(2)}, u32[]{:S(2)}) collective-permute-start(f32[75,2,128]{2,1,0:T(2,128)S(1)} %reshape.304), channel_id=1, source_target_pairs={{16,0},{32,16},{48,32},{64,48},{80,64},{96,80},{112,96},{128,112},... | collective-permute-start | bytes 230408 | tf_op jit(solution)/shard_map/ppermute | solution.py:22
  32.7 11.2 %collective-permute-start.6 = (f32[37,12,128]{2,0,1:T(8,128)S(1)}, f32[37,12,128]{2,0,1:T(8,128)S(1)}, u32[]{:S(2)}, u32[]{:S(2)}) collective-permute-start(f32[37,12,128]{2,0,1:T(8,128)S(1)} %pad_maximum_fusion.3), channel_id=1, source_target_pairs={{32,0},{48,16},{64,32},{80,48},{96,64},{112,80},{128,96},{144,112}... | collective-permute-start | bytes 681992 | tf_op jit(solution)/shard_map/ppermute | solution.py:22
  34.1 3.7 %collective-permute-start.7 = (f32[5,256]{1,0:T(8,128)S(1)}, f32[5,256]{1,0:T(8,128)S(1)}, u32[]{:S(2)}, u32[]{:S(2)}) collective-permute-start(f32[5,256]{1,0:T(8,128)S(1)} %add.285), channel_id=1, source_target_pairs={{0,2},{1,3},{2,0},{3,1},{4,6},{5,7},{6,4},{7,5},{8,10},{9,11},{10,... | collective-permute-start | bytes 15368 | tf_op jit(solution)/shard_map/ppermute | solution.py:229
  37.8 10.2 %collective-permute-start.5 = (f32[37,12,128]{2,0,1:T(8,128)S(1)}, f32[37,12,128]{2,0,1:T(8,128)S(1)}, u32[]{:S(2)}, u32[]{:S(2)}) collective-permute-start(f32[37,12,128]{2,0,1:T(8,128)S(1)} %pad_maximum_fusion.2), channel_id=1, source_target_pairs={{0,32},{16,48},{32,64},{48,80},{64,96},{80,112},{96,128},{112,144}... | collective-permute-start | bytes 681992 | tf_op jit(solution)/shard_map/ppermute | solution.py:22
  48.1 14.6 %collective-permute-start.9 = (f32[37,12,128]{2,0,1:T(8,128)S(1)}, f32[37,12,128]{2,0,1:T(8,128)S(1)}, u32[]{:S(2)}, u32[]{:S(2)}) collective-permute-start(f32[37,12,128]{2,0,1:T(8,128)S(1)} %pad_maximum_fusion.5), channel_id=1, source_target_pairs={{64,0},{80,16},{96,32},{112,48},{128,64},{144,80},{160,96},{176,11... | collective-permute-start | bytes 681992 | tf_op jit(solution)/shard_map/ppermute | solution.py:22
  50.3 5.0 %collective-permute-start.10 = (f32[5,256]{1,0:T(8,128)S(1)}, f32[5,256]{1,0:T(8,128)S(1)}, u32[]{:S(2)}, u32[]{:S(2)}) collective-permute-start(f32[5,256]{1,0:T(8,128)S(1)} %add.288), channel_id=1, source_target_pairs={{0,4},{1,5},{2,6},{3,7},{4,0},{5,1},{6,2},{7,3},{8,12},{9,13},{10,... | collective-permute-start | bytes 15368 | tf_op jit(solution)/shard_map/ppermute | solution.py:229
  55.3 11.0 %collective-permute-start.8 = (f32[37,12,128]{2,0,1:T(8,128)S(1)}, f32[37,12,128]{2,0,1:T(8,128)S(1)}, u32[]{:S(2)}, u32[]{:S(2)}) collective-permute-start(f32[37,12,128]{2,0,1:T(8,128)S(1)} %pad_maximum_fusion.4), channel_id=1, source_target_pairs={{0,64},{16,80},{32,96},{48,112},{64,128},{80,144},{96,160},{112,17... | collective-permute-start | bytes 681992 | tf_op jit(solution)/shard_map/ppermute | solution.py:22
  66.4 17.1 %collective-permute-start.12 = (f32[37,12,128]{2,0,1:T(8,128)S(1)}, f32[37,12,128]{2,0,1:T(8,128)S(1)}, u32[]{:S(2)}, u32[]{:S(2)}) collective-permute-start(f32[37,12,128]{2,0,1:T(8,128)S(1)} %pad_maximum_fusion.7), channel_id=1, source_target_pairs={{128,0},{144,16},{160,32},{176,48},{192,64},{208,80},{224,96},{240... | collective-permute-start | bytes 681992 | tf_op jit(solution)/shard_map/ppermute | solution.py:22
  67.7 7.7 %collective-permute-start.13 = (f32[5,256]{1,0:T(8,128)S(1)}, f32[5,256]{1,0:T(8,128)S(1)}, u32[]{:S(2)}, u32[]{:S(2)}) collective-permute-start(f32[5,256]{1,0:T(8,128)S(1)} %add.291), channel_id=1, source_target_pairs={{0,8},{1,9},{2,10},{3,11},{4,12},{5,13},{6,14},{7,15},{8,0},{9,1},... | collective-permute-start | bytes 15368 | tf_op jit(solution)/shard_map/ppermute | solution.py:229
  73.8 13.4 %copy-start.4 = (f32[256]{0:T(256)S(1)}, f32[256]{0:T(256)}, u32[]{:S(2)}) copy-start(f32[256]{0:T(256)} %param.10) | copy-start | bytes 3076
  75.4 11.8 %collective-permute-start.11 = (f32[37,12,128]{2,0,1:T(8,128)S(1)}, f32[37,12,128]{2,0,1:T(8,128)S(1)}, u32[]{:S(2)}, u32[]{:S(2)}) collective-permute-start(f32[37,12,128]{2,0,1:T(8,128)S(1)} %pad_maximum_fusion.6), channel_id=1, source_target_pairs={{0,128},{16,144},{32,160},{48,176},{64,192},{80,208},{96,224},{112... | collective-permute-start | bytes 681992 | tf_op jit(solution)/shard_map/ppermute | solution.py:22
  87.3 6.9 %collective-permute-start.19 = (f32[6,12,128]{2,1,0:T(8,128)S(1)}, f32[6,12,128]{2,1,0:T(8,128)S(1)}, u32[]{:S(2)}, u32[]{:S(2)}) collective-permute-start(f32[6,12,128]{2,1,0:T(8,128)S(1)} %pad_maximum_fusion.14), channel_id=1, source_target_pairs={{0,16},{16,32},{32,48},{48,64},{64,80},{80,96},{96,112},{112,128},... | collective-permute-start | bytes 110600 | tf_op jit(solution)/shard_map/ppermute | solution.py:22
  90.4 5.3 %collective-permute-start.20 = (f32[6,12,128]{2,1,0:T(8,128)S(1)}, f32[6,12,128]{2,1,0:T(8,128)S(1)}, u32[]{:S(2)}, u32[]{:S(2)}) collective-permute-start(f32[6,12,128]{2,1,0:T(8,128)S(1)} %pad_maximum_fusion.14), channel_id=1, source_target_pairs={{0,32},{16,48},{32,64},{48,80},{64,96},{80,112},{96,128},{112,144}... | collective-permute-start | bytes 110600 | tf_op jit(solution)/shard_map/ppermute | solution.py:22
  94.2 6.6 %collective-permute-start.14 = (f32[6,12,128]{2,1,0:T(8,128)S(1)}, f32[6,12,128]{2,1,0:T(8,128)S(1)}, u32[]{:S(2)}, u32[]{:S(2)}) collective-permute-start(f32[6,12,128]{2,1,0:T(8,128)S(1)} %pad_maximum_fusion.10), channel_id=1, source_target_pairs={{16,0},{32,16},{48,32},{64,48},{80,64},{96,80},{112,96},{128,112},... | collective-permute-start | bytes 110600 | tf_op jit(solution)/shard_map/ppermute | solution.py:22
  95.7 9.2 %collective-permute-start.15 = (f32[6,12,128]{2,1,0:T(8,128)S(1)}, f32[6,12,128]{2,1,0:T(8,128)S(1)}, u32[]{:S(2)}, u32[]{:S(2)}) collective-permute-start(f32[6,12,128]{2,1,0:T(8,128)S(1)} %pad_maximum_fusion.10), channel_id=1, source_target_pairs={{32,0},{48,16},{64,32},{80,48},{96,64},{112,80},{128,96},{144,112}... | collective-permute-start | bytes 110600 | tf_op jit(solution)/shard_map/ppermute | solution.py:22
  100.9 67.1 %collective-permute-start.27 = (f32[75,2,128]{2,1,0:T(2,128)S(1)}, f32[75,2,128]{2,1,0:T(2,128)S(1)}, u32[]{:S(2)}, u32[]{:S(2)}) collective-permute-start(f32[75,2,128]{2,1,0:T(2,128)S(1)} %reshape.304), channel_id=1, source_target_pairs={{32,0},{48,16},{64,32},{80,48},{96,64},{112,80},{128,96},{144,112}... | collective-permute-start | bytes 230408 | tf_op jit(solution)/shard_map/ppermute | solution.py:22
  104.9 8.1 %collective-permute-start.21 = (f32[6,12,128]{2,1,0:T(8,128)S(1)}, f32[6,12,128]{2,1,0:T(8,128)S(1)}, u32[]{:S(2)}, u32[]{:S(2)}) collective-permute-start(f32[6,12,128]{2,1,0:T(8,128)S(1)} %pad_maximum_fusion.15), channel_id=1, source_target_pairs={{0,32},{16,48},{32,64},{48,80},{64,96},{80,112},{96,128},{112,144}... | collective-permute-start | bytes 110600 | tf_op jit(solution)/shard_map/ppermute | solution.py:22
  112.9 7.8 %collective-permute-start.16 = (f32[6,12,128]{2,1,0:T(8,128)S(1)}, f32[6,12,128]{2,1,0:T(8,128)S(1)}, u32[]{:S(2)}, u32[]{:S(2)}) collective-permute-start(f32[6,12,128]{2,1,0:T(8,128)S(1)} %pad_maximum_fusion.11), channel_id=1, source_target_pairs={{32,0},{48,16},{64,32},{80,48},{96,64},{112,80},{128,96},{144,112}... | collective-permute-start | bytes 110600 | tf_op jit(solution)/shard_map/ppermute | solution.py:22
  120.7 6.9 %collective-permute-start.22 = (f32[6,12,128]{2,1,0:T(8,128)S(1)}, f32[6,12,128]{2,1,0:T(8,128)S(1)}, u32[]{:S(2)}, u32[]{:S(2)}) collective-permute-start(f32[6,12,128]{2,1,0:T(8,128)S(1)} %pad_maximum_fusion.16), channel_id=1, source_target_pairs={{0,64},{16,80},{32,96},{48,112},{64,128},{80,144},{96,160},{112,17... | collective-permute-start | bytes 110600 | tf_op jit(solution)/shard_map/ppermute | solution.py:22
  127.6 6.6 %collective-permute-start.17 = (f32[6,12,128]{2,1,0:T(8,128)S(1)}, f32[6,12,128]{2,1,0:T(8,128)S(1)}, u32[]{:S(2)}, u32[]{:S(2)}) collective-permute-start(f32[6,12,128]{2,1,0:T(8,128)S(1)} %pad_maximum_fusion.12), channel_id=1, source_target_pairs={{64,0},{80,16},{96,32},{112,48},{128,64},{144,80},{160,96},{176,11... | collective-permute-start | bytes 110600 | tf_op jit(solution)/shard_map/ppermute | solution.py:22
  134.2 8.4 %collective-permute-start.23 = (f32[6,12,128]{2,1,0:T(8,128)S(1)}, f32[6,12,128]{2,1,0:T(8,128)S(1)}, u32[]{:S(2)}, u32[]{:S(2)}) collective-permute-start(f32[6,12,128]{2,1,0:T(8,128)S(1)} %pad_maximum_fusion.17), channel_id=1, source_target_pairs={{0,128},{16,144},{32,160},{48,176},{64,192},{80,208},{96,224},{112... | collective-permute-start | bytes 110600 | tf_op jit(solution)/shard_map/ppermute | solution.py:22
  142.6 7.5 %collective-permute-start.18 = (f32[6,12,128]{2,1,0:T(8,128)S(1)}, f32[6,12,128]{2,1,0:T(8,128)S(1)}, u32[]{:S(2)}, u32[]{:S(2)}) collective-permute-start(f32[6,12,128]{2,1,0:T(8,128)S(1)} %pad_maximum_fusion.13), channel_id=1, source_target_pairs={{128,0},{144,16},{160,32},{176,48},{192,64},{208,80},{224,96},{240... | collective-permute-start | bytes 110600 | tf_op jit(solution)/shard_map/ppermute | solution.py:22
  152.9 1.2 collective-permute-start.28
  154.1 3.7 %collective-permute-start.29 = (f32[5,256]{1,0:T(8,128)S(1)}, f32[5,256]{1,0:T(8,128)S(1)}, u32[]{:S(2)}, u32[]{:S(2)}) collective-permute-start(f32[5,256]{1,0:T(8,128)S(1)} %add.313), channel_id=1, source_target_pairs={{0,2},{1,3},{2,0},{3,1},{4,6},{5,7},{6,4},{7,5},{8,10},{9,11},{10,... | collective-permute-start | bytes 15368 | tf_op jit(solution)/shard_map/ppermute | solution.py:174
  157.7 4.5 %collective-permute-start.30 = (f32[5,256]{1,0:T(8,128)S(1)}, f32[5,256]{1,0:T(8,128)S(1)}, u32[]{:S(2)}, u32[]{:S(2)}) collective-permute-start(f32[5,256]{1,0:T(8,128)S(1)} %add.314), channel_id=1, source_target_pairs={{0,4},{1,5},{2,6},{3,7},{4,0},{5,1},{6,2},{7,3},{8,12},{9,13},{10,... | collective-permute-start | bytes 15368 | tf_op jit(solution)/shard_map/ppermute | solution.py:174
  162.3 7.6 %collective-permute-start.31 = (f32[5,256]{1,0:T(8,128)S(1)}, f32[5,256]{1,0:T(8,128)S(1)}, u32[]{:S(2)}, u32[]{:S(2)}) collective-permute-start(f32[5,256]{1,0:T(8,128)S(1)} %add.315), channel_id=1, source_target_pairs={{0,8},{1,9},{2,10},{3,11},{4,12},{5,13},{6,14},{7,15},{8,0},{9,1},... | collective-permute-start | bytes 15368 | tf_op jit(solution)/shard_map/ppermute | solution.py:174
  169.9 10.5 %collective-permute-start.32 = (f32[5,2,128]{2,1,0:T(2,128)S(1)}, f32[5,2,128]{2,1,0:T(2,128)S(1)}, u32[]{:S(2)}, u32[]{:S(2)}) collective-permute-start(f32[5,2,128]{2,1,0:T(2,128)S(1)} %reshape.306), channel_id=1, source_target_pairs={{0,32},{16,48},{32,64},{48,80},{64,96},{80,112},{96,128},{112,144}... | collective-permute-start | bytes 15368 | tf_op jit(solution)/shard_map/ppermute | solution.py:22
  174.5 6.0 %collective-permute-start.33 = (f32[5,2,128]{2,1,0:T(2,128)S(1)}, f32[5,2,128]{2,1,0:T(2,128)S(1)}, u32[]{:S(2)}, u32[]{:S(2)}) collective-permute-start(f32[5,2,128]{2,1,0:T(2,128)S(1)} %reshape.306), channel_id=1, source_target_pairs={{0,16},{16,32},{32,48},{48,64},{64,80},{80,96},{96,112},{112,128},... | collective-permute-start | bytes 15368 | tf_op jit(solution)/shard_map/ppermute | solution.py:22
  177.6 5.5 %collective-permute-start.34 = (f32[5,2,128]{2,1,0:T(2,128)S(1)}, f32[5,2,128]{2,1,0:T(2,128)S(1)}, u32[]{:S(2)}, u32[]{:S(2)}) collective-permute-start(f32[5,2,128]{2,1,0:T(2,128)S(1)} %reshape.306), channel_id=1, source_target_pairs={{16,0},{32,16},{48,32},{64,48},{80,64},{96,80},{112,96},{128,112},... | collective-permute-start | bytes 15368 | tf_op jit(solution)/shard_map/ppermute | solution.py:22
  178.9 7.0 %collective-permute-start.35 = (f32[5,2,128]{2,1,0:T(2,128)S(1)}, f32[5,2,128]{2,1,0:T(2,128)S(1)}, u32[]{:S(2)}, u32[]{:S(2)}) collective-permute-start(f32[5,2,128]{2,1,0:T(2,128)S(1)} %reshape.306), channel_id=1, source_target_pairs={{32,0},{48,16},{64,32},{80,48},{96,64},{112,80},{128,96},{144,112}... | collective-permute-start | bytes 15368 | tf_op jit(solution)/shard_map/ppermute | solution.py:22
  186.6 38.8 %copy-start.5 = (f32[24]{0:T(128)S(1)}, f32[24]{0:T(128)}, u32[]{:S(2)}) copy-start(f32[24]{0:T(128)} %constant.36.clone) | copy-start | bytes 292
  186.6 38.8 %copy-start.7 = (f32[24]{0:T(128)S(1)}, f32[24]{0:T(128)}, u32[]{:S(2)}) copy-start(f32[24]{0:T(128)} %constant.81) | copy-start | bytes 292
  186.7 38.9 %copy-start.6 = (f32[1,24]{1,0:T(1,128)S(1)}, f32[1,24]{1,0:T(1,128)}, u32[]{:S(2)}) copy-start(f32[1,24]{1,0:T(1,128)} %constant.85) | copy-start | bytes 292
  190.3 1.1 collective-permute-start.36
  191.5 3.6 %collective-permute-start.37 = (f32[26]{0:T(128)S(1)}, f32[26]{0:T(128)S(1)}, u32[]{:S(2)}, u32[]{:S(2)}) collective-permute-start(f32[26]{0:T(128)S(1)} %fusion.63), channel_id=1, source_target_pairs={{0,2},{1,3},{2,0},{3,1},{4,6},{5,7},{6,4},{7,5},{8,10},{9,11},{10,... | collective-permute-start | bytes 320 | tf_op jit(solution)/shard_map/ppermute | solution.py:174
  195.1 4.4 %collective-permute-start.38 = (f32[26]{0:T(128)S(1)}, f32[26]{0:T(128)S(1)}, u32[]{:S(2)}, u32[]{:S(2)}) collective-permute-start(f32[26]{0:T(128)S(1)} %add.320), channel_id=1, source_target_pairs={{0,4},{1,5},{2,6},{3,7},{4,0},{5,1},{6,2},{7,3},{8,12},{9,13},{10,... | collective-permute-start | bytes 320 | tf_op jit(solution)/shard_map/ppermute | solution.py:174
  199.5 7.4 %collective-permute-start.39 = (f32[26]{0:T(128)S(1)}, f32[26]{0:T(128)S(1)}, u32[]{:S(2)}, u32[]{:S(2)}) collective-permute-start(f32[26]{0:T(128)S(1)} %add.321), channel_id=1, source_target_pairs={{0,8},{1,9},{2,10},{3,11},{4,12},{5,13},{6,14},{7,15},{8,0},{9,1},... | collective-permute-start | bytes 320 | tf_op jit(solution)/shard_map/ppermute | solution.py:174
  207.0 4.2 %collective-permute-start.40 = (f32[26]{0:T(128)S(1)}, f32[26]{0:T(128)S(1)}, u32[]{:S(2)}, u32[]{:S(2)}) collective-permute-start(f32[26]{0:T(128)S(1)} %add.322), channel_id=1, source_target_pairs={{0,16},{16,0},{32,48},{48,32},{64,80},{80,64},{96,112},{112,96},{1... | collective-permute-start | bytes 320 | tf_op jit(solution)/shard_map/ppermute | solution.py:174
  211.2 5.0 %collective-permute-start.41 = (f32[26]{0:T(128)S(1)}, f32[26]{0:T(128)S(1)}, u32[]{:S(2)}, u32[]{:S(2)}) collective-permute-start(f32[26]{0:T(128)S(1)} %add.323), channel_id=1, source_target_pairs={{0,32},{16,48},{32,0},{48,16},{64,96},{80,112},{96,64},{112,80},{1... | collective-permute-start | bytes 320 | tf_op jit(solution)/shard_map/ppermute | solution.py:174
  216.2 3.5 %collective-permute-start.42 = (f32[26]{0:T(128)S(1)}, f32[26]{0:T(128)S(1)}, u32[]{:S(2)}, u32[]{:S(2)}) collective-permute-start(f32[26]{0:T(128)S(1)} %add.324), channel_id=1, source_target_pairs={{0,64},{16,80},{32,96},{48,112},{64,0},{80,16},{96,32},{112,48},{1... | collective-permute-start | bytes 320 | tf_op jit(solution)/shard_map/ppermute | solution.py:174
  219.7 5.0 %collective-permute-start.43 = (f32[26]{0:T(128)S(1)}, f32[26]{0:T(128)S(1)}, u32[]{:S(2)}, u32[]{:S(2)}) collective-permute-start(f32[26]{0:T(128)S(1)} %add.325), channel_id=1, source_target_pairs={{0,128},{16,144},{32,160},{48,176},{64,192},{80,208},{96,224},{112... | collective-permute-start | bytes 320 | tf_op jit(solution)/shard_map/ppermute | solution.py:174
  (4 other events, 52.3 us)

commit v5 on v4

--- a/solution.py
+++ b/solution.py
@@ -207,31 +207,6 @@
     return joined_field(sweep, inflow_neg, inflow_pos)
 
 
-def scan_beside_sum(sweep, block, axis):
-    count = lax.axis_size("sec")
-    pos, span = scan_first(sweep[2][:, :, -1], sweep[3][:, :, -1], 1)
-    neg, _ = scan_first(sweep[0][:, :, 0], sweep[1][:, :, 0], -1)
-    members = lax.axis_size(axis)
-    bit = 1
-    if members & (members - 1):
-        block = lax.psum(block, axis)
-        bit = members
-    elif bit < members:
-        block = block + lax.ppermute(block, axis, [(i, i ^ bit) for i in range(members)])
-        bit *= 2
-    pos, neg, block = lax.optimization_barrier((pos, neg, block))
-    while span < count - 1 or bit < members:
-        if span < count - 1:
-            pos, next_span = scan_next(pos, span, 1)
-            neg, _ = scan_next(neg, span, -1)
-            span = next_span
-        if bit < members:
-            block = block + lax.ppermute(block, axis, [(i, i ^ bit) for i in range(members)])
-            bit *= 2
-        pos, neg, block = lax.optimization_barrier((pos, neg, block))
-    return joined_field(sweep, neg[1], pos[1]), block
-
-
 def body(distribution, collision, lower_blocks, upper_blocks, diag_inverse):
     node_count = distribution.shape[0]
     cell_count = distribution.shape[1]
@@ -253,13 +228,32 @@
     denominator = node_speed * total_length + thickness + pseudo_rate
     carry_rate = node_speed * total_length / denominator
     own_drive = pseudo_rate * distribution.reshape(node_rows, NXI, length, TUBES) / denominator
-    own_field, old_moments = scan_beside_sum(
-        local_sweep(carry_rate, own_drive),
-        jnp.dot(weighted, distribution, precision=HIGH),
-        "vel",
-    )
+    count = lax.axis_size("sec")
+    own_sweep = local_sweep(carry_rate, own_drive)
+    own_pos, own_span = scan_first(own_sweep[2][:, :, -1], own_sweep[3][:, :, -1], 1)
+    own_neg, _ = scan_first(own_sweep[0][:, :, 0], own_sweep[1][:, :, 0], -1)
+    old_moments = tree_sum(jnp.dot(weighted, distribution, precision=HIGH), ("vel",))
+    own_pos, own_neg, old_moments = lax.optimization_barrier((own_pos, own_neg, old_moments))
     moment_drive = thickness * old_moments.reshape(5, 1, length, TUBES) / denominator
-    moment_field = swept_field(carry_rate, moment_drive)
+    moment_sweep = local_sweep(carry_rate, moment_drive)
+    moment_pos, moment_span = scan_first(moment_sweep[2][:, :, -1], moment_sweep[3][:, :, -1], 1)
+    moment_neg, _ = scan_first(moment_sweep[0][:, :, 0], moment_sweep[1][:, :, 0], -1)
+    while True:
+        if own_span < count - 1:
+            own_pos, next_span = scan_next(own_pos, own_span, 1)
+            own_neg, _ = scan_next(own_neg, own_span, -1)
+            own_span = next_span
+        own_pos, own_neg, moment_pos, moment_neg = lax.optimization_barrier(
+            (own_pos, own_neg, moment_pos, moment_neg)
+        )
+        if moment_span >= count - 1 and own_span >= count - 1:
+            break
+        if moment_span < count - 1:
+            moment_pos, next_span = scan_next(moment_pos, moment_span, 1)
+            moment_neg, _ = scan_next(moment_neg, moment_span, -1)
+            moment_span = next_span
+    own_field = joined_field(own_sweep, own_neg[1], own_pos[1])
+    moment_field = joined_field(moment_sweep, moment_neg[1], moment_pos[1])
     basis = rebuild.reshape(5, node_rows, NXI, 1, 1)
     half_field = own_field + jnp.sum(basis * moment_field[:, None], axis=0)
     half_field = half_field.reshape(node_count, cell_count)
@@ -267,11 +261,13 @@
     residual = (half_moments - old_moments).reshape(5, length, TUBES)
     width = min(-(-JACOBI // length), lax.axis_size("sec") - 1)
     blocks = jnp.concatenate([lower_blocks, upper_blocks, diag_inverse], axis=0)
-    blocks_wide = with_halo(blocks.reshape(75, length, TUBES), width)
-    lower_r = blocks_wide[:25]
-    upper_r = blocks_wide[25:50]
-    inverse_r = blocks_wide[50:]
-    residual_wide = with_halo(residual, width)
+    wide = with_halo(
+        jnp.concatenate([blocks.reshape(75, length, TUBES), residual], axis=0), width
+    )
+    lower_r = wide[:25]
+    upper_r = wide[25:50]
+    inverse_r = wide[50:75]
+    residual_wide = wide[75:]
     correction = apply_block(inverse_r, residual_wide)
     edge_zero = jnp.zeros((5, 1, TUBES), jnp.float32)
     for sweep_index in range(JACOBI):

time: 232 us -> 197 us (0.85)
  waiting for transfers between devices: 75.3 us -> 44.6 us
  starting transfers between devices: 131 us -> 128 us
    ppermute x28 -> x24, waiting for transfers between devices: 46.3 us -> 20 us  [passed_along(): return lax.ppermute(block, axis, route)]
    ppermute x12 -> x16, starting transfers between devices: 28.2 us -> 44 us  [tree_sum(): lax.ppermute(block, axis, [(i, i ^ bit) for i in range(count)])]
    ppermute x4 -> x0, starting transfers between devices: 9.61 us -> none  [scan_beside_sum(): lax.ppermute(block, axis, [(i, i ^ bit) for i in range(members)])]
    ppermute x28 -> x24, starting transfers between devices: 93.1 us -> 84 us  [passed_along(): return lax.ppermute(block, axis, route)]
    ppermute x4 -> x0, waiting for transfers between devices: 7.68 us -> none  [scan_beside_sum(): lax.ppermute(block, axis, [(i, i ^ bit) for i in range(members)])]
    ppermute x12 -> x16, waiting for transfers between devices: 21.3 us -> 24.6 us  [tree_sum(): lax.ppermute(block, axis, [(i, i ^ bit) for i in range(count)])]
  transfers between devices with their start and end apart: 44 -> 40, of which waited for: 29 -> 25; matrix products, arithmetic and copies ran while one was open for 4% -> 2% of each run, Pallas kernels for 0% -> 0%
where the time goes in v5:
time: 197 us; the launch traced here: 194 us
  starting transfers between devices  128 us (65%)
  waiting for transfers between devices  44.6 us (23%)
  other arithmetic  9.82 us (5%)
  local copies, waits for them, and re-layouts  4.87 us (2%)
  matrix products  4.74 us (2%)
    ppermute x24, starting transfers between devices, passed_along(): return lax.ppermute(block, axis, route)  84 us
    ppermute x16, starting transfers between devices, tree_sum(): lax.ppermute(block, axis, [(i, i ^ bit) for i in range(count)])  44 us
    ppermute x16, waiting for transfers between devices, tree_sum(): lax.ppermute(block, axis, [(i, i ^ bit) for i in range(count)])  24.6 us
    ppermute x24, waiting for transfers between devices, passed_along(): return lax.ppermute(block, axis, route)  20 us
  transfers between devices with their start and end apart: 40, of which 25 were waited for; matrix products, arithmetic and copies ran while one was open for 2% of the time, Pallas kernels for 0%

profile of v5, /device:TPU:32, one launch (start us, length us, event | category | flops | bytes accessed | tf_op | source)
XLA Modules:
  0.0 194.0 jit_solution(2446114482033846573)
XLA Ops:
  2.2 1.6 reshape.138
  4.2 1.4 collective-permute-start.2
  8.4 4.6 %collective-permute-start = (f32[37,12,128]{2,0,1:T(8,128)S(1)}, f32[37,12,128]{2,0,1:T(8,128)S(1)}, u32[]{:S(2)}, u32[]{:S(2)}) collective-permute-start(f32[37,12,128]{2,0,1:T(8,128)S(1)} %pad_maximum_fusion), channel_id=1, source_target_pairs={{0,16},{16,32},{32,48},{48,64},{64,80},{80,96},{96,112},{112,128},... | collective-permute-start | bytes 681992 | tf_op jit(solution)/shard_map/ppermute | solution.py:22
  13.0 6.7 %collective-permute-start.1 = (f32[37,12,128]{2,0,1:T(8,128)S(1)}, f32[37,12,128]{2,0,1:T(8,128)S(1)}, u32[]{:S(2)}, u32[]{:S(2)}) collective-permute-start(f32[37,12,128]{2,0,1:T(8,128)S(1)} %pad_maximum_fusion), channel_id=1, source_target_pairs={{0,32},{16,48},{32,64},{48,80},{64,96},{80,112},{96,128},{112,144}... | collective-permute-start | bytes 681992 | tf_op jit(solution)/shard_map/ppermute | solution.py:22
  19.7 1.9 collective-permute-start.5
  21.6 1.8 collective-permute-done.5
  23.4 3.3 %collective-permute-start.6 = (f32[5,256]{1,0:T(8,128)S(1)}, f32[5,256]{1,0:T(8,128)S(1)}, u32[]{:S(2)}, u32[]{:S(2)}) collective-permute-start(f32[5,256]{1,0:T(8,128)S(1)} %add.286), channel_id=1, source_target_pairs={{0,4},{1,5},{2,6},{3,7},{4,0},{5,1},{6,2},{7,3},{8,12},{9,13},{10,... | collective-permute-start | bytes 15368 | tf_op jit(solution)/shard_map/ppermute | solution.py:174
  28.3 5.9 %collective-permute-start.7 = (f32[5,256]{1,0:T(8,128)S(1)}, f32[5,256]{1,0:T(8,128)S(1)}, u32[]{:S(2)}, u32[]{:S(2)}) collective-permute-start(f32[5,256]{1,0:T(8,128)S(1)} %add.287), channel_id=1, source_target_pairs={{0,8},{1,9},{2,10},{3,11},{4,12},{5,13},{6,14},{7,15},{8,0},{9,1},... | collective-permute-start | bytes 15368 | tf_op jit(solution)/shard_map/ppermute | solution.py:174
  34.4 1.4 collective-permute-done.7
  38.8 5.0 %collective-permute-start.10 = (f32[6,12,128]{2,1,0:T(8,128)S(1)}, f32[6,12,128]{2,1,0:T(8,128)S(1)}, u32[]{:S(2)}, u32[]{:S(2)}) collective-permute-start(f32[6,12,128]{2,1,0:T(8,128)S(1)} %pad_maximum_fusion.10), channel_id=1, source_target_pairs={{0,16},{16,32},{32,48},{48,64},{64,80},{80,96},{96,112},{112,128},... | collective-permute-start | bytes 110600 | tf_op jit(solution)/shard_map/ppermute | solution.py:22
  43.8 6.7 %collective-permute-start.11 = (f32[6,12,128]{2,1,0:T(8,128)S(1)}, f32[6,12,128]{2,1,0:T(8,128)S(1)}, u32[]{:S(2)}, u32[]{:S(2)}) collective-permute-start(f32[6,12,128]{2,1,0:T(8,128)S(1)} %pad_maximum_fusion.10), channel_id=1, source_target_pairs={{0,32},{16,48},{32,64},{48,80},{64,96},{80,112},{96,128},{112,144}... | collective-permute-start | bytes 110600 | tf_op jit(solution)/shard_map/ppermute | solution.py:22
  51.9 6.1 %collective-permute-start.8 = (f32[37,12,128]{2,0,1:T(8,128)S(1)}, f32[37,12,128]{2,0,1:T(8,128)S(1)}, u32[]{:S(2)}, u32[]{:S(2)}) collective-permute-start(f32[37,12,128]{2,0,1:T(8,128)S(1)} %pad_maximum_fusion.2), channel_id=1, source_target_pairs={{0,32},{16,48},{32,64},{48,80},{64,96},{80,112},{96,128},{112,144}... | collective-permute-start | bytes 681992 | tf_op jit(solution)/shard_map/ppermute | solution.py:22
  58.1 2.1 %collective-permute-done.9 = f32[37,12,128]{2,0,1:T(8,128)S(1)} collective-permute-done((f32[37,12,128]{2,0,1:T(8,128)S(1)}, f32[37,12,128]{2,0,1:T(8,128)S(1)}, u32[]{:S(2)}, u32[]{:S(2)}) %collective-permute-start.9) | collective-permute-done | bytes 227360 | tf_op jit(solution)/shard_map/ppermute | solution.py:22
  60.2 2.6 %collective-permute-done.8 = f32[37,12,128]{2,0,1:T(8,128)S(1)} collective-permute-done((f32[37,12,128]{2,0,1:T(8,128)S(1)}, f32[37,12,128]{2,0,1:T(8,128)S(1)}, u32[]{:S(2)}, u32[]{:S(2)}) %collective-permute-start.8) | collective-permute-done | bytes 227360 | tf_op jit(solution)/shard_map/ppermute | solution.py:22
  64.2 6.5 %collective-permute-start.16 = (f32[6,12,128]{2,1,0:T(8,128)S(1)}, f32[6,12,128]{2,1,0:T(8,128)S(1)}, u32[]{:S(2)}, u32[]{:S(2)}) collective-permute-start(f32[6,12,128]{2,1,0:T(8,128)S(1)} %pad_maximum_fusion.12), channel_id=1, source_target_pairs={{0,32},{16,48},{32,64},{48,80},{64,96},{80,112},{96,128},{112,144}... | collective-permute-start | bytes 110600 | tf_op jit(solution)/shard_map/ppermute | solution.py:22
  72.1 6.7 %collective-permute-start.14 = (f32[37,12,128]{2,0,1:T(8,128)S(1)}, f32[37,12,128]{2,0,1:T(8,128)S(1)}, u32[]{:S(2)}, u32[]{:S(2)}) collective-permute-start(f32[37,12,128]{2,0,1:T(8,128)S(1)} %pad_maximum_fusion.4), channel_id=1, source_target_pairs={{0,64},{16,80},{32,96},{48,112},{64,128},{80,144},{96,160},{112,17... | collective-permute-start | bytes 681992 | tf_op jit(solution)/shard_map/ppermute | solution.py:22
  78.9 2.1 %collective-permute-done.15 = f32[37,12,128]{2,0,1:T(8,128)S(1)} collective-permute-done((f32[37,12,128]{2,0,1:T(8,128)S(1)}, f32[37,12,128]{2,0,1:T(8,128)S(1)}, u32[]{:S(2)}, u32[]{:S(2)}) %collective-permute-start.15) | collective-permute-done | bytes 227360 | tf_op jit(solution)/shard_map/ppermute | solution.py:22
  81.1 1.4 collective-permute-done.14
  83.9 5.0 %collective-permute-start.20 = (f32[6,12,128]{2,1,0:T(8,128)S(1)}, f32[6,12,128]{2,1,0:T(8,128)S(1)}, u32[]{:S(2)}, u32[]{:S(2)}) collective-permute-start(f32[6,12,128]{2,1,0:T(8,128)S(1)} %pad_maximum_fusion.14), channel_id=1, source_target_pairs={{0,64},{16,80},{32,96},{48,112},{64,128},{80,144},{96,160},{112,17... | collective-permute-start | bytes 110600 | tf_op jit(solution)/shard_map/ppermute | solution.py:22
  90.3 6.1 %collective-permute-start.18 = (f32[37,12,128]{2,0,1:T(8,128)S(1)}, f32[37,12,128]{2,0,1:T(8,128)S(1)}, u32[]{:S(2)}, u32[]{:S(2)}) collective-permute-start(f32[37,12,128]{2,0,1:T(8,128)S(1)} %pad_maximum_fusion.6), channel_id=1, source_target_pairs={{0,128},{16,144},{32,160},{48,176},{64,192},{80,208},{96,224},{112... | collective-permute-start | bytes 681992 | tf_op jit(solution)/shard_map/ppermute | solution.py:22
  96.5 2.1 %collective-permute-done.19 = f32[37,12,128]{2,0,1:T(8,128)S(1)} collective-permute-done((f32[37,12,128]{2,0,1:T(8,128)S(1)}, f32[37,12,128]{2,0,1:T(8,128)S(1)}, u32[]{:S(2)}, u32[]{:S(2)}) %collective-permute-start.19) | collective-permute-done | bytes 227360 | tf_op jit(solution)/shard_map/ppermute | solution.py:22
  98.6 1.5 collective-permute-done.18
  101.4 6.1 %collective-permute-start.22 = (f32[6,12,128]{2,1,0:T(8,128)S(1)}, f32[6,12,128]{2,1,0:T(8,128)S(1)}, u32[]{:S(2)}, u32[]{:S(2)}) collective-permute-start(f32[6,12,128]{2,1,0:T(8,128)S(1)} %pad_maximum_fusion.16), channel_id=1, source_target_pairs={{0,128},{16,144},{32,160},{48,176},{64,192},{80,208},{96,224},{112... | collective-permute-start | bytes 110600 | tf_op jit(solution)/shard_map/ppermute | solution.py:22
  107.6 1.6 collective-permute-done.22
  114.5 2.6 %collective-permute-done.25 = f32[5,256]{1,0:T(8,128)S(1)} collective-permute-done((f32[5,256]{1,0:T(8,128)S(1)}, f32[5,256]{1,0:T(8,128)S(1)}, u32[]{:S(2)}, u32[]{:S(2)}) %collective-permute-start.25) | collective-permute-done | bytes 5152 | tf_op jit(solution)/shard_map/ppermute | solution.py:174
  117.2 2.7 %collective-permute-start.26 = (f32[5,256]{1,0:T(8,128)S(1)}, f32[5,256]{1,0:T(8,128)S(1)}, u32[]{:S(2)}, u32[]{:S(2)}) collective-permute-start(f32[5,256]{1,0:T(8,128)S(1)} %add.314), channel_id=1, source_target_pairs={{0,4},{1,5},{2,6},{3,7},{4,0},{5,1},{6,2},{7,3},{8,12},{9,13},{10,... | collective-permute-start | bytes 15368 | tf_op jit(solution)/shard_map/ppermute | solution.py:174
  119.9 1.8 collective-permute-done.26
  121.7 5.6 %collective-permute-start.27 = (f32[5,256]{1,0:T(8,128)S(1)}, f32[5,256]{1,0:T(8,128)S(1)}, u32[]{:S(2)}, u32[]{:S(2)}) collective-permute-start(f32[5,256]{1,0:T(8,128)S(1)} %add.315), channel_id=1, source_target_pairs={{0,8},{1,9},{2,10},{3,11},{4,12},{5,13},{6,14},{7,15},{8,0},{9,1},... | collective-permute-start | bytes 15368 | tf_op jit(solution)/shard_map/ppermute | solution.py:174
  127.4 1.9 collective-permute-done.27
  129.3 4.3 %collective-permute-start.28 = (f32[80,2,128]{2,1,0:T(2,128)S(1)}, f32[80,2,128]{2,1,0:T(2,128)S(1)}, u32[]{:S(2)}, u32[]{:S(2)}) collective-permute-start(f32[80,2,128]{2,1,0:T(2,128)S(1)} %constant_dynamic-update-slice_fusion), channel_id=1, source_target_pairs={{0,32},{16,48},{32,64},{48,80},{64,96},{80,112},{96,128},{112,144}... | collective-permute-start | bytes 245768 | tf_op jit(solution)/shard_map/ppermute | solution.py:22
  133.6 4.5 %collective-permute-start.29 = (f32[80,2,128]{2,1,0:T(2,128)S(1)}, f32[80,2,128]{2,1,0:T(2,128)S(1)}, u32[]{:S(2)}, u32[]{:S(2)}) collective-permute-start(f32[80,2,128]{2,1,0:T(2,128)S(1)} %constant_dynamic-update-slice_fusion), channel_id=1, source_target_pairs={{0,16},{16,32},{32,48},{48,64},{64,80},{80,96},{96,112},{112,128},... | collective-permute-start | bytes 245768 | tf_op jit(solution)/shard_map/ppermute | solution.py:22
  139.5 1.5 collective-permute-start.31
  141.0 4.4 %collective-permute-done.30 = f32[80,2,128]{2,1,0:T(2,128)S(1)} collective-permute-done((f32[80,2,128]{2,1,0:T(2,128)S(1)}, f32[80,2,128]{2,1,0:T(2,128)S(1)}, u32[]{:S(2)}, u32[]{:S(2)}) %collective-permute-start.30) | collective-permute-done | bytes 81952 | tf_op jit(solution)/shard_map/ppermute | solution.py:22
  145.4 2.1 %collective-permute-done.31 = f32[80,2,128]{2,1,0:T(2,128)S(1)} collective-permute-done((f32[80,2,128]{2,1,0:T(2,128)S(1)}, f32[80,2,128]{2,1,0:T(2,128)S(1)}, u32[]{:S(2)}, u32[]{:S(2)}) %collective-permute-start.31) | collective-permute-done | bytes 81952 | tf_op jit(solution)/shard_map/ppermute | solution.py:22
  148.7 1.9 %abs_reduce_fusion = (f32[864]{0:T(1024)S(1)}, f32[864,256]{1,0:T(8,128)S(1)}) fusion(f32[1,5,2,128]{3,2,1,0:T(2,128)S(1)} %slice_bitcast_fusion.2, f32[5,13824]{1,0:T(8,128)} %constant.35.clone, s32[]{:T(128)S(6)} %select_n.2, f32[108,8,2,128]{3,2,1,0:T(2,128)S(1)} %bitcast.116), kind=kOutput, calls=%fused_computation.8 | convolution fusion | flops 13933728 | bytes 1806724 | tf_op jit(solution)/shard_map/dot_general | solution.py:282
  154.4 2.7 %collective-permute-done.33 = f32[26]{0:T(128)S(1)} collective-permute-done((f32[26]{0:T(128)S(1)}, f32[26]{0:T(128)S(1)}, u32[]{:S(2)}, u32[]{:S(2)}) %collective-permute-start.33) | collective-permute-done | bytes 136 | tf_op jit(solution)/shard_map/ppermute | solution.py:174
  157.1 2.9 %collective-permute-start.34 = (f32[26]{0:T(128)S(1)}, f32[26]{0:T(128)S(1)}, u32[]{:S(2)}, u32[]{:S(2)}) collective-permute-start(f32[26]{0:T(128)S(1)} %add.320), channel_id=1, source_target_pairs={{0,4},{1,5},{2,6},{3,7},{4,0},{5,1},{6,2},{7,3},{8,12},{9,13},{10,... | collective-permute-start | bytes 320 | tf_op jit(solution)/shard_map/ppermute | solution.py:174
  160.0 1.5 collective-permute-done.34
  161.5 5.7 %collective-permute-start.35 = (f32[26]{0:T(128)S(1)}, f32[26]{0:T(128)S(1)}, u32[]{:S(2)}, u32[]{:S(2)}) collective-permute-start(f32[26]{0:T(128)S(1)} %add.321), channel_id=1, source_target_pairs={{0,8},{1,9},{2,10},{3,11},{4,12},{5,13},{6,14},{7,15},{8,0},{9,1},... | collective-permute-start | bytes 320 | tf_op jit(solution)/shard_map/ppermute | solution.py:174
  167.3 1.7 collective-permute-done.35
  169.0 2.5 %collective-permute-start.36 = (f32[26]{0:T(128)S(1)}, f32[26]{0:T(128)S(1)}, u32[]{:S(2)}, u32[]{:S(2)}) collective-permute-start(f32[26]{0:T(128)S(1)} %add.322), channel_id=1, source_target_pairs={{0,16},{16,0},{32,48},{48,32},{64,80},{80,64},{96,112},{112,96},{1... | collective-permute-start | bytes 320 | tf_op jit(solution)/shard_map/ppermute | solution.py:174
  171.5 1.5 collective-permute-done.36
  173.0 4.0 %collective-permute-start.37 = (f32[26]{0:T(128)S(1)}, f32[26]{0:T(128)S(1)}, u32[]{:S(2)}, u32[]{:S(2)}) collective-permute-start(f32[26]{0:T(128)S(1)} %add.323), channel_id=1, source_target_pairs={{0,32},{16,48},{32,0},{48,16},{64,96},{80,112},{96,64},{112,80},{1... | collective-permute-start | bytes 320 | tf_op jit(solution)/shard_map/ppermute | solution.py:174
  177.0 1.5 collective-permute-done.37
  178.5 3.1 %collective-permute-start.38 = (f32[26]{0:T(128)S(1)}, f32[26]{0:T(128)S(1)}, u32[]{:S(2)}, u32[]{:S(2)}) collective-permute-start(f32[26]{0:T(128)S(1)} %add.324), channel_id=1, source_target_pairs={{0,64},{16,80},{32,96},{48,112},{64,0},{80,16},{96,32},{112,48},{1... | collective-permute-start | bytes 320 | tf_op jit(solution)/shard_map/ppermute | solution.py:174
  181.6 1.5 collective-permute-done.38
  183.1 4.5 %collective-permute-start.39 = (f32[26]{0:T(128)S(1)}, f32[26]{0:T(128)S(1)}, u32[]{:S(2)}, u32[]{:S(2)}) collective-permute-start(f32[26]{0:T(128)S(1)} %add.325), channel_id=1, source_target_pairs={{0,128},{16,144},{32,160},{48,176},{64,192},{80,208},{96,224},{112... | collective-permute-start | bytes 320 | tf_op jit(solution)/shard_map/ppermute | solution.py:174
  187.5 1.5 collective-permute-done.39
  (214 shorter events, 34.0 us)
Async XLA Ops:
  4.0 2.9 %copy-start = (f32[864,256]{1,0:T(8,128)S(1)}, f32[864,256]{1,0:T(8,128)}, u32[]{:S(2)}) copy-start(f32[864,256]{1,0:T(8,128)} %param.9) | copy-start | bytes 2654212
  4.2 31.7 %collective-permute-start.2 = (f32[37,12,128]{2,0,1:T(8,128)S(1)}, f32[37,12,128]{2,0,1:T(8,128)S(1)}, u32[]{:S(2)}, u32[]{:S(2)}) collective-permute-start(f32[37,12,128]{2,0,1:T(8,128)S(1)} %pad_maximum_fusion.1), channel_id=1, source_target_pairs={{16,0},{32,16},{48,32},{64,48},{80,64},{96,80},{112,96},{128,112},... | collective-permute-start | bytes 681992 | tf_op jit(solution)/shard_map/ppermute | solution.py:22
  5.6 30.3 %collective-permute-start.3 = (f32[37,12,128]{2,0,1:T(8,128)S(1)}, f32[37,12,128]{2,0,1:T(8,128)S(1)}, u32[]{:S(2)}, u32[]{:S(2)}) collective-permute-start(f32[37,12,128]{2,0,1:T(8,128)S(1)} %pad_maximum_fusion.1), channel_id=1, source_target_pairs={{32,0},{48,16},{64,32},{80,48},{96,64},{112,80},{128,96},{144,112}... | collective-permute-start | bytes 681992 | tf_op jit(solution)/shard_map/ppermute | solution.py:22
  8.2 11.4 %collective-permute-start.4 = (f32[5,256]{1,0:T(8,128)S(1)}, f32[5,256]{1,0:T(8,128)S(1)}, u32[]{:S(2)}, u32[]{:S(2)}) collective-permute-start(f32[5,256]{1,0:T(8,128)S(1)} %fusion.14), channel_id=1, source_target_pairs={{0,1},{1,0},{2,3},{3,2},{4,5},{5,4},{6,7},{7,6},{8,9},{9,8},{10,11... | collective-permute-start | bytes 15368 | tf_op jit(solution)/shard_map/ppermute | solution.py:174
  8.4 27.5 %collective-permute-start = (f32[37,12,128]{2,0,1:T(8,128)S(1)}, f32[37,12,128]{2,0,1:T(8,128)S(1)}, u32[]{:S(2)}, u32[]{:S(2)}) collective-permute-start(f32[37,12,128]{2,0,1:T(8,128)S(1)} %pad_maximum_fusion), channel_id=1, source_target_pairs={{0,16},{16,32},{32,48},{48,64},{64,80},{80,96},{96,112},{112,128},... | collective-permute-start | bytes 681992 | tf_op jit(solution)/shard_map/ppermute | solution.py:22
  13.0 23.0 %collective-permute-start.1 = (f32[37,12,128]{2,0,1:T(8,128)S(1)}, f32[37,12,128]{2,0,1:T(8,128)S(1)}, u32[]{:S(2)}, u32[]{:S(2)}) collective-permute-start(f32[37,12,128]{2,0,1:T(8,128)S(1)} %pad_maximum_fusion), channel_id=1, source_target_pairs={{0,32},{16,48},{32,64},{48,80},{64,96},{80,112},{96,128},{112,144}... | collective-permute-start | bytes 681992 | tf_op jit(solution)/shard_map/ppermute | solution.py:22
  19.7 3.7 %collective-permute-start.5 = (f32[5,256]{1,0:T(8,128)S(1)}, f32[5,256]{1,0:T(8,128)S(1)}, u32[]{:S(2)}, u32[]{:S(2)}) collective-permute-start(f32[5,256]{1,0:T(8,128)S(1)} %add.285), channel_id=1, source_target_pairs={{0,2},{1,3},{2,0},{3,1},{4,6},{5,7},{6,4},{7,5},{8,10},{9,11},{10,... | collective-permute-start | bytes 15368 | tf_op jit(solution)/shard_map/ppermute | solution.py:174
  23.4 4.9 %collective-permute-start.6 = (f32[5,256]{1,0:T(8,128)S(1)}, f32[5,256]{1,0:T(8,128)S(1)}, u32[]{:S(2)}, u32[]{:S(2)}) collective-permute-start(f32[5,256]{1,0:T(8,128)S(1)} %add.286), channel_id=1, source_target_pairs={{0,4},{1,5},{2,6},{3,7},{4,0},{5,1},{6,2},{7,3},{8,12},{9,13},{10,... | collective-permute-start | bytes 15368 | tf_op jit(solution)/shard_map/ppermute | solution.py:174
  28.3 7.6 %collective-permute-start.7 = (f32[5,256]{1,0:T(8,128)S(1)}, f32[5,256]{1,0:T(8,128)S(1)}, u32[]{:S(2)}, u32[]{:S(2)}) collective-permute-start(f32[5,256]{1,0:T(8,128)S(1)} %add.287), channel_id=1, source_target_pairs={{0,8},{1,9},{2,10},{3,11},{4,12},{5,13},{6,14},{7,15},{8,0},{9,1},... | collective-permute-start | bytes 15368 | tf_op jit(solution)/shard_map/ppermute | solution.py:174
  34.3 1.8 copy-start.4
  36.2 15.7 %collective-permute-start.12 = (f32[6,12,128]{2,1,0:T(8,128)S(1)}, f32[6,12,128]{2,1,0:T(8,128)S(1)}, u32[]{:S(2)}, u32[]{:S(2)}) collective-permute-start(f32[6,12,128]{2,1,0:T(8,128)S(1)} %pad_maximum_fusion.11), channel_id=1, source_target_pairs={{16,0},{32,16},{48,32},{64,48},{80,64},{96,80},{112,96},{128,112},... | collective-permute-start | bytes 110600 | tf_op jit(solution)/shard_map/ppermute | solution.py:22
  37.5 20.5 %collective-permute-start.13 = (f32[6,12,128]{2,1,0:T(8,128)S(1)}, f32[6,12,128]{2,1,0:T(8,128)S(1)}, u32[]{:S(2)}, u32[]{:S(2)}) collective-permute-start(f32[6,12,128]{2,1,0:T(8,128)S(1)} %pad_maximum_fusion.11), channel_id=1, source_target_pairs={{32,0},{48,16},{64,32},{80,48},{96,64},{112,80},{128,96},{144,112}... | collective-permute-start | bytes 110600 | tf_op jit(solution)/shard_map/ppermute | solution.py:22
  38.8 19.2 %collective-permute-start.10 = (f32[6,12,128]{2,1,0:T(8,128)S(1)}, f32[6,12,128]{2,1,0:T(8,128)S(1)}, u32[]{:S(2)}, u32[]{:S(2)}) collective-permute-start(f32[6,12,128]{2,1,0:T(8,128)S(1)} %pad_maximum_fusion.10), channel_id=1, source_target_pairs={{0,16},{16,32},{32,48},{48,64},{64,80},{80,96},{96,112},{112,128},... | collective-permute-start | bytes 110600 | tf_op jit(solution)/shard_map/ppermute | solution.py:22
  43.8 14.2 %collective-permute-start.11 = (f32[6,12,128]{2,1,0:T(8,128)S(1)}, f32[6,12,128]{2,1,0:T(8,128)S(1)}, u32[]{:S(2)}, u32[]{:S(2)}) collective-permute-start(f32[6,12,128]{2,1,0:T(8,128)S(1)} %pad_maximum_fusion.10), channel_id=1, source_target_pairs={{0,32},{16,48},{32,64},{48,80},{64,96},{80,112},{96,128},{112,144}... | collective-permute-start | bytes 110600 | tf_op jit(solution)/shard_map/ppermute | solution.py:22
  50.6 9.6 %collective-permute-start.9 = (f32[37,12,128]{2,0,1:T(8,128)S(1)}, f32[37,12,128]{2,0,1:T(8,128)S(1)}, u32[]{:S(2)}, u32[]{:S(2)}) collective-permute-start(f32[37,12,128]{2,0,1:T(8,128)S(1)} %pad_maximum_fusion.3), channel_id=1, source_target_pairs={{32,0},{48,16},{64,32},{80,48},{96,64},{112,80},{128,96},{144,112}... | collective-permute-start | bytes 681992 | tf_op jit(solution)/shard_map/ppermute | solution.py:22
  51.9 10.9 %collective-permute-start.8 = (f32[37,12,128]{2,0,1:T(8,128)S(1)}, f32[37,12,128]{2,0,1:T(8,128)S(1)}, u32[]{:S(2)}, u32[]{:S(2)}) collective-permute-start(f32[37,12,128]{2,0,1:T(8,128)S(1)} %pad_maximum_fusion.2), channel_id=1, source_target_pairs={{0,32},{16,48},{32,64},{48,80},{64,96},{80,112},{96,128},{112,144}... | collective-permute-start | bytes 681992 | tf_op jit(solution)/shard_map/ppermute | solution.py:22
  62.9 15.9 %collective-permute-start.17 = (f32[6,12,128]{2,1,0:T(8,128)S(1)}, f32[6,12,128]{2,1,0:T(8,128)S(1)}, u32[]{:S(2)}, u32[]{:S(2)}) collective-permute-start(f32[6,12,128]{2,1,0:T(8,128)S(1)} %pad_maximum_fusion.13), channel_id=1, source_target_pairs={{32,0},{48,16},{64,32},{80,48},{96,64},{112,80},{128,96},{144,112}... | collective-permute-start | bytes 110600 | tf_op jit(solution)/shard_map/ppermute | solution.py:22
  64.2 14.6 %collective-permute-start.16 = (f32[6,12,128]{2,1,0:T(8,128)S(1)}, f32[6,12,128]{2,1,0:T(8,128)S(1)}, u32[]{:S(2)}, u32[]{:S(2)}) collective-permute-start(f32[6,12,128]{2,1,0:T(8,128)S(1)} %pad_maximum_fusion.12), channel_id=1, source_target_pairs={{0,32},{16,48},{32,64},{48,80},{64,96},{80,112},{96,128},{112,144}... | collective-permute-start | bytes 110600 | tf_op jit(solution)/shard_map/ppermute | solution.py:22
  70.8 10.2 %collective-permute-start.15 = (f32[37,12,128]{2,0,1:T(8,128)S(1)}, f32[37,12,128]{2,0,1:T(8,128)S(1)}, u32[]{:S(2)}, u32[]{:S(2)}) collective-permute-start(f32[37,12,128]{2,0,1:T(8,128)S(1)} %pad_maximum_fusion.5), channel_id=1, source_target_pairs={{64,0},{80,16},{96,32},{112,48},{128,64},{144,80},{160,96},{176,11... | collective-permute-start | bytes 681992 | tf_op jit(solution)/shard_map/ppermute | solution.py:22
  72.1 10.4 %collective-permute-start.14 = (f32[37,12,128]{2,0,1:T(8,128)S(1)}, f32[37,12,128]{2,0,1:T(8,128)S(1)}, u32[]{:S(2)}, u32[]{:S(2)}) collective-permute-start(f32[37,12,128]{2,0,1:T(8,128)S(1)} %pad_maximum_fusion.4), channel_id=1, source_target_pairs={{0,64},{16,80},{32,96},{48,112},{64,128},{80,144},{96,160},{112,17... | collective-permute-start | bytes 681992 | tf_op jit(solution)/shard_map/ppermute | solution.py:22
  82.6 13.8 %collective-permute-start.21 = (f32[6,12,128]{2,1,0:T(8,128)S(1)}, f32[6,12,128]{2,1,0:T(8,128)S(1)}, u32[]{:S(2)}, u32[]{:S(2)}) collective-permute-start(f32[6,12,128]{2,1,0:T(8,128)S(1)} %pad_maximum_fusion.15), channel_id=1, source_target_pairs={{64,0},{80,16},{96,32},{112,48},{128,64},{144,80},{160,96},{176,11... | collective-permute-start | bytes 110600 | tf_op jit(solution)/shard_map/ppermute | solution.py:22
  83.9 12.5 %collective-permute-start.20 = (f32[6,12,128]{2,1,0:T(8,128)S(1)}, f32[6,12,128]{2,1,0:T(8,128)S(1)}, u32[]{:S(2)}, u32[]{:S(2)}) collective-permute-start(f32[6,12,128]{2,1,0:T(8,128)S(1)} %pad_maximum_fusion.14), channel_id=1, source_target_pairs={{0,64},{16,80},{32,96},{48,112},{64,128},{80,144},{96,160},{112,17... | collective-permute-start | bytes 110600 | tf_op jit(solution)/shard_map/ppermute | solution.py:22
  89.0 9.6 %collective-permute-start.19 = (f32[37,12,128]{2,0,1:T(8,128)S(1)}, f32[37,12,128]{2,0,1:T(8,128)S(1)}, u32[]{:S(2)}, u32[]{:S(2)}) collective-permute-start(f32[37,12,128]{2,0,1:T(8,128)S(1)} %pad_maximum_fusion.7), channel_id=1, source_target_pairs={{128,0},{144,16},{160,32},{176,48},{192,64},{208,80},{224,96},{240... | collective-permute-start | bytes 681992 | tf_op jit(solution)/shard_map/ppermute | solution.py:22
  90.3 9.8 %collective-permute-start.18 = (f32[37,12,128]{2,0,1:T(8,128)S(1)}, f32[37,12,128]{2,0,1:T(8,128)S(1)}, u32[]{:S(2)}, u32[]{:S(2)}) collective-permute-start(f32[37,12,128]{2,0,1:T(8,128)S(1)} %pad_maximum_fusion.6), channel_id=1, source_target_pairs={{0,128},{16,144},{32,160},{48,176},{64,192},{80,208},{96,224},{112... | collective-permute-start | bytes 681992 | tf_op jit(solution)/shard_map/ppermute | solution.py:22
  100.1 7.5 %collective-permute-start.23 = (f32[6,12,128]{2,1,0:T(8,128)S(1)}, f32[6,12,128]{2,1,0:T(8,128)S(1)}, u32[]{:S(2)}, u32[]{:S(2)}) collective-permute-start(f32[6,12,128]{2,1,0:T(8,128)S(1)} %pad_maximum_fusion.17), channel_id=1, source_target_pairs={{128,0},{144,16},{160,32},{176,48},{192,64},{208,80},{224,96},{240... | collective-permute-start | bytes 110600 | tf_op jit(solution)/shard_map/ppermute | solution.py:22
  101.4 7.8 %collective-permute-start.22 = (f32[6,12,128]{2,1,0:T(8,128)S(1)}, f32[6,12,128]{2,1,0:T(8,128)S(1)}, u32[]{:S(2)}, u32[]{:S(2)}) collective-permute-start(f32[6,12,128]{2,1,0:T(8,128)S(1)} %pad_maximum_fusion.16), channel_id=1, source_target_pairs={{0,128},{16,144},{32,160},{48,176},{64,192},{80,208},{96,224},{112... | collective-permute-start | bytes 110600 | tf_op jit(solution)/shard_map/ppermute | solution.py:22
  111.0 8.8 %copy-start.1 = (f32[25,256]{1,0:T(8,128)S(1)}, f32[25,256]{1,0:T(8,128)}, u32[]{:S(2)}) copy-start(f32[25,256]{1,0:T(8,128)} %param.13) | copy-start | bytes 76804
  111.0 8.8 %copy-start.2 = (f32[25,256]{1,0:T(8,128)S(1)}, f32[25,256]{1,0:T(8,128)}, u32[]{:S(2)}) copy-start(f32[25,256]{1,0:T(8,128)} %param.12) | copy-start | bytes 76804
  111.0 8.8 %copy-start.3 = (f32[25,256]{1,0:T(8,128)S(1)}, f32[25,256]{1,0:T(8,128)}, u32[]{:S(2)}) copy-start(f32[25,256]{1,0:T(8,128)} %param.11) | copy-start | bytes 76804
  112.3 1.2 collective-permute-start.24
  113.5 3.7 %collective-permute-start.25 = (f32[5,256]{1,0:T(8,128)S(1)}, f32[5,256]{1,0:T(8,128)S(1)}, u32[]{:S(2)}, u32[]{:S(2)}) collective-permute-start(f32[5,256]{1,0:T(8,128)S(1)} %add.313), channel_id=1, source_target_pairs={{0,2},{1,3},{2,0},{3,1},{4,6},{5,7},{6,4},{7,5},{8,10},{9,11},{10,... | collective-permute-start | bytes 15368 | tf_op jit(solution)/shard_map/ppermute | solution.py:174
  117.2 4.5 %collective-permute-start.26 = (f32[5,256]{1,0:T(8,128)S(1)}, f32[5,256]{1,0:T(8,128)S(1)}, u32[]{:S(2)}, u32[]{:S(2)}) collective-permute-start(f32[5,256]{1,0:T(8,128)S(1)} %add.314), channel_id=1, source_target_pairs={{0,4},{1,5},{2,6},{3,7},{4,0},{5,1},{6,2},{7,3},{8,12},{9,13},{10,... | collective-permute-start | bytes 15368 | tf_op jit(solution)/shard_map/ppermute | solution.py:174
  121.7 7.6 %collective-permute-start.27 = (f32[5,256]{1,0:T(8,128)S(1)}, f32[5,256]{1,0:T(8,128)S(1)}, u32[]{:S(2)}, u32[]{:S(2)}) collective-permute-start(f32[5,256]{1,0:T(8,128)S(1)} %add.315), channel_id=1, source_target_pairs={{0,8},{1,9},{2,10},{3,11},{4,12},{5,13},{6,14},{7,15},{8,0},{9,1},... | collective-permute-start | bytes 15368 | tf_op jit(solution)/shard_map/ppermute | solution.py:174
  129.3 11.7 %collective-permute-start.28 = (f32[80,2,128]{2,1,0:T(2,128)S(1)}, f32[80,2,128]{2,1,0:T(2,128)S(1)}, u32[]{:S(2)}, u32[]{:S(2)}) collective-permute-start(f32[80,2,128]{2,1,0:T(2,128)S(1)} %constant_dynamic-update-slice_fusion), channel_id=1, source_target_pairs={{0,32},{16,48},{32,64},{48,80},{64,96},{80,112},{96,128},{112,144}... | collective-permute-start | bytes 245768 | tf_op jit(solution)/shard_map/ppermute | solution.py:22
  133.6 7.4 %collective-permute-start.29 = (f32[80,2,128]{2,1,0:T(2,128)S(1)}, f32[80,2,128]{2,1,0:T(2,128)S(1)}, u32[]{:S(2)}, u32[]{:S(2)}) collective-permute-start(f32[80,2,128]{2,1,0:T(2,128)S(1)} %constant_dynamic-update-slice_fusion), channel_id=1, source_target_pairs={{0,16},{16,32},{32,48},{48,64},{64,80},{80,96},{96,112},{112,128},... | collective-permute-start | bytes 245768 | tf_op jit(solution)/shard_map/ppermute | solution.py:22
  138.2 7.2 %collective-permute-start.30 = (f32[80,2,128]{2,1,0:T(2,128)S(1)}, f32[80,2,128]{2,1,0:T(2,128)S(1)}, u32[]{:S(2)}, u32[]{:S(2)}) collective-permute-start(f32[80,2,128]{2,1,0:T(2,128)S(1)} %constant_dynamic-update-slice_fusion), channel_id=1, source_target_pairs={{16,0},{32,16},{48,32},{64,48},{80,64},{96,80},{112,96},{128,112},... | collective-permute-start | bytes 245768 | tf_op jit(solution)/shard_map/ppermute | solution.py:22
  139.5 8.0 %collective-permute-start.31 = (f32[80,2,128]{2,1,0:T(2,128)S(1)}, f32[80,2,128]{2,1,0:T(2,128)S(1)}, u32[]{:S(2)}, u32[]{:S(2)}) collective-permute-start(f32[80,2,128]{2,1,0:T(2,128)S(1)} %constant_dynamic-update-slice_fusion), channel_id=1, source_target_pairs={{32,0},{48,16},{64,32},{80,48},{96,64},{112,80},{128,96},{144,112}... | collective-permute-start | bytes 245768 | tf_op jit(solution)/shard_map/ppermute | solution.py:22
  148.6 41.1 %copy-start.5 = (f32[24]{0:T(128)S(1)}, f32[24]{0:T(128)}, u32[]{:S(2)}) copy-start(f32[24]{0:T(128)} %constant.36.clone) | copy-start | bytes 292
  148.6 41.1 %copy-start.7 = (f32[24]{0:T(128)S(1)}, f32[24]{0:T(128)}, u32[]{:S(2)}) copy-start(f32[24]{0:T(128)} %constant.81) | copy-start | bytes 292
  148.7 41.2 %copy-start.6 = (f32[1,24]{1,0:T(1,128)S(1)}, f32[1,24]{1,0:T(1,128)}, u32[]{:S(2)}) copy-start(f32[1,24]{1,0:T(1,128)} %constant.85) | copy-start | bytes 292
  152.3 1.1 collective-permute-start.32
  153.5 3.6 %collective-permute-start.33 = (f32[26]{0:T(128)S(1)}, f32[26]{0:T(128)S(1)}, u32[]{:S(2)}, u32[]{:S(2)}) collective-permute-start(f32[26]{0:T(128)S(1)} %fusion.62), channel_id=1, source_target_pairs={{0,2},{1,3},{2,0},{3,1},{4,6},{5,7},{6,4},{7,5},{8,10},{9,11},{10,... | collective-permute-start | bytes 320 | tf_op jit(solution)/shard_map/ppermute | solution.py:174
  157.1 4.4 %collective-permute-start.34 = (f32[26]{0:T(128)S(1)}, f32[26]{0:T(128)S(1)}, u32[]{:S(2)}, u32[]{:S(2)}) collective-permute-start(f32[26]{0:T(128)S(1)} %add.320), channel_id=1, source_target_pairs={{0,4},{1,5},{2,6},{3,7},{4,0},{5,1},{6,2},{7,3},{8,12},{9,13},{10,... | collective-permute-start | bytes 320 | tf_op jit(solution)/shard_map/ppermute | solution.py:174
  161.5 7.4 %collective-permute-start.35 = (f32[26]{0:T(128)S(1)}, f32[26]{0:T(128)S(1)}, u32[]{:S(2)}, u32[]{:S(2)}) collective-permute-start(f32[26]{0:T(128)S(1)} %add.321), channel_id=1, source_target_pairs={{0,8},{1,9},{2,10},{3,11},{4,12},{5,13},{6,14},{7,15},{8,0},{9,1},... | collective-permute-start | bytes 320 | tf_op jit(solution)/shard_map/ppermute | solution.py:174
  169.0 4.0 %collective-permute-start.36 = (f32[26]{0:T(128)S(1)}, f32[26]{0:T(128)S(1)}, u32[]{:S(2)}, u32[]{:S(2)}) collective-permute-start(f32[26]{0:T(128)S(1)} %add.322), channel_id=1, source_target_pairs={{0,16},{16,0},{32,48},{48,32},{64,80},{80,64},{96,112},{112,96},{1... | collective-permute-start | bytes 320 | tf_op jit(solution)/shard_map/ppermute | solution.py:174
  173.0 5.5 %collective-permute-start.37 = (f32[26]{0:T(128)S(1)}, f32[26]{0:T(128)S(1)}, u32[]{:S(2)}, u32[]{:S(2)}) collective-permute-start(f32[26]{0:T(128)S(1)} %add.323), channel_id=1, source_target_pairs={{0,32},{16,48},{32,0},{48,16},{64,96},{80,112},{96,64},{112,80},{1... | collective-permute-start | bytes 320 | tf_op jit(solution)/shard_map/ppermute | solution.py:174
  178.5 4.6 %collective-permute-start.38 = (f32[26]{0:T(128)S(1)}, f32[26]{0:T(128)S(1)}, u32[]{:S(2)}, u32[]{:S(2)}) collective-permute-start(f32[26]{0:T(128)S(1)} %add.324), channel_id=1, source_target_pairs={{0,64},{16,80},{32,96},{48,112},{64,0},{80,16},{96,32},{112,48},{1... | collective-permute-start | bytes 320 | tf_op jit(solution)/shard_map/ppermute | solution.py:174
  183.1 6.0 %collective-permute-start.39 = (f32[26]{0:T(128)S(1)}, f32[26]{0:T(128)S(1)}, u32[]{:S(2)}, u32[]{:S(2)}) collective-permute-start(f32[26]{0:T(128)S(1)} %add.325), channel_id=1, source_target_pairs={{0,128},{16,144},{32,160},{48,176},{64,192},{80,208},{96,224},{112... | collective-permute-start | bytes 320 | tf_op jit(solution)/shard_map/ppermute | solution.py:174

commit v6 on v5

--- a/solution.py
+++ b/solution.py
@@ -207,6 +207,50 @@
     return joined_field(sweep, inflow_neg, inflow_pos)
 
 
+def caught_up_side(own, own_span, rate, drive, count, sign):
+    reach = min(2 * own_span, count - 1)
+    own_rows = own[1].shape[0]
+    moment_rows = drive.shape[0]
+    fetched_maps = {}
+    for distance in range(1, reach + 1):
+        if distance == own_span and own_span < count - 1:
+            packed = jnp.concatenate([own[0], own[1], rate, drive], axis=0)
+            got = received(packed, sign * distance)
+            got_own = (got[:1], got[1 : 1 + own_rows])
+            fetched_maps[distance] = (got[1 + own_rows : 2 + own_rows], got[2 + own_rows :])
+        else:
+            got = received(jnp.concatenate([rate, drive], axis=0), sign * distance)
+            fetched_maps[distance] = (got[:1], got[1:])
+    if own_span < count - 1:
+        own = (own[0] * got_own[0], own[0] * got_own[1] + own[1])
+    acc_a, acc_b = fetched_maps[reach]
+    for distance in range(reach - 1, 0, -1):
+        near_a, near_b = fetched_maps[distance]
+        acc_a, acc_b = near_a * acc_a, near_a * acc_b + near_b
+    return own, (acc_a, acc_b)
+
+
+def caught_up(own_pos, own_neg, own_span, moment_sweep, count):
+    own_pos, moment_pos = caught_up_side(
+        own_pos, own_span, moment_sweep[2][:, :, -1], moment_sweep[3][:, :, -1], count, 1
+    )
+    own_neg, moment_neg = caught_up_side(
+        own_neg, own_span, moment_sweep[0][:, :, 0], moment_sweep[1][:, :, 0], count, -1
+    )
+    return lax.optimization_barrier((own_pos, own_neg, moment_pos, moment_neg))
+
+
+def joint_next(own, moment, span, sign):
+    own_rows = own[1].shape[0]
+    packed = jnp.concatenate([own[0], own[1], moment[1]], axis=0)
+    got = received(packed, sign * span)
+    got_a, got_own, got_moment = got[:1], got[1 : 1 + own_rows], got[1 + own_rows :]
+    return (
+        (own[0] * got_a, own[0] * got_own + own[1]),
+        (own[0] * got_a, own[0] * got_moment + moment[1]),
+    )
+
+
 def body(distribution, collision, lower_blocks, upper_blocks, diag_inverse):
     node_count = distribution.shape[0]
     cell_count = distribution.shape[1]
@@ -236,22 +280,17 @@
     own_pos, own_neg, old_moments = lax.optimization_barrier((own_pos, own_neg, old_moments))
     moment_drive = thickness * old_moments.reshape(5, 1, length, TUBES) / denominator
     moment_sweep = local_sweep(carry_rate, moment_drive)
-    moment_pos, moment_span = scan_first(moment_sweep[2][:, :, -1], moment_sweep[3][:, :, -1], 1)
-    moment_neg, _ = scan_first(moment_sweep[0][:, :, 0], moment_sweep[1][:, :, 0], -1)
-    while True:
-        if own_span < count - 1:
-            own_pos, next_span = scan_next(own_pos, own_span, 1)
-            own_neg, _ = scan_next(own_neg, own_span, -1)
-            own_span = next_span
+    own_pos, own_neg, moment_pos, moment_neg = caught_up(
+        own_pos, own_neg, own_span, moment_sweep, count
+    )
+    span = min(2 * own_span, count)
+    while span < count - 1:
+        own_pos, moment_pos = joint_next(own_pos, moment_pos, span, 1)
+        own_neg, moment_neg = joint_next(own_neg, moment_neg, span, -1)
+        span *= 2
         own_pos, own_neg, moment_pos, moment_neg = lax.optimization_barrier(
             (own_pos, own_neg, moment_pos, moment_neg)
         )
-        if moment_span >= count - 1 and own_span >= count - 1:
-            break
-        if moment_span < count - 1:
-            moment_pos, next_span = scan_next(moment_pos, moment_span, 1)
-            moment_neg, _ = scan_next(moment_neg, moment_span, -1)
-            moment_span = next_span
     own_field = joined_field(own_sweep, own_neg[1], own_pos[1])
     moment_field = joined_field(moment_sweep, moment_neg[1], moment_pos[1])
     basis = rebuild.reshape(5, node_rows, NXI, 1, 1)

time: 197 us -> 182 us (0.924)
  starting transfers between devices: 128 us -> 101 us
  waiting for transfers between devices: 44.6 us -> 58.3 us
    ppermute x24 -> x20, starting transfers between devices: 84 us -> 70.4 us  [passed_along(): return lax.ppermute(block, axis, route)]
    ppermute x16, starting transfers between devices: 44 us -> 31 us  [tree_sum(): lax.ppermute(block, axis, [(i, i ^ bit) for i in range(count)])]
    ppermute x16, waiting for transfers between devices: 24.6 us -> 36.8 us  [tree_sum(): lax.ppermute(block, axis, [(i, i ^ bit) for i in range(count)])]
    ppermute x24 -> x20, waiting for transfers between devices: 20 us -> 21.5 us  [passed_along(): return lax.ppermute(block, axis, route)]
  transfers between devices with their start and end apart: 40 -> 36, of which waited for: 25 -> 22; matrix products, arithmetic and copies ran while one was open for 2% -> 2% of each run, Pallas kernels for 0% -> 0%
where the time goes in v6:
time: 182 us; the launch traced here: 179 us
  starting transfers between devices  101 us (55%)
  waiting for transfers between devices  58.3 us (32%)
  other arithmetic  8.56 us (5%)
  matrix products  5.23 us (3%)
  local copies, waits for them, and re-layouts  3.78 us (2%)
  between operations  1.86 us (1%)
    ppermute x20, starting transfers between devices, passed_along(): return lax.ppermute(block, axis, route)  70.4 us
    ppermute x16, waiting for transfers between devices, tree_sum(): lax.ppermute(block, axis, [(i, i ^ bit) for i in range(count)])  36.8 us
    ppermute x16, starting transfers between devices, tree_sum(): lax.ppermute(block, axis, [(i, i ^ bit) for i in range(count)])  31 us
    ppermute x20, waiting for transfers between devices, passed_along(): return lax.ppermute(block, axis, route)  21.5 us
  transfers between devices with their start and end apart: 36, of which 22 were waited for; matrix products, arithmetic and copies ran while one was open for 2% of the time, Pallas kernels for 0%

profile of v6, /device:TPU:32, one launch (start us, length us, event | category | flops | bytes accessed | tf_op | source)
XLA Modules:
  0.0 179.1 jit_solution(3826976442082438572)
XLA Ops:
  0.7 1.8 fusion.26
  3.6 1.3 collective-permute-start.2
  4.9 1.3 collective-permute-start.3
  6.2 1.9 %collective-permute-start.5 = (f32[5,256]{1,0:T(8,128)S(1)}, f32[5,256]{1,0:T(8,128)S(1)}, u32[]{:S(2)}, u32[]{:S(2)}) collective-permute-start(f32[5,256]{1,0:T(8,128)S(1)} %add.291), channel_id=1, source_target_pairs={{0,2},{1,3},{2,0},{3,1},{4,6},{5,7},{6,4},{7,5},{8,10},{9,11},{10,... | collective-permute-start | bytes 15368 | tf_op jit(solution)/shard_map/ppermute | solution.py:174
  8.1 1.8 collective-permute-done.5
  9.9 3.3 %collective-permute-start.6 = (f32[5,256]{1,0:T(8,128)S(1)}, f32[5,256]{1,0:T(8,128)S(1)}, u32[]{:S(2)}, u32[]{:S(2)}) collective-permute-start(f32[5,256]{1,0:T(8,128)S(1)} %add.292), channel_id=1, source_target_pairs={{0,4},{1,5},{2,6},{3,7},{4,0},{5,1},{6,2},{7,3},{8,12},{9,13},{10,... | collective-permute-start | bytes 15368 | tf_op jit(solution)/shard_map/ppermute | solution.py:174
  13.3 1.6 collective-permute-done.6
  14.8 5.9 %collective-permute-start.7 = (f32[5,256]{1,0:T(8,128)S(1)}, f32[5,256]{1,0:T(8,128)S(1)}, u32[]{:S(2)}, u32[]{:S(2)}) collective-permute-start(f32[5,256]{1,0:T(8,128)S(1)} %add.293), channel_id=1, source_target_pairs={{0,8},{1,9},{2,10},{3,11},{4,12},{5,13},{6,14},{7,15},{8,0},{9,1},... | collective-permute-start | bytes 15368 | tf_op jit(solution)/shard_map/ppermute | solution.py:174
  20.8 4.6 %collective-permute-start = (f32[37,12,128]{2,0,1:T(8,128)S(1)}, f32[37,12,128]{2,0,1:T(8,128)S(1)}, u32[]{:S(2)}, u32[]{:S(2)}) collective-permute-start(f32[37,12,128]{2,0,1:T(8,128)S(1)} %pad_maximum_fusion.6), channel_id=1, source_target_pairs={{0,16},{16,32},{32,48},{48,64},{64,80},{80,96},{96,112},{112,128},... | collective-permute-start | bytes 681992 | tf_op jit(solution)/shard_map/ppermute | solution.py:22
  25.4 6.7 %collective-permute-start.1 = (f32[37,12,128]{2,0,1:T(8,128)S(1)}, f32[37,12,128]{2,0,1:T(8,128)S(1)}, u32[]{:S(2)}, u32[]{:S(2)}) collective-permute-start(f32[37,12,128]{2,0,1:T(8,128)S(1)} %pad_maximum_fusion.6), channel_id=1, source_target_pairs={{0,32},{16,48},{32,64},{48,80},{64,96},{80,112},{96,128},{112,144}... | collective-permute-start | bytes 681992 | tf_op jit(solution)/shard_map/ppermute | solution.py:22
  32.1 3.6 %collective-permute-done.1 = f32[37,12,128]{2,0,1:T(8,128)S(1)} collective-permute-done((f32[37,12,128]{2,0,1:T(8,128)S(1)}, f32[37,12,128]{2,0,1:T(8,128)S(1)}, u32[]{:S(2)}, u32[]{:S(2)}) %collective-permute-start.1) | collective-permute-done | bytes 227360 | tf_op jit(solution)/shard_map/ppermute | solution.py:22
  38.7 1.3 collective-permute-start.9
  40.0 9.4 %collective-permute-start.11 = (f32[6,12,128]{2,0,1:T(8,128)S(1)}, f32[6,12,128]{2,0,1:T(8,128)S(1)}, u32[]{:S(2)}, u32[]{:S(2)}) collective-permute-start(f32[6,12,128]{2,0,1:T(8,128)S(1)} %pad_maximum_fusion.10), channel_id=1, source_target_pairs={{0,48},{16,64},{32,80},{48,96},{64,112},{80,128},{96,144},{112,160... | collective-permute-start | bytes 110600 | tf_op jit(solution)/shard_map/ppermute | solution.py:22
  49.4 4.8 %collective-permute-start.10 = (f32[6,12,128]{2,0,1:T(8,128)S(1)}, f32[6,12,128]{2,0,1:T(8,128)S(1)}, u32[]{:S(2)}, u32[]{:S(2)}) collective-permute-start(f32[6,12,128]{2,0,1:T(8,128)S(1)} %pad_maximum_fusion.10), channel_id=1, source_target_pairs={{0,16},{16,32},{32,48},{48,64},{64,80},{80,96},{96,112},{112,128},... | collective-permute-start | bytes 110600 | tf_op jit(solution)/shard_map/ppermute | solution.py:22
  54.3 5.4 %collective-permute-start.8 = (f32[43,12,128]{2,0,1:T(8,128)S(1)}, f32[43,12,128]{2,0,1:T(8,128)S(1)}, u32[]{:S(2)}, u32[]{:S(2)}) collective-permute-start(f32[43,12,128]{2,0,1:T(8,128)S(1)} %pad_maximum_fusion), channel_id=1, source_target_pairs={{0,32},{16,48},{32,64},{48,80},{64,96},{80,112},{96,128},{112,144}... | collective-permute-start | bytes 792584 | tf_op jit(solution)/shard_map/ppermute | solution.py:22
  61.1 7.0 %collective-permute-start.12 = (f32[6,12,128]{2,0,1:T(8,128)S(1)}, f32[6,12,128]{2,0,1:T(8,128)S(1)}, u32[]{:S(2)}, u32[]{:S(2)}) collective-permute-start(f32[6,12,128]{2,0,1:T(8,128)S(1)} %pad_maximum_fusion.10), channel_id=1, source_target_pairs={{0,64},{16,80},{32,96},{48,112},{64,128},{80,144},{96,160},{112,17... | collective-permute-start | bytes 110600 | tf_op jit(solution)/shard_map/ppermute | solution.py:22
  68.4 1.4 collective-permute-done.12
  72.2 4.9 %collective-permute-start.16 = (f32[42,12,128]{2,0,1:T(8,128)S(1)}, f32[42,12,128]{2,0,1:T(8,128)S(1)}, u32[]{:S(2)}, u32[]{:S(2)}) collective-permute-start(f32[42,12,128]{2,0,1:T(8,128)S(1)} %pad_maximum_fusion.2), channel_id=1, source_target_pairs={{0,64},{16,80},{32,96},{48,112},{64,128},{80,144},{96,160},{112,17... | collective-permute-start | bytes 774152 | tf_op jit(solution)/shard_map/ppermute | solution.py:22
  77.1 1.8 collective-permute-done.17
  79.0 2.3 %collective-permute-done.16 = f32[42,12,128]{2,0,1:T(8,128)S(1)} collective-permute-done((f32[42,12,128]{2,0,1:T(8,128)S(1)}, f32[42,12,128]{2,0,1:T(8,128)S(1)}, u32[]{:S(2)}, u32[]{:S(2)}) %collective-permute-start.16) | collective-permute-done | bytes 258080 | tf_op jit(solution)/shard_map/ppermute | solution.py:22
  83.0 7.0 %collective-permute-start.18 = (f32[42,12,128]{2,0,1:T(8,128)S(1)}, f32[42,12,128]{2,0,1:T(8,128)S(1)}, u32[]{:S(2)}, u32[]{:S(2)}) collective-permute-start(f32[42,12,128]{2,0,1:T(8,128)S(1)} %pad_maximum_fusion.4), channel_id=1, source_target_pairs={{0,128},{16,144},{32,160},{48,176},{64,192},{80,208},{96,224},{112... | collective-permute-start | bytes 774152 | tf_op jit(solution)/shard_map/ppermute | solution.py:22
  90.1 2.5 %collective-permute-done.19 = f32[42,12,128]{2,0,1:T(8,128)S(1)} collective-permute-done((f32[42,12,128]{2,0,1:T(8,128)S(1)}, f32[42,12,128]{2,0,1:T(8,128)S(1)}, u32[]{:S(2)}, u32[]{:S(2)}) %collective-permute-start.19) | collective-permute-done | bytes 258080 | tf_op jit(solution)/shard_map/ppermute | solution.py:22
  92.6 1.7 collective-permute-done.18
  99.7 2.6 %collective-permute-done.21 = f32[5,256]{1,0:T(8,128)S(1)} collective-permute-done((f32[5,256]{1,0:T(8,128)S(1)}, f32[5,256]{1,0:T(8,128)S(1)}, u32[]{:S(2)}, u32[]{:S(2)}) %collective-permute-start.21) | collective-permute-done | bytes 5152 | tf_op jit(solution)/shard_map/ppermute | solution.py:174
  102.4 1.5 collective-permute-start.22
  103.9 3.0 %collective-permute-done.22 = f32[5,256]{1,0:T(8,128)S(1)} collective-permute-done((f32[5,256]{1,0:T(8,128)S(1)}, f32[5,256]{1,0:T(8,128)S(1)}, u32[]{:S(2)}, u32[]{:S(2)}) %collective-permute-start.22) | collective-permute-done | bytes 5152 | tf_op jit(solution)/shard_map/ppermute | solution.py:174
  106.9 1.5 collective-permute-start.23
  108.5 6.0 %collective-permute-done.23 = f32[5,256]{1,0:T(8,128)S(1)} collective-permute-done((f32[5,256]{1,0:T(8,128)S(1)}, f32[5,256]{1,0:T(8,128)S(1)}, u32[]{:S(2)}, u32[]{:S(2)}) %collective-permute-start.23) | collective-permute-done | bytes 5152 | tf_op jit(solution)/shard_map/ppermute | solution.py:174
  114.5 4.4 %collective-permute-start.24 = (f32[80,2,128]{2,1,0:T(2,128)S(1)}, f32[80,2,128]{2,1,0:T(2,128)S(1)}, u32[]{:S(2)}, u32[]{:S(2)}) collective-permute-start(f32[80,2,128]{2,1,0:T(2,128)S(1)} %constant_dynamic-update-slice_fusion), channel_id=1, source_target_pairs={{0,32},{16,48},{32,64},{48,80},{64,96},{80,112},{96,128},{112,144}... | collective-permute-start | bytes 245768 | tf_op jit(solution)/shard_map/ppermute | solution.py:22
  118.9 3.1 %collective-permute-start.25 = (f32[80,2,128]{2,1,0:T(2,128)S(1)}, f32[80,2,128]{2,1,0:T(2,128)S(1)}, u32[]{:S(2)}, u32[]{:S(2)}) collective-permute-start(f32[80,2,128]{2,1,0:T(2,128)S(1)} %constant_dynamic-update-slice_fusion), channel_id=1, source_target_pairs={{0,16},{16,32},{32,48},{48,64},{64,80},{80,96},{96,112},{112,128},... | collective-permute-start | bytes 245768 | tf_op jit(solution)/shard_map/ppermute | solution.py:22
  123.3 1.5 collective-permute-start.27
  124.8 3.5 %collective-permute-done.26 = f32[80,2,128]{2,1,0:T(2,128)S(1)} collective-permute-done((f32[80,2,128]{2,1,0:T(2,128)S(1)}, f32[80,2,128]{2,1,0:T(2,128)S(1)}, u32[]{:S(2)}, u32[]{:S(2)}) %collective-permute-start.26) | collective-permute-done | bytes 81952 | tf_op jit(solution)/shard_map/ppermute | solution.py:22
  128.4 4.6 %collective-permute-done.27 = f32[80,2,128]{2,1,0:T(2,128)S(1)} collective-permute-done((f32[80,2,128]{2,1,0:T(2,128)S(1)}, f32[80,2,128]{2,1,0:T(2,128)S(1)}, u32[]{:S(2)}, u32[]{:S(2)}) %collective-permute-start.27) | collective-permute-done | bytes 81952 | tf_op jit(solution)/shard_map/ppermute | solution.py:22
  134.2 1.9 %abs_reduce_fusion = (f32[864]{0:T(1024)S(1)}, f32[864,256]{1,0:T(8,128)S(1)}) fusion(f32[1,5,2,128]{3,2,1,0:T(2,128)S(1)} %slice_bitcast_fusion, f32[5,13824]{1,0:T(8,128)} %constant.35.clone, s32[]{:T(128)S(6)} %select_n.2, f32[108,8,2,128]{3,2,1,0:T(2,128)S(1)} %bitcast.124), kind=kOutput, calls=%fused_computation.8 | convolution fusion | flops 13933728 | bytes 1806724 | tf_op jit(solution)/shard_map/dot_general | solution.py:321
  140.1 2.5 %collective-permute-done.29 = f32[26]{0:T(128)S(1)} collective-permute-done((f32[26]{0:T(128)S(1)}, f32[26]{0:T(128)S(1)}, u32[]{:S(2)}, u32[]{:S(2)}) %collective-permute-start.29) | collective-permute-done | bytes 136 | tf_op jit(solution)/shard_map/ppermute | solution.py:174
  142.6 1.5 collective-permute-start.30
  144.1 3.0 %collective-permute-done.30 = f32[26]{0:T(128)S(1)} collective-permute-done((f32[26]{0:T(128)S(1)}, f32[26]{0:T(128)S(1)}, u32[]{:S(2)}, u32[]{:S(2)}) %collective-permute-start.30) | collective-permute-done | bytes 136 | tf_op jit(solution)/shard_map/ppermute | solution.py:174
  147.1 7.4 %collective-permute-done.31 = f32[26]{0:T(128)S(1)} collective-permute-done((f32[26]{0:T(128)S(1)}, f32[26]{0:T(128)S(1)}, u32[]{:S(2)}, u32[]{:S(2)}) %collective-permute-start.31) | collective-permute-done | bytes 136 | tf_op jit(solution)/shard_map/ppermute | solution.py:174
  154.5 1.4 collective-permute-start.32
  155.9 2.1 %collective-permute-done.32 = f32[26]{0:T(128)S(1)} collective-permute-done((f32[26]{0:T(128)S(1)}, f32[26]{0:T(128)S(1)}, u32[]{:S(2)}, u32[]{:S(2)}) %collective-permute-start.32) | collective-permute-done | bytes 136 | tf_op jit(solution)/shard_map/ppermute | solution.py:174
  158.0 4.4 %collective-permute-start.33 = (f32[26]{0:T(128)S(1)}, f32[26]{0:T(128)S(1)}, u32[]{:S(2)}, u32[]{:S(2)}) collective-permute-start(f32[26]{0:T(128)S(1)} %add.331), channel_id=1, source_target_pairs={{0,32},{16,48},{32,0},{48,16},{64,96},{80,112},{96,64},{112,80},{1... | collective-permute-start | bytes 320 | tf_op jit(solution)/shard_map/ppermute | solution.py:174
  162.4 1.5 collective-permute-done.33
  164.0 2.7 %collective-permute-start.34 = (f32[26]{0:T(128)S(1)}, f32[26]{0:T(128)S(1)}, u32[]{:S(2)}, u32[]{:S(2)}) collective-permute-start(f32[26]{0:T(128)S(1)} %add.332), channel_id=1, source_target_pairs={{0,64},{16,80},{32,96},{48,112},{64,0},{80,16},{96,32},{112,48},{1... | collective-permute-start | bytes 320 | tf_op jit(solution)/shard_map/ppermute | solution.py:174
  166.7 1.5 collective-permute-done.34
  168.2 4.6 %collective-permute-start.35 = (f32[26]{0:T(128)S(1)}, f32[26]{0:T(128)S(1)}, u32[]{:S(2)}, u32[]{:S(2)}) collective-permute-start(f32[26]{0:T(128)S(1)} %add.333), channel_id=1, source_target_pairs={{0,128},{16,144},{32,160},{48,176},{64,192},{80,208},{96,224},{112... | collective-permute-start | bytes 320 | tf_op jit(solution)/shard_map/ppermute | solution.py:174
  172.8 1.5 collective-permute-done.35
  175.1 1.3 multiply_bitcast_fusion.2
  176.6 1.3 add_bitcast_fusion
  (204 shorter events, 23.5 us)
Async XLA Ops:
  0.6 1.9 %copy-start.7 = (f32[24]{0:T(128)S(1)}, f32[24]{0:T(128)}, u32[]{:S(2)}) copy-start(f32[24]{0:T(128)} %constant.78) | copy-start | bytes 292
  0.6 2.1 %copy-start = (f32[864,256]{1,0:T(8,128)S(1)}, f32[864,256]{1,0:T(8,128)}, u32[]{:S(2)}) copy-start(f32[864,256]{1,0:T(8,128)} %param.9) | copy-start | bytes 2654212
  0.7 1.9 %copy-start.4 = (f32[256]{0:T(256)S(1)}, f32[256]{0:T(256)}, u32[]{:S(2)}) copy-start(f32[256]{0:T(256)} %param.10) | copy-start | bytes 3076
  2.4 3.7 %collective-permute-start.4 = (f32[5,256]{1,0:T(8,128)S(1)}, f32[5,256]{1,0:T(8,128)S(1)}, u32[]{:S(2)}, u32[]{:S(2)}) collective-permute-start(f32[5,256]{1,0:T(8,128)S(1)} %fusion.26), channel_id=1, source_target_pairs={{0,1},{1,0},{2,3},{3,2},{4,5},{5,4},{6,7},{7,6},{8,9},{9,8},{10,11... | collective-permute-start | bytes 15368 | tf_op jit(solution)/shard_map/ppermute | solution.py:174
  3.6 28.5 %collective-permute-start.2 = (f32[37,12,128]{2,0,1:T(8,128)S(1)}, f32[37,12,128]{2,0,1:T(8,128)S(1)}, u32[]{:S(2)}, u32[]{:S(2)}) collective-permute-start(f32[37,12,128]{2,0,1:T(8,128)S(1)} %pad_maximum_fusion.7), channel_id=1, source_target_pairs={{16,0},{32,16},{48,32},{64,48},{80,64},{96,80},{112,96},{128,112},... | collective-permute-start | bytes 681992 | tf_op jit(solution)/shard_map/ppermute | solution.py:22
  4.9 27.2 %collective-permute-start.3 = (f32[37,12,128]{2,0,1:T(8,128)S(1)}, f32[37,12,128]{2,0,1:T(8,128)S(1)}, u32[]{:S(2)}, u32[]{:S(2)}) collective-permute-start(f32[37,12,128]{2,0,1:T(8,128)S(1)} %pad_maximum_fusion.7), channel_id=1, source_target_pairs={{32,0},{48,16},{64,32},{80,48},{96,64},{112,80},{128,96},{144,112}... | collective-permute-start | bytes 681992 | tf_op jit(solution)/shard_map/ppermute | solution.py:22
  6.2 3.7 %collective-permute-start.5 = (f32[5,256]{1,0:T(8,128)S(1)}, f32[5,256]{1,0:T(8,128)S(1)}, u32[]{:S(2)}, u32[]{:S(2)}) collective-permute-start(f32[5,256]{1,0:T(8,128)S(1)} %add.291), channel_id=1, source_target_pairs={{0,2},{1,3},{2,0},{3,1},{4,6},{5,7},{6,4},{7,5},{8,10},{9,11},{10,... | collective-permute-start | bytes 15368 | tf_op jit(solution)/shard_map/ppermute | solution.py:174
  9.9 4.9 %collective-permute-start.6 = (f32[5,256]{1,0:T(8,128)S(1)}, f32[5,256]{1,0:T(8,128)S(1)}, u32[]{:S(2)}, u32[]{:S(2)}) collective-permute-start(f32[5,256]{1,0:T(8,128)S(1)} %add.292), channel_id=1, source_target_pairs={{0,4},{1,5},{2,6},{3,7},{4,0},{5,1},{6,2},{7,3},{8,12},{9,13},{10,... | collective-permute-start | bytes 15368 | tf_op jit(solution)/shard_map/ppermute | solution.py:174
  14.8 17.2 %collective-permute-start.7 = (f32[5,256]{1,0:T(8,128)S(1)}, f32[5,256]{1,0:T(8,128)S(1)}, u32[]{:S(2)}, u32[]{:S(2)}) collective-permute-start(f32[5,256]{1,0:T(8,128)S(1)} %add.293), channel_id=1, source_target_pairs={{0,8},{1,9},{2,10},{3,11},{4,12},{5,13},{6,14},{7,15},{8,0},{9,1},... | collective-permute-start | bytes 15368 | tf_op jit(solution)/shard_map/ppermute | solution.py:174
  20.8 11.3 %collective-permute-start = (f32[37,12,128]{2,0,1:T(8,128)S(1)}, f32[37,12,128]{2,0,1:T(8,128)S(1)}, u32[]{:S(2)}, u32[]{:S(2)}) collective-permute-start(f32[37,12,128]{2,0,1:T(8,128)S(1)} %pad_maximum_fusion.6), channel_id=1, source_target_pairs={{0,16},{16,32},{32,48},{48,64},{64,80},{80,96},{96,112},{112,128},... | collective-permute-start | bytes 681992 | tf_op jit(solution)/shard_map/ppermute | solution.py:22
  25.4 10.4 %collective-permute-start.1 = (f32[37,12,128]{2,0,1:T(8,128)S(1)}, f32[37,12,128]{2,0,1:T(8,128)S(1)}, u32[]{:S(2)}, u32[]{:S(2)}) collective-permute-start(f32[37,12,128]{2,0,1:T(8,128)S(1)} %pad_maximum_fusion.6), channel_id=1, source_target_pairs={{0,32},{16,48},{32,64},{48,80},{64,96},{80,112},{96,128},{112,144}... | collective-permute-start | bytes 681992 | tf_op jit(solution)/shard_map/ppermute | solution.py:22
  36.0 18.3 %collective-permute-start.14 = (f32[6,12,128]{2,0,1:T(8,128)S(1)}, f32[6,12,128]{2,0,1:T(8,128)S(1)}, u32[]{:S(2)}, u32[]{:S(2)}) collective-permute-start(f32[6,12,128]{2,0,1:T(8,128)S(1)} %pad_maximum_fusion.11), channel_id=1, source_target_pairs={{48,0},{64,16},{80,32},{96,48},{112,64},{128,80},{144,96},{160,112... | collective-permute-start | bytes 110600 | tf_op jit(solution)/shard_map/ppermute | solution.py:22
  37.3 22.5 %collective-permute-start.13 = (f32[6,12,128]{2,0,1:T(8,128)S(1)}, f32[6,12,128]{2,0,1:T(8,128)S(1)}, u32[]{:S(2)}, u32[]{:S(2)}) collective-permute-start(f32[6,12,128]{2,0,1:T(8,128)S(1)} %pad_maximum_fusion.11), channel_id=1, source_target_pairs={{16,0},{32,16},{48,32},{64,48},{80,64},{96,80},{112,96},{128,112},... | collective-permute-start | bytes 110600 | tf_op jit(solution)/shard_map/ppermute | solution.py:22
  38.7 29.5 %collective-permute-start.9 = (f32[43,12,128]{2,0,1:T(8,128)S(1)}, f32[43,12,128]{2,0,1:T(8,128)S(1)}, u32[]{:S(2)}, u32[]{:S(2)}) collective-permute-start(f32[43,12,128]{2,0,1:T(8,128)S(1)} %pad_maximum_fusion.1), channel_id=1, source_target_pairs={{32,0},{48,16},{64,32},{80,48},{96,64},{112,80},{128,96},{144,112}... | collective-permute-start | bytes 792584 | tf_op jit(solution)/shard_map/ppermute | solution.py:22
  40.0 21.1 %collective-permute-start.11 = (f32[6,12,128]{2,0,1:T(8,128)S(1)}, f32[6,12,128]{2,0,1:T(8,128)S(1)}, u32[]{:S(2)}, u32[]{:S(2)}) collective-permute-start(f32[6,12,128]{2,0,1:T(8,128)S(1)} %pad_maximum_fusion.10), channel_id=1, source_target_pairs={{0,48},{16,64},{32,80},{48,96},{64,112},{80,128},{96,144},{112,160... | collective-permute-start | bytes 110600 | tf_op jit(solution)/shard_map/ppermute | solution.py:22
  49.4 18.8 %collective-permute-start.10 = (f32[6,12,128]{2,0,1:T(8,128)S(1)}, f32[6,12,128]{2,0,1:T(8,128)S(1)}, u32[]{:S(2)}, u32[]{:S(2)}) collective-permute-start(f32[6,12,128]{2,0,1:T(8,128)S(1)} %pad_maximum_fusion.10), channel_id=1, source_target_pairs={{0,16},{16,32},{32,48},{48,64},{64,80},{80,96},{96,112},{112,128},... | collective-permute-start | bytes 110600 | tf_op jit(solution)/shard_map/ppermute | solution.py:22
  54.3 14.0 %collective-permute-start.8 = (f32[43,12,128]{2,0,1:T(8,128)S(1)}, f32[43,12,128]{2,0,1:T(8,128)S(1)}, u32[]{:S(2)}, u32[]{:S(2)}) collective-permute-start(f32[43,12,128]{2,0,1:T(8,128)S(1)} %pad_maximum_fusion), channel_id=1, source_target_pairs={{0,32},{16,48},{32,64},{48,80},{64,96},{80,112},{96,128},{112,144}... | collective-permute-start | bytes 792584 | tf_op jit(solution)/shard_map/ppermute | solution.py:22
  59.8 8.6 %collective-permute-start.15 = (f32[6,12,128]{2,0,1:T(8,128)S(1)}, f32[6,12,128]{2,0,1:T(8,128)S(1)}, u32[]{:S(2)}, u32[]{:S(2)}) collective-permute-start(f32[6,12,128]{2,0,1:T(8,128)S(1)} %pad_maximum_fusion.11), channel_id=1, source_target_pairs={{64,0},{80,16},{96,32},{112,48},{128,64},{144,80},{160,96},{176,11... | collective-permute-start | bytes 110600 | tf_op jit(solution)/shard_map/ppermute | solution.py:22
  61.1 8.7 %collective-permute-start.12 = (f32[6,12,128]{2,0,1:T(8,128)S(1)}, f32[6,12,128]{2,0,1:T(8,128)S(1)}, u32[]{:S(2)}, u32[]{:S(2)}) collective-permute-start(f32[6,12,128]{2,0,1:T(8,128)S(1)} %pad_maximum_fusion.10), channel_id=1, source_target_pairs={{0,64},{16,80},{32,96},{48,112},{64,128},{80,144},{96,160},{112,17... | collective-permute-start | bytes 110600 | tf_op jit(solution)/shard_map/ppermute | solution.py:22
  70.0 8.9 %collective-permute-start.17 = (f32[42,12,128]{2,0,1:T(8,128)S(1)}, f32[42,12,128]{2,0,1:T(8,128)S(1)}, u32[]{:S(2)}, u32[]{:S(2)}) collective-permute-start(f32[42,12,128]{2,0,1:T(8,128)S(1)} %pad_maximum_fusion.3), channel_id=1, source_target_pairs={{64,0},{80,16},{96,32},{112,48},{128,64},{144,80},{160,96},{176,11... | collective-permute-start | bytes 774152 | tf_op jit(solution)/shard_map/ppermute | solution.py:22
  72.2 9.1 %collective-permute-start.16 = (f32[42,12,128]{2,0,1:T(8,128)S(1)}, f32[42,12,128]{2,0,1:T(8,128)S(1)}, u32[]{:S(2)}, u32[]{:S(2)}) collective-permute-start(f32[42,12,128]{2,0,1:T(8,128)S(1)} %pad_maximum_fusion.2), channel_id=1, source_target_pairs={{0,64},{16,80},{32,96},{48,112},{64,128},{80,144},{96,160},{112,17... | collective-permute-start | bytes 774152 | tf_op jit(solution)/shard_map/ppermute | solution.py:22
  81.5 11.1 %collective-permute-start.19 = (f32[42,12,128]{2,0,1:T(8,128)S(1)}, f32[42,12,128]{2,0,1:T(8,128)S(1)}, u32[]{:S(2)}, u32[]{:S(2)}) collective-permute-start(f32[42,12,128]{2,0,1:T(8,128)S(1)} %pad_maximum_fusion.5), channel_id=1, source_target_pairs={{128,0},{144,16},{160,32},{176,48},{192,64},{208,80},{224,96},{240... | collective-permute-start | bytes 774152 | tf_op jit(solution)/shard_map/ppermute | solution.py:22
  83.0 11.3 %collective-permute-start.18 = (f32[42,12,128]{2,0,1:T(8,128)S(1)}, f32[42,12,128]{2,0,1:T(8,128)S(1)}, u32[]{:S(2)}, u32[]{:S(2)}) collective-permute-start(f32[42,12,128]{2,0,1:T(8,128)S(1)} %pad_maximum_fusion.4), channel_id=1, source_target_pairs={{0,128},{16,144},{32,160},{48,176},{64,192},{80,208},{96,224},{112... | collective-permute-start | bytes 774152 | tf_op jit(solution)/shard_map/ppermute | solution.py:22
  96.2 7.6 %copy-start.1 = (f32[25,256]{1,0:T(8,128)S(1)}, f32[25,256]{1,0:T(8,128)}, u32[]{:S(2)}) copy-start(f32[25,256]{1,0:T(8,128)} %param.13) | copy-start | bytes 76804
  96.2 7.6 %copy-start.2 = (f32[25,256]{1,0:T(8,128)S(1)}, f32[25,256]{1,0:T(8,128)}, u32[]{:S(2)}) copy-start(f32[25,256]{1,0:T(8,128)} %param.12) | copy-start | bytes 76804
  96.2 7.6 %copy-start.3 = (f32[25,256]{1,0:T(8,128)S(1)}, f32[25,256]{1,0:T(8,128)}, u32[]{:S(2)}) copy-start(f32[25,256]{1,0:T(8,128)} %param.11) | copy-start | bytes 76804
  97.5 1.2 collective-permute-start.20
  98.7 3.7 %collective-permute-start.21 = (f32[5,256]{1,0:T(8,128)S(1)}, f32[5,256]{1,0:T(8,128)S(1)}, u32[]{:S(2)}, u32[]{:S(2)}) collective-permute-start(f32[5,256]{1,0:T(8,128)S(1)} %add.321), channel_id=1, source_target_pairs={{0,2},{1,3},{2,0},{3,1},{4,6},{5,7},{6,4},{7,5},{8,10},{9,11},{10,... | collective-permute-start | bytes 15368 | tf_op jit(solution)/shard_map/ppermute | solution.py:174
  102.4 4.5 %collective-permute-start.22 = (f32[5,256]{1,0:T(8,128)S(1)}, f32[5,256]{1,0:T(8,128)S(1)}, u32[]{:S(2)}, u32[]{:S(2)}) collective-permute-start(f32[5,256]{1,0:T(8,128)S(1)} %add.322), channel_id=1, source_target_pairs={{0,4},{1,5},{2,6},{3,7},{4,0},{5,1},{6,2},{7,3},{8,12},{9,13},{10,... | collective-permute-start | bytes 15368 | tf_op jit(solution)/shard_map/ppermute | solution.py:174
  106.9 7.6 %collective-permute-start.23 = (f32[5,256]{1,0:T(8,128)S(1)}, f32[5,256]{1,0:T(8,128)S(1)}, u32[]{:S(2)}, u32[]{:S(2)}) collective-permute-start(f32[5,256]{1,0:T(8,128)S(1)} %add.323), channel_id=1, source_target_pairs={{0,8},{1,9},{2,10},{3,11},{4,12},{5,13},{6,14},{7,15},{8,0},{9,1},... | collective-permute-start | bytes 15368 | tf_op jit(solution)/shard_map/ppermute | solution.py:174
  114.5 10.3 %collective-permute-start.24 = (f32[80,2,128]{2,1,0:T(2,128)S(1)}, f32[80,2,128]{2,1,0:T(2,128)S(1)}, u32[]{:S(2)}, u32[]{:S(2)}) collective-permute-start(f32[80,2,128]{2,1,0:T(2,128)S(1)} %constant_dynamic-update-slice_fusion), channel_id=1, source_target_pairs={{0,32},{16,48},{32,64},{48,80},{64,96},{80,112},{96,128},{112,144}... | collective-permute-start | bytes 245768 | tf_op jit(solution)/shard_map/ppermute | solution.py:22
  118.9 5.9 %collective-permute-start.25 = (f32[80,2,128]{2,1,0:T(2,128)S(1)}, f32[80,2,128]{2,1,0:T(2,128)S(1)}, u32[]{:S(2)}, u32[]{:S(2)}) collective-permute-start(f32[80,2,128]{2,1,0:T(2,128)S(1)} %constant_dynamic-update-slice_fusion), channel_id=1, source_target_pairs={{0,16},{16,32},{32,48},{48,64},{64,80},{80,96},{96,112},{112,128},... | collective-permute-start | bytes 245768 | tf_op jit(solution)/shard_map/ppermute | solution.py:22
  122.0 6.3 %collective-permute-start.26 = (f32[80,2,128]{2,1,0:T(2,128)S(1)}, f32[80,2,128]{2,1,0:T(2,128)S(1)}, u32[]{:S(2)}, u32[]{:S(2)}) collective-permute-start(f32[80,2,128]{2,1,0:T(2,128)S(1)} %constant_dynamic-update-slice_fusion), channel_id=1, source_target_pairs={{16,0},{32,16},{48,32},{64,48},{80,64},{96,80},{112,96},{128,112},... | collective-permute-start | bytes 245768 | tf_op jit(solution)/shard_map/ppermute | solution.py:22
  123.3 9.6 %collective-permute-start.27 = (f32[80,2,128]{2,1,0:T(2,128)S(1)}, f32[80,2,128]{2,1,0:T(2,128)S(1)}, u32[]{:S(2)}, u32[]{:S(2)}) collective-permute-start(f32[80,2,128]{2,1,0:T(2,128)S(1)} %constant_dynamic-update-slice_fusion), channel_id=1, source_target_pairs={{32,0},{48,16},{64,32},{80,48},{96,64},{112,80},{128,96},{144,112}... | collective-permute-start | bytes 245768 | tf_op jit(solution)/shard_map/ppermute | solution.py:22
  134.1 40.9 %copy-start.5 = (f32[24]{0:T(128)S(1)}, f32[24]{0:T(128)}, u32[]{:S(2)}) copy-start(f32[24]{0:T(128)} %constant.36.clone) | copy-start | bytes 292
  134.1 40.8 %copy-start.8 = (f32[24]{0:T(128)S(1)}, f32[24]{0:T(128)}, u32[]{:S(2)}) copy-start(f32[24]{0:T(128)} %constant.81) | copy-start | bytes 292
  134.1 41.0 %copy-start.6 = (f32[1,24]{1,0:T(1,128)S(1)}, f32[1,24]{1,0:T(1,128)}, u32[]{:S(2)}) copy-start(f32[1,24]{1,0:T(1,128)} %constant.85) | copy-start | bytes 292
  137.8 1.1 collective-permute-start.28
  139.0 3.6 %collective-permute-start.29 = (f32[26]{0:T(128)S(1)}, f32[26]{0:T(128)S(1)}, u32[]{:S(2)}, u32[]{:S(2)}) collective-permute-start(f32[26]{0:T(128)S(1)} %fusion.66), channel_id=1, source_target_pairs={{0,2},{1,3},{2,0},{3,1},{4,6},{5,7},{6,4},{7,5},{8,10},{9,11},{10,... | collective-permute-start | bytes 320 | tf_op jit(solution)/shard_map/ppermute | solution.py:174
  142.6 4.4 %collective-permute-start.30 = (f32[26]{0:T(128)S(1)}, f32[26]{0:T(128)S(1)}, u32[]{:S(2)}, u32[]{:S(2)}) collective-permute-start(f32[26]{0:T(128)S(1)} %add.328), channel_id=1, source_target_pairs={{0,4},{1,5},{2,6},{3,7},{4,0},{5,1},{6,2},{7,3},{8,12},{9,13},{10,... | collective-permute-start | bytes 320 | tf_op jit(solution)/shard_map/ppermute | solution.py:174
  147.0 7.4 %collective-permute-start.31 = (f32[26]{0:T(128)S(1)}, f32[26]{0:T(128)S(1)}, u32[]{:S(2)}, u32[]{:S(2)}) collective-permute-start(f32[26]{0:T(128)S(1)} %add.329), channel_id=1, source_target_pairs={{0,8},{1,9},{2,10},{3,11},{4,12},{5,13},{6,14},{7,15},{8,0},{9,1},... | collective-permute-start | bytes 320 | tf_op jit(solution)/shard_map/ppermute | solution.py:174
  154.5 3.5 %collective-permute-start.32 = (f32[26]{0:T(128)S(1)}, f32[26]{0:T(128)S(1)}, u32[]{:S(2)}, u32[]{:S(2)}) collective-permute-start(f32[26]{0:T(128)S(1)} %add.330), channel_id=1, source_target_pairs={{0,16},{16,0},{32,48},{48,32},{64,80},{80,64},{96,112},{112,96},{1... | collective-permute-start | bytes 320 | tf_op jit(solution)/shard_map/ppermute | solution.py:174
  158.0 5.9 %collective-permute-start.33 = (f32[26]{0:T(128)S(1)}, f32[26]{0:T(128)S(1)}, u32[]{:S(2)}, u32[]{:S(2)}) collective-permute-start(f32[26]{0:T(128)S(1)} %add.331), channel_id=1, source_target_pairs={{0,32},{16,48},{32,0},{48,16},{64,96},{80,112},{96,64},{112,80},{1... | collective-permute-start | bytes 320 | tf_op jit(solution)/shard_map/ppermute | solution.py:174
  164.0 4.2 %collective-permute-start.34 = (f32[26]{0:T(128)S(1)}, f32[26]{0:T(128)S(1)}, u32[]{:S(2)}, u32[]{:S(2)}) collective-permute-start(f32[26]{0:T(128)S(1)} %add.332), channel_id=1, source_target_pairs={{0,64},{16,80},{32,96},{48,112},{64,0},{80,16},{96,32},{112,48},{1... | collective-permute-start | bytes 320 | tf_op jit(solution)/shard_map/ppermute | solution.py:174
  168.2 6.1 %collective-permute-start.35 = (f32[26]{0:T(128)S(1)}, f32[26]{0:T(128)S(1)}, u32[]{:S(2)}, u32[]{:S(2)}) collective-permute-start(f32[26]{0:T(128)S(1)} %add.333), channel_id=1, source_target_pairs={{0,128},{16,144},{32,160},{48,176},{64,192},{80,208},{96,224},{112... | collective-permute-start | bytes 320 | tf_op jit(solution)/shard_map/ppermute | solution.py:174

commit v7 on v6

--- a/solution.py
+++ b/solution.py
@@ -251,6 +251,19 @@
     )
 
 
+def paired_inflow(pos, neg):
+    count = lax.axis_size("sec")
+    pos, span = scan_first(pos[0], pos[1], 1)
+    neg, _ = scan_first(neg[0], neg[1], -1)
+    pos, neg = lax.optimization_barrier((pos, neg))
+    while span < count - 1:
+        pos, next_span = scan_next(pos, span, 1)
+        neg, _ = scan_next(neg, span, -1)
+        span = next_span
+        pos, neg = lax.optimization_barrier((pos, neg))
+    return pos[1], neg[1]
+
+
 def body(distribution, collision, lower_blocks, upper_blocks, diag_inverse):
     node_count = distribution.shape[0]
     cell_count = distribution.shape[1]
@@ -272,31 +285,39 @@
     denominator = node_speed * total_length + thickness + pseudo_rate
     carry_rate = node_speed * total_length / denominator
     own_drive = pseudo_rate * distribution.reshape(node_rows, NXI, length, TUBES) / denominator
-    count = lax.axis_size("sec")
     own_sweep = local_sweep(carry_rate, own_drive)
-    own_pos, own_span = scan_first(own_sweep[2][:, :, -1], own_sweep[3][:, :, -1], 1)
-    own_neg, _ = scan_first(own_sweep[0][:, :, 0], own_sweep[1][:, :, 0], -1)
-    old_moments = tree_sum(jnp.dot(weighted, distribution, precision=HIGH), ("vel",))
-    own_pos, own_neg, old_moments = lax.optimization_barrier((own_pos, own_neg, old_moments))
-    moment_drive = thickness * old_moments.reshape(5, 1, length, TUBES) / denominator
+    old_part = jnp.dot(weighted, distribution, precision=HIGH)
+    moment_drive = thickness * old_part.reshape(5, 1, length, TUBES) / denominator
     moment_sweep = local_sweep(carry_rate, moment_drive)
-    own_pos, own_neg, moment_pos, moment_neg = caught_up(
-        own_pos, own_neg, own_span, moment_sweep, count
-    )
-    span = min(2 * own_span, count)
-    while span < count - 1:
-        own_pos, moment_pos = joint_next(own_pos, moment_pos, span, 1)
-        own_neg, moment_neg = joint_next(own_neg, moment_neg, span, -1)
-        span *= 2
-        own_pos, own_neg, moment_pos, moment_neg = lax.optimization_barrier(
-            (own_pos, own_neg, moment_pos, moment_neg)
-        )
-    own_field = joined_field(own_sweep, own_neg[1], own_pos[1])
-    moment_field = joined_field(moment_sweep, moment_neg[1], moment_pos[1])
+    own_rows = own_sweep[1].shape[0]
+    inflow_pos, inflow_neg = paired_inflow(
+        (own_sweep[2][:, :, -1],
+         jnp.concatenate([own_sweep[3][:, :, -1], moment_sweep[3][:, :, -1]], axis=0)),
+        (own_sweep[0][:, :, 0],
+         jnp.concatenate([own_sweep[1][:, :, 0], moment_sweep[1][:, :, 0]], axis=0)),
+    )
+    own_field = joined_field(own_sweep, inflow_neg[:own_rows], inflow_pos[:own_rows])
+    moment_part = joined_field(moment_sweep, inflow_neg[own_rows:], inflow_pos[own_rows:])
+    coupling = jnp.asarray(np.einsum(
+        "irx,jrx->ijx",
+        weighted_np.reshape(5, -1, NXI),
+        rebuild_np.reshape(5, -1, NXI),
+    ), jnp.float32)
+    half_part = jnp.dot(
+        weighted, own_field.reshape(node_count, cell_count), precision=HIGH
+    ) + jnp.tensordot(coupling, moment_part, axes=([1, 2], [0, 1]), precision=HIGH).reshape(
+        5, cell_count
+    )
+    summed = tree_sum(
+        jnp.concatenate([half_part, old_part, moment_part.reshape(5 * NXI, cell_count)], axis=0),
+        ("vel",),
+    )
+    half_moments = summed[:5]
+    old_moments = summed[5:10]
+    moment_field = summed[10:].reshape(5, NXI, length, TUBES)
     basis = rebuild.reshape(5, node_rows, NXI, 1, 1)
     half_field = own_field + jnp.sum(basis * moment_field[:, None], axis=0)
     half_field = half_field.reshape(node_count, cell_count)
-    half_moments = tree_sum(jnp.dot(weighted, half_field, precision=HIGH), ("vel",))
     residual = (half_moments - old_moments).reshape(5, length, TUBES)
     width = min(-(-JACOBI // length), lax.axis_size("sec") - 1)
     blocks = jnp.concatenate([lower_blocks, upper_blocks, diag_inverse], axis=0)

time: 182 us -> 188 us (1.033)
  waiting for transfers between devices: 58.3 us -> 101 us
  starting transfers between devices: 101 us -> 62.2 us
  local copies, waits for them, and re-layouts: 3.78 us -> 7.05 us
    ppermute x20 -> x14, waiting for transfers between devices: 21.5 us -> 66.5 us  [passed_along(): return lax.ppermute(block, axis, route)]
    ppermute x20 -> x14, starting transfers between devices: 70.4 us -> 33.8 us  [passed_along(): return lax.ppermute(block, axis, route)]
    ppermute x16 -> x12, waiting for transfers between devices: 36.8 us -> 34.1 us  [tree_sum(): lax.ppermute(block, axis, [(i, i ^ bit) for i in range(count)])]
    ppermute x16 -> x12, starting transfers between devices: 31 us -> 28.4 us  [tree_sum(): lax.ppermute(block, axis, [(i, i ^ bit) for i in range(count)])]
  transfers between devices with their start and end apart: 36 -> 26, of which waited for: 22 -> 22; matrix products, arithmetic and copies ran while one was open for 2% -> 1% of each run, Pallas kernels for 0% -> 0%
where the time goes in v7:
time: 188 us; the launch traced here: 186 us
  waiting for transfers between devices  101 us (54%)
  starting transfers between devices  62.2 us (33%)
  other arithmetic  9.51 us (5%)
  local copies, waits for them, and re-layouts  7.05 us (4%)
  matrix products  4.99 us (3%)
    ppermute x14, waiting for transfers between devices, passed_along(): return lax.ppermute(block, axis, route)  66.5 us
    ppermute x12, waiting for transfers between devices, tree_sum(): lax.ppermute(block, axis, [(i, i ^ bit) for i in range(count)])  34.1 us
    ppermute x14, starting transfers between devices, passed_along(): return lax.ppermute(block, axis, route)  33.8 us
    ppermute x12, starting transfers between devices, tree_sum(): lax.ppermute(block, axis, [(i, i ^ bit) for i in range(count)])  28.4 us
  transfers between devices with their start and end apart: 26, of which 22 were waited for; matrix products, arithmetic and copies ran while one was open for 1% of the time, Pallas kernels for 0%

profile of v7, /device:TPU:32, one launch (start us, length us, event | category | flops | bytes accessed | tf_op | source)
XLA Modules:
  0.0 186.1 jit_solution(6068468564057551589)
XLA Ops:
  2.2 1.7 reshape.144
  5.5 3.5 %collective-permute-start = (f32[42,12,128]{2,1,0:T(8,128)S(1)}, f32[42,12,128]{2,1,0:T(8,128)S(1)}, u32[]{:S(2)}, u32[]{:S(2)}) collective-permute-start(f32[42,12,128]{2,1,0:T(8,128)S(1)} %pad_maximum_fusion.1), channel_id=1, source_target_pairs={{0,16},{16,32},{32,48},{48,64},{64,80},{80,96},{96,112},{112,128},... | collective-permute-start | bytes 774152 | tf_op jit(solution)/shard_map/ppermute | solution.py:22
  9.1 4.8 %collective-permute-start.1 = (f32[42,12,128]{2,1,0:T(8,128)S(1)}, f32[42,12,128]{2,1,0:T(8,128)S(1)}, u32[]{:S(2)}, u32[]{:S(2)}) collective-permute-start(f32[42,12,128]{2,1,0:T(8,128)S(1)} %pad_maximum_fusion.1), channel_id=1, source_target_pairs={{0,32},{16,48},{32,64},{48,80},{64,96},{80,112},{96,128},{112,144}... | collective-permute-start | bytes 774152 | tf_op jit(solution)/shard_map/ppermute | solution.py:22
  14.0 1.3 collective-permute-start.2
  15.3 1.3 collective-permute-start.3
  17.5 6.3 %collective-permute-done.1 = f32[42,12,128]{2,1,0:T(8,128)S(1)} collective-permute-done((f32[42,12,128]{2,1,0:T(8,128)S(1)}, f32[42,12,128]{2,1,0:T(8,128)S(1)}, u32[]{:S(2)}, u32[]{:S(2)}) %collective-permute-start.1) | collective-permute-done | bytes 258080 | tf_op jit(solution)/shard_map/ppermute | solution.py:22
  23.8 18.9 %collective-permute-done.2 = f32[42,12,128]{2,1,0:T(8,128)S(1)} collective-permute-done((f32[42,12,128]{2,1,0:T(8,128)S(1)}, f32[42,12,128]{2,1,0:T(8,128)S(1)}, u32[]{:S(2)}, u32[]{:S(2)}) %collective-permute-start.2) | collective-permute-done | bytes 258080 | tf_op jit(solution)/shard_map/ppermute | solution.py:22
  42.8 2.5 %collective-permute-start.4 = (f32[42,12,128]{2,1,0:T(8,128)S(1)}, f32[42,12,128]{2,1,0:T(8,128)S(1)}, u32[]{:S(2)}, u32[]{:S(2)}) collective-permute-start(f32[42,12,128]{2,1,0:T(8,128)S(1)} %pad_maximum_fusion.3), channel_id=1, source_target_pairs={{0,32},{16,48},{32,64},{48,80},{64,96},{80,112},{96,128},{112,144}... | collective-permute-start | bytes 774152 | tf_op jit(solution)/shard_map/ppermute | solution.py:22
  45.3 1.3 collective-permute-start.5
  46.6 12.2 %collective-permute-done.4 = f32[42,12,128]{2,1,0:T(8,128)S(1)} collective-permute-done((f32[42,12,128]{2,1,0:T(8,128)S(1)}, f32[42,12,128]{2,1,0:T(8,128)S(1)}, u32[]{:S(2)}, u32[]{:S(2)}) %collective-permute-start.4) | collective-permute-done | bytes 258080 | tf_op jit(solution)/shard_map/ppermute | solution.py:22
  59.0 7.6 %collective-permute-start.6 = (f32[42,12,128]{2,1,0:T(8,128)S(1)}, f32[42,12,128]{2,1,0:T(8,128)S(1)}, u32[]{:S(2)}, u32[]{:S(2)}) collective-permute-start(f32[42,12,128]{2,1,0:T(8,128)S(1)} %pad_maximum_fusion.5), channel_id=1, source_target_pairs={{0,64},{16,80},{32,96},{48,112},{64,128},{80,144},{96,160},{112,17... | collective-permute-start | bytes 774152 | tf_op jit(solution)/shard_map/ppermute | solution.py:22
  66.7 1.3 collective-permute-start.7
  68.0 6.1 %collective-permute-done.6 = f32[42,12,128]{2,1,0:T(8,128)S(1)} collective-permute-done((f32[42,12,128]{2,1,0:T(8,128)S(1)}, f32[42,12,128]{2,1,0:T(8,128)S(1)}, u32[]{:S(2)}, u32[]{:S(2)}) %collective-permute-start.6) | collective-permute-done | bytes 258080 | tf_op jit(solution)/shard_map/ppermute | solution.py:22
  74.1 4.2 %collective-permute-done.7 = f32[42,12,128]{2,1,0:T(8,128)S(1)} collective-permute-done((f32[42,12,128]{2,1,0:T(8,128)S(1)}, f32[42,12,128]{2,1,0:T(8,128)S(1)}, u32[]{:S(2)}, u32[]{:S(2)}) %collective-permute-start.7) | collective-permute-done | bytes 258080 | tf_op jit(solution)/shard_map/ppermute | solution.py:22
  78.3 3.4 %collective-permute-start.8 = (f32[42,12,128]{2,1,0:T(8,128)S(1)}, f32[42,12,128]{2,1,0:T(8,128)S(1)}, u32[]{:S(2)}, u32[]{:S(2)}) collective-permute-start(f32[42,12,128]{2,1,0:T(8,128)S(1)} %pad_maximum_fusion.7), channel_id=1, source_target_pairs={{0,128},{16,144},{32,160},{48,176},{64,192},{80,208},{96,224},{112... | collective-permute-start | bytes 774152 | tf_op jit(solution)/shard_map/ppermute | solution.py:22
  81.8 1.3 collective-permute-start.9
  83.1 5.3 %collective-permute-done.8 = f32[42,12,128]{2,1,0:T(8,128)S(1)} collective-permute-done((f32[42,12,128]{2,1,0:T(8,128)S(1)}, f32[42,12,128]{2,1,0:T(8,128)S(1)}, u32[]{:S(2)}, u32[]{:S(2)}) %collective-permute-start.8) | collective-permute-done | bytes 258080 | tf_op jit(solution)/shard_map/ppermute | solution.py:22
  88.5 5.6 %collective-permute-done.9 = f32[42,12,128]{2,1,0:T(8,128)S(1)} collective-permute-done((f32[42,12,128]{2,1,0:T(8,128)S(1)}, f32[42,12,128]{2,1,0:T(8,128)S(1)}, u32[]{:S(2)}, u32[]{:S(2)}) %collective-permute-start.9) | collective-permute-done | bytes 258080 | tf_op jit(solution)/shard_map/ppermute | solution.py:22
  96.8 1.3 fusion.1
  98.5 1.3 collective-permute-done.10
  100.1 5.6 %collective-permute-done.11 = f32[130,256]{1,0:T(8,128)S(1)} collective-permute-done((f32[130,256]{1,0:T(8,128)S(1)}, f32[130,256]{1,0:T(8,128)S(1)}, u32[]{:S(2)}, u32[]{:S(2)}) %collective-permute-start.11) | collective-permute-done | bytes 133152 | tf_op jit(solution)/shard_map/ppermute | solution.py:174
  105.7 3.4 %collective-permute-start.12 = (f32[130,256]{1,0:T(8,128)S(1)}, f32[130,256]{1,0:T(8,128)S(1)}, u32[]{:S(2)}, u32[]{:S(2)}) collective-permute-start(f32[130,256]{1,0:T(8,128)S(1)} %add.265), channel_id=1, source_target_pairs={{0,4},{1,5},{2,6},{3,7},{4,0},{5,1},{6,2},{7,3},{8,12},{9,13},{10,... | collective-permute-start | bytes 399368 | tf_op jit(solution)/shard_map/ppermute | solution.py:174
  109.1 5.3 %collective-permute-done.12 = f32[130,256]{1,0:T(8,128)S(1)} collective-permute-done((f32[130,256]{1,0:T(8,128)S(1)}, f32[130,256]{1,0:T(8,128)S(1)}, u32[]{:S(2)}, u32[]{:S(2)}) %collective-permute-start.12) | collective-permute-done | bytes 133152 | tf_op jit(solution)/shard_map/ppermute | solution.py:174
  114.4 4.6 %collective-permute-start.13 = (f32[130,256]{1,0:T(8,128)S(1)}, f32[130,256]{1,0:T(8,128)S(1)}, u32[]{:S(2)}, u32[]{:S(2)}) collective-permute-start(f32[130,256]{1,0:T(8,128)S(1)} %add.266), channel_id=1, source_target_pairs={{0,8},{1,9},{2,10},{3,11},{4,12},{5,13},{6,14},{7,15},{8,0},{9,1},... | collective-permute-start | bytes 399368 | tf_op jit(solution)/shard_map/ppermute | solution.py:174
  120.0 4.8 %collective-permute-done.13 = f32[130,256]{1,0:T(8,128)S(1)} collective-permute-done((f32[130,256]{1,0:T(8,128)S(1)}, f32[130,256]{1,0:T(8,128)S(1)}, u32[]{:S(2)}, u32[]{:S(2)}) %collective-permute-start.13) | collective-permute-done | bytes 133152 | tf_op jit(solution)/shard_map/ppermute | solution.py:174
  124.9 1.3 collective-permute-start.14
  126.2 1.6 collective-permute-start.15
  127.8 1.3 collective-permute-start.16
  129.1 1.3 collective-permute-start.17
  131.8 3.2 %collective-permute-done.16 = f32[80,2,128]{2,1,0:T(2,128)S(1)} collective-permute-done((f32[80,2,128]{2,1,0:T(2,128)S(1)}, f32[80,2,128]{2,1,0:T(2,128)S(1)}, u32[]{:S(2)}, u32[]{:S(2)}) %collective-permute-start.16) | collective-permute-done | bytes 81952 | tf_op jit(solution)/shard_map/ppermute | solution.py:22
  135.0 4.0 %collective-permute-done.17 = f32[80,2,128]{2,1,0:T(2,128)S(1)} collective-permute-done((f32[80,2,128]{2,1,0:T(2,128)S(1)}, f32[80,2,128]{2,1,0:T(2,128)S(1)}, u32[]{:S(2)}, u32[]{:S(2)}) %collective-permute-start.17) | collective-permute-done | bytes 81952 | tf_op jit(solution)/shard_map/ppermute | solution.py:22
  140.8 2.0 %abs_reduce_fusion = (f32[864]{0:T(1024)S(1)}, f32[864,256]{1,0:T(8,128)S(1)}) fusion(f32[1,5,2,128]{3,2,1,0:T(2,128)S(1)} %slice_bitcast_fusion.4, f32[5,13824]{1,0:T(8,128)} %constant.37.clone, s32[]{:T(128)S(6)} %select_n.2, f32[108,8,2,128]{3,2,1,0:T(2,128)S(1)} %bitcast.127, f32[108,8,2,128]{3,2,1,0:T(2,128)S(1)} %bitcast.113), kind=kOutput, calls=%fused_computation.11 | convolution fusion | flops 14154912 | bytes 2691460 | tf_op jit(solution)/shard_map/dot_general | solution.py:342
  145.0 3.5 %collective-permute-start.19 = (f32[26]{0:T(128)S(1)}, f32[26]{0:T(128)S(1)}, u32[]{:S(2)}, u32[]{:S(2)}) collective-permute-start(f32[26]{0:T(128)S(1)} %fusion.59), channel_id=1, source_target_pairs={{0,2},{1,3},{2,0},{3,1},{4,6},{5,7},{6,4},{7,5},{8,10},{9,11},{10,... | collective-permute-start | bytes 320 | tf_op jit(solution)/shard_map/ppermute | solution.py:174
  148.5 1.5 collective-permute-done.19
  150.0 4.1 %collective-permute-start.20 = (f32[26]{0:T(128)S(1)}, f32[26]{0:T(128)S(1)}, u32[]{:S(2)}, u32[]{:S(2)}) collective-permute-start(f32[26]{0:T(128)S(1)} %add.272), channel_id=1, source_target_pairs={{0,4},{1,5},{2,6},{3,7},{4,0},{5,1},{6,2},{7,3},{8,12},{9,13},{10,... | collective-permute-start | bytes 320 | tf_op jit(solution)/shard_map/ppermute | solution.py:174
  154.1 1.5 collective-permute-done.20
  155.6 2.6 %collective-permute-start.21 = (f32[26]{0:T(128)S(1)}, f32[26]{0:T(128)S(1)}, u32[]{:S(2)}, u32[]{:S(2)}) collective-permute-start(f32[26]{0:T(128)S(1)} %add.273), channel_id=1, source_target_pairs={{0,8},{1,9},{2,10},{3,11},{4,12},{5,13},{6,14},{7,15},{8,0},{9,1},... | collective-permute-start | bytes 320 | tf_op jit(solution)/shard_map/ppermute | solution.py:174
  158.2 4.9 %collective-permute-done.21 = f32[26]{0:T(128)S(1)} collective-permute-done((f32[26]{0:T(128)S(1)}, f32[26]{0:T(128)S(1)}, u32[]{:S(2)}, u32[]{:S(2)}) %collective-permute-start.21) | collective-permute-done | bytes 136 | tf_op jit(solution)/shard_map/ppermute | solution.py:174
  163.1 1.5 collective-permute-start.22
  164.6 2.1 %collective-permute-done.22 = f32[26]{0:T(128)S(1)} collective-permute-done((f32[26]{0:T(128)S(1)}, f32[26]{0:T(128)S(1)}, u32[]{:S(2)}, u32[]{:S(2)}) %collective-permute-start.22) | collective-permute-done | bytes 136 | tf_op jit(solution)/shard_map/ppermute | solution.py:174
  166.6 4.4 %collective-permute-start.23 = (f32[26]{0:T(128)S(1)}, f32[26]{0:T(128)S(1)}, u32[]{:S(2)}, u32[]{:S(2)}) collective-permute-start(f32[26]{0:T(128)S(1)} %add.275), channel_id=1, source_target_pairs={{0,32},{16,48},{32,0},{48,16},{64,96},{80,112},{96,64},{112,80},{1... | collective-permute-start | bytes 320 | tf_op jit(solution)/shard_map/ppermute | solution.py:174
  171.0 1.5 collective-permute-done.23
  172.6 1.8 collective-permute-start.24
  174.4 1.8 collective-permute-done.24
  176.1 2.3 %collective-permute-start.25 = (f32[26]{0:T(128)S(1)}, f32[26]{0:T(128)S(1)}, u32[]{:S(2)}, u32[]{:S(2)}) collective-permute-start(f32[26]{0:T(128)S(1)} %add.277), channel_id=1, source_target_pairs={{0,128},{16,144},{32,160},{48,176},{64,192},{80,208},{96,224},{112... | collective-permute-start | bytes 320 | tf_op jit(solution)/shard_map/ppermute | solution.py:174
  178.4 2.7 %collective-permute-done.25 = f32[26]{0:T(128)S(1)} collective-permute-done((f32[26]{0:T(128)S(1)}, f32[26]{0:T(128)S(1)}, u32[]{:S(2)}, u32[]{:S(2)}) %collective-permute-start.25) | collective-permute-done | bytes 136 | tf_op jit(solution)/shard_map/ppermute | solution.py:174
  182.0 1.4 multiply_bitcast_fusion.2
  183.5 1.4 add_bitcast_fusion
  (164 shorter events, 16.3 us)
Async XLA Ops:
  2.2 1.7 copy-start
  3.9 1.3 copy-start.7
  5.5 11.9 %collective-permute-start = (f32[42,12,128]{2,1,0:T(8,128)S(1)}, f32[42,12,128]{2,1,0:T(8,128)S(1)}, u32[]{:S(2)}, u32[]{:S(2)}) collective-permute-start(f32[42,12,128]{2,1,0:T(8,128)S(1)} %pad_maximum_fusion.1), channel_id=1, source_target_pairs={{0,16},{16,32},{32,48},{48,64},{64,80},{80,96},{96,112},{112,128},... | collective-permute-start | bytes 774152 | tf_op jit(solution)/shard_map/ppermute | solution.py:22
  9.1 14.7 %collective-permute-start.1 = (f32[42,12,128]{2,1,0:T(8,128)S(1)}, f32[42,12,128]{2,1,0:T(8,128)S(1)}, u32[]{:S(2)}, u32[]{:S(2)}) collective-permute-start(f32[42,12,128]{2,1,0:T(8,128)S(1)} %pad_maximum_fusion.1), channel_id=1, source_target_pairs={{0,32},{16,48},{32,64},{48,80},{64,96},{80,112},{96,128},{112,144}... | collective-permute-start | bytes 774152 | tf_op jit(solution)/shard_map/ppermute | solution.py:22
  14.0 28.7 %collective-permute-start.2 = (f32[42,12,128]{2,1,0:T(8,128)S(1)}, f32[42,12,128]{2,1,0:T(8,128)S(1)}, u32[]{:S(2)}, u32[]{:S(2)}) collective-permute-start(f32[42,12,128]{2,1,0:T(8,128)S(1)} %pad_maximum_fusion.2), channel_id=1, source_target_pairs={{16,0},{32,16},{48,32},{64,48},{80,64},{96,80},{112,96},{128,112},... | collective-permute-start | bytes 774152 | tf_op jit(solution)/shard_map/ppermute | solution.py:22
  15.3 27.4 %collective-permute-start.3 = (f32[42,12,128]{2,1,0:T(8,128)S(1)}, f32[42,12,128]{2,1,0:T(8,128)S(1)}, u32[]{:S(2)}, u32[]{:S(2)}) collective-permute-start(f32[42,12,128]{2,1,0:T(8,128)S(1)} %pad_maximum_fusion.2), channel_id=1, source_target_pairs={{32,0},{48,16},{64,32},{80,48},{96,64},{112,80},{128,96},{144,112}... | collective-permute-start | bytes 774152 | tf_op jit(solution)/shard_map/ppermute | solution.py:22
  42.8 16.0 %collective-permute-start.4 = (f32[42,12,128]{2,1,0:T(8,128)S(1)}, f32[42,12,128]{2,1,0:T(8,128)S(1)}, u32[]{:S(2)}, u32[]{:S(2)}) collective-permute-start(f32[42,12,128]{2,1,0:T(8,128)S(1)} %pad_maximum_fusion.3), channel_id=1, source_target_pairs={{0,32},{16,48},{32,64},{48,80},{64,96},{80,112},{96,128},{112,144}... | collective-permute-start | bytes 774152 | tf_op jit(solution)/shard_map/ppermute | solution.py:22
  45.3 13.5 %collective-permute-start.5 = (f32[42,12,128]{2,1,0:T(8,128)S(1)}, f32[42,12,128]{2,1,0:T(8,128)S(1)}, u32[]{:S(2)}, u32[]{:S(2)}) collective-permute-start(f32[42,12,128]{2,1,0:T(8,128)S(1)} %pad_maximum_fusion.4), channel_id=1, source_target_pairs={{32,0},{48,16},{64,32},{80,48},{96,64},{112,80},{128,96},{144,112}... | collective-permute-start | bytes 774152 | tf_op jit(solution)/shard_map/ppermute | solution.py:22
  59.0 15.1 %collective-permute-start.6 = (f32[42,12,128]{2,1,0:T(8,128)S(1)}, f32[42,12,128]{2,1,0:T(8,128)S(1)}, u32[]{:S(2)}, u32[]{:S(2)}) collective-permute-start(f32[42,12,128]{2,1,0:T(8,128)S(1)} %pad_maximum_fusion.5), channel_id=1, source_target_pairs={{0,64},{16,80},{32,96},{48,112},{64,128},{80,144},{96,160},{112,17... | collective-permute-start | bytes 774152 | tf_op jit(solution)/shard_map/ppermute | solution.py:22
  66.7 11.6 %collective-permute-start.7 = (f32[42,12,128]{2,1,0:T(8,128)S(1)}, f32[42,12,128]{2,1,0:T(8,128)S(1)}, u32[]{:S(2)}, u32[]{:S(2)}) collective-permute-start(f32[42,12,128]{2,1,0:T(8,128)S(1)} %pad_maximum_fusion.6), channel_id=1, source_target_pairs={{64,0},{80,16},{96,32},{112,48},{128,64},{144,80},{160,96},{176,11... | collective-permute-start | bytes 774152 | tf_op jit(solution)/shard_map/ppermute | solution.py:22
  78.3 10.1 %collective-permute-start.8 = (f32[42,12,128]{2,1,0:T(8,128)S(1)}, f32[42,12,128]{2,1,0:T(8,128)S(1)}, u32[]{:S(2)}, u32[]{:S(2)}) collective-permute-start(f32[42,12,128]{2,1,0:T(8,128)S(1)} %pad_maximum_fusion.7), channel_id=1, source_target_pairs={{0,128},{16,144},{32,160},{48,176},{64,192},{80,208},{96,224},{112... | collective-permute-start | bytes 774152 | tf_op jit(solution)/shard_map/ppermute | solution.py:22
  81.8 12.3 %collective-permute-start.9 = (f32[42,12,128]{2,1,0:T(8,128)S(1)}, f32[42,12,128]{2,1,0:T(8,128)S(1)}, u32[]{:S(2)}, u32[]{:S(2)}) collective-permute-start(f32[42,12,128]{2,1,0:T(8,128)S(1)} %pad_maximum_fusion.8), channel_id=1, source_target_pairs={{128,0},{144,16},{160,32},{176,48},{192,64},{208,80},{224,96},{240... | collective-permute-start | bytes 774152 | tf_op jit(solution)/shard_map/ppermute | solution.py:22
  88.4 5.7 %copy-start.1 = (f32[41,12,128]{2,1,0:T(8,128)}, f32[41,12,128]{2,1,0:T(8,128)S(1)}, u32[]{:S(2)}) copy-start(f32[41,12,128]{2,1,0:T(8,128)S(1)} %fusion.6) | copy-start | bytes 755716
  94.1 0.7 copy-start.2
  94.2 1.1 slice-start
  94.9 1.0 slice-start.1
  96.8 1.3 copy-start.6
  96.8 12.3 %copy-start.3 = (f32[25,256]{1,0:T(8,128)S(1)}, f32[25,256]{1,0:T(8,128)}, u32[]{:S(2)}) copy-start(f32[25,256]{1,0:T(8,128)} %param.14) | copy-start | bytes 76804
  96.8 12.3 %copy-start.4 = (f32[25,256]{1,0:T(8,128)S(1)}, f32[25,256]{1,0:T(8,128)}, u32[]{:S(2)}) copy-start(f32[25,256]{1,0:T(8,128)} %param.13) | copy-start | bytes 76804
  96.8 12.3 %copy-start.5 = (f32[25,256]{1,0:T(8,128)S(1)}, f32[25,256]{1,0:T(8,128)}, u32[]{:S(2)}) copy-start(f32[25,256]{1,0:T(8,128)} %param.12) | copy-start | bytes 76804
  98.4 1.4 collective-permute-start.10
  99.9 5.8 %collective-permute-start.11 = (f32[130,256]{1,0:T(8,128)S(1)}, f32[130,256]{1,0:T(8,128)S(1)}, u32[]{:S(2)}, u32[]{:S(2)}) collective-permute-start(f32[130,256]{1,0:T(8,128)S(1)} %fusion.45), channel_id=1, source_target_pairs={{0,2},{1,3},{2,0},{3,1},{4,6},{5,7},{6,4},{7,5},{8,10},{9,11},{10,... | collective-permute-start | bytes 399368 | tf_op jit(solution)/shard_map/ppermute | solution.py:174
  105.7 8.7 %collective-permute-start.12 = (f32[130,256]{1,0:T(8,128)S(1)}, f32[130,256]{1,0:T(8,128)S(1)}, u32[]{:S(2)}, u32[]{:S(2)}) collective-permute-start(f32[130,256]{1,0:T(8,128)S(1)} %add.265), channel_id=1, source_target_pairs={{0,4},{1,5},{2,6},{3,7},{4,0},{5,1},{6,2},{7,3},{8,12},{9,13},{10,... | collective-permute-start | bytes 399368 | tf_op jit(solution)/shard_map/ppermute | solution.py:174
  114.4 10.4 %collective-permute-start.13 = (f32[130,256]{1,0:T(8,128)S(1)}, f32[130,256]{1,0:T(8,128)S(1)}, u32[]{:S(2)}, u32[]{:S(2)}) collective-permute-start(f32[130,256]{1,0:T(8,128)S(1)} %add.266), channel_id=1, source_target_pairs={{0,8},{1,9},{2,10},{3,11},{4,12},{5,13},{6,14},{7,15},{8,0},{9,1},... | collective-permute-start | bytes 399368 | tf_op jit(solution)/shard_map/ppermute | solution.py:174
  124.9 6.9 %collective-permute-start.14 = (f32[80,2,128]{2,1,0:T(2,128)S(1)}, f32[80,2,128]{2,1,0:T(2,128)S(1)}, u32[]{:S(2)}, u32[]{:S(2)}) collective-permute-start(f32[80,2,128]{2,1,0:T(2,128)S(1)} %constant_dynamic-update-slice_fusion), channel_id=1, source_target_pairs={{0,32},{16,48},{32,64},{48,80},{64,96},{80,112},{96,128},{112,144}... | collective-permute-start | bytes 245768 | tf_op jit(solution)/shard_map/ppermute | solution.py:22
  126.2 5.6 %collective-permute-start.15 = (f32[80,2,128]{2,1,0:T(2,128)S(1)}, f32[80,2,128]{2,1,0:T(2,128)S(1)}, u32[]{:S(2)}, u32[]{:S(2)}) collective-permute-start(f32[80,2,128]{2,1,0:T(2,128)S(1)} %constant_dynamic-update-slice_fusion), channel_id=1, source_target_pairs={{0,16},{16,32},{32,48},{48,64},{64,80},{80,96},{96,112},{112,128},... | collective-permute-start | bytes 245768 | tf_op jit(solution)/shard_map/ppermute | solution.py:22
  127.8 7.2 %collective-permute-start.16 = (f32[80,2,128]{2,1,0:T(2,128)S(1)}, f32[80,2,128]{2,1,0:T(2,128)S(1)}, u32[]{:S(2)}, u32[]{:S(2)}) collective-permute-start(f32[80,2,128]{2,1,0:T(2,128)S(1)} %constant_dynamic-update-slice_fusion), channel_id=1, source_target_pairs={{16,0},{32,16},{48,32},{64,48},{80,64},{96,80},{112,96},{128,112},... | collective-permute-start | bytes 245768 | tf_op jit(solution)/shard_map/ppermute | solution.py:22
  129.1 9.8 %collective-permute-start.17 = (f32[80,2,128]{2,1,0:T(2,128)S(1)}, f32[80,2,128]{2,1,0:T(2,128)S(1)}, u32[]{:S(2)}, u32[]{:S(2)}) collective-permute-start(f32[80,2,128]{2,1,0:T(2,128)S(1)} %constant_dynamic-update-slice_fusion), channel_id=1, source_target_pairs={{32,0},{48,16},{64,32},{80,48},{96,64},{112,80},{128,96},{144,112}... | collective-permute-start | bytes 245768 | tf_op jit(solution)/shard_map/ppermute | solution.py:22
  140.8 41.0 %copy-start.8 = (f32[24]{0:T(128)S(1)}, f32[24]{0:T(128)}, u32[]{:S(2)}) copy-start(f32[24]{0:T(128)} %constant.38.clone) | copy-start | bytes 292
  140.8 41.0 %copy-start.10 = (f32[24]{0:T(128)S(1)}, f32[24]{0:T(128)}, u32[]{:S(2)}) copy-start(f32[24]{0:T(128)} %constant.84) | copy-start | bytes 292
  140.8 41.2 %copy-start.9 = (f32[1,24]{1,0:T(1,128)S(1)}, f32[1,24]{1,0:T(1,128)}, u32[]{:S(2)}) copy-start(f32[1,24]{1,0:T(1,128)} %constant.88) | copy-start | bytes 292
  143.8 1.1 collective-permute-start.18
  145.0 5.0 %collective-permute-start.19 = (f32[26]{0:T(128)S(1)}, f32[26]{0:T(128)S(1)}, u32[]{:S(2)}, u32[]{:S(2)}) collective-permute-start(f32[26]{0:T(128)S(1)} %fusion.59), channel_id=1, source_target_pairs={{0,2},{1,3},{2,0},{3,1},{4,6},{5,7},{6,4},{7,5},{8,10},{9,11},{10,... | collective-permute-start | bytes 320 | tf_op jit(solution)/shard_map/ppermute | solution.py:174
  150.0 5.6 %collective-permute-start.20 = (f32[26]{0:T(128)S(1)}, f32[26]{0:T(128)S(1)}, u32[]{:S(2)}, u32[]{:S(2)}) collective-permute-start(f32[26]{0:T(128)S(1)} %add.272), channel_id=1, source_target_pairs={{0,4},{1,5},{2,6},{3,7},{4,0},{5,1},{6,2},{7,3},{8,12},{9,13},{10,... | collective-permute-start | bytes 320 | tf_op jit(solution)/shard_map/ppermute | solution.py:174
  155.6 7.4 %collective-permute-start.21 = (f32[26]{0:T(128)S(1)}, f32[26]{0:T(128)S(1)}, u32[]{:S(2)}, u32[]{:S(2)}) collective-permute-start(f32[26]{0:T(128)S(1)} %add.273), channel_id=1, source_target_pairs={{0,8},{1,9},{2,10},{3,11},{4,12},{5,13},{6,14},{7,15},{8,0},{9,1},... | collective-permute-start | bytes 320 | tf_op jit(solution)/shard_map/ppermute | solution.py:174
  163.1 3.5 %collective-permute-start.22 = (f32[26]{0:T(128)S(1)}, f32[26]{0:T(128)S(1)}, u32[]{:S(2)}, u32[]{:S(2)}) collective-permute-start(f32[26]{0:T(128)S(1)} %add.274), channel_id=1, source_target_pairs={{0,16},{16,0},{32,48},{48,32},{64,80},{80,64},{96,112},{112,96},{1... | collective-permute-start | bytes 320 | tf_op jit(solution)/shard_map/ppermute | solution.py:174
  166.6 5.9 %collective-permute-start.23 = (f32[26]{0:T(128)S(1)}, f32[26]{0:T(128)S(1)}, u32[]{:S(2)}, u32[]{:S(2)}) collective-permute-start(f32[26]{0:T(128)S(1)} %add.275), channel_id=1, source_target_pairs={{0,32},{16,48},{32,0},{48,16},{64,96},{80,112},{96,64},{112,80},{1... | collective-permute-start | bytes 320 | tf_op jit(solution)/shard_map/ppermute | solution.py:174
  172.6 3.5 %collective-permute-start.24 = (f32[26]{0:T(128)S(1)}, f32[26]{0:T(128)S(1)}, u32[]{:S(2)}, u32[]{:S(2)}) collective-permute-start(f32[26]{0:T(128)S(1)} %add.276), channel_id=1, source_target_pairs={{0,64},{16,80},{32,96},{48,112},{64,0},{80,16},{96,32},{112,48},{1... | collective-permute-start | bytes 320 | tf_op jit(solution)/shard_map/ppermute | solution.py:174
  176.1 5.0 %collective-permute-start.25 = (f32[26]{0:T(128)S(1)}, f32[26]{0:T(128)S(1)}, u32[]{:S(2)}, u32[]{:S(2)}) collective-permute-start(f32[26]{0:T(128)S(1)} %add.277), channel_id=1, source_target_pairs={{0,128},{16,144},{32,160},{48,176},{64,192},{80,208},{96,224},{112... | collective-permute-start | bytes 320 | tf_op jit(solution)/shard_map/ppermute | solution.py:174

commit v8 on v6

--- a/solution.py
+++ b/solution.py
@@ -163,16 +163,54 @@
     return jnp.concatenate(parts, axis=1)
 
 
+def group_sum(block, axis, low_bit, members):
+    count = lax.axis_size(axis)
+    if members == 2:
+        pairs = [(i, i ^ (1 << low_bit)) for i in range(count)]
+        return block + lax.ppermute(block, axis, pairs)
+    mine = (lax.axis_index(axis) >> low_bit) % members
+    shifted = [block]
+    for step in range(1, members):
+        pairs = []
+        for i in range(count):
+            place = (i >> low_bit) % members
+            base = i - (place << low_bit)
+            pairs.append((base + (((place + step) % members) << low_bit), i))
+        shifted.append(lax.ppermute(block, axis, pairs))
+    stacked = jnp.stack(shifted)
+    total = None
+    for member in range(members):
+        value = lax.dynamic_index_in_dim(stacked, (member - mine) % members, 0, keepdims=False)
+        total = value if total is None else total + value
+    return total
+
+
+def sum_plan(axis, count):
+    bits = count.bit_length() - 1
+    plan = []
+    bit = 0
+    if axis == "vel" and bits % 2 == 1:
+        plan.append((0, 2))
+        bit = 1
+    elif axis == "vel" and bits >= 2:
+        plan.append((0, 2))
+        bit = 1
+    while bit + 1 < bits:
+        plan.append((bit, 4))
+        bit += 2
+    if bit < bits:
+        plan.append((bit, 2))
+    return plan
+
+
 def tree_sum(block, axes):
     for axis in axes:
         count = lax.axis_size(axis)
         if count & (count - 1):
             block = lax.psum(block, axis)
             continue
-        bit = 1
-        while bit < count:
-            block = block + lax.ppermute(block, axis, [(i, i ^ bit) for i in range(count)])
-            bit *= 2
+        for low_bit, members in sum_plan(axis, count):
+            block = group_sum(block, axis, low_bit, members)
     return block
 
 

time: 182 us -> 180 us (0.989)
  waiting for transfers between devices: 58.3 us -> 50.6 us
  starting transfers between devices: 101 us -> 105 us
    ppermute x16 -> x21, waiting for transfers between devices: 36.8 us -> 28.5 us  [the longest x6 16 us: group_sum(): return block + lax.ppermute(block, axis, pairs)]
    ppermute x16 -> x21, starting transfers between devices: 31 us -> 35.5 us  [the longest x15 27.9 us: group_sum(): shifted.append(lax.ppermute(block, axis, pairs))]
  transfers between devices with their start and end apart: 36 -> 41, of which waited for: 22 -> 22; matrix products, arithmetic and copies ran while one was open for 2% -> 2% of each run, Pallas kernels for 0% -> 0%
where the time goes in v8:
time: 180 us; the launch traced here: 178 us
  starting transfers between devices  105 us (58%)
  waiting for transfers between devices  50.6 us (28%)
  other arithmetic  10.1 us (6%)
  local copies, waits for them, and re-layouts  4.95 us (3%)
  matrix products  4.73 us (3%)
  between operations  2.11 us (1%)
    ppermute x20, starting transfers between devices, passed_along(): return lax.ppermute(block, axis, route)  69.8 us
    ppermute x15, starting transfers between devices, group_sum(): shifted.append(lax.ppermute(block, axis, pairs))  27.9 us
    ppermute x20, waiting for transfers between devices, passed_along(): return lax.ppermute(block, axis, route)  22.1 us
    ppermute x6, waiting for transfers between devices, group_sum(): return block + lax.ppermute(block, axis, pairs)  16 us
    ppermute x15, waiting for transfers between devices, group_sum(): shifted.append(lax.ppermute(block, axis, pairs))  12.4 us
    ppermute x6, starting transfers between devices, group_sum(): return block + lax.ppermute(block, axis, pairs)  7.57 us
  transfers between devices with their start and end apart: 41, of which 22 were waited for; matrix products, arithmetic and copies ran while one was open for 2% of the time, Pallas kernels for 0%

profile of v8, /device:TPU:32, one launch (start us, length us, event | category | flops | bytes accessed | tf_op | source)
XLA Modules:
  0.0 177.8 jit_solution(10783896654535930959)
XLA Ops:
  2.2 1.6 reshape.158
  4.2 1.4 collective-permute-start.2
  5.6 1.3 collective-permute-start.3
  9.4 1.8 %collective-permute-start.5 = (f32[5,256]{1,0:T(8,128)S(1)}, f32[5,256]{1,0:T(8,128)S(1)}, u32[]{:S(2)}, u32[]{:S(2)}) collective-permute-start(f32[5,256]{1,0:T(8,128)S(1)} %add.434), channel_id=1, source_target_pairs={{2,0},{3,1},{4,2},{5,3},{6,4},{7,5},{0,6},{1,7},{10,8},{11,9},{12,... | collective-permute-start | bytes 15368 | tf_op jit(solution)/shard_map/ppermute | solution.py:179
  11.3 1.5 collective-permute-start.6
  12.8 2.8 %collective-permute-start.7 = (f32[5,256]{1,0:T(8,128)S(1)}, f32[5,256]{1,0:T(8,128)S(1)}, u32[]{:S(2)}, u32[]{:S(2)}) collective-permute-start(f32[5,256]{1,0:T(8,128)S(1)} %add.434), channel_id=1, source_target_pairs={{6,0},{7,1},{0,2},{1,3},{2,4},{3,5},{4,6},{5,7},{14,8},{15,9},{8,1... | collective-permute-start | bytes 15368 | tf_op jit(solution)/shard_map/ppermute | solution.py:179
  17.0 4.9 %collective-permute-start.8 = (f32[5,256]{1,0:T(8,128)S(1)}, f32[5,256]{1,0:T(8,128)S(1)}, u32[]{:S(2)}, u32[]{:S(2)}) collective-permute-start(f32[5,256]{1,0:T(8,128)S(1)} %add_bitcast_fusion.1), channel_id=1, source_target_pairs={{0,8},{1,9},{2,10},{3,11},{4,12},{5,13},{6,14},{7,15},{8,0},{9,1},... | collective-permute-start | bytes 15368 | tf_op jit(solution)/shard_map/ppermute | solution.py:170
  22.0 4.6 %collective-permute-start = (f32[37,12,128]{2,0,1:T(8,128)S(1)}, f32[37,12,128]{2,0,1:T(8,128)S(1)}, u32[]{:S(2)}, u32[]{:S(2)}) collective-permute-start(f32[37,12,128]{2,0,1:T(8,128)S(1)} %pad_maximum_fusion.6), channel_id=1, source_target_pairs={{0,16},{16,32},{32,48},{48,64},{64,80},{80,96},{96,112},{112,128},... | collective-permute-start | bytes 681992 | tf_op jit(solution)/shard_map/ppermute | solution.py:22
  26.5 6.7 %collective-permute-start.1 = (f32[37,12,128]{2,0,1:T(8,128)S(1)}, f32[37,12,128]{2,0,1:T(8,128)S(1)}, u32[]{:S(2)}, u32[]{:S(2)}) collective-permute-start(f32[37,12,128]{2,0,1:T(8,128)S(1)} %pad_maximum_fusion.6), channel_id=1, source_target_pairs={{0,32},{16,48},{32,64},{48,80},{64,96},{80,112},{96,128},{112,144}... | collective-permute-start | bytes 681992 | tf_op jit(solution)/shard_map/ppermute | solution.py:22
  33.3 3.6 %collective-permute-done.1 = f32[37,12,128]{2,0,1:T(8,128)S(1)} collective-permute-done((f32[37,12,128]{2,0,1:T(8,128)S(1)}, f32[37,12,128]{2,0,1:T(8,128)S(1)}, u32[]{:S(2)}, u32[]{:S(2)}) %collective-permute-start.1) | collective-permute-done | bytes 227360 | tf_op jit(solution)/shard_map/ppermute | solution.py:22
  37.2 1.3 collective-permute-start.15
  38.5 1.3 collective-permute-start.14
  39.8 1.3 collective-permute-start.10
  41.2 9.4 %collective-permute-start.12 = (f32[6,12,128]{2,0,1:T(8,128)S(1)}, f32[6,12,128]{2,0,1:T(8,128)S(1)}, u32[]{:S(2)}, u32[]{:S(2)}) collective-permute-start(f32[6,12,128]{2,0,1:T(8,128)S(1)} %pad_maximum_fusion.10), channel_id=1, source_target_pairs={{0,48},{16,64},{32,80},{48,96},{64,112},{80,128},{96,144},{112,160... | collective-permute-start | bytes 110600 | tf_op jit(solution)/shard_map/ppermute | solution.py:22
  50.6 4.8 %collective-permute-start.11 = (f32[6,12,128]{2,0,1:T(8,128)S(1)}, f32[6,12,128]{2,0,1:T(8,128)S(1)}, u32[]{:S(2)}, u32[]{:S(2)}) collective-permute-start(f32[6,12,128]{2,0,1:T(8,128)S(1)} %pad_maximum_fusion.10), channel_id=1, source_target_pairs={{0,16},{16,32},{32,48},{48,64},{64,80},{80,96},{96,112},{112,128},... | collective-permute-start | bytes 110600 | tf_op jit(solution)/shard_map/ppermute | solution.py:22
  55.5 5.4 %collective-permute-start.9 = (f32[43,12,128]{2,0,1:T(8,128)S(1)}, f32[43,12,128]{2,0,1:T(8,128)S(1)}, u32[]{:S(2)}, u32[]{:S(2)}) collective-permute-start(f32[43,12,128]{2,0,1:T(8,128)S(1)} %pad_maximum_fusion), channel_id=1, source_target_pairs={{0,32},{16,48},{32,64},{48,80},{64,96},{80,112},{96,128},{112,144}... | collective-permute-start | bytes 792584 | tf_op jit(solution)/shard_map/ppermute | solution.py:22
  61.0 1.3 collective-permute-start.16
  62.3 7.2 %collective-permute-start.13 = (f32[6,12,128]{2,0,1:T(8,128)S(1)}, f32[6,12,128]{2,0,1:T(8,128)S(1)}, u32[]{:S(2)}, u32[]{:S(2)}) collective-permute-start(f32[6,12,128]{2,0,1:T(8,128)S(1)} %pad_maximum_fusion.10), channel_id=1, source_target_pairs={{0,64},{16,80},{32,96},{48,112},{64,128},{80,144},{96,160},{112,17... | collective-permute-start | bytes 110600 | tf_op jit(solution)/shard_map/ppermute | solution.py:22
  69.8 1.4 collective-permute-done.13
  71.3 1.3 collective-permute-start.18
  73.6 4.9 %collective-permute-start.17 = (f32[42,12,128]{2,0,1:T(8,128)S(1)}, f32[42,12,128]{2,0,1:T(8,128)S(1)}, u32[]{:S(2)}, u32[]{:S(2)}) collective-permute-start(f32[42,12,128]{2,0,1:T(8,128)S(1)} %pad_maximum_fusion.2), channel_id=1, source_target_pairs={{0,64},{16,80},{32,96},{48,112},{64,128},{80,144},{96,160},{112,17... | collective-permute-start | bytes 774152 | tf_op jit(solution)/shard_map/ppermute | solution.py:22
  78.5 1.8 %collective-permute-done.18 = f32[42,12,128]{2,0,1:T(8,128)S(1)} collective-permute-done((f32[42,12,128]{2,0,1:T(8,128)S(1)}, f32[42,12,128]{2,0,1:T(8,128)S(1)}, u32[]{:S(2)}, u32[]{:S(2)}) %collective-permute-start.18) | collective-permute-done | bytes 258080 | tf_op jit(solution)/shard_map/ppermute | solution.py:22
  80.3 2.3 %collective-permute-done.17 = f32[42,12,128]{2,0,1:T(8,128)S(1)} collective-permute-done((f32[42,12,128]{2,0,1:T(8,128)S(1)}, f32[42,12,128]{2,0,1:T(8,128)S(1)}, u32[]{:S(2)}, u32[]{:S(2)}) %collective-permute-start.17) | collective-permute-done | bytes 258080 | tf_op jit(solution)/shard_map/ppermute | solution.py:22
  82.8 1.3 collective-permute-start.20
  84.4 8.0 %collective-permute-start.19 = (f32[42,12,128]{2,0,1:T(8,128)S(1)}, f32[42,12,128]{2,0,1:T(8,128)S(1)}, u32[]{:S(2)}, u32[]{:S(2)}) collective-permute-start(f32[42,12,128]{2,0,1:T(8,128)S(1)} %pad_maximum_fusion.4), channel_id=1, source_target_pairs={{0,128},{16,144},{32,160},{48,176},{64,192},{80,208},{96,224},{112... | collective-permute-start | bytes 774152 | tf_op jit(solution)/shard_map/ppermute | solution.py:22
  92.4 2.5 %collective-permute-done.20 = f32[42,12,128]{2,0,1:T(8,128)S(1)} collective-permute-done((f32[42,12,128]{2,0,1:T(8,128)S(1)}, f32[42,12,128]{2,0,1:T(8,128)S(1)}, u32[]{:S(2)}, u32[]{:S(2)}) %collective-permute-start.20) | collective-permute-done | bytes 258080 | tf_op jit(solution)/shard_map/ppermute | solution.py:22
  95.0 1.7 collective-permute-done.19
  101.0 2.5 %collective-permute-start.22 = (f32[5,256]{1,0:T(8,128)S(1)}, f32[5,256]{1,0:T(8,128)S(1)}, u32[]{:S(2)}, u32[]{:S(2)}) collective-permute-start(f32[5,256]{1,0:T(8,128)S(1)} %add.475), channel_id=1, source_target_pairs={{2,0},{3,1},{4,2},{5,3},{6,4},{7,5},{0,6},{1,7},{10,8},{11,9},{12,... | collective-permute-start | bytes 15368 | tf_op jit(solution)/shard_map/ppermute | solution.py:179
  105.8 2.4 %collective-permute-done.23 = f32[5,256]{1,0:T(8,128)S(1)} collective-permute-done((f32[5,256]{1,0:T(8,128)S(1)}, f32[5,256]{1,0:T(8,128)S(1)}, u32[]{:S(2)}, u32[]{:S(2)}) %collective-permute-start.23) | collective-permute-done | bytes 5152 | tf_op jit(solution)/shard_map/ppermute | solution.py:179
  109.5 6.3 %collective-permute-done.25 = f32[5,256]{1,0:T(8,128)S(1)} collective-permute-done((f32[5,256]{1,0:T(8,128)S(1)}, f32[5,256]{1,0:T(8,128)S(1)}, u32[]{:S(2)}, u32[]{:S(2)}) %collective-permute-start.25) | collective-permute-done | bytes 5152 | tf_op jit(solution)/shard_map/ppermute | solution.py:170
  115.8 2.4 %collective-permute-start.26 = (f32[80,2,128]{2,1,0:T(2,128)S(1)}, f32[80,2,128]{2,1,0:T(2,128)S(1)}, u32[]{:S(2)}, u32[]{:S(2)}) collective-permute-start(f32[80,2,128]{2,1,0:T(2,128)S(1)} %constant_dynamic-update-slice_fusion), channel_id=1, source_target_pairs={{0,32},{16,48},{32,64},{48,80},{64,96},{80,112},{96,128},{112,144}... | collective-permute-start | bytes 245768 | tf_op jit(solution)/shard_map/ppermute | solution.py:22
  118.3 3.4 %collective-permute-start.27 = (f32[80,2,128]{2,1,0:T(2,128)S(1)}, f32[80,2,128]{2,1,0:T(2,128)S(1)}, u32[]{:S(2)}, u32[]{:S(2)}) collective-permute-start(f32[80,2,128]{2,1,0:T(2,128)S(1)} %constant_dynamic-update-slice_fusion), channel_id=1, source_target_pairs={{0,16},{16,32},{32,48},{48,64},{64,80},{80,96},{96,112},{112,128},... | collective-permute-start | bytes 245768 | tf_op jit(solution)/shard_map/ppermute | solution.py:22
  121.7 1.3 collective-permute-start.28
  124.5 4.3 %collective-permute-done.28 = f32[80,2,128]{2,1,0:T(2,128)S(1)} collective-permute-done((f32[80,2,128]{2,1,0:T(2,128)S(1)}, f32[80,2,128]{2,1,0:T(2,128)S(1)}, u32[]{:S(2)}, u32[]{:S(2)}) %collective-permute-start.28) | collective-permute-done | bytes 81952 | tf_op jit(solution)/shard_map/ppermute | solution.py:22
  128.8 4.5 %collective-permute-done.29 = f32[80,2,128]{2,1,0:T(2,128)S(1)} collective-permute-done((f32[80,2,128]{2,1,0:T(2,128)S(1)}, f32[80,2,128]{2,1,0:T(2,128)S(1)}, u32[]{:S(2)}, u32[]{:S(2)}) %collective-permute-start.29) | collective-permute-done | bytes 81952 | tf_op jit(solution)/shard_map/ppermute | solution.py:22
  134.5 1.9 %abs_reduce_fusion = (f32[864]{0:T(1024)S(1)}, f32[864,256]{1,0:T(8,128)S(1)}) fusion(f32[1,5,2,128]{3,2,1,0:T(2,128)S(1)} %slice_bitcast_fusion, f32[5,13824]{1,0:T(8,128)} %constant.175.clone, s32[]{:T(128)S(6)} %select_n.134, f32[108,8,2,128]{3,2,1,0:T(2,128)S(1)} %bitcast.180), kind=kOutput, calls=%fused_computation.8 | convolution fusion | flops 13933728 | bytes 1806724 | tf_op jit(solution)/shard_map/dot_general | solution.py:359
  139.4 1.6 collective-permute-start.31
  141.6 2.7 %collective-permute-start.33 = (f32[26]{0:T(128)S(1)}, f32[26]{0:T(128)S(1)}, u32[]{:S(2)}, u32[]{:S(2)}) collective-permute-start(f32[26]{0:T(128)S(1)} %fusion.81), channel_id=1, source_target_pairs={{6,0},{7,1},{0,2},{1,3},{2,4},{3,5},{4,6},{5,7},{14,8},{15,9},{8,1... | collective-permute-start | bytes 320 | tf_op jit(solution)/shard_map/ppermute | solution.py:179
  146.9 6.3 %collective-permute-done.34 = f32[26]{0:T(128)S(1)} collective-permute-done((f32[26]{0:T(128)S(1)}, f32[26]{0:T(128)S(1)}, u32[]{:S(2)}, u32[]{:S(2)}) %collective-permute-start.34) | collective-permute-done | bytes 136 | tf_op jit(solution)/shard_map/ppermute | solution.py:170
  153.2 5.0 %collective-permute-start.35 = (f32[26]{0:T(128)S(1)}, f32[26]{0:T(128)S(1)}, u32[]{:S(2)}, u32[]{:S(2)}) collective-permute-start(f32[26]{0:T(128)S(1)} %fusion.80), channel_id=1, source_target_pairs={{16,0},{32,16},{48,32},{0,48},{80,64},{96,80},{112,96},{64,112},{1... | collective-permute-start | bytes 320 | tf_op jit(solution)/shard_map/ppermute | solution.py:179
  159.5 3.7 %collective-permute-done.36 = f32[26]{0:T(128)S(1)} collective-permute-done((f32[26]{0:T(128)S(1)}, f32[26]{0:T(128)S(1)}, u32[]{:S(2)}, u32[]{:S(2)}) %collective-permute-start.36) | collective-permute-done | bytes 136 | tf_op jit(solution)/shard_map/ppermute | solution.py:179
  163.4 2.9 %collective-permute-start.38 = (f32[26]{0:T(128)S(1)}, f32[26]{0:T(128)S(1)}, u32[]{:S(2)}, u32[]{:S(2)}) collective-permute-start(f32[26]{0:T(128)S(1)} %fusion.79), channel_id=1, source_target_pairs={{64,0},{80,16},{96,32},{112,48},{128,64},{144,80},{160,96},{176,11... | collective-permute-start | bytes 320 | tf_op jit(solution)/shard_map/ppermute | solution.py:179
  166.3 1.8 %collective-permute-start.39 = (f32[26]{0:T(128)S(1)}, f32[26]{0:T(128)S(1)}, u32[]{:S(2)}, u32[]{:S(2)}) collective-permute-start(f32[26]{0:T(128)S(1)} %fusion.79), channel_id=1, source_target_pairs={{128,0},{144,16},{160,32},{176,48},{192,64},{208,80},{224,96},{240... | collective-permute-start | bytes 320 | tf_op jit(solution)/shard_map/ppermute | solution.py:179
  168.1 1.3 collective-permute-start.40
  169.5 1.9 %collective-permute-done.39 = f32[26]{0:T(128)S(1)} collective-permute-done((f32[26]{0:T(128)S(1)}, f32[26]{0:T(128)S(1)}, u32[]{:S(2)}, u32[]{:S(2)}) %collective-permute-start.39) | collective-permute-done | bytes 136 | tf_op jit(solution)/shard_map/ppermute | solution.py:179
  171.3 1.6 collective-permute-done.40
  173.7 1.4 multiply_bitcast_fusion.1
  175.3 1.4 add_bitcast_fusion.2
  (213 shorter events, 27.5 us)
Async XLA Ops:
  4.2 29.1 %collective-permute-start.2 = (f32[37,12,128]{2,0,1:T(8,128)S(1)}, f32[37,12,128]{2,0,1:T(8,128)S(1)}, u32[]{:S(2)}, u32[]{:S(2)}) collective-permute-start(f32[37,12,128]{2,0,1:T(8,128)S(1)} %pad_maximum_fusion.7), channel_id=1, source_target_pairs={{16,0},{32,16},{48,32},{64,48},{80,64},{96,80},{112,96},{128,112},... | collective-permute-start | bytes 681992 | tf_op jit(solution)/shard_map/ppermute | solution.py:22
  5.6 27.6 %collective-permute-start.3 = (f32[37,12,128]{2,0,1:T(8,128)S(1)}, f32[37,12,128]{2,0,1:T(8,128)S(1)}, u32[]{:S(2)}, u32[]{:S(2)}) collective-permute-start(f32[37,12,128]{2,0,1:T(8,128)S(1)} %pad_maximum_fusion.7), channel_id=1, source_target_pairs={{32,0},{48,16},{64,32},{80,48},{96,64},{112,80},{128,96},{144,112}... | collective-permute-start | bytes 681992 | tf_op jit(solution)/shard_map/ppermute | solution.py:22
  8.2 1.2 collective-permute-start.4
  9.4 6.3 %collective-permute-start.5 = (f32[5,256]{1,0:T(8,128)S(1)}, f32[5,256]{1,0:T(8,128)S(1)}, u32[]{:S(2)}, u32[]{:S(2)}) collective-permute-start(f32[5,256]{1,0:T(8,128)S(1)} %add.434), channel_id=1, source_target_pairs={{2,0},{3,1},{4,2},{5,3},{6,4},{7,5},{0,6},{1,7},{10,8},{11,9},{12,... | collective-permute-start | bytes 15368 | tf_op jit(solution)/shard_map/ppermute | solution.py:179
  11.3 4.5 %collective-permute-start.6 = (f32[5,256]{1,0:T(8,128)S(1)}, f32[5,256]{1,0:T(8,128)S(1)}, u32[]{:S(2)}, u32[]{:S(2)}) collective-permute-start(f32[5,256]{1,0:T(8,128)S(1)} %add.434), channel_id=1, source_target_pairs={{4,0},{5,1},{6,2},{7,3},{0,4},{1,5},{2,6},{3,7},{12,8},{13,9},{14,... | collective-permute-start | bytes 15368 | tf_op jit(solution)/shard_map/ppermute | solution.py:179
  12.8 4.2 %collective-permute-start.7 = (f32[5,256]{1,0:T(8,128)S(1)}, f32[5,256]{1,0:T(8,128)S(1)}, u32[]{:S(2)}, u32[]{:S(2)}) collective-permute-start(f32[5,256]{1,0:T(8,128)S(1)} %add.434), channel_id=1, source_target_pairs={{6,0},{7,1},{0,2},{1,3},{2,4},{3,5},{4,6},{5,7},{14,8},{15,9},{8,1... | collective-permute-start | bytes 15368 | tf_op jit(solution)/shard_map/ppermute | solution.py:179
  17.0 16.2 %collective-permute-start.8 = (f32[5,256]{1,0:T(8,128)S(1)}, f32[5,256]{1,0:T(8,128)S(1)}, u32[]{:S(2)}, u32[]{:S(2)}) collective-permute-start(f32[5,256]{1,0:T(8,128)S(1)} %add_bitcast_fusion.1), channel_id=1, source_target_pairs={{0,8},{1,9},{2,10},{3,11},{4,12},{5,13},{6,14},{7,15},{8,0},{9,1},... | collective-permute-start | bytes 15368 | tf_op jit(solution)/shard_map/ppermute | solution.py:170
  22.0 15.1 %copy-start.4 = (f32[256]{0:T(256)S(1)}, f32[256]{0:T(256)}, u32[]{:S(2)}) copy-start(f32[256]{0:T(256)} %param.10) | copy-start | bytes 3076
  22.0 11.3 %collective-permute-start = (f32[37,12,128]{2,0,1:T(8,128)S(1)}, f32[37,12,128]{2,0,1:T(8,128)S(1)}, u32[]{:S(2)}, u32[]{:S(2)}) collective-permute-start(f32[37,12,128]{2,0,1:T(8,128)S(1)} %pad_maximum_fusion.6), channel_id=1, source_target_pairs={{0,16},{16,32},{32,48},{48,64},{64,80},{80,96},{96,112},{112,128},... | collective-permute-start | bytes 681992 | tf_op jit(solution)/shard_map/ppermute | solution.py:22
  26.5 10.4 %collective-permute-start.1 = (f32[37,12,128]{2,0,1:T(8,128)S(1)}, f32[37,12,128]{2,0,1:T(8,128)S(1)}, u32[]{:S(2)}, u32[]{:S(2)}) collective-permute-start(f32[37,12,128]{2,0,1:T(8,128)S(1)} %pad_maximum_fusion.6), channel_id=1, source_target_pairs={{0,32},{16,48},{32,64},{48,80},{64,96},{80,112},{96,128},{112,144}... | collective-permute-start | bytes 681992 | tf_op jit(solution)/shard_map/ppermute | solution.py:22
  37.2 18.3 %collective-permute-start.15 = (f32[6,12,128]{2,0,1:T(8,128)S(1)}, f32[6,12,128]{2,0,1:T(8,128)S(1)}, u32[]{:S(2)}, u32[]{:S(2)}) collective-permute-start(f32[6,12,128]{2,0,1:T(8,128)S(1)} %pad_maximum_fusion.11), channel_id=1, source_target_pairs={{48,0},{64,16},{80,32},{96,48},{112,64},{128,80},{144,96},{160,112... | collective-permute-start | bytes 110600 | tf_op jit(solution)/shard_map/ppermute | solution.py:22
  38.5 22.5 %collective-permute-start.14 = (f32[6,12,128]{2,0,1:T(8,128)S(1)}, f32[6,12,128]{2,0,1:T(8,128)S(1)}, u32[]{:S(2)}, u32[]{:S(2)}) collective-permute-start(f32[6,12,128]{2,0,1:T(8,128)S(1)} %pad_maximum_fusion.11), channel_id=1, source_target_pairs={{16,0},{32,16},{48,32},{64,48},{80,64},{96,80},{112,96},{128,112},... | collective-permute-start | bytes 110600 | tf_op jit(solution)/shard_map/ppermute | solution.py:22
  39.8 29.7 %collective-permute-start.10 = (f32[43,12,128]{2,0,1:T(8,128)S(1)}, f32[43,12,128]{2,0,1:T(8,128)S(1)}, u32[]{:S(2)}, u32[]{:S(2)}) collective-permute-start(f32[43,12,128]{2,0,1:T(8,128)S(1)} %pad_maximum_fusion.1), channel_id=1, source_target_pairs={{32,0},{48,16},{64,32},{80,48},{96,64},{112,80},{128,96},{144,112}... | collective-permute-start | bytes 792584 | tf_op jit(solution)/shard_map/ppermute | solution.py:22
  41.2 21.1 %collective-permute-start.12 = (f32[6,12,128]{2,0,1:T(8,128)S(1)}, f32[6,12,128]{2,0,1:T(8,128)S(1)}, u32[]{:S(2)}, u32[]{:S(2)}) collective-permute-start(f32[6,12,128]{2,0,1:T(8,128)S(1)} %pad_maximum_fusion.10), channel_id=1, source_target_pairs={{0,48},{16,64},{32,80},{48,96},{64,112},{80,128},{96,144},{112,160... | collective-permute-start | bytes 110600 | tf_op jit(solution)/shard_map/ppermute | solution.py:22
  50.6 18.9 %collective-permute-start.11 = (f32[6,12,128]{2,0,1:T(8,128)S(1)}, f32[6,12,128]{2,0,1:T(8,128)S(1)}, u32[]{:S(2)}, u32[]{:S(2)}) collective-permute-start(f32[6,12,128]{2,0,1:T(8,128)S(1)} %pad_maximum_fusion.10), channel_id=1, source_target_pairs={{0,16},{16,32},{32,48},{48,64},{64,80},{80,96},{96,112},{112,128},... | collective-permute-start | bytes 110600 | tf_op jit(solution)/shard_map/ppermute | solution.py:22
  55.5 14.1 %collective-permute-start.9 = (f32[43,12,128]{2,0,1:T(8,128)S(1)}, f32[43,12,128]{2,0,1:T(8,128)S(1)}, u32[]{:S(2)}, u32[]{:S(2)}) collective-permute-start(f32[43,12,128]{2,0,1:T(8,128)S(1)} %pad_maximum_fusion), channel_id=1, source_target_pairs={{0,32},{16,48},{32,64},{48,80},{64,96},{80,112},{96,128},{112,144}... | collective-permute-start | bytes 792584 | tf_op jit(solution)/shard_map/ppermute | solution.py:22
  61.0 8.7 %collective-permute-start.16 = (f32[6,12,128]{2,0,1:T(8,128)S(1)}, f32[6,12,128]{2,0,1:T(8,128)S(1)}, u32[]{:S(2)}, u32[]{:S(2)}) collective-permute-start(f32[6,12,128]{2,0,1:T(8,128)S(1)} %pad_maximum_fusion.11), channel_id=1, source_target_pairs={{64,0},{80,16},{96,32},{112,48},{128,64},{144,80},{160,96},{176,11... | collective-permute-start | bytes 110600 | tf_op jit(solution)/shard_map/ppermute | solution.py:22
  62.3 8.9 %collective-permute-start.13 = (f32[6,12,128]{2,0,1:T(8,128)S(1)}, f32[6,12,128]{2,0,1:T(8,128)S(1)}, u32[]{:S(2)}, u32[]{:S(2)}) collective-permute-start(f32[6,12,128]{2,0,1:T(8,128)S(1)} %pad_maximum_fusion.10), channel_id=1, source_target_pairs={{0,64},{16,80},{32,96},{48,112},{64,128},{80,144},{96,160},{112,17... | collective-permute-start | bytes 110600 | tf_op jit(solution)/shard_map/ppermute | solution.py:22
  71.3 8.9 %collective-permute-start.18 = (f32[42,12,128]{2,0,1:T(8,128)S(1)}, f32[42,12,128]{2,0,1:T(8,128)S(1)}, u32[]{:S(2)}, u32[]{:S(2)}) collective-permute-start(f32[42,12,128]{2,0,1:T(8,128)S(1)} %pad_maximum_fusion.3), channel_id=1, source_target_pairs={{64,0},{80,16},{96,32},{112,48},{128,64},{144,80},{160,96},{176,11... | collective-permute-start | bytes 774152 | tf_op jit(solution)/shard_map/ppermute | solution.py:22
  73.6 9.1 %collective-permute-start.17 = (f32[42,12,128]{2,0,1:T(8,128)S(1)}, f32[42,12,128]{2,0,1:T(8,128)S(1)}, u32[]{:S(2)}, u32[]{:S(2)}) collective-permute-start(f32[42,12,128]{2,0,1:T(8,128)S(1)} %pad_maximum_fusion.2), channel_id=1, source_target_pairs={{0,64},{16,80},{32,96},{48,112},{64,128},{80,144},{96,160},{112,17... | collective-permute-start | bytes 774152 | tf_op jit(solution)/shard_map/ppermute | solution.py:22
  82.8 12.1 %collective-permute-start.20 = (f32[42,12,128]{2,0,1:T(8,128)S(1)}, f32[42,12,128]{2,0,1:T(8,128)S(1)}, u32[]{:S(2)}, u32[]{:S(2)}) collective-permute-start(f32[42,12,128]{2,0,1:T(8,128)S(1)} %pad_maximum_fusion.5), channel_id=1, source_target_pairs={{128,0},{144,16},{160,32},{176,48},{192,64},{208,80},{224,96},{240... | collective-permute-start | bytes 774152 | tf_op jit(solution)/shard_map/ppermute | solution.py:22
  84.4 12.2 %collective-permute-start.19 = (f32[42,12,128]{2,0,1:T(8,128)S(1)}, f32[42,12,128]{2,0,1:T(8,128)S(1)}, u32[]{:S(2)}, u32[]{:S(2)}) collective-permute-start(f32[42,12,128]{2,0,1:T(8,128)S(1)} %pad_maximum_fusion.4), channel_id=1, source_target_pairs={{0,128},{16,144},{32,160},{48,176},{64,192},{80,208},{96,224},{112... | collective-permute-start | bytes 774152 | tf_op jit(solution)/shard_map/ppermute | solution.py:22
  98.5 7.2 %copy-start.1 = (f32[25,256]{1,0:T(8,128)S(1)}, f32[25,256]{1,0:T(8,128)}, u32[]{:S(2)}) copy-start(f32[25,256]{1,0:T(8,128)} %param.13) | copy-start | bytes 76804
  98.5 7.2 %copy-start.2 = (f32[25,256]{1,0:T(8,128)S(1)}, f32[25,256]{1,0:T(8,128)}, u32[]{:S(2)}) copy-start(f32[25,256]{1,0:T(8,128)} %param.12) | copy-start | bytes 76804
  98.5 7.2 %copy-start.3 = (f32[25,256]{1,0:T(8,128)S(1)}, f32[25,256]{1,0:T(8,128)}, u32[]{:S(2)}) copy-start(f32[25,256]{1,0:T(8,128)} %param.11) | copy-start | bytes 76804
  99.8 1.2 collective-permute-start.21
  101.0 4.7 %collective-permute-start.22 = (f32[5,256]{1,0:T(8,128)S(1)}, f32[5,256]{1,0:T(8,128)S(1)}, u32[]{:S(2)}, u32[]{:S(2)}) collective-permute-start(f32[5,256]{1,0:T(8,128)S(1)} %add.475), channel_id=1, source_target_pairs={{2,0},{3,1},{4,2},{5,3},{6,4},{7,5},{0,6},{1,7},{10,8},{11,9},{12,... | collective-permute-start | bytes 15368 | tf_op jit(solution)/shard_map/ppermute | solution.py:179
  103.6 4.5 %collective-permute-start.23 = (f32[5,256]{1,0:T(8,128)S(1)}, f32[5,256]{1,0:T(8,128)S(1)}, u32[]{:S(2)}, u32[]{:S(2)}) collective-permute-start(f32[5,256]{1,0:T(8,128)S(1)} %add.475), channel_id=1, source_target_pairs={{4,0},{5,1},{6,2},{7,3},{0,4},{1,5},{2,6},{3,7},{12,8},{13,9},{14,... | collective-permute-start | bytes 15368 | tf_op jit(solution)/shard_map/ppermute | solution.py:179
  104.4 3.7 %collective-permute-start.24 = (f32[5,256]{1,0:T(8,128)S(1)}, f32[5,256]{1,0:T(8,128)S(1)}, u32[]{:S(2)}, u32[]{:S(2)}) collective-permute-start(f32[5,256]{1,0:T(8,128)S(1)} %add.475), channel_id=1, source_target_pairs={{6,0},{7,1},{0,2},{1,3},{2,4},{3,5},{4,6},{5,7},{14,8},{15,9},{8,1... | collective-permute-start | bytes 15368 | tf_op jit(solution)/shard_map/ppermute | solution.py:179
  108.2 7.6 %collective-permute-start.25 = (f32[5,256]{1,0:T(8,128)S(1)}, f32[5,256]{1,0:T(8,128)S(1)}, u32[]{:S(2)}, u32[]{:S(2)}) collective-permute-start(f32[5,256]{1,0:T(8,128)S(1)} %add_bitcast_fusion), channel_id=1, source_target_pairs={{0,8},{1,9},{2,10},{3,11},{4,12},{5,13},{6,14},{7,15},{8,0},{9,1},... | collective-permute-start | bytes 15368 | tf_op jit(solution)/shard_map/ppermute | solution.py:170
  115.8 8.6 %collective-permute-start.26 = (f32[80,2,128]{2,1,0:T(2,128)S(1)}, f32[80,2,128]{2,1,0:T(2,128)S(1)}, u32[]{:S(2)}, u32[]{:S(2)}) collective-permute-start(f32[80,2,128]{2,1,0:T(2,128)S(1)} %constant_dynamic-update-slice_fusion), channel_id=1, source_target_pairs={{0,32},{16,48},{32,64},{48,80},{64,96},{80,112},{96,128},{112,144}... | collective-permute-start | bytes 245768 | tf_op jit(solution)/shard_map/ppermute | solution.py:22
  118.3 6.2 %collective-permute-start.27 = (f32[80,2,128]{2,1,0:T(2,128)S(1)}, f32[80,2,128]{2,1,0:T(2,128)S(1)}, u32[]{:S(2)}, u32[]{:S(2)}) collective-permute-start(f32[80,2,128]{2,1,0:T(2,128)S(1)} %constant_dynamic-update-slice_fusion), channel_id=1, source_target_pairs={{0,16},{16,32},{32,48},{48,64},{64,80},{80,96},{96,112},{112,128},... | collective-permute-start | bytes 245768 | tf_op jit(solution)/shard_map/ppermute | solution.py:22
  121.7 7.1 %collective-permute-start.28 = (f32[80,2,128]{2,1,0:T(2,128)S(1)}, f32[80,2,128]{2,1,0:T(2,128)S(1)}, u32[]{:S(2)}, u32[]{:S(2)}) collective-permute-start(f32[80,2,128]{2,1,0:T(2,128)S(1)} %constant_dynamic-update-slice_fusion), channel_id=1, source_target_pairs={{16,0},{32,16},{48,32},{64,48},{80,64},{96,80},{112,96},{128,112},... | collective-permute-start | bytes 245768 | tf_op jit(solution)/shard_map/ppermute | solution.py:22
  123.0 10.3 %collective-permute-start.29 = (f32[80,2,128]{2,1,0:T(2,128)S(1)}, f32[80,2,128]{2,1,0:T(2,128)S(1)}, u32[]{:S(2)}, u32[]{:S(2)}) collective-permute-start(f32[80,2,128]{2,1,0:T(2,128)S(1)} %constant_dynamic-update-slice_fusion), channel_id=1, source_target_pairs={{32,0},{48,16},{64,32},{80,48},{96,64},{112,80},{128,96},{144,112}... | collective-permute-start | bytes 245768 | tf_op jit(solution)/shard_map/ppermute | solution.py:22
  134.5 39.1 %copy-start.5 = (f32[24]{0:T(128)S(1)}, f32[24]{0:T(128)}, u32[]{:S(2)}) copy-start(f32[24]{0:T(128)} %constant.176.clone) | copy-start | bytes 292
  134.5 39.1 %copy-start.7 = (f32[24]{0:T(128)S(1)}, f32[24]{0:T(128)}, u32[]{:S(2)}) copy-start(f32[24]{0:T(128)} %constant.221) | copy-start | bytes 292
  134.5 39.2 %copy-start.6 = (f32[1,24]{1,0:T(1,128)S(1)}, f32[1,24]{1,0:T(1,128)}, u32[]{:S(2)}) copy-start(f32[1,24]{1,0:T(1,128)} %constant.225) | copy-start | bytes 292
  138.2 1.1 collective-permute-start.30
  139.4 4.9 %collective-permute-start.31 = (f32[26]{0:T(128)S(1)}, f32[26]{0:T(128)S(1)}, u32[]{:S(2)}, u32[]{:S(2)}) collective-permute-start(f32[26]{0:T(128)S(1)} %fusion.81), channel_id=1, source_target_pairs={{2,0},{3,1},{4,2},{5,3},{6,4},{7,5},{0,6},{1,7},{10,8},{11,9},{12,... | collective-permute-start | bytes 320 | tf_op jit(solution)/shard_map/ppermute | solution.py:179
  141.0 4.4 %collective-permute-start.32 = (f32[26]{0:T(128)S(1)}, f32[26]{0:T(128)S(1)}, u32[]{:S(2)}, u32[]{:S(2)}) collective-permute-start(f32[26]{0:T(128)S(1)} %fusion.81), channel_id=1, source_target_pairs={{4,0},{5,1},{6,2},{7,3},{0,4},{1,5},{2,6},{3,7},{12,8},{13,9},{14,... | collective-permute-start | bytes 320 | tf_op jit(solution)/shard_map/ppermute | solution.py:179
  141.6 4.0 %collective-permute-start.33 = (f32[26]{0:T(128)S(1)}, f32[26]{0:T(128)S(1)}, u32[]{:S(2)}, u32[]{:S(2)}) collective-permute-start(f32[26]{0:T(128)S(1)} %fusion.81), channel_id=1, source_target_pairs={{6,0},{7,1},{0,2},{1,3},{2,4},{3,5},{4,6},{5,7},{14,8},{15,9},{8,1... | collective-permute-start | bytes 320 | tf_op jit(solution)/shard_map/ppermute | solution.py:179
  145.7 7.5 %collective-permute-start.34 = (f32[26]{0:T(128)S(1)}, f32[26]{0:T(128)S(1)}, u32[]{:S(2)}, u32[]{:S(2)}) collective-permute-start(f32[26]{0:T(128)S(1)} %fusion.56), channel_id=1, source_target_pairs={{0,8},{1,9},{2,10},{3,11},{4,12},{5,13},{6,14},{7,15},{8,0},{9,1},... | collective-permute-start | bytes 320 | tf_op jit(solution)/shard_map/ppermute | solution.py:170
  153.2 6.3 %collective-permute-start.35 = (f32[26]{0:T(128)S(1)}, f32[26]{0:T(128)S(1)}, u32[]{:S(2)}, u32[]{:S(2)}) collective-permute-start(f32[26]{0:T(128)S(1)} %fusion.80), channel_id=1, source_target_pairs={{16,0},{32,16},{48,32},{0,48},{80,64},{96,80},{112,96},{64,112},{1... | collective-permute-start | bytes 320 | tf_op jit(solution)/shard_map/ppermute | solution.py:179
  158.3 5.0 %collective-permute-start.36 = (f32[26]{0:T(128)S(1)}, f32[26]{0:T(128)S(1)}, u32[]{:S(2)}, u32[]{:S(2)}) collective-permute-start(f32[26]{0:T(128)S(1)} %fusion.80), channel_id=1, source_target_pairs={{32,0},{48,16},{0,32},{16,48},{96,64},{112,80},{64,96},{80,112},{1... | collective-permute-start | bytes 320 | tf_op jit(solution)/shard_map/ppermute | solution.py:179
  158.3 5.0 %collective-permute-start.37 = (f32[26]{0:T(128)S(1)}, f32[26]{0:T(128)S(1)}, u32[]{:S(2)}, u32[]{:S(2)}) collective-permute-start(f32[26]{0:T(128)S(1)} %fusion.80), channel_id=1, source_target_pairs={{48,0},{0,16},{16,32},{32,48},{112,64},{64,80},{80,96},{96,112},{1... | collective-permute-start | bytes 320 | tf_op jit(solution)/shard_map/ppermute | solution.py:179
  163.4 6.1 %collective-permute-start.38 = (f32[26]{0:T(128)S(1)}, f32[26]{0:T(128)S(1)}, u32[]{:S(2)}, u32[]{:S(2)}) collective-permute-start(f32[26]{0:T(128)S(1)} %fusion.79), channel_id=1, source_target_pairs={{64,0},{80,16},{96,32},{112,48},{128,64},{144,80},{160,96},{176,11... | collective-permute-start | bytes 320 | tf_op jit(solution)/shard_map/ppermute | solution.py:179
  166.3 5.0 %collective-permute-start.39 = (f32[26]{0:T(128)S(1)}, f32[26]{0:T(128)S(1)}, u32[]{:S(2)}, u32[]{:S(2)}) collective-permute-start(f32[26]{0:T(128)S(1)} %fusion.79), channel_id=1, source_target_pairs={{128,0},{144,16},{160,32},{176,48},{192,64},{208,80},{224,96},{240... | collective-permute-start | bytes 320 | tf_op jit(solution)/shard_map/ppermute | solution.py:179
  168.1 4.8 %collective-permute-start.40 = (f32[26]{0:T(128)S(1)}, f32[26]{0:T(128)S(1)}, u32[]{:S(2)}, u32[]{:S(2)}) collective-permute-start(f32[26]{0:T(128)S(1)} %fusion.79), channel_id=1, source_target_pairs={{192,0},{208,16},{224,32},{240,48},{0,64},{16,80},{32,96},{48,112}... | collective-permute-start | bytes 320 | tf_op jit(solution)/shard_map/ppermute | solution.py:179
  (1 other events, 2.9 us)

commit v9 on v8

--- a/solution.py
+++ b/solution.py
@@ -312,8 +312,9 @@
     own_drive = pseudo_rate * distribution.reshape(node_rows, NXI, length, TUBES) / denominator
     count = lax.axis_size("sec")
     own_sweep = local_sweep(carry_rate, own_drive)
-    own_pos, own_span = scan_first(own_sweep[2][:, :, -1], own_sweep[3][:, :, -1], 1)
-    own_neg, _ = scan_first(own_sweep[0][:, :, 0], own_sweep[1][:, :, 0], -1)
+    own_pos = fetched((own_sweep[2][:, :, -1], own_sweep[3][:, :, -1]), 1, 1)
+    own_neg = fetched((own_sweep[0][:, :, 0], own_sweep[1][:, :, 0]), 1, -1)
+    own_span = 1
     old_moments = tree_sum(jnp.dot(weighted, distribution, precision=HIGH), ("vel",))
     own_pos, own_neg, old_moments = lax.optimization_barrier((own_pos, own_neg, old_moments))
     moment_drive = thickness * old_moments.reshape(5, 1, length, TUBES) / denominator

time: 180 us -> 172 us (0.956)
  starting transfers between devices: 105 us -> 89.2 us
  waiting for transfers between devices: 50.6 us -> 60.7 us
    ppermute x20 -> x16, starting transfers between devices: 69.8 us -> 53.1 us  [passed_along(): return lax.ppermute(block, axis, route)]
    ppermute x20 -> x16, waiting for transfers between devices: 22.1 us -> 33.2 us  [passed_along(): return lax.ppermute(block, axis, route)]
  transfers between devices with their start and end apart: 41 -> 37, of which waited for: 22 -> 23; matrix products, arithmetic and copies ran while one was open for 2% -> 2% of each run, Pallas kernels for 0% -> 0%
where the time goes in v9:
time: 172 us; the launch traced here: 170 us
  starting transfers between devices  89.2 us (52%)
  waiting for transfers between devices  60.7 us (35%)
  other arithmetic  8.77 us (5%)
  matrix products  5.24 us (3%)
  local copies, waits for them, and re-layouts  3.77 us (2%)
  between operations  2.05 us (1%)
    ppermute x16, starting transfers between devices, passed_along(): return lax.ppermute(block, axis, route)  53.1 us
    ppermute x16, waiting for transfers between devices, passed_along(): return lax.ppermute(block, axis, route)  33.2 us
    ppermute x15, starting transfers between devices, group_sum(): shifted.append(lax.ppermute(block, axis, pairs))  28.4 us
    ppermute x6, waiting for transfers between devices, group_sum(): return block + lax.ppermute(block, axis, pairs)  15 us
    ppermute x15, waiting for transfers between devices, group_sum(): shifted.append(lax.ppermute(block, axis, pairs))  12.4 us
    ppermute x6, starting transfers between devices, group_sum(): return block + lax.ppermute(block, axis, pairs)  7.68 us
  transfers between devices with their start and end apart: 37, of which 23 were waited for; matrix products, arithmetic and copies ran while one was open for 2% of the time, Pallas kernels for 0%

profile of v9, /device:TPU:32, one launch (start us, length us, event | category | flops | bytes accessed | tf_op | source)
XLA Modules:
  0.0 169.7 jit_solution(9164833923663617509)
XLA Ops:
  0.7 1.8 %fusion.26 = f32[5,256]{1,0:T(8,128)S(1)} fusion(f32[864,256]{1,0:T(8,128)} %param.9, f32[5,13824]{1,0:T(8,128)} %constant.174.clone, s32[]{:T(128)S(6)} %select_n.134), kind=kOutput, calls=%fused_computation.98 | convolution fusion | flops 13271040 | bytes 918532 | tf_op jit(solution)/shard_map/dot_general | solution.py:318
  3.6 1.3 collective-permute-start.1
  4.9 1.9 %collective-permute-start.3 = (f32[5,256]{1,0:T(8,128)S(1)}, f32[5,256]{1,0:T(8,128)S(1)}, u32[]{:S(2)}, u32[]{:S(2)}) collective-permute-start(f32[5,256]{1,0:T(8,128)S(1)} %add.426), channel_id=1, source_target_pairs={{2,0},{3,1},{4,2},{5,3},{6,4},{7,5},{0,6},{1,7},{10,8},{11,9},{12,... | collective-permute-start | bytes 15368 | tf_op jit(solution)/shard_map/ppermute | solution.py:179
  6.8 1.5 collective-permute-start.4
  8.4 2.8 %collective-permute-start.5 = (f32[5,256]{1,0:T(8,128)S(1)}, f32[5,256]{1,0:T(8,128)S(1)}, u32[]{:S(2)}, u32[]{:S(2)}) collective-permute-start(f32[5,256]{1,0:T(8,128)S(1)} %add.426), channel_id=1, source_target_pairs={{6,0},{7,1},{0,2},{1,3},{2,4},{3,5},{4,6},{5,7},{14,8},{15,9},{8,1... | collective-permute-start | bytes 15368 | tf_op jit(solution)/shard_map/ppermute | solution.py:179
  12.6 4.9 %collective-permute-start.6 = (f32[5,256]{1,0:T(8,128)S(1)}, f32[5,256]{1,0:T(8,128)S(1)}, u32[]{:S(2)}, u32[]{:S(2)}) collective-permute-start(f32[5,256]{1,0:T(8,128)S(1)} %add_bitcast_fusion.1), channel_id=1, source_target_pairs={{0,8},{1,9},{2,10},{3,11},{4,12},{5,13},{6,14},{7,15},{8,0},{9,1},... | collective-permute-start | bytes 15368 | tf_op jit(solution)/shard_map/ppermute | solution.py:170
  17.5 4.6 %collective-permute-start = (f32[37,12,128]{2,0,1:T(8,128)S(1)}, f32[37,12,128]{2,0,1:T(8,128)S(1)}, u32[]{:S(2)}, u32[]{:S(2)}) collective-permute-start(f32[37,12,128]{2,0,1:T(8,128)S(1)} %pad_maximum_fusion.8), channel_id=1, source_target_pairs={{0,16},{16,32},{32,48},{48,64},{64,80},{80,96},{96,112},{112,128},... | collective-permute-start | bytes 681992 | tf_op jit(solution)/shard_map/ppermute | solution.py:22
  22.2 3.8 %collective-permute-done = f32[37,12,128]{2,0,1:T(8,128)S(1)} collective-permute-done((f32[37,12,128]{2,0,1:T(8,128)S(1)}, f32[37,12,128]{2,0,1:T(8,128)S(1)}, u32[]{:S(2)}, u32[]{:S(2)}) %collective-permute-start) | collective-permute-done | bytes 227360 | tf_op jit(solution)/shard_map/ppermute | solution.py:22
  26.2 1.3 collective-permute-start.8
  27.5 1.3 collective-permute-start.10
  28.9 5.0 %collective-permute-start.7 = (f32[43,12,128]{2,0,1:T(8,128)S(1)}, f32[43,12,128]{2,0,1:T(8,128)S(1)}, u32[]{:S(2)}, u32[]{:S(2)}) collective-permute-start(f32[43,12,128]{2,0,1:T(8,128)S(1)} %pad_maximum_fusion), channel_id=1, source_target_pairs={{0,16},{16,32},{32,48},{48,64},{64,80},{80,96},{96,112},{112,128},... | collective-permute-start | bytes 792584 | tf_op jit(solution)/shard_map/ppermute | solution.py:22
  34.0 6.6 %collective-permute-start.9 = (f32[6,12,128]{2,0,1:T(8,128)S(1)}, f32[6,12,128]{2,0,1:T(8,128)S(1)}, u32[]{:S(2)}, u32[]{:S(2)}) collective-permute-start(f32[6,12,128]{2,0,1:T(8,128)S(1)} %pad_maximum_fusion.12), channel_id=1, source_target_pairs={{0,32},{16,48},{32,64},{48,80},{64,96},{80,112},{96,128},{112,144}... | collective-permute-start | bytes 110600 | tf_op jit(solution)/shard_map/ppermute | solution.py:22
  40.8 1.5 collective-permute-done.9
  42.4 1.3 collective-permute-start.12
  43.8 8.0 %collective-permute-start.11 = (f32[42,12,128]{2,0,1:T(8,128)S(1)}, f32[42,12,128]{2,0,1:T(8,128)S(1)}, u32[]{:S(2)}, u32[]{:S(2)}) collective-permute-start(f32[42,12,128]{2,0,1:T(8,128)S(1)} %pad_maximum_fusion.2), channel_id=1, source_target_pairs={{0,32},{16,48},{32,64},{48,80},{64,96},{80,112},{96,128},{112,144}... | collective-permute-start | bytes 774152 | tf_op jit(solution)/shard_map/ppermute | solution.py:22
  51.8 2.7 %collective-permute-done.12 = f32[42,12,128]{2,0,1:T(8,128)S(1)} collective-permute-done((f32[42,12,128]{2,0,1:T(8,128)S(1)}, f32[42,12,128]{2,0,1:T(8,128)S(1)}, u32[]{:S(2)}, u32[]{:S(2)}) %collective-permute-start.12) | collective-permute-done | bytes 258080 | tf_op jit(solution)/shard_map/ppermute | solution.py:22
  54.5 6.0 %collective-permute-done.11 = f32[42,12,128]{2,0,1:T(8,128)S(1)} collective-permute-done((f32[42,12,128]{2,0,1:T(8,128)S(1)}, f32[42,12,128]{2,0,1:T(8,128)S(1)}, u32[]{:S(2)}, u32[]{:S(2)}) %collective-permute-start.11) | collective-permute-done | bytes 258080 | tf_op jit(solution)/shard_map/ppermute | solution.py:22
  60.6 1.3 collective-permute-start.14
  62.9 6.9 %collective-permute-start.13 = (f32[42,12,128]{2,0,1:T(8,128)S(1)}, f32[42,12,128]{2,0,1:T(8,128)S(1)}, u32[]{:S(2)}, u32[]{:S(2)}) collective-permute-start(f32[42,12,128]{2,0,1:T(8,128)S(1)} %pad_maximum_fusion.4), channel_id=1, source_target_pairs={{0,64},{16,80},{32,96},{48,112},{64,128},{80,144},{96,160},{112,17... | collective-permute-start | bytes 774152 | tf_op jit(solution)/shard_map/ppermute | solution.py:22
  69.8 2.3 %collective-permute-done.14 = f32[42,12,128]{2,0,1:T(8,128)S(1)} collective-permute-done((f32[42,12,128]{2,0,1:T(8,128)S(1)}, f32[42,12,128]{2,0,1:T(8,128)S(1)}, u32[]{:S(2)}, u32[]{:S(2)}) %collective-permute-start.14) | collective-permute-done | bytes 258080 | tf_op jit(solution)/shard_map/ppermute | solution.py:22
  72.2 2.1 %collective-permute-done.13 = f32[42,12,128]{2,0,1:T(8,128)S(1)} collective-permute-done((f32[42,12,128]{2,0,1:T(8,128)S(1)}, f32[42,12,128]{2,0,1:T(8,128)S(1)}, u32[]{:S(2)}, u32[]{:S(2)}) %collective-permute-start.13) | collective-permute-done | bytes 258080 | tf_op jit(solution)/shard_map/ppermute | solution.py:22
  74.4 1.3 collective-permute-start.16
  75.9 8.4 %collective-permute-start.15 = (f32[42,12,128]{2,0,1:T(8,128)S(1)}, f32[42,12,128]{2,0,1:T(8,128)S(1)}, u32[]{:S(2)}, u32[]{:S(2)}) collective-permute-start(f32[42,12,128]{2,0,1:T(8,128)S(1)} %pad_maximum_fusion.6), channel_id=1, source_target_pairs={{0,128},{16,144},{32,160},{48,176},{64,192},{80,208},{96,224},{112... | collective-permute-start | bytes 774152 | tf_op jit(solution)/shard_map/ppermute | solution.py:22
  84.3 2.5 %collective-permute-done.16 = f32[42,12,128]{2,0,1:T(8,128)S(1)} collective-permute-done((f32[42,12,128]{2,0,1:T(8,128)S(1)}, f32[42,12,128]{2,0,1:T(8,128)S(1)}, u32[]{:S(2)}, u32[]{:S(2)}) %collective-permute-start.16) | collective-permute-done | bytes 258080 | tf_op jit(solution)/shard_map/ppermute | solution.py:22
  86.9 1.7 collective-permute-done.15
  90.5 1.3 fusion
  93.0 3.8 %collective-permute-start.18 = (f32[5,256]{1,0:T(8,128)S(1)}, f32[5,256]{1,0:T(8,128)S(1)}, u32[]{:S(2)}, u32[]{:S(2)}) collective-permute-start(f32[5,256]{1,0:T(8,128)S(1)} %add.467), channel_id=1, source_target_pairs={{2,0},{3,1},{4,2},{5,3},{6,4},{7,5},{0,6},{1,7},{10,8},{11,9},{12,... | collective-permute-start | bytes 15368 | tf_op jit(solution)/shard_map/ppermute | solution.py:179
  98.3 3.0 %collective-permute-done.19 = f32[5,256]{1,0:T(8,128)S(1)} collective-permute-done((f32[5,256]{1,0:T(8,128)S(1)}, f32[5,256]{1,0:T(8,128)S(1)}, u32[]{:S(2)}, u32[]{:S(2)}) %collective-permute-start.19) | collective-permute-done | bytes 5152 | tf_op jit(solution)/shard_map/ppermute | solution.py:179
  101.3 1.4 collective-permute-start.21
  102.7 6.5 %collective-permute-done.21 = f32[5,256]{1,0:T(8,128)S(1)} collective-permute-done((f32[5,256]{1,0:T(8,128)S(1)}, f32[5,256]{1,0:T(8,128)S(1)}, u32[]{:S(2)}, u32[]{:S(2)}) %collective-permute-start.21) | collective-permute-done | bytes 5152 | tf_op jit(solution)/shard_map/ppermute | solution.py:170
  109.2 1.8 %collective-permute-start.22 = (f32[80,2,128]{2,1,0:T(2,128)S(1)}, f32[80,2,128]{2,1,0:T(2,128)S(1)}, u32[]{:S(2)}, u32[]{:S(2)}) collective-permute-start(f32[80,2,128]{2,1,0:T(2,128)S(1)} %constant_dynamic-update-slice_fusion), channel_id=1, source_target_pairs={{0,32},{16,48},{32,64},{48,80},{64,96},{80,112},{96,128},{112,144}... | collective-permute-start | bytes 245768 | tf_op jit(solution)/shard_map/ppermute | solution.py:22
  111.0 1.4 collective-permute-start.23
  112.5 1.3 collective-permute-start.24
  113.8 1.3 collective-permute-start.25
  115.3 7.7 %collective-permute-done.24 = f32[80,2,128]{2,1,0:T(2,128)S(1)} collective-permute-done((f32[80,2,128]{2,1,0:T(2,128)S(1)}, f32[80,2,128]{2,1,0:T(2,128)S(1)}, u32[]{:S(2)}, u32[]{:S(2)}) %collective-permute-start.24) | collective-permute-done | bytes 81952 | tf_op jit(solution)/shard_map/ppermute | solution.py:22
  123.0 3.1 %collective-permute-done.25 = f32[80,2,128]{2,1,0:T(2,128)S(1)} collective-permute-done((f32[80,2,128]{2,1,0:T(2,128)S(1)}, f32[80,2,128]{2,1,0:T(2,128)S(1)}, u32[]{:S(2)}, u32[]{:S(2)}) %collective-permute-start.25) | collective-permute-done | bytes 81952 | tf_op jit(solution)/shard_map/ppermute | solution.py:22
  127.3 1.9 %abs_reduce_fusion = (f32[864]{0:T(1024)S(1)}, f32[864,256]{1,0:T(8,128)S(1)}) fusion(f32[1,5,2,128]{3,2,1,0:T(2,128)S(1)} %slice_bitcast_fusion, f32[5,13824]{1,0:T(8,128)} %constant.175.clone, s32[]{:T(128)S(6)} %select_n.134, f32[108,8,2,128]{3,2,1,0:T(2,128)S(1)} %bitcast.168), kind=kOutput, calls=%fused_computation.8 | convolution fusion | flops 13933728 | bytes 1806724 | tf_op jit(solution)/shard_map/dot_general | solution.py:360
  132.2 1.5 collective-permute-start.27
  134.3 2.8 %collective-permute-start.29 = (f32[26]{0:T(128)S(1)}, f32[26]{0:T(128)S(1)}, u32[]{:S(2)}, u32[]{:S(2)}) collective-permute-start(f32[26]{0:T(128)S(1)} %fusion.79), channel_id=1, source_target_pairs={{6,0},{7,1},{0,2},{1,3},{2,4},{3,5},{4,6},{5,7},{14,8},{15,9},{8,1... | collective-permute-start | bytes 320 | tf_op jit(solution)/shard_map/ppermute | solution.py:179
  139.7 6.3 %collective-permute-done.30 = f32[26]{0:T(128)S(1)} collective-permute-done((f32[26]{0:T(128)S(1)}, f32[26]{0:T(128)S(1)}, u32[]{:S(2)}, u32[]{:S(2)}) %collective-permute-start.30) | collective-permute-done | bytes 136 | tf_op jit(solution)/shard_map/ppermute | solution.py:170
  146.0 3.5 %collective-permute-start.31 = (f32[26]{0:T(128)S(1)}, f32[26]{0:T(128)S(1)}, u32[]{:S(2)}, u32[]{:S(2)}) collective-permute-start(f32[26]{0:T(128)S(1)} %fusion.78), channel_id=1, source_target_pairs={{16,0},{32,16},{48,32},{0,48},{80,64},{96,80},{112,96},{64,112},{1... | collective-permute-start | bytes 320 | tf_op jit(solution)/shard_map/ppermute | solution.py:179
  150.6 1.3 collective-permute-start.33
  151.9 2.6 %collective-permute-done.32 = f32[26]{0:T(128)S(1)} collective-permute-done((f32[26]{0:T(128)S(1)}, f32[26]{0:T(128)S(1)}, u32[]{:S(2)}, u32[]{:S(2)}) %collective-permute-start.32) | collective-permute-done | bytes 136 | tf_op jit(solution)/shard_map/ppermute | solution.py:179
  155.4 4.1 %collective-permute-start.34 = (f32[26]{0:T(128)S(1)}, f32[26]{0:T(128)S(1)}, u32[]{:S(2)}, u32[]{:S(2)}) collective-permute-start(f32[26]{0:T(128)S(1)} %fusion.77), channel_id=1, source_target_pairs={{64,0},{80,16},{96,32},{112,48},{128,64},{144,80},{160,96},{176,11... | collective-permute-start | bytes 320 | tf_op jit(solution)/shard_map/ppermute | solution.py:179
  160.2 1.3 collective-permute-start.36
  161.5 3.1 %collective-permute-done.35 = f32[26]{0:T(128)S(1)} collective-permute-done((f32[26]{0:T(128)S(1)}, f32[26]{0:T(128)S(1)}, u32[]{:S(2)}, u32[]{:S(2)}) %collective-permute-start.35) | collective-permute-done | bytes 136 | tf_op jit(solution)/shard_map/ppermute | solution.py:179
  165.7 1.3 multiply_bitcast_fusion.1
  167.2 1.3 add_bitcast_fusion.2
  (207 shorter events, 21.3 us)
Async XLA Ops:
  0.6 1.9 %copy-start.7 = (f32[24]{0:T(128)S(1)}, f32[24]{0:T(128)}, u32[]{:S(2)}) copy-start(f32[24]{0:T(128)} %constant.218) | copy-start | bytes 292
  0.6 2.1 %copy-start = (f32[864,256]{1,0:T(8,128)S(1)}, f32[864,256]{1,0:T(8,128)}, u32[]{:S(2)}) copy-start(f32[864,256]{1,0:T(8,128)} %param.9) | copy-start | bytes 2654212
  0.7 1.9 %copy-start.4 = (f32[256]{0:T(256)S(1)}, f32[256]{0:T(256)}, u32[]{:S(2)}) copy-start(f32[256]{0:T(256)} %param.10) | copy-start | bytes 3076
  2.4 2.4 %collective-permute-start.2 = (f32[5,256]{1,0:T(8,128)S(1)}, f32[5,256]{1,0:T(8,128)S(1)}, u32[]{:S(2)}, u32[]{:S(2)}) collective-permute-start(f32[5,256]{1,0:T(8,128)S(1)} %fusion.26), channel_id=1, source_target_pairs={{0,1},{1,0},{2,3},{3,2},{4,5},{5,4},{6,7},{7,6},{8,9},{9,8},{10,11... | collective-permute-start | bytes 15368 | tf_op jit(solution)/shard_map/ppermute | solution.py:170
  3.6 18.6 %collective-permute-start.1 = (f32[37,12,128]{2,0,1:T(8,128)S(1)}, f32[37,12,128]{2,0,1:T(8,128)S(1)}, u32[]{:S(2)}, u32[]{:S(2)}) collective-permute-start(f32[37,12,128]{2,0,1:T(8,128)S(1)} %pad_maximum_fusion.9), channel_id=1, source_target_pairs={{16,0},{32,16},{48,32},{64,48},{80,64},{96,80},{112,96},{128,112},... | collective-permute-start | bytes 681992 | tf_op jit(solution)/shard_map/ppermute | solution.py:22
  4.9 6.4 %collective-permute-start.3 = (f32[5,256]{1,0:T(8,128)S(1)}, f32[5,256]{1,0:T(8,128)S(1)}, u32[]{:S(2)}, u32[]{:S(2)}) collective-permute-start(f32[5,256]{1,0:T(8,128)S(1)} %add.426), channel_id=1, source_target_pairs={{2,0},{3,1},{4,2},{5,3},{6,4},{7,5},{0,6},{1,7},{10,8},{11,9},{12,... | collective-permute-start | bytes 15368 | tf_op jit(solution)/shard_map/ppermute | solution.py:179
  6.8 4.5 %collective-permute-start.4 = (f32[5,256]{1,0:T(8,128)S(1)}, f32[5,256]{1,0:T(8,128)S(1)}, u32[]{:S(2)}, u32[]{:S(2)}) collective-permute-start(f32[5,256]{1,0:T(8,128)S(1)} %add.426), channel_id=1, source_target_pairs={{4,0},{5,1},{6,2},{7,3},{0,4},{1,5},{2,6},{3,7},{12,8},{13,9},{14,... | collective-permute-start | bytes 15368 | tf_op jit(solution)/shard_map/ppermute | solution.py:179
  8.4 4.2 %collective-permute-start.5 = (f32[5,256]{1,0:T(8,128)S(1)}, f32[5,256]{1,0:T(8,128)S(1)}, u32[]{:S(2)}, u32[]{:S(2)}) collective-permute-start(f32[5,256]{1,0:T(8,128)S(1)} %add.426), channel_id=1, source_target_pairs={{6,0},{7,1},{0,2},{1,3},{2,4},{3,5},{4,6},{5,7},{14,8},{15,9},{8,1... | collective-permute-start | bytes 15368 | tf_op jit(solution)/shard_map/ppermute | solution.py:179
  12.6 9.5 %collective-permute-start.6 = (f32[5,256]{1,0:T(8,128)S(1)}, f32[5,256]{1,0:T(8,128)S(1)}, u32[]{:S(2)}, u32[]{:S(2)}) collective-permute-start(f32[5,256]{1,0:T(8,128)S(1)} %add_bitcast_fusion.1), channel_id=1, source_target_pairs={{0,8},{1,9},{2,10},{3,11},{4,12},{5,13},{6,14},{7,15},{8,0},{9,1},... | collective-permute-start | bytes 15368 | tf_op jit(solution)/shard_map/ppermute | solution.py:170
  17.5 8.4 %collective-permute-start = (f32[37,12,128]{2,0,1:T(8,128)S(1)}, f32[37,12,128]{2,0,1:T(8,128)S(1)}, u32[]{:S(2)}, u32[]{:S(2)}) collective-permute-start(f32[37,12,128]{2,0,1:T(8,128)S(1)} %pad_maximum_fusion.8), channel_id=1, source_target_pairs={{0,16},{16,32},{32,48},{48,64},{64,80},{80,96},{96,112},{112,128},... | collective-permute-start | bytes 681992 | tf_op jit(solution)/shard_map/ppermute | solution.py:22
  26.2 14.4 %collective-permute-start.8 = (f32[43,12,128]{2,0,1:T(8,128)S(1)}, f32[43,12,128]{2,0,1:T(8,128)S(1)}, u32[]{:S(2)}, u32[]{:S(2)}) collective-permute-start(f32[43,12,128]{2,0,1:T(8,128)S(1)} %pad_maximum_fusion.1), channel_id=1, source_target_pairs={{16,0},{32,16},{48,32},{64,48},{80,64},{96,80},{112,96},{128,112},... | collective-permute-start | bytes 792584 | tf_op jit(solution)/shard_map/ppermute | solution.py:22
  27.5 13.1 %collective-permute-start.10 = (f32[6,12,128]{2,0,1:T(8,128)S(1)}, f32[6,12,128]{2,0,1:T(8,128)S(1)}, u32[]{:S(2)}, u32[]{:S(2)}) collective-permute-start(f32[6,12,128]{2,0,1:T(8,128)S(1)} %pad_maximum_fusion.13), channel_id=1, source_target_pairs={{32,0},{48,16},{64,32},{80,48},{96,64},{112,80},{128,96},{144,112}... | collective-permute-start | bytes 110600 | tf_op jit(solution)/shard_map/ppermute | solution.py:22
  28.9 11.8 %collective-permute-start.7 = (f32[43,12,128]{2,0,1:T(8,128)S(1)}, f32[43,12,128]{2,0,1:T(8,128)S(1)}, u32[]{:S(2)}, u32[]{:S(2)}) collective-permute-start(f32[43,12,128]{2,0,1:T(8,128)S(1)} %pad_maximum_fusion), channel_id=1, source_target_pairs={{0,16},{16,32},{32,48},{48,64},{64,80},{80,96},{96,112},{112,128},... | collective-permute-start | bytes 792584 | tf_op jit(solution)/shard_map/ppermute | solution.py:22
  34.0 8.4 %collective-permute-start.9 = (f32[6,12,128]{2,0,1:T(8,128)S(1)}, f32[6,12,128]{2,0,1:T(8,128)S(1)}, u32[]{:S(2)}, u32[]{:S(2)}) collective-permute-start(f32[6,12,128]{2,0,1:T(8,128)S(1)} %pad_maximum_fusion.12), channel_id=1, source_target_pairs={{0,32},{16,48},{32,64},{48,80},{64,96},{80,112},{96,128},{112,144}... | collective-permute-start | bytes 110600 | tf_op jit(solution)/shard_map/ppermute | solution.py:22
  42.4 12.0 %collective-permute-start.12 = (f32[42,12,128]{2,0,1:T(8,128)S(1)}, f32[42,12,128]{2,0,1:T(8,128)S(1)}, u32[]{:S(2)}, u32[]{:S(2)}) collective-permute-start(f32[42,12,128]{2,0,1:T(8,128)S(1)} %pad_maximum_fusion.3), channel_id=1, source_target_pairs={{32,0},{48,16},{64,32},{80,48},{96,64},{112,80},{128,96},{144,112}... | collective-permute-start | bytes 774152 | tf_op jit(solution)/shard_map/ppermute | solution.py:22
  43.8 16.7 %collective-permute-start.11 = (f32[42,12,128]{2,0,1:T(8,128)S(1)}, f32[42,12,128]{2,0,1:T(8,128)S(1)}, u32[]{:S(2)}, u32[]{:S(2)}) collective-permute-start(f32[42,12,128]{2,0,1:T(8,128)S(1)} %pad_maximum_fusion.2), channel_id=1, source_target_pairs={{0,32},{16,48},{32,64},{48,80},{64,96},{80,112},{96,128},{112,144}... | collective-permute-start | bytes 774152 | tf_op jit(solution)/shard_map/ppermute | solution.py:22
  60.6 11.5 %collective-permute-start.14 = (f32[42,12,128]{2,0,1:T(8,128)S(1)}, f32[42,12,128]{2,0,1:T(8,128)S(1)}, u32[]{:S(2)}, u32[]{:S(2)}) collective-permute-start(f32[42,12,128]{2,0,1:T(8,128)S(1)} %pad_maximum_fusion.5), channel_id=1, source_target_pairs={{64,0},{80,16},{96,32},{112,48},{128,64},{144,80},{160,96},{176,11... | collective-permute-start | bytes 774152 | tf_op jit(solution)/shard_map/ppermute | solution.py:22
  62.9 11.3 %collective-permute-start.13 = (f32[42,12,128]{2,0,1:T(8,128)S(1)}, f32[42,12,128]{2,0,1:T(8,128)S(1)}, u32[]{:S(2)}, u32[]{:S(2)}) collective-permute-start(f32[42,12,128]{2,0,1:T(8,128)S(1)} %pad_maximum_fusion.4), channel_id=1, source_target_pairs={{0,64},{16,80},{32,96},{48,112},{64,128},{80,144},{96,160},{112,17... | collective-permute-start | bytes 774152 | tf_op jit(solution)/shard_map/ppermute | solution.py:22
  74.4 12.4 %collective-permute-start.16 = (f32[42,12,128]{2,0,1:T(8,128)S(1)}, f32[42,12,128]{2,0,1:T(8,128)S(1)}, u32[]{:S(2)}, u32[]{:S(2)}) collective-permute-start(f32[42,12,128]{2,0,1:T(8,128)S(1)} %pad_maximum_fusion.7), channel_id=1, source_target_pairs={{128,0},{144,16},{160,32},{176,48},{192,64},{208,80},{224,96},{240... | collective-permute-start | bytes 774152 | tf_op jit(solution)/shard_map/ppermute | solution.py:22
  75.9 12.6 %collective-permute-start.15 = (f32[42,12,128]{2,0,1:T(8,128)S(1)}, f32[42,12,128]{2,0,1:T(8,128)S(1)}, u32[]{:S(2)}, u32[]{:S(2)}) collective-permute-start(f32[42,12,128]{2,0,1:T(8,128)S(1)} %pad_maximum_fusion.6), channel_id=1, source_target_pairs={{0,128},{16,144},{32,160},{48,176},{64,192},{80,208},{96,224},{112... | collective-permute-start | bytes 774152 | tf_op jit(solution)/shard_map/ppermute | solution.py:22
  90.5 7.8 %copy-start.1 = (f32[25,256]{1,0:T(8,128)S(1)}, f32[25,256]{1,0:T(8,128)}, u32[]{:S(2)}) copy-start(f32[25,256]{1,0:T(8,128)} %param.13) | copy-start | bytes 76804
  90.5 7.7 %copy-start.2 = (f32[25,256]{1,0:T(8,128)S(1)}, f32[25,256]{1,0:T(8,128)}, u32[]{:S(2)}) copy-start(f32[25,256]{1,0:T(8,128)} %param.12) | copy-start | bytes 76804
  90.5 7.7 %copy-start.3 = (f32[25,256]{1,0:T(8,128)S(1)}, f32[25,256]{1,0:T(8,128)}, u32[]{:S(2)}) copy-start(f32[25,256]{1,0:T(8,128)} %param.11) | copy-start | bytes 76804
  91.8 1.2 collective-permute-start.17
  93.0 5.3 %collective-permute-start.18 = (f32[5,256]{1,0:T(8,128)S(1)}, f32[5,256]{1,0:T(8,128)S(1)}, u32[]{:S(2)}, u32[]{:S(2)}) collective-permute-start(f32[5,256]{1,0:T(8,128)S(1)} %add.467), channel_id=1, source_target_pairs={{2,0},{3,1},{4,2},{5,3},{6,4},{7,5},{0,6},{1,7},{10,8},{11,9},{12,... | collective-permute-start | bytes 15368 | tf_op jit(solution)/shard_map/ppermute | solution.py:179
  96.8 4.5 %collective-permute-start.19 = (f32[5,256]{1,0:T(8,128)S(1)}, f32[5,256]{1,0:T(8,128)S(1)}, u32[]{:S(2)}, u32[]{:S(2)}) collective-permute-start(f32[5,256]{1,0:T(8,128)S(1)} %add.467), channel_id=1, source_target_pairs={{4,0},{5,1},{6,2},{7,3},{0,4},{1,5},{2,6},{3,7},{12,8},{13,9},{14,... | collective-permute-start | bytes 15368 | tf_op jit(solution)/shard_map/ppermute | solution.py:179
  97.1 4.2 %collective-permute-start.20 = (f32[5,256]{1,0:T(8,128)S(1)}, f32[5,256]{1,0:T(8,128)S(1)}, u32[]{:S(2)}, u32[]{:S(2)}) collective-permute-start(f32[5,256]{1,0:T(8,128)S(1)} %add.467), channel_id=1, source_target_pairs={{6,0},{7,1},{0,2},{1,3},{2,4},{3,5},{4,6},{5,7},{14,8},{15,9},{8,1... | collective-permute-start | bytes 15368 | tf_op jit(solution)/shard_map/ppermute | solution.py:179
  101.3 7.8 %collective-permute-start.21 = (f32[5,256]{1,0:T(8,128)S(1)}, f32[5,256]{1,0:T(8,128)S(1)}, u32[]{:S(2)}, u32[]{:S(2)}) collective-permute-start(f32[5,256]{1,0:T(8,128)S(1)} %add_bitcast_fusion), channel_id=1, source_target_pairs={{0,8},{1,9},{2,10},{3,11},{4,12},{5,13},{6,14},{7,15},{8,0},{9,1},... | collective-permute-start | bytes 15368 | tf_op jit(solution)/shard_map/ppermute | solution.py:170
  109.2 6.1 %collective-permute-start.22 = (f32[80,2,128]{2,1,0:T(2,128)S(1)}, f32[80,2,128]{2,1,0:T(2,128)S(1)}, u32[]{:S(2)}, u32[]{:S(2)}) collective-permute-start(f32[80,2,128]{2,1,0:T(2,128)S(1)} %constant_dynamic-update-slice_fusion), channel_id=1, source_target_pairs={{0,32},{16,48},{32,64},{48,80},{64,96},{80,112},{96,128},{112,144}... | collective-permute-start | bytes 245768 | tf_op jit(solution)/shard_map/ppermute | solution.py:22
  111.0 4.2 %collective-permute-start.23 = (f32[80,2,128]{2,1,0:T(2,128)S(1)}, f32[80,2,128]{2,1,0:T(2,128)S(1)}, u32[]{:S(2)}, u32[]{:S(2)}) collective-permute-start(f32[80,2,128]{2,1,0:T(2,128)S(1)} %constant_dynamic-update-slice_fusion), channel_id=1, source_target_pairs={{0,16},{16,32},{32,48},{48,64},{64,80},{80,96},{96,112},{112,128},... | collective-permute-start | bytes 245768 | tf_op jit(solution)/shard_map/ppermute | solution.py:22
  112.5 10.5 %collective-permute-start.24 = (f32[80,2,128]{2,1,0:T(2,128)S(1)}, f32[80,2,128]{2,1,0:T(2,128)S(1)}, u32[]{:S(2)}, u32[]{:S(2)}) collective-permute-start(f32[80,2,128]{2,1,0:T(2,128)S(1)} %constant_dynamic-update-slice_fusion), channel_id=1, source_target_pairs={{16,0},{32,16},{48,32},{64,48},{80,64},{96,80},{112,96},{128,112},... | collective-permute-start | bytes 245768 | tf_op jit(solution)/shard_map/ppermute | solution.py:22
  113.8 12.3 %collective-permute-start.25 = (f32[80,2,128]{2,1,0:T(2,128)S(1)}, f32[80,2,128]{2,1,0:T(2,128)S(1)}, u32[]{:S(2)}, u32[]{:S(2)}) collective-permute-start(f32[80,2,128]{2,1,0:T(2,128)S(1)} %constant_dynamic-update-slice_fusion), channel_id=1, source_target_pairs={{32,0},{48,16},{64,32},{80,48},{96,64},{112,80},{128,96},{144,112}... | collective-permute-start | bytes 245768 | tf_op jit(solution)/shard_map/ppermute | solution.py:22
  127.3 38.3 %copy-start.5 = (f32[24]{0:T(128)S(1)}, f32[24]{0:T(128)}, u32[]{:S(2)}) copy-start(f32[24]{0:T(128)} %constant.176.clone) | copy-start | bytes 292
  127.3 38.3 %copy-start.8 = (f32[24]{0:T(128)S(1)}, f32[24]{0:T(128)}, u32[]{:S(2)}) copy-start(f32[24]{0:T(128)} %constant.221) | copy-start | bytes 292
  127.3 38.4 %copy-start.6 = (f32[1,24]{1,0:T(1,128)S(1)}, f32[1,24]{1,0:T(1,128)}, u32[]{:S(2)}) copy-start(f32[1,24]{1,0:T(1,128)} %constant.225) | copy-start | bytes 292
  131.0 1.1 collective-permute-start.26
  132.2 4.9 %collective-permute-start.27 = (f32[26]{0:T(128)S(1)}, f32[26]{0:T(128)S(1)}, u32[]{:S(2)}, u32[]{:S(2)}) collective-permute-start(f32[26]{0:T(128)S(1)} %fusion.79), channel_id=1, source_target_pairs={{2,0},{3,1},{4,2},{5,3},{6,4},{7,5},{0,6},{1,7},{10,8},{11,9},{12,... | collective-permute-start | bytes 320 | tf_op jit(solution)/shard_map/ppermute | solution.py:179
  133.7 4.4 %collective-permute-start.28 = (f32[26]{0:T(128)S(1)}, f32[26]{0:T(128)S(1)}, u32[]{:S(2)}, u32[]{:S(2)}) collective-permute-start(f32[26]{0:T(128)S(1)} %fusion.79), channel_id=1, source_target_pairs={{4,0},{5,1},{6,2},{7,3},{0,4},{1,5},{2,6},{3,7},{12,8},{13,9},{14,... | collective-permute-start | bytes 320 | tf_op jit(solution)/shard_map/ppermute | solution.py:179
  134.3 4.1 %collective-permute-start.29 = (f32[26]{0:T(128)S(1)}, f32[26]{0:T(128)S(1)}, u32[]{:S(2)}, u32[]{:S(2)}) collective-permute-start(f32[26]{0:T(128)S(1)} %fusion.79), channel_id=1, source_target_pairs={{6,0},{7,1},{0,2},{1,3},{2,4},{3,5},{4,6},{5,7},{14,8},{15,9},{8,1... | collective-permute-start | bytes 320 | tf_op jit(solution)/shard_map/ppermute | solution.py:179
  138.4 7.5 %collective-permute-start.30 = (f32[26]{0:T(128)S(1)}, f32[26]{0:T(128)S(1)}, u32[]{:S(2)}, u32[]{:S(2)}) collective-permute-start(f32[26]{0:T(128)S(1)} %fusion.56), channel_id=1, source_target_pairs={{0,8},{1,9},{2,10},{3,11},{4,12},{5,13},{6,14},{7,15},{8,0},{9,1},... | collective-permute-start | bytes 320 | tf_op jit(solution)/shard_map/ppermute | solution.py:170
  146.0 5.9 %collective-permute-start.31 = (f32[26]{0:T(128)S(1)}, f32[26]{0:T(128)S(1)}, u32[]{:S(2)}, u32[]{:S(2)}) collective-permute-start(f32[26]{0:T(128)S(1)} %fusion.78), channel_id=1, source_target_pairs={{16,0},{32,16},{48,32},{0,48},{80,64},{96,80},{112,96},{64,112},{1... | collective-permute-start | bytes 320 | tf_op jit(solution)/shard_map/ppermute | solution.py:179
  149.5 5.0 %collective-permute-start.32 = (f32[26]{0:T(128)S(1)}, f32[26]{0:T(128)S(1)}, u32[]{:S(2)}, u32[]{:S(2)}) collective-permute-start(f32[26]{0:T(128)S(1)} %fusion.78), channel_id=1, source_target_pairs={{32,0},{48,16},{0,32},{16,48},{96,64},{112,80},{64,96},{80,112},{1... | collective-permute-start | bytes 320 | tf_op jit(solution)/shard_map/ppermute | solution.py:179
  150.6 4.8 %collective-permute-start.33 = (f32[26]{0:T(128)S(1)}, f32[26]{0:T(128)S(1)}, u32[]{:S(2)}, u32[]{:S(2)}) collective-permute-start(f32[26]{0:T(128)S(1)} %fusion.78), channel_id=1, source_target_pairs={{48,0},{0,16},{16,32},{32,48},{112,64},{64,80},{80,96},{96,112},{1... | collective-permute-start | bytes 320 | tf_op jit(solution)/shard_map/ppermute | solution.py:179
  155.4 6.1 %collective-permute-start.34 = (f32[26]{0:T(128)S(1)}, f32[26]{0:T(128)S(1)}, u32[]{:S(2)}, u32[]{:S(2)}) collective-permute-start(f32[26]{0:T(128)S(1)} %fusion.77), channel_id=1, source_target_pairs={{64,0},{80,16},{96,32},{112,48},{128,64},{144,80},{160,96},{176,11... | collective-permute-start | bytes 320 | tf_op jit(solution)/shard_map/ppermute | solution.py:179
  159.5 5.0 %collective-permute-start.35 = (f32[26]{0:T(128)S(1)}, f32[26]{0:T(128)S(1)}, u32[]{:S(2)}, u32[]{:S(2)}) collective-permute-start(f32[26]{0:T(128)S(1)} %fusion.77), channel_id=1, source_target_pairs={{128,0},{144,16},{160,32},{176,48},{192,64},{208,80},{224,96},{240... | collective-permute-start | bytes 320 | tf_op jit(solution)/shard_map/ppermute | solution.py:179
  160.2 4.8 %collective-permute-start.36 = (f32[26]{0:T(128)S(1)}, f32[26]{0:T(128)S(1)}, u32[]{:S(2)}, u32[]{:S(2)}) collective-permute-start(f32[26]{0:T(128)S(1)} %fusion.77), channel_id=1, source_target_pairs={{192,0},{208,16},{224,32},{240,48},{0,64},{16,80},{32,96},{48,112}... | collective-permute-start | bytes 320 | tf_op jit(solution)/shard_map/ppermute | solution.py:179

commit v10 on v8

--- a/solution.py
+++ b/solution.py
@@ -289,78 +289,79 @@
     )
 
 
+def line_block(matrices, vector):
+    shaped = matrices.reshape(matrices.shape[:-1] + (5, 5))
+    return jnp.sum(shaped * vector[..., None, :], axis=-1)
+
+
 def body(distribution, collision, lower_blocks, upper_blocks, diag_inverse):
     node_count = distribution.shape[0]
     cell_count = distribution.shape[1]
     length = cell_count // TUBES
     node_rows = node_count // NXI
-    half_nodes = NXI // 2
+    count = lax.axis_size("sec")
+    total_length = length * count
+    share = TUBES // count
     along_x, node_weight, weighted_np, rebuild_np = node_tables(NXI)
-    all_mass = jnp.asarray(node_weight, jnp.float32)
     offset = lax.axis_index("vel") * node_count
     weighted = lax.dynamic_slice_in_dim(
         jnp.asarray(weighted_np, jnp.float32), offset, node_count, 1
     )
     rebuild = lax.dynamic_slice_in_dim(jnp.asarray(rebuild_np, jnp.float32), offset, node_count, 1)
-    node_mass = lax.dynamic_slice_in_dim(all_mass, offset, node_count, 0)
+    node_mass = lax.dynamic_slice_in_dim(jnp.asarray(node_weight, jnp.float32), offset, node_count, 0)
     line_signed = jnp.asarray(along_x[:NXI], jnp.float32)
-    total_length = length * lax.axis_size("sec")
-    thickness = collision.reshape(1, 1, length, TUBES)
-    node_speed = jnp.abs(line_signed).reshape(1, NXI, 1, 1)
+    node_signed = jnp.asarray(np.tile(along_x[:NXI], node_rows), jnp.float32)
+    packed = jnp.concatenate(
+        [distribution, collision.reshape(1, cell_count), lower_blocks, upper_blocks, diag_inverse],
+        axis=0,
+    )
+    rows = packed.shape[0]
+    packed = packed.reshape(rows, length, TUBES).transpose(1, 2, 0)
+    lines = lax.all_to_all(packed, "sec", 1, 0, tiled=True)
+    dist_t = lines[:, :, :node_count]
+    thickness = lines[:, :, node_count : node_count + 1]
+    lower_t = lines[:, :, node_count + 1 : node_count + 26]
+    upper_t = lines[:, :, node_count + 26 : node_count + 51]
+    inverse_t = lines[:, :, node_count + 51 : node_count + 76]
+    cells = total_length * share
+    old_moments = tree_sum(
+        jnp.dot(dist_t.reshape(cells, node_count), weighted.T, precision=HIGH), ("vel",)
+    )
+    target = jnp.dot(old_moments, rebuild, precision=HIGH).reshape(total_length, share, node_count)
+    node_speed = jnp.abs(node_signed)
     denominator = node_speed * total_length + thickness + pseudo_rate
     carry_rate = node_speed * total_length / denominator
-    own_drive = pseudo_rate * distribution.reshape(node_rows, NXI, length, TUBES) / denominator
-    count = lax.axis_size("sec")
-    own_sweep = local_sweep(carry_rate, own_drive)
-    own_pos, own_span = scan_first(own_sweep[2][:, :, -1], own_sweep[3][:, :, -1], 1)
-    own_neg, _ = scan_first(own_sweep[0][:, :, 0], own_sweep[1][:, :, 0], -1)
-    old_moments = tree_sum(jnp.dot(weighted, distribution, precision=HIGH), ("vel",))
-    own_pos, own_neg, old_moments = lax.optimization_barrier((own_pos, own_neg, old_moments))
-    moment_drive = thickness * old_moments.reshape(5, 1, length, TUBES) / denominator
-    moment_sweep = local_sweep(carry_rate, moment_drive)
-    own_pos, own_neg, moment_pos, moment_neg = caught_up(
-        own_pos, own_neg, own_span, moment_sweep, count
-    )
-    span = min(2 * own_span, count)
-    while span < count - 1:
-        own_pos, moment_pos = joint_next(own_pos, moment_pos, span, 1)
-        own_neg, moment_neg = joint_next(own_neg, moment_neg, span, -1)
-        span *= 2
-        own_pos, own_neg, moment_pos, moment_neg = lax.optimization_barrier(
-            (own_pos, own_neg, moment_pos, moment_neg)
+    drive_term = (thickness * target + pseudo_rate * dist_t) / denominator
+    _, forward = lax.associative_scan(affine_combine, (carry_rate, drive_term), axis=0)
+    _, backward = lax.associative_scan(
+        affine_combine, (carry_rate, drive_term), reverse=True, axis=0
+    )
+    half_field = jnp.where(node_signed > 0, forward, backward)
+    half_moments = tree_sum(
+        jnp.dot(half_field.reshape(cells, node_count), weighted.T, precision=HIGH), ("vel",)
+    )
+    residual = (half_moments - old_moments).reshape(total_length, share, 5)
+    correction = line_block(inverse_t, residual)
+    edge_zero = jnp.zeros((1, share, 5), jnp.float32)
+    for sweep_index in range(JACOBI):
+        from_left = jnp.concatenate([edge_zero, correction[:-1]], axis=0)
+        from_right = jnp.concatenate([correction[1:], edge_zero], axis=0)
+        correction = line_block(
+            inverse_t,
+            residual - line_block(lower_t, from_left) - line_block(upper_t, from_right),
         )
-    own_field = joined_field(own_sweep, own_neg[1], own_pos[1])
-    moment_field = joined_field(moment_sweep, moment_neg[1], moment_pos[1])
-    basis = rebuild.reshape(5, node_rows, NXI, 1, 1)
-    half_field = own_field + jnp.sum(basis * moment_field[:, None], axis=0)
-    half_field = half_field.reshape(node_count, cell_count)
-    half_moments = tree_sum(jnp.dot(weighted, half_field, precision=HIGH), ("vel",))
-    residual = (half_moments - old_moments).reshape(5, length, TUBES)
-    width = min(-(-JACOBI // length), lax.axis_size("sec") - 1)
-    blocks = jnp.concatenate([lower_blocks, upper_blocks, diag_inverse], axis=0)
-    wide = with_halo(
-        jnp.concatenate([blocks.reshape(75, length, TUBES), residual], axis=0), width
-    )
-    lower_r = wide[:25]
-    upper_r = wide[25:50]
-    inverse_r = wide[50:75]
-    residual_wide = wide[75:]
-    correction = apply_block(inverse_r, residual_wide)
-    edge_zero = jnp.zeros((5, 1, TUBES), jnp.float32)
-    for sweep_index in range(JACOBI):
-        from_left = jnp.concatenate([edge_zero, correction[:, :-1]], axis=1)
-        from_right = jnp.concatenate([correction[:, 1:], edge_zero], axis=1)
-        correction = apply_block(
-            inverse_r,
-            residual_wide - apply_block(lower_r, from_left) - apply_block(upper_r, from_right),
-        )
-    correction = correction[:, width * length : (width + 1) * length].reshape(5, cell_count)
+    correction = correction.reshape(cells, 5)
     macro = half_moments + correction
-    synthetic = half_field + jnp.dot(rebuild.T, correction, precision=HIGH)
-    local_totals = jnp.sum(old_moments - macro, axis=1)[0:2]
-    magnitude = jnp.sum(jnp.abs(synthetic), axis=1)
+    synthetic = half_field + jnp.dot(correction, rebuild, precision=HIGH).reshape(
+        total_length, share, node_count
+    )
+    local_totals = jnp.sum(old_moments - macro, axis=0)[0:2]
+    magnitude = jnp.sum(jnp.abs(synthetic), axis=(0, 1))
     line_loaded = jnp.sum((node_mass * magnitude).reshape(node_rows, NXI), axis=0)
     first_copy = (lax.axis_index("vel") == 0).astype(jnp.float32)
+    back = jnp.concatenate([synthetic, macro.reshape(total_length, share, 5)], axis=2)
+    back = lax.all_to_all(back, "sec", 0, 1, tiled=True)
+    back = back.transpose(2, 0, 1).reshape(node_count + 5, cell_count)
     gathered = tree_sum(
         jnp.concatenate([line_loaded, local_totals * first_copy]), ("vel", "sec")
     )
@@ -380,9 +381,9 @@
         sums = jnp.dot(terms, spread, precision=HIGH)
         shift_mass, shift_flow = newton_update(shift_mass, shift_flow, sums, goal_mass, goal_flow)
     growth = jnp.exp(shift_mass + shift_flow * line_signed)
-    synthetic_rows = synthetic.reshape(node_rows, NXI, cell_count)
+    synthetic_rows = back[:node_count].reshape(node_rows, NXI, cell_count)
     new_distribution = synthetic_rows + jnp.abs(synthetic_rows) * (growth[None, :, None] - 1.0)
-    return (new_distribution.reshape(node_count, cell_count), macro)
+    return (new_distribution.reshape(node_count, cell_count), back[node_count:])
 
 
 def solution(mesh):

time: 180 us -> 164 us (0.911)
  starting transfers between devices: 105 us -> 52.8 us
  local copies, waits for them, and re-layouts: 4.95 us -> 41.6 us
  waiting for transfers between devices: 50.6 us -> 39.6 us
  other arithmetic: 10.1 us -> 19.7 us
  matrix products: 4.73 us -> 7.05 us
    ppermute x20 -> x0, starting transfers between devices: 69.8 us -> none  [passed_along(): return lax.ppermute(block, axis, route)]
    ppermute x20 -> x0, waiting for transfers between devices: 22.1 us -> none  [passed_along(): return lax.ppermute(block, axis, route)]
    pad x0 -> x16, local copies, waits for them, and re-layouts: none -> 21.9 us  [the longest x8 14 us: body(): lax.associative_scan(affine_combine, (carry_rate, drive_term), axis=0)]
    all_to_all x0 -> x2, waiting for transfers between devices: none -> 17.7 us  [the longest x1 17.7 us: body(): lines = lax.all_to_all(packed, 'sec', 1, 0, tiled=True)]
    all_to_all x0 -> x2, starting transfers between devices: none -> 10.7 us  [the longest x1 7.03 us: body(): lines = lax.all_to_all(packed, 'sec', 1, 0, tiled=True)]
    unnamed x33 -> x62, local copies, waits for them, and re-layouts: 0.11 us -> 9.95 us
    ppermute x6, starting transfers between devices: 7.57 us -> 16.6 us  [group_sum(): return block + lax.ppermute(block, axis, pairs)]
    ppermute x6, waiting for transfers between devices: 16 us -> 7.19 us  [group_sum(): return block + lax.ppermute(block, axis, pairs)]
  transfers between devices with their start and end apart: 41 -> 23, of which waited for: 22 -> 17; matrix products, arithmetic and copies ran while one was open for 2% -> 4% of each run, Pallas kernels for 0% -> 0%
where the time goes in v10:
time: 164 us; the launch traced here: 162 us
  starting transfers between devices  52.8 us (32%)
  local copies, waits for them, and re-layouts  41.6 us (25%)
  waiting for transfers between devices  39.6 us (24%)
  other arithmetic  19.7 us (12%)
  matrix products  7.05 us (4%)
    ppermute x15, starting transfers between devices, group_sum(): shifted.append(lax.ppermute(block, axis, pairs))  25.5 us
    all_to_all x1, waiting for transfers between devices, body(): lines = lax.all_to_all(packed, 'sec', 1, 0, tiled=True)  17.7 us
    ppermute x6, starting transfers between devices, group_sum(): return block + lax.ppermute(block, axis, pairs)  16.6 us
    ppermute x15, waiting for transfers between devices, group_sum(): shifted.append(lax.ppermute(block, axis, pairs))  14.7 us
    pad x8, local copies, waits for them, and re-layouts, body(): lax.associative_scan(affine_combine, (carry_rate, drive_term), axis=0)  14 us
    unnamed x62, local copies, waits for them, and re-layouts  9.95 us
    pad x8, local copies, waits for them, and re-layouts, body(): lax.associative_scan(affine_combine, (carry_rate, drive_term), reverse=Tr...  7.89 us
    add x8, other arithmetic, affine_combine(): later_map[0] * earlier_map[1] + later_map[1]  7.46 us
  transfers between devices with their start and end apart: 23, of which 17 were waited for; matrix products, arithmetic and copies ran while one was open for 4% of the time, Pallas kernels for 0%

profile of v10, /device:TPU:32, one launch (start us, length us, event | category | flops | bytes accessed | tf_op | source)
XLA Modules:
  0.0 162.2 jit_solution(14543600937856071219)
XLA Ops:
  3.7 1.5 copy.86
  5.6 1.8 %copy.91 = f32[2,128,940]{2,0,1:T(2,128)} copy(f32[2,128,940]{2,1,0:T(8,128)S(1)} %bitcast.157) | data formatting | bytes 1925120 | tf_op jit(solution)/shard_map/transpose | solution.py:319
  7.4 7.0 %all-to-all-start = ((f32[2,128,940]{2,0,1:T(2,128)}), f32[2,128,940]{2,0,1:T(2,128)S(1)}, u32[]{:S(2)}, u32[]{:S(2)}) async-start(f32[2,128,940]{2,0,1:T(2,128)} %copy.91), calls=%async_computation | async-start | bytes 2097152 | tf_op jit(solution)/shard_map/all_to_all | solution.py:320
  14.5 17.7 %all-to-all-done = f32[2,128,940]{2,0,1:T(2,128)S(1)} async-done(((f32[2,128,940]{2,0,1:T(2,128)}), f32[2,128,940]{2,0,1:T(2,128)S(1)}, u32[]{:S(2)}, u32[]{:S(2)}) %all-to-all-start) | async-done | bytes 962592 | tf_op jit(solution)/shard_map/all_to_all | solution.py:320
  32.6 1.6 fusion.5
  34.2 1.2 collective-permute-done
  35.4 1.9 %collective-permute-start.3 = (f32[256,5]{0,1:T(8,128)S(1)}, f32[256,5]{0,1:T(8,128)S(1)}, u32[]{:S(2)}, u32[]{:S(2)}) collective-permute-start(f32[256,5]{0,1:T(8,128)S(1)} %add.377), channel_id=1, source_target_pairs={{6,0},{7,1},{0,2},{1,3},{2,4},{3,5},{4,6},{5,7},{14,8},{15,9},{8,1... | collective-permute-start | bytes 15368 | tf_op jit(solution)/shard_map/ppermute | solution.py:179
  37.4 1.4 collective-permute-start.2
  38.7 2.0 %collective-permute-start.1 = (f32[256,5]{0,1:T(8,128)S(1)}, f32[256,5]{0,1:T(8,128)S(1)}, u32[]{:S(2)}, u32[]{:S(2)}) collective-permute-start(f32[256,5]{0,1:T(8,128)S(1)} %add.377), channel_id=1, source_target_pairs={{2,0},{3,1},{4,2},{5,3},{6,4},{7,5},{0,6},{1,7},{10,8},{11,9},{12,... | collective-permute-start | bytes 15368 | tf_op jit(solution)/shard_map/ppermute | solution.py:179
  42.4 6.5 %collective-permute-start.4 = (f32[256,5]{0,1:T(8,128)S(1)}, f32[256,5]{0,1:T(8,128)S(1)}, u32[]{:S(2)}, u32[]{:S(2)}) collective-permute-start(f32[256,5]{0,1:T(8,128)S(1)} %add_bitcast_fusion.1), channel_id=1, source_target_pairs={{0,8},{1,9},{2,10},{3,11},{4,12},{5,13},{6,14},{7,15},{8,0},{9,1},... | collective-permute-start | bytes 15368 | tf_op jit(solution)/shard_map/ppermute | solution.py:170
  49.1 1.4 collective-permute-done.4
  50.5 1.9 %fusion.2 = f32[32,8,864]{2,1,0:T(8,128)S(1)} fusion(f32[256,5]{0,1:T(8,128)S(1)} %fusion.75, f32[32,8,940]{2,1,0:T(8,128)S(1)} %bitcast.153, f32[864]{0:T(1024)S(1)} %copy-done.25, f32[32,8]{1,0:T(8,128)S(1)} %bitcast.180, f32[5,13824]{1,0:T(8,128)} %constant.177.clone, s32[]{:T(128)S(6)} %select_n.138), kind=kOutput, calls=%fused_computation.4 | convolution fusion | flops 14376960 | bytes 1807748 | tf_op jit(solution)/shard_map/dot_general | solution.py:330
  56.5 1.3 pad.83
  57.8 1.0 fusion.13
  59.6 1.9 %pad.84 = f32[8,8,864]{2,1,0:T(8,128)} pad(f32[4,8,864]{2,1,0:T(8,128)S(1)} %pad_maximum_fusion.6, f32[]{:T(128)} %constant.163.clone.1), padding=0_1_1x0_0_0x0_0_0 | pad | bytes 331780 | tf_op jit(solution)/shard_map/pad | solution.py:336
  61.5 3.4 %pad.85 = f32[8,8,864]{2,1,0:T(8,128)} pad(f32[4,8,864]{2,1,0:T(8,128)} %add.418, f32[]{:T(128)} %constant.163.clone.1), padding=1_0_1x0_0_0x0_0_0 | pad | bytes 331780 | tf_op jit(solution)/shard_map/pad | solution.py:336
  65.0 1.9 %fusion.11 = f32[7,8,864]{2,1,0:T(8,128)} fusion(f32[8,8,864]{2,1,0:T(8,128)} %pad.85, f32[8,8,864]{2,1,0:T(8,128)} %pad.84, f32[16,8,864]{2,1,0:T(8,128)S(1)} %get-tuple-element.37, f32[16,8,864]{2,1,0:T(8,128)} %copy-done.3), kind=kLoop, calls=%fused_computation.34 | loop fusion | flops 145152 | bytes 967680 | tf_op jit(solution)/shard_map/add | solution.py:99
  70.3 1.3 pad.73
  76.2 2.2 %fusion.10 = (f32[15,8,864]{2,1,0:T(8,128)}, f32[15,8,864]{2,1,0:T(8,128)}, f32[15,8,864]{2,1,0:T(8,128)}) fusion(f32[16,8,864]{2,1,0:T(8,128)S(1)} %pad.77, f32[16,8,864]{2,1,0:T(8,128)S(1)} %pad.76, f32[32,8,864]{2,1,0:T(8,128)} %copy-done.2, f32[32,8,864]{2,1,0:T(8,128)S(1)} %fusion.7), kind=kLoop, calls=%fused_computation.26 | loop fusion | flops 311040 | bytes 3732480 | tf_op jit(solution)/shard_map/add | solution.py:99
  80.7 1.3 fusion.9
  82.1 5.8 %pad.78 = f32[32,8,864]{2,1,0:T(8,128)} pad(f32[16,8,864]{2,1,0:T(8,128)S(1)} %get-tuple-element.76, f32[]{:T(128)} %constant.163.clone.1), padding=0_1_1x0_0_0x0_0_0 | pad | bytes 1327108 | tf_op jit(solution)/shard_map/pad | solution.py:335
  87.9 5.9 %pad.79 = f32[32,8,864]{2,1,0:T(8,128)} pad(f32[16,8,864]{2,1,0:T(8,128)S(1)} %copy-done.6, f32[]{:T(128)} %constant.163.clone.1), padding=1_0_1x0_0_0x0_0_0 | pad | bytes 1327108 | tf_op jit(solution)/shard_map/pad | solution.py:335
  94.1 1.0 copy-done
  95.5 1.6 fusion.3
  97.2 1.1 collective-permute-done.5
  99.4 2.9 %collective-permute-start.7 = (f32[256,5]{0,1:T(8,128)S(1)}, f32[256,5]{0,1:T(8,128)S(1)}, u32[]{:S(2)}, u32[]{:S(2)}) collective-permute-start(f32[256,5]{0,1:T(8,128)S(1)} %add.425), channel_id=1, source_target_pairs={{4,0},{5,1},{6,2},{7,3},{0,4},{1,5},{2,6},{3,7},{12,8},{13,9},{14,... | collective-permute-start | bytes 15368 | tf_op jit(solution)/shard_map/ppermute | solution.py:179
  104.0 1.9 %collective-permute-done.6 = f32[256,5]{0,1:T(8,128)S(1)} collective-permute-done((f32[256,5]{0,1:T(8,128)S(1)}, f32[256,5]{0,1:T(8,128)S(1)}, u32[]{:S(2)}, u32[]{:S(2)}) %collective-permute-start.6) | collective-permute-done | bytes 5152 | tf_op jit(solution)/shard_map/ppermute | solution.py:179
  106.0 4.6 %collective-permute-start.9 = (f32[256,5]{0,1:T(8,128)S(1)}, f32[256,5]{0,1:T(8,128)S(1)}, u32[]{:S(2)}, u32[]{:S(2)}) collective-permute-start(f32[256,5]{0,1:T(8,128)S(1)} %add_bitcast_fusion), channel_id=1, source_target_pairs={{0,8},{1,9},{2,10},{3,11},{4,12},{5,13},{6,14},{7,15},{8,0},{9,1},... | collective-permute-start | bytes 15368 | tf_op jit(solution)/shard_map/ppermute | solution.py:170
  111.1 2.5 %collective-permute-done.9 = f32[256,5]{0,1:T(8,128)S(1)} collective-permute-done((f32[256,5]{0,1:T(8,128)S(1)}, f32[256,5]{0,1:T(8,128)S(1)}, u32[]{:S(2)}, u32[]{:S(2)}) %collective-permute-start.9) | collective-permute-done | bytes 5152 | tf_op jit(solution)/shard_map/ppermute | solution.py:170
  115.1 1.7 %abs_reduce_fusion = (f32[864]{0:T(1024)S(1)}, f32[32,8,864]{2,1,0:T(8,128)S(1)}) fusion(f32[32,8,864]{2,1,0:T(8,128)S(1)} %reverse_select_fusion, f32[32,8,5]{2,1,0:T(8,128)S(1)} %copy.105, f32[5,13824]{1,0:T(8,128)} %constant.177.clone, s32[]{:T(128)S(6)} %select_n.138), kind=kOutput, calls=%fused_computation.12 | convolution fusion | flops 13933728 | bytes 1806724 | tf_op jit(solution)/shard_map/dot_general | solution.py:355
  119.6 2.9 %collective-permute-start.12 = (f32[26]{0:T(128)S(1)}, f32[26]{0:T(128)S(1)}, u32[]{:S(2)}, u32[]{:S(2)}) collective-permute-start(f32[26]{0:T(128)S(1)} %fusion.74), channel_id=1, source_target_pairs={{4,0},{5,1},{6,2},{7,3},{0,4},{1,5},{2,6},{3,7},{12,8},{13,9},{14,... | collective-permute-start | bytes 320 | tf_op jit(solution)/shard_map/ppermute | solution.py:179
  123.0 1.1 collective-permute-done.12
  124.1 2.0 %collective-permute-done.11 = f32[26]{0:T(128)S(1)} collective-permute-done((f32[26]{0:T(128)S(1)}, f32[26]{0:T(128)S(1)}, u32[]{:S(2)}, u32[]{:S(2)}) %collective-permute-start.11) | collective-permute-done | bytes 136 | tf_op jit(solution)/shard_map/ppermute | solution.py:179
  126.1 5.5 %collective-permute-start.14 = (f32[26]{0:T(128)S(1)}, f32[26]{0:T(128)S(1)}, u32[]{:S(2)}, u32[]{:S(2)}) collective-permute-start(f32[26]{0:T(128)S(1)} %fusion.48), channel_id=1, source_target_pairs={{0,8},{1,9},{2,10},{3,11},{4,12},{5,13},{6,14},{7,15},{8,0},{9,1},... | collective-permute-start | bytes 320 | tf_op jit(solution)/shard_map/ppermute | solution.py:170
  131.6 1.0 pad_maximum_fusion
  132.6 3.6 %all-to-all-start.1 = ((f32[32,8,869]{2,1,0:T(8,128)}), f32[32,8,869]{2,1,0:T(8,128)S(1)}, u32[]{:S(2)}, u32[]{:S(2)}) async-start(f32[32,8,869]{2,1,0:T(8,128)} %pad_maximum_fusion), calls=%async_computation.1 | async-start | bytes 1835008 | tf_op jit(solution)/shard_map/all_to_all | solution.py:363
  136.3 1.9 %collective-permute-start.17 = (f32[26]{0:T(128)S(1)}, f32[26]{0:T(128)S(1)}, u32[]{:S(2)}, u32[]{:S(2)}) collective-permute-start(f32[26]{0:T(128)S(1)} %fusion.73), channel_id=1, source_target_pairs={{48,0},{0,16},{16,32},{32,48},{112,64},{64,80},{80,96},{96,112},{1... | collective-permute-start | bytes 320 | tf_op jit(solution)/shard_map/ppermute | solution.py:179
  138.2 2.7 %collective-permute-start.16 = (f32[26]{0:T(128)S(1)}, f32[26]{0:T(128)S(1)}, u32[]{:S(2)}, u32[]{:S(2)}) collective-permute-start(f32[26]{0:T(128)S(1)} %fusion.73), channel_id=1, source_target_pairs={{32,0},{48,16},{0,32},{16,48},{96,64},{112,80},{64,96},{80,112},{1... | collective-permute-start | bytes 320 | tf_op jit(solution)/shard_map/ppermute | solution.py:179
  140.9 1.5 collective-permute-start.15
  142.3 1.6 collective-permute-done.17
  144.3 2.4 %collective-permute-done.15 = f32[26]{0:T(128)S(1)} collective-permute-done((f32[26]{0:T(128)S(1)}, f32[26]{0:T(128)S(1)}, u32[]{:S(2)}, u32[]{:S(2)}) %collective-permute-start.15) | collective-permute-done | bytes 136 | tf_op jit(solution)/shard_map/ppermute | solution.py:179
  146.7 2.1 %collective-permute-start.20 = (f32[26]{0:T(128)S(1)}, f32[26]{0:T(128)S(1)}, u32[]{:S(2)}, u32[]{:S(2)}) collective-permute-start(f32[26]{0:T(128)S(1)} %fusion.72), channel_id=1, source_target_pairs={{192,0},{208,16},{224,32},{240,48},{0,64},{16,80},{32,96},{48,112}... | collective-permute-start | bytes 320 | tf_op jit(solution)/shard_map/ppermute | solution.py:179
  148.8 3.2 %collective-permute-start.19 = (f32[26]{0:T(128)S(1)}, f32[26]{0:T(128)S(1)}, u32[]{:S(2)}, u32[]{:S(2)}) collective-permute-start(f32[26]{0:T(128)S(1)} %fusion.72), channel_id=1, source_target_pairs={{128,0},{144,16},{160,32},{176,48},{192,64},{208,80},{224,96},{240... | collective-permute-start | bytes 320 | tf_op jit(solution)/shard_map/ppermute | solution.py:179
  152.1 1.7 %collective-permute-done.19 = f32[26]{0:T(128)S(1)} collective-permute-done((f32[26]{0:T(128)S(1)}, f32[26]{0:T(128)S(1)}, u32[]{:S(2)}, u32[]{:S(2)}) %collective-permute-start.19) | collective-permute-done | bytes 136 | tf_op jit(solution)/shard_map/ppermute | solution.py:179
  153.9 1.6 %collective-permute-done.18 = f32[26]{0:T(128)S(1)} collective-permute-done((f32[26]{0:T(128)S(1)}, f32[26]{0:T(128)S(1)}, u32[]{:S(2)}, u32[]{:S(2)}) %collective-permute-start.18) | collective-permute-done | bytes 136 | tf_op jit(solution)/shard_map/ppermute | solution.py:179
  157.0 1.3 multiply_bitcast_fusion.1
  158.5 1.3 add_bitcast_fusion.2
  161.1 1.1 multiply_add_fusion
  (209 shorter events, 33.0 us)
Async XLA Ops:
  1.3 0.8 copy-start.21
  2.1 0.8 copy-start.22
  2.8 0.8 copy-start.23
  7.4 24.7 %all-to-all-start = ((f32[2,128,940]{2,0,1:T(2,128)}), f32[2,128,940]{2,0,1:T(2,128)S(1)}, u32[]{:S(2)}, u32[]{:S(2)}) async-start(f32[2,128,940]{2,0,1:T(2,128)} %copy.91), calls=%async_computation | async-start | bytes 2097152 | tf_op jit(solution)/shard_map/all_to_all | solution.py:320
  34.2 1.2 collective-permute-start
  35.4 5.6 %collective-permute-start.3 = (f32[256,5]{0,1:T(8,128)S(1)}, f32[256,5]{0,1:T(8,128)S(1)}, u32[]{:S(2)}, u32[]{:S(2)}) collective-permute-start(f32[256,5]{0,1:T(8,128)S(1)} %add.377), channel_id=1, source_target_pairs={{6,0},{7,1},{0,2},{1,3},{2,4},{3,5},{4,6},{5,7},{14,8},{15,9},{8,1... | collective-permute-start | bytes 15368 | tf_op jit(solution)/shard_map/ppermute | solution.py:179
  37.4 4.5 %collective-permute-start.2 = (f32[256,5]{0,1:T(8,128)S(1)}, f32[256,5]{0,1:T(8,128)S(1)}, u32[]{:S(2)}, u32[]{:S(2)}) collective-permute-start(f32[256,5]{0,1:T(8,128)S(1)} %add.377), channel_id=1, source_target_pairs={{4,0},{5,1},{6,2},{7,3},{0,4},{1,5},{2,6},{3,7},{12,8},{13,9},{14,... | collective-permute-start | bytes 15368 | tf_op jit(solution)/shard_map/ppermute | solution.py:179
  38.7 3.7 %collective-permute-start.1 = (f32[256,5]{0,1:T(8,128)S(1)}, f32[256,5]{0,1:T(8,128)S(1)}, u32[]{:S(2)}, u32[]{:S(2)}) collective-permute-start(f32[256,5]{0,1:T(8,128)S(1)} %add.377), channel_id=1, source_target_pairs={{2,0},{3,1},{4,2},{5,3},{6,4},{7,5},{0,6},{1,7},{10,8},{11,9},{12,... | collective-permute-start | bytes 15368 | tf_op jit(solution)/shard_map/ppermute | solution.py:179
  42.4 6.5 %copy-start.25 = (f32[864]{0:T(1024)S(1)}, f32[864]{0:T(1024)}, u32[]{:S(2)}) copy-start(f32[864]{0:T(1024)} %constant.239) | copy-start | bytes 10372
  42.4 8.1 %collective-permute-start.4 = (f32[256,5]{0,1:T(8,128)S(1)}, f32[256,5]{0,1:T(8,128)S(1)}, u32[]{:S(2)}, u32[]{:S(2)}) collective-permute-start(f32[256,5]{0,1:T(8,128)S(1)} %add_bitcast_fusion.1), channel_id=1, source_target_pairs={{0,8},{1,9},{2,10},{3,11},{4,12},{5,13},{6,14},{7,15},{8,0},{9,1},... | collective-permute-start | bytes 15368 | tf_op jit(solution)/shard_map/ppermute | solution.py:170
  52.4 1.0 copy-start.2
  53.5 0.8 copy-start.3
  54.3 0.8 copy-start.9
  57.8 1.0 copy-start.12
  58.9 0.7 copy-start.19
  64.9 1.9 %copy-start.4 = (f32[8,8,864]{2,1,0:T(8,128)S(1)}, f32[8,8,864]{2,1,0:T(8,128)}, u32[]{:S(2)}) copy-start(f32[8,8,864]{2,1,0:T(8,128)} %pad.84) | copy-start | bytes 663556
  65.0 1.9 %copy-start.5 = (f32[8,8,864]{2,1,0:T(8,128)S(1)}, f32[8,8,864]{2,1,0:T(8,128)}, u32[]{:S(2)}) copy-start(f32[8,8,864]{2,1,0:T(8,128)} %pad.85) | copy-start | bytes 663556
  71.6 1.0 copy-start.13
  72.6 0.7 copy-start.20
  73.4 0.9 copy-start.15
  74.4 0.7 copy-start.18
  75.1 0.9 copy-start.11
  78.4 1.0 copy-start.14
  78.4 1.0 copy-start.17
  79.4 0.9 copy-start.10
  80.7 1.3 copy-start.7
  80.7 1.3 copy-start.16
  82.1 5.8 %copy-start.6 = (f32[16,8,864]{2,1,0:T(8,128)S(1)}, f32[16,8,864]{2,1,0:T(8,128)}, u32[]{:S(2)}) copy-start(f32[16,8,864]{2,1,0:T(8,128)} %add.408) | copy-start | bytes 1327108
  93.9 1.2 copy-start
  93.9 1.4 copy-start.1
  94.0 1.4 copy-start.29
  97.1 1.2 collective-permute-start.5
  98.4 4.9 %collective-permute-start.8 = (f32[256,5]{0,1:T(8,128)S(1)}, f32[256,5]{0,1:T(8,128)S(1)}, u32[]{:S(2)}, u32[]{:S(2)}) collective-permute-start(f32[256,5]{0,1:T(8,128)S(1)} %add.425), channel_id=1, source_target_pairs={{6,0},{7,1},{0,2},{1,3},{2,4},{3,5},{4,6},{5,7},{14,8},{15,9},{8,1... | collective-permute-start | bytes 15368 | tf_op jit(solution)/shard_map/ppermute | solution.py:179
  99.4 4.6 %collective-permute-start.7 = (f32[256,5]{0,1:T(8,128)S(1)}, f32[256,5]{0,1:T(8,128)S(1)}, u32[]{:S(2)}, u32[]{:S(2)}) collective-permute-start(f32[256,5]{0,1:T(8,128)S(1)} %add.425), channel_id=1, source_target_pairs={{4,0},{5,1},{6,2},{7,3},{0,4},{1,5},{2,6},{3,7},{12,8},{13,9},{14,... | collective-permute-start | bytes 15368 | tf_op jit(solution)/shard_map/ppermute | solution.py:179
  102.3 3.7 %collective-permute-start.6 = (f32[256,5]{0,1:T(8,128)S(1)}, f32[256,5]{0,1:T(8,128)S(1)}, u32[]{:S(2)}, u32[]{:S(2)}) collective-permute-start(f32[256,5]{0,1:T(8,128)S(1)} %add.425), channel_id=1, source_target_pairs={{2,0},{3,1},{4,2},{5,3},{6,4},{7,5},{0,6},{1,7},{10,8},{11,9},{12,... | collective-permute-start | bytes 15368 | tf_op jit(solution)/shard_map/ppermute | solution.py:179
  106.0 7.6 %collective-permute-start.9 = (f32[256,5]{0,1:T(8,128)S(1)}, f32[256,5]{0,1:T(8,128)S(1)}, u32[]{:S(2)}, u32[]{:S(2)}) collective-permute-start(f32[256,5]{0,1:T(8,128)S(1)} %add_bitcast_fusion), channel_id=1, source_target_pairs={{0,8},{1,9},{2,10},{3,11},{4,12},{5,13},{6,14},{7,15},{8,0},{9,1},... | collective-permute-start | bytes 15368 | tf_op jit(solution)/shard_map/ppermute | solution.py:170
  117.9 1.1 collective-permute-start.10
  119.2 3.9 %collective-permute-start.13 = (f32[26]{0:T(128)S(1)}, f32[26]{0:T(128)S(1)}, u32[]{:S(2)}, u32[]{:S(2)}) collective-permute-start(f32[26]{0:T(128)S(1)} %fusion.74), channel_id=1, source_target_pairs={{6,0},{7,1},{0,2},{1,3},{2,4},{3,5},{4,6},{5,7},{14,8},{15,9},{8,1... | collective-permute-start | bytes 320 | tf_op jit(solution)/shard_map/ppermute | solution.py:179
  119.6 4.4 %collective-permute-start.12 = (f32[26]{0:T(128)S(1)}, f32[26]{0:T(128)S(1)}, u32[]{:S(2)}, u32[]{:S(2)}) collective-permute-start(f32[26]{0:T(128)S(1)} %fusion.74), channel_id=1, source_target_pairs={{4,0},{5,1},{6,2},{7,3},{0,4},{1,5},{2,6},{3,7},{12,8},{13,9},{14,... | collective-permute-start | bytes 320 | tf_op jit(solution)/shard_map/ppermute | solution.py:179
  122.5 3.5 %collective-permute-start.11 = (f32[26]{0:T(128)S(1)}, f32[26]{0:T(128)S(1)}, u32[]{:S(2)}, u32[]{:S(2)}) collective-permute-start(f32[26]{0:T(128)S(1)} %fusion.74), channel_id=1, source_target_pairs={{2,0},{3,1},{4,2},{5,3},{6,4},{7,5},{0,6},{1,7},{10,8},{11,9},{12,... | collective-permute-start | bytes 320 | tf_op jit(solution)/shard_map/ppermute | solution.py:179
  126.1 10.2 %collective-permute-start.14 = (f32[26]{0:T(128)S(1)}, f32[26]{0:T(128)S(1)}, u32[]{:S(2)}, u32[]{:S(2)}) collective-permute-start(f32[26]{0:T(128)S(1)} %fusion.48), channel_id=1, source_target_pairs={{0,8},{1,9},{2,10},{3,11},{4,12},{5,13},{6,14},{7,15},{8,0},{9,1},... | collective-permute-start | bytes 320 | tf_op jit(solution)/shard_map/ppermute | solution.py:170
  132.6 27.3 %all-to-all-start.1 = ((f32[32,8,869]{2,1,0:T(8,128)}), f32[32,8,869]{2,1,0:T(8,128)S(1)}, u32[]{:S(2)}, u32[]{:S(2)}) async-start(f32[32,8,869]{2,1,0:T(8,128)} %pad_maximum_fusion), calls=%async_computation.1 | async-start | bytes 1835008 | tf_op jit(solution)/shard_map/all_to_all | solution.py:363
  136.3 7.6 %collective-permute-start.17 = (f32[26]{0:T(128)S(1)}, f32[26]{0:T(128)S(1)}, u32[]{:S(2)}, u32[]{:S(2)}) collective-permute-start(f32[26]{0:T(128)S(1)} %fusion.73), channel_id=1, source_target_pairs={{48,0},{0,16},{16,32},{32,48},{112,64},{64,80},{80,96},{96,112},{1... | collective-permute-start | bytes 320 | tf_op jit(solution)/shard_map/ppermute | solution.py:179
  138.2 6.1 %collective-permute-start.16 = (f32[26]{0:T(128)S(1)}, f32[26]{0:T(128)S(1)}, u32[]{:S(2)}, u32[]{:S(2)}) collective-permute-start(f32[26]{0:T(128)S(1)} %fusion.73), channel_id=1, source_target_pairs={{32,0},{48,16},{0,32},{16,48},{96,64},{112,80},{64,96},{80,112},{1... | collective-permute-start | bytes 320 | tf_op jit(solution)/shard_map/ppermute | solution.py:179
  140.9 5.8 %collective-permute-start.15 = (f32[26]{0:T(128)S(1)}, f32[26]{0:T(128)S(1)}, u32[]{:S(2)}, u32[]{:S(2)}) collective-permute-start(f32[26]{0:T(128)S(1)} %fusion.73), channel_id=1, source_target_pairs={{16,0},{32,16},{48,32},{0,48},{80,64},{96,80},{112,96},{64,112},{1... | collective-permute-start | bytes 320 | tf_op jit(solution)/shard_map/ppermute | solution.py:179
  146.7 5.4 %collective-permute-start.20 = (f32[26]{0:T(128)S(1)}, f32[26]{0:T(128)S(1)}, u32[]{:S(2)}, u32[]{:S(2)}) collective-permute-start(f32[26]{0:T(128)S(1)} %fusion.72), channel_id=1, source_target_pairs={{192,0},{208,16},{224,32},{240,48},{0,64},{16,80},{32,96},{48,112}... | collective-permute-start | bytes 320 | tf_op jit(solution)/shard_map/ppermute | solution.py:179
  148.8 5.0 %collective-permute-start.19 = (f32[26]{0:T(128)S(1)}, f32[26]{0:T(128)S(1)}, u32[]{:S(2)}, u32[]{:S(2)}) collective-permute-start(f32[26]{0:T(128)S(1)} %fusion.72), channel_id=1, source_target_pairs={{128,0},{144,16},{160,32},{176,48},{192,64},{208,80},{224,96},{240... | collective-permute-start | bytes 320 | tf_op jit(solution)/shard_map/ppermute | solution.py:179
  152.0 3.5 %collective-permute-start.18 = (f32[26]{0:T(128)S(1)}, f32[26]{0:T(128)S(1)}, u32[]{:S(2)}, u32[]{:S(2)}) collective-permute-start(f32[26]{0:T(128)S(1)} %fusion.72), channel_id=1, source_target_pairs={{64,0},{80,16},{96,32},{112,48},{128,64},{144,80},{160,96},{176,11... | collective-permute-start | bytes 320 | tf_op jit(solution)/shard_map/ppermute | solution.py:179
  (5 other events, 3.4 us)

commit v11 on v10

--- a/solution.py
+++ b/solution.py
@@ -4,6 +4,7 @@
 import jax.numpy as jnp
 import numpy as np
 from jax import lax
+from jax.experimental import pallas as pl
 from jax.sharding import PartitionSpec as P
 
 NXI = 24
@@ -289,6 +290,34 @@
     )
 
 
+def sweep_kernel(rate_ref, drive_ref, sign_ref, out_ref):
+    positions = rate_ref.shape[0]
+    start = jnp.zeros(rate_ref.shape[1:], jnp.float32)
+
+    def forward(p, carried):
+        value = rate_ref[p] * carried + drive_ref[p]
+        out_ref[p] = value
+        return value
+
+    lax.fori_loop(0, positions, forward, start)
+    heading = sign_ref[...] > 0
+
+    def backward(i, carried):
+        p = positions - 1 - i
+        value = rate_ref[p] * carried + drive_ref[p]
+        out_ref[p] = jnp.where(heading, out_ref[p], value)
+        return value
+
+    lax.fori_loop(0, positions, backward, start)
+
+
+def line_sweep(carry_rate, drive_term, node_signed):
+    return pl.pallas_call(
+        sweep_kernel,
+        out_shape=jax.ShapeDtypeStruct(drive_term.shape, jnp.float32),
+    )(carry_rate, drive_term, node_signed.reshape(1, -1))
+
+
 def line_block(matrices, vector):
     shaped = matrices.reshape(matrices.shape[:-1] + (5, 5))
     return jnp.sum(shaped * vector[..., None, :], axis=-1)
@@ -332,11 +361,8 @@
     denominator = node_speed * total_length + thickness + pseudo_rate
     carry_rate = node_speed * total_length / denominator
     drive_term = (thickness * target + pseudo_rate * dist_t) / denominator
-    _, forward = lax.associative_scan(affine_combine, (carry_rate, drive_term), axis=0)
-    _, backward = lax.associative_scan(
-        affine_combine, (carry_rate, drive_term), reverse=True, axis=0
-    )
-    half_field = jnp.where(node_signed > 0, forward, backward)
+    carry_rate = jnp.broadcast_to(carry_rate, drive_term.shape)
+    half_field = line_sweep(carry_rate, drive_term, node_signed)
     half_moments = tree_sum(
         jnp.dot(half_field.reshape(cells, node_count), weighted.T, precision=HIGH), ("vel",)
     )

time: 164 us -> 125 us (0.76)
  local copies, waits for them, and re-layouts: 41.6 us -> 12.3 us
  other arithmetic: 19.7 us -> 7.38 us
  Pallas kernels: 0 us -> 2.94 us
    pad x16 -> x0, local copies, waits for them, and re-layouts: 21.9 us -> none  [the longest x8 14 us: body(): lax.associative_scan(affine_combine, (carry_rate, drive_term), axis=0)]
    add x17 -> x0, other arithmetic: 11.2 us -> none  [the longest x8 7.46 us: affine_combine(): later_map[0] * earlier_map[1] + later_map[1]]
    unnamed x62 -> x20, local copies, waits for them, and re-layouts: 9.95 us -> 5.78 us
    slice x5 -> x0, local copies, waits for them, and re-layouts: 3.18 us -> none  [the longest x3 1.87 us: body(): lax.associative_scan(affine_combine, (carry_rate, drive_term), axis=0)]
    pallas_call x0 -> x1, Pallas kernels: none -> 2.94 us  [line_sweep(): pl.pallas_call(sweep_kernel, out_shape=jax.ShapeDtypeStruct(drive_term.sh...]
  transfers between devices with their start and end apart: 23 -> 23, of which waited for: 17 -> 17; matrix products, arithmetic and copies ran while one was open for 4% -> 6% of each run, Pallas kernels for 0% -> 0%
where the time goes in v11:
time: 125 us; the launch traced here: 124 us
  starting transfers between devices  53 us (42%)
  waiting for transfers between devices  38.6 us (31%)
  local copies, waits for them, and re-layouts  12.3 us (10%)
  matrix products  8.41 us (7%)
  other arithmetic  7.38 us (6%)
  Pallas kernels  2.94 us (2%)
    ppermute x15, starting transfers between devices, group_sum(): shifted.append(lax.ppermute(block, axis, pairs))  25.5 us
    all_to_all x1, waiting for transfers between devices, body(): lines = lax.all_to_all(packed, 'sec', 1, 0, tiled=True)  17.7 us
    ppermute x6, starting transfers between devices, group_sum(): return block + lax.ppermute(block, axis, pairs)  16.8 us
    ppermute x15, waiting for transfers between devices, group_sum(): shifted.append(lax.ppermute(block, axis, pairs))  14.7 us
    all_to_all x1, starting transfers between devices, body(): lines = lax.all_to_all(packed, 'sec', 1, 0, tiled=True)  7.03 us
    ppermute x6, waiting for transfers between devices, group_sum(): return block + lax.ppermute(block, axis, pairs)  6.26 us
    unnamed x20, local copies, waits for them, and re-layouts  5.78 us
    all_to_all x1, starting transfers between devices, body(): back = lax.all_to_all(back, 'sec', 0, 1, tiled=True)  3.63 us
  transfers between devices with their start and end apart: 23, of which 17 were waited for; matrix products, arithmetic and copies ran while one was open for 6% of the time, Pallas kernels for 0%

profile of v11, /device:TPU:32, one launch (start us, length us, event | category | flops | bytes accessed | tf_op | source)
XLA Modules:
  0.0 123.8 jit_solution(4254410957117862556)
XLA Ops:
  0.6 0.7 copy-done.8
  2.2 0.6 copy-done.2
  3.7 1.5 %copy.86 = f32[864,256]{0,1:T(8,128)S(1)} copy(f32[864,256]{1,0:T(8,128)} %param.10) | data formatting | bytes 1769472 | tf_op args[0]
  5.6 1.8 %copy.91 = f32[2,128,940]{2,0,1:T(2,128)} copy(f32[2,128,940]{2,1,0:T(8,128)S(1)} %bitcast.157) | data formatting | bytes 1925120 | tf_op jit(solution)/shard_map/transpose | solution.py:348
  7.4 7.0 %all-to-all-start = ((f32[2,128,940]{2,0,1:T(2,128)}), f32[2,128,940]{2,0,1:T(2,128)S(1)}, u32[]{:S(2)}, u32[]{:S(2)}) async-start(f32[2,128,940]{2,0,1:T(2,128)} %copy.91), calls=%async_computation | async-start | bytes 2097152 | tf_op jit(solution)/shard_map/all_to_all | solution.py:349
  14.5 17.7 %all-to-all-done = f32[2,128,940]{2,0,1:T(2,128)S(1)} async-done(((f32[2,128,940]{2,0,1:T(2,128)}), f32[2,128,940]{2,0,1:T(2,128)S(1)}, u32[]{:S(2)}, u32[]{:S(2)}) %all-to-all-start) | async-done | bytes 962592 | tf_op jit(solution)/shard_map/all_to_all | solution.py:349
  32.6 1.6 %fusion.5 = f32[256,5]{0,1:T(8,128)S(1)} fusion(f32[32,8,940]{2,1,0:T(8,128)S(1)} %bitcast.151, f32[5,13824]{1,0:T(8,128)} %constant.175.clone, s32[]{:T(128)S(6)} %select_n.134), kind=kOutput, calls=%fused_computation.9 | convolution fusion | flops 13271040 | bytes 951300 | tf_op jit(solution)/shard_map/dot_general | solution.py:357
  34.2 1.2 collective-permute-done
  35.4 1.9 %collective-permute-start.3 = (f32[256,5]{0,1:T(8,128)S(1)}, f32[256,5]{0,1:T(8,128)S(1)}, u32[]{:S(2)}, u32[]{:S(2)}) collective-permute-start(f32[256,5]{0,1:T(8,128)S(1)} %add.260), channel_id=1, source_target_pairs={{6,0},{7,1},{0,2},{1,3},{2,4},{3,5},{4,6},{5,7},{14,8},{15,9},{8,1... | collective-permute-start | bytes 15368 | tf_op jit(solution)/shard_map/ppermute | solution.py:180
  37.3 1.4 %collective-permute-start.2 = (f32[256,5]{0,1:T(8,128)S(1)}, f32[256,5]{0,1:T(8,128)S(1)}, u32[]{:S(2)}, u32[]{:S(2)}) collective-permute-start(f32[256,5]{0,1:T(8,128)S(1)} %add.260), channel_id=1, source_target_pairs={{4,0},{5,1},{6,2},{7,3},{0,4},{1,5},{2,6},{3,7},{12,8},{13,9},{14,... | collective-permute-start | bytes 15368 | tf_op jit(solution)/shard_map/ppermute | solution.py:180
  38.7 2.0 %collective-permute-start.1 = (f32[256,5]{0,1:T(8,128)S(1)}, f32[256,5]{0,1:T(8,128)S(1)}, u32[]{:S(2)}, u32[]{:S(2)}) collective-permute-start(f32[256,5]{0,1:T(8,128)S(1)} %add.260), channel_id=1, source_target_pairs={{2,0},{3,1},{4,2},{5,3},{6,4},{7,5},{0,6},{1,7},{10,8},{11,9},{12,... | collective-permute-start | bytes 15368 | tf_op jit(solution)/shard_map/ppermute | solution.py:180
  41.1 0.8 collective-permute-done.2
  42.4 6.5 %collective-permute-start.4 = (f32[256,5]{0,1:T(8,128)S(1)}, f32[256,5]{0,1:T(8,128)S(1)}, u32[]{:S(2)}, u32[]{:S(2)}) collective-permute-start(f32[256,5]{0,1:T(8,128)S(1)} %add_bitcast_fusion.1), channel_id=1, source_target_pairs={{0,8},{1,9},{2,10},{3,11},{4,12},{5,13},{6,14},{7,15},{8,0},{9,1},... | collective-permute-start | bytes 15368 | tf_op jit(solution)/shard_map/ppermute | solution.py:171
  48.8 1.1 fusion.7.rate_ref
  50.5 2.9 %fusion.2.drive_ref = f32[32,8,864]{2,1,0:T(8,128)} fusion(f32[256,5]{0,1:T(8,128)S(1)} %fusion.56, f32[32,8,940]{2,1,0:T(8,128)S(1)} %bitcast.153, f32[32,8]{1,0:T(8,128)S(1)} %bitcast.180, f32[864]{0:T(1024)S(1)} %copy-done.5, f32[5,13824]{1,0:T(8,128)} %constant.176.clone, s32[]{:T(128)S(6)} %select_n.134), kind=kOutput, calls=%fused_computation.4 | convolution fusion | flops 14376960 | bytes 1807748 | tf_op jit(solution)/shard_map/dot_general | solution.py:359
  53.4 2.9 %shard_map.113 = f32[32,8,864]{2,1,0:T(8,128)} custom-call(f32[32,8,864]{2,1,0:T(8,128)} %fusion.7.rate_ref, f32[32,8,864]{2,1,0:T(8,128)} %fusion.2.drive_ref, f32[1,864]{1,0:T(1,128)} %constant.198.sign_ref), custom_call_target="tpu_custom_call" | custom-call | tf_op jit(solution)/shard_map/pallas_call | solution.py:315
  56.3 2.0 %fusion.3 = f32[256,5]{0,1:T(8,128)S(1)} fusion(f32[32,8,864]{2,1,0:T(8,128)} %shard_map.113, f32[5,13824]{1,0:T(8,128)} %constant.175.clone, s32[]{:T(128)S(6)} %select_n.134), kind=kOutput, calls=%fused_computation.7 | convolution fusion | flops 13271040 | bytes 951300 | tf_op jit(solution)/shard_map/dot_general | solution.py:367
  58.4 1.1 collective-permute-done.5
  59.5 1.0 collective-permute-start.8
  60.6 2.9 %collective-permute-start.7 = (f32[256,5]{0,1:T(8,128)S(1)}, f32[256,5]{0,1:T(8,128)S(1)}, u32[]{:S(2)}, u32[]{:S(2)}) collective-permute-start(f32[256,5]{0,1:T(8,128)S(1)} %add.276), channel_id=1, source_target_pairs={{4,0},{5,1},{6,2},{7,3},{0,4},{1,5},{2,6},{3,7},{12,8},{13,9},{14,... | collective-permute-start | bytes 15368 | tf_op jit(solution)/shard_map/ppermute | solution.py:180
  63.5 1.0 collective-permute-start.6
  64.5 0.7 collective-permute-done.7
  65.2 1.9 %collective-permute-done.6 = f32[256,5]{0,1:T(8,128)S(1)} collective-permute-done((f32[256,5]{0,1:T(8,128)S(1)}, f32[256,5]{0,1:T(8,128)S(1)}, u32[]{:S(2)}, u32[]{:S(2)}) %collective-permute-start.6) | collective-permute-done | bytes 5152 | tf_op jit(solution)/shard_map/ppermute | solution.py:180
  67.1 4.8 %collective-permute-start.9 = (f32[256,5]{0,1:T(8,128)S(1)}, f32[256,5]{0,1:T(8,128)S(1)}, u32[]{:S(2)}, u32[]{:S(2)}) collective-permute-start(f32[256,5]{0,1:T(8,128)S(1)} %add_bitcast_fusion), channel_id=1, source_target_pairs={{0,8},{1,9},{2,10},{3,11},{4,12},{5,13},{6,14},{7,15},{8,0},{9,1},... | collective-permute-start | bytes 15368 | tf_op jit(solution)/shard_map/ppermute | solution.py:171
  72.5 2.5 %collective-permute-done.9 = f32[256,5]{0,1:T(8,128)S(1)} collective-permute-done((f32[256,5]{0,1:T(8,128)S(1)}, f32[256,5]{0,1:T(8,128)S(1)}, u32[]{:S(2)}, u32[]{:S(2)}) %collective-permute-start.9) | collective-permute-done | bytes 5152 | tf_op jit(solution)/shard_map/ppermute | solution.py:171
  76.8 1.7 %abs_reduce_fusion = (f32[864]{0:T(1024)S(1)}, f32[32,8,864]{2,1,0:T(8,128)S(1)}) fusion(f32[32,8,864]{2,1,0:T(8,128)S(1)} %copy-done, f32[32,8,5]{2,1,0:T(8,128)S(1)} %copy.105, f32[5,13824]{1,0:T(8,128)} %constant.176.clone, s32[]{:T(128)S(6)} %select_n.134), kind=kOutput, calls=%fused_computation.12 | convolution fusion | flops 13933728 | bytes 1806724 | tf_op jit(solution)/shard_map/dot_general | solution.py:381
  78.5 0.8 dynamic-slice_multiply_fusion
  79.8 1.0 collective-permute-done.10
  81.3 2.9 %collective-permute-start.12 = (f32[26]{0:T(128)S(1)}, f32[26]{0:T(128)S(1)}, u32[]{:S(2)}, u32[]{:S(2)}) collective-permute-start(f32[26]{0:T(128)S(1)} %fusion.55), channel_id=1, source_target_pairs={{4,0},{5,1},{6,2},{7,3},{0,4},{1,5},{2,6},{3,7},{12,8},{13,9},{14,... | collective-permute-start | bytes 320 | tf_op jit(solution)/shard_map/ppermute | solution.py:180
  84.7 1.1 collective-permute-done.12
  85.8 2.0 %collective-permute-done.11 = f32[26]{0:T(128)S(1)} collective-permute-done((f32[26]{0:T(128)S(1)}, f32[26]{0:T(128)S(1)}, u32[]{:S(2)}, u32[]{:S(2)}) %collective-permute-start.11) | collective-permute-done | bytes 136 | tf_op jit(solution)/shard_map/ppermute | solution.py:180
  87.8 5.5 %collective-permute-start.14 = (f32[26]{0:T(128)S(1)}, f32[26]{0:T(128)S(1)}, u32[]{:S(2)}, u32[]{:S(2)}) collective-permute-start(f32[26]{0:T(128)S(1)} %fusion.34), channel_id=1, source_target_pairs={{0,8},{1,9},{2,10},{3,11},{4,12},{5,13},{6,14},{7,15},{8,0},{9,1},... | collective-permute-start | bytes 320 | tf_op jit(solution)/shard_map/ppermute | solution.py:171
  93.3 1.0 pad_maximum_fusion
  94.3 3.6 %all-to-all-start.1 = ((f32[32,8,869]{2,1,0:T(8,128)}), f32[32,8,869]{2,1,0:T(8,128)S(1)}, u32[]{:S(2)}, u32[]{:S(2)}) async-start(f32[32,8,869]{2,1,0:T(8,128)} %pad_maximum_fusion), calls=%async_computation.1 | async-start | bytes 1835008 | tf_op jit(solution)/shard_map/all_to_all | solution.py:389
  98.0 1.9 %collective-permute-start.17 = (f32[26]{0:T(128)S(1)}, f32[26]{0:T(128)S(1)}, u32[]{:S(2)}, u32[]{:S(2)}) collective-permute-start(f32[26]{0:T(128)S(1)} %fusion.54), channel_id=1, source_target_pairs={{48,0},{0,16},{16,32},{32,48},{112,64},{64,80},{80,96},{96,112},{1... | collective-permute-start | bytes 320 | tf_op jit(solution)/shard_map/ppermute | solution.py:180
  99.9 2.7 %collective-permute-start.16 = (f32[26]{0:T(128)S(1)}, f32[26]{0:T(128)S(1)}, u32[]{:S(2)}, u32[]{:S(2)}) collective-permute-start(f32[26]{0:T(128)S(1)} %fusion.54), channel_id=1, source_target_pairs={{32,0},{48,16},{0,32},{16,48},{96,64},{112,80},{64,96},{80,112},{1... | collective-permute-start | bytes 320 | tf_op jit(solution)/shard_map/ppermute | solution.py:180
  102.5 1.5 %collective-permute-start.15 = (f32[26]{0:T(128)S(1)}, f32[26]{0:T(128)S(1)}, u32[]{:S(2)}, u32[]{:S(2)}) collective-permute-start(f32[26]{0:T(128)S(1)} %fusion.54), channel_id=1, source_target_pairs={{16,0},{32,16},{48,32},{0,48},{80,64},{96,80},{112,96},{64,112},{1... | collective-permute-start | bytes 320 | tf_op jit(solution)/shard_map/ppermute | solution.py:180
  104.0 1.6 %collective-permute-done.17 = f32[26]{0:T(128)S(1)} collective-permute-done((f32[26]{0:T(128)S(1)}, f32[26]{0:T(128)S(1)}, u32[]{:S(2)}, u32[]{:S(2)}) %collective-permute-start.17) | collective-permute-done | bytes 136 | tf_op jit(solution)/shard_map/ppermute | solution.py:180
  106.0 2.4 %collective-permute-done.15 = f32[26]{0:T(128)S(1)} collective-permute-done((f32[26]{0:T(128)S(1)}, f32[26]{0:T(128)S(1)}, u32[]{:S(2)}, u32[]{:S(2)}) %collective-permute-start.15) | collective-permute-done | bytes 136 | tf_op jit(solution)/shard_map/ppermute | solution.py:180
  108.4 2.1 %collective-permute-start.20 = (f32[26]{0:T(128)S(1)}, f32[26]{0:T(128)S(1)}, u32[]{:S(2)}, u32[]{:S(2)}) collective-permute-start(f32[26]{0:T(128)S(1)} %fusion.53), channel_id=1, source_target_pairs={{192,0},{208,16},{224,32},{240,48},{0,64},{16,80},{32,96},{48,112}... | collective-permute-start | bytes 320 | tf_op jit(solution)/shard_map/ppermute | solution.py:180
  110.5 3.2 %collective-permute-start.19 = (f32[26]{0:T(128)S(1)}, f32[26]{0:T(128)S(1)}, u32[]{:S(2)}, u32[]{:S(2)}) collective-permute-start(f32[26]{0:T(128)S(1)} %fusion.53), channel_id=1, source_target_pairs={{128,0},{144,16},{160,32},{176,48},{192,64},{208,80},{224,96},{240... | collective-permute-start | bytes 320 | tf_op jit(solution)/shard_map/ppermute | solution.py:180
  113.8 1.7 %collective-permute-done.19 = f32[26]{0:T(128)S(1)} collective-permute-done((f32[26]{0:T(128)S(1)}, f32[26]{0:T(128)S(1)}, u32[]{:S(2)}, u32[]{:S(2)}) %collective-permute-start.19) | collective-permute-done | bytes 136 | tf_op jit(solution)/shard_map/ppermute | solution.py:180
  115.5 1.6 %collective-permute-done.18 = f32[26]{0:T(128)S(1)} collective-permute-done((f32[26]{0:T(128)S(1)}, f32[26]{0:T(128)S(1)}, u32[]{:S(2)}, u32[]{:S(2)}) %collective-permute-start.18) | collective-permute-done | bytes 136 | tf_op jit(solution)/shard_map/ppermute | solution.py:180
  118.0 0.7 copy-done.6
  118.7 1.3 %multiply_bitcast_fusion.1 = (f32[1,24]{1,0:T(1,128)S(1)}, f32[1,24]{1,0:T(1,128)S(1)}, f32[1,24]{1,0:T(1,128)S(1)}, f32[1,24]{1,0:T(1,128)S(1)}) fusion(f32[24]{0:T(128)S(1)} %copy-done.4, f32[1,26]{1,0:T(1,128)S(1)} %fusion.20, f32[1,24]{1,0:T(1,128)S(1)} %copy-done.6, f32[5,24]{1,0:T(8,128)S(1)} %fusion.14, f32[]{:T(128)} %bitcast.52, f32[]{:T(128)} %bitcast.53), kind=kLoop, calls=%fused_computation.88 | loop fusion | flops 480 | bytes 1160 | tf_op jit(solution)/shard_map/stack | solution.py:404
  120.2 1.3 %add_bitcast_fusion.2 = f32[24]{0:T(128)S(1)} fusion(f32[1,24]{1,0:T(1,128)S(1)} %copy-done.6, f32[1,24]{1,0:T(1,128)S(1)} %get-tuple-element.13, f32[1,24]{1,0:T(1,128)S(1)} %get-tuple-element.12, f32[5,24]{1,0:T(8,128)S(1)} %fusion.12, f32[]{:T(128)} %bitcast.53, f32[]{:T(128)} %bitcast.52), kind=kLoop, calls=%fused_computation.85 | loop fusion | flops 432 | bytes 872 | tf_op jit(solution)/shard_map/sub | solution.py:411
  121.8 0.7 copy.111
  122.7 1.1 multiply_add_fusion
  (111 shorter events, 9.9 us)
Async XLA Ops:
  0.6 0.7 copy-start.8
  1.3 0.8 copy-start.1
  2.1 0.8 copy-start.2
  2.8 0.8 copy-start.3
  7.4 24.7 %all-to-all-start = ((f32[2,128,940]{2,0,1:T(2,128)}), f32[2,128,940]{2,0,1:T(2,128)S(1)}, u32[]{:S(2)}, u32[]{:S(2)}) async-start(f32[2,128,940]{2,0,1:T(2,128)} %copy.91), calls=%async_computation | async-start | bytes 2097152 | tf_op jit(solution)/shard_map/all_to_all | solution.py:349
  34.2 1.2 collective-permute-start
  35.4 5.6 %collective-permute-start.3 = (f32[256,5]{0,1:T(8,128)S(1)}, f32[256,5]{0,1:T(8,128)S(1)}, u32[]{:S(2)}, u32[]{:S(2)}) collective-permute-start(f32[256,5]{0,1:T(8,128)S(1)} %add.260), channel_id=1, source_target_pairs={{6,0},{7,1},{0,2},{1,3},{2,4},{3,5},{4,6},{5,7},{14,8},{15,9},{8,1... | collective-permute-start | bytes 15368 | tf_op jit(solution)/shard_map/ppermute | solution.py:180
  37.3 4.5 %collective-permute-start.2 = (f32[256,5]{0,1:T(8,128)S(1)}, f32[256,5]{0,1:T(8,128)S(1)}, u32[]{:S(2)}, u32[]{:S(2)}) collective-permute-start(f32[256,5]{0,1:T(8,128)S(1)} %add.260), channel_id=1, source_target_pairs={{4,0},{5,1},{6,2},{7,3},{0,4},{1,5},{2,6},{3,7},{12,8},{13,9},{14,... | collective-permute-start | bytes 15368 | tf_op jit(solution)/shard_map/ppermute | solution.py:180
  38.7 3.7 %collective-permute-start.1 = (f32[256,5]{0,1:T(8,128)S(1)}, f32[256,5]{0,1:T(8,128)S(1)}, u32[]{:S(2)}, u32[]{:S(2)}) collective-permute-start(f32[256,5]{0,1:T(8,128)S(1)} %add.260), channel_id=1, source_target_pairs={{2,0},{3,1},{4,2},{5,3},{6,4},{7,5},{0,6},{1,7},{10,8},{11,9},{12,... | collective-permute-start | bytes 15368 | tf_op jit(solution)/shard_map/ppermute | solution.py:180
  42.3 6.5 %copy-start.5 = (f32[864]{0:T(1024)S(1)}, f32[864]{0:T(1024)}, u32[]{:S(2)}) copy-start(f32[864]{0:T(1024)} %constant.197) | copy-start | bytes 10372
  42.4 8.1 %collective-permute-start.4 = (f32[256,5]{0,1:T(8,128)S(1)}, f32[256,5]{0,1:T(8,128)S(1)}, u32[]{:S(2)}, u32[]{:S(2)}) collective-permute-start(f32[256,5]{0,1:T(8,128)S(1)} %add_bitcast_fusion.1), channel_id=1, source_target_pairs={{0,8},{1,9},{2,10},{3,11},{4,12},{5,13},{6,14},{7,15},{8,0},{9,1},... | collective-permute-start | bytes 15368 | tf_op jit(solution)/shard_map/ppermute | solution.py:171
  58.3 1.2 collective-permute-start.5
  59.5 4.9 %collective-permute-start.8 = (f32[256,5]{0,1:T(8,128)S(1)}, f32[256,5]{0,1:T(8,128)S(1)}, u32[]{:S(2)}, u32[]{:S(2)}) collective-permute-start(f32[256,5]{0,1:T(8,128)S(1)} %add.276), channel_id=1, source_target_pairs={{6,0},{7,1},{0,2},{1,3},{2,4},{3,5},{4,6},{5,7},{14,8},{15,9},{8,1... | collective-permute-start | bytes 15368 | tf_op jit(solution)/shard_map/ppermute | solution.py:180
  60.6 4.6 %collective-permute-start.7 = (f32[256,5]{0,1:T(8,128)S(1)}, f32[256,5]{0,1:T(8,128)S(1)}, u32[]{:S(2)}, u32[]{:S(2)}) collective-permute-start(f32[256,5]{0,1:T(8,128)S(1)} %add.276), channel_id=1, source_target_pairs={{4,0},{5,1},{6,2},{7,3},{0,4},{1,5},{2,6},{3,7},{12,8},{13,9},{14,... | collective-permute-start | bytes 15368 | tf_op jit(solution)/shard_map/ppermute | solution.py:180
  63.5 3.7 %collective-permute-start.6 = (f32[256,5]{0,1:T(8,128)S(1)}, f32[256,5]{0,1:T(8,128)S(1)}, u32[]{:S(2)}, u32[]{:S(2)}) collective-permute-start(f32[256,5]{0,1:T(8,128)S(1)} %add.276), channel_id=1, source_target_pairs={{2,0},{3,1},{4,2},{5,3},{6,4},{7,5},{0,6},{1,7},{10,8},{11,9},{12,... | collective-permute-start | bytes 15368 | tf_op jit(solution)/shard_map/ppermute | solution.py:180
  67.1 7.8 %collective-permute-start.9 = (f32[256,5]{0,1:T(8,128)S(1)}, f32[256,5]{0,1:T(8,128)S(1)}, u32[]{:S(2)}, u32[]{:S(2)}) collective-permute-start(f32[256,5]{0,1:T(8,128)S(1)} %add_bitcast_fusion), channel_id=1, source_target_pairs={{0,8},{1,9},{2,10},{3,11},{4,12},{5,13},{6,14},{7,15},{8,0},{9,1},... | collective-permute-start | bytes 15368 | tf_op jit(solution)/shard_map/ppermute | solution.py:171
  75.6 1.2 copy-start
  79.6 1.1 collective-permute-start.10
  80.8 3.9 %collective-permute-start.13 = (f32[26]{0:T(128)S(1)}, f32[26]{0:T(128)S(1)}, u32[]{:S(2)}, u32[]{:S(2)}) collective-permute-start(f32[26]{0:T(128)S(1)} %fusion.55), channel_id=1, source_target_pairs={{6,0},{7,1},{0,2},{1,3},{2,4},{3,5},{4,6},{5,7},{14,8},{15,9},{8,1... | collective-permute-start | bytes 320 | tf_op jit(solution)/shard_map/ppermute | solution.py:180
  81.3 4.4 %collective-permute-start.12 = (f32[26]{0:T(128)S(1)}, f32[26]{0:T(128)S(1)}, u32[]{:S(2)}, u32[]{:S(2)}) collective-permute-start(f32[26]{0:T(128)S(1)} %fusion.55), channel_id=1, source_target_pairs={{4,0},{5,1},{6,2},{7,3},{0,4},{1,5},{2,6},{3,7},{12,8},{13,9},{14,... | collective-permute-start | bytes 320 | tf_op jit(solution)/shard_map/ppermute | solution.py:180
  84.2 3.5 %collective-permute-start.11 = (f32[26]{0:T(128)S(1)}, f32[26]{0:T(128)S(1)}, u32[]{:S(2)}, u32[]{:S(2)}) collective-permute-start(f32[26]{0:T(128)S(1)} %fusion.55), channel_id=1, source_target_pairs={{2,0},{3,1},{4,2},{5,3},{6,4},{7,5},{0,6},{1,7},{10,8},{11,9},{12,... | collective-permute-start | bytes 320 | tf_op jit(solution)/shard_map/ppermute | solution.py:180
  87.8 10.2 %collective-permute-start.14 = (f32[26]{0:T(128)S(1)}, f32[26]{0:T(128)S(1)}, u32[]{:S(2)}, u32[]{:S(2)}) collective-permute-start(f32[26]{0:T(128)S(1)} %fusion.34), channel_id=1, source_target_pairs={{0,8},{1,9},{2,10},{3,11},{4,12},{5,13},{6,14},{7,15},{8,0},{9,1},... | collective-permute-start | bytes 320 | tf_op jit(solution)/shard_map/ppermute | solution.py:171
  94.3 27.3 %all-to-all-start.1 = ((f32[32,8,869]{2,1,0:T(8,128)}), f32[32,8,869]{2,1,0:T(8,128)S(1)}, u32[]{:S(2)}, u32[]{:S(2)}) async-start(f32[32,8,869]{2,1,0:T(8,128)} %pad_maximum_fusion), calls=%async_computation.1 | async-start | bytes 1835008 | tf_op jit(solution)/shard_map/all_to_all | solution.py:389
  98.0 7.6 %collective-permute-start.17 = (f32[26]{0:T(128)S(1)}, f32[26]{0:T(128)S(1)}, u32[]{:S(2)}, u32[]{:S(2)}) collective-permute-start(f32[26]{0:T(128)S(1)} %fusion.54), channel_id=1, source_target_pairs={{48,0},{0,16},{16,32},{32,48},{112,64},{64,80},{80,96},{96,112},{1... | collective-permute-start | bytes 320 | tf_op jit(solution)/shard_map/ppermute | solution.py:180
  99.9 6.1 %collective-permute-start.16 = (f32[26]{0:T(128)S(1)}, f32[26]{0:T(128)S(1)}, u32[]{:S(2)}, u32[]{:S(2)}) collective-permute-start(f32[26]{0:T(128)S(1)} %fusion.54), channel_id=1, source_target_pairs={{32,0},{48,16},{0,32},{16,48},{96,64},{112,80},{64,96},{80,112},{1... | collective-permute-start | bytes 320 | tf_op jit(solution)/shard_map/ppermute | solution.py:180
  102.5 5.8 %collective-permute-start.15 = (f32[26]{0:T(128)S(1)}, f32[26]{0:T(128)S(1)}, u32[]{:S(2)}, u32[]{:S(2)}) collective-permute-start(f32[26]{0:T(128)S(1)} %fusion.54), channel_id=1, source_target_pairs={{16,0},{32,16},{48,32},{0,48},{80,64},{96,80},{112,96},{64,112},{1... | collective-permute-start | bytes 320 | tf_op jit(solution)/shard_map/ppermute | solution.py:180
  108.4 5.4 %collective-permute-start.20 = (f32[26]{0:T(128)S(1)}, f32[26]{0:T(128)S(1)}, u32[]{:S(2)}, u32[]{:S(2)}) collective-permute-start(f32[26]{0:T(128)S(1)} %fusion.53), channel_id=1, source_target_pairs={{192,0},{208,16},{224,32},{240,48},{0,64},{16,80},{32,96},{48,112}... | collective-permute-start | bytes 320 | tf_op jit(solution)/shard_map/ppermute | solution.py:180
  110.5 5.0 %collective-permute-start.19 = (f32[26]{0:T(128)S(1)}, f32[26]{0:T(128)S(1)}, u32[]{:S(2)}, u32[]{:S(2)}) collective-permute-start(f32[26]{0:T(128)S(1)} %fusion.53), channel_id=1, source_target_pairs={{128,0},{144,16},{160,32},{176,48},{192,64},{208,80},{224,96},{240... | collective-permute-start | bytes 320 | tf_op jit(solution)/shard_map/ppermute | solution.py:180
  113.6 3.5 %collective-permute-start.18 = (f32[26]{0:T(128)S(1)}, f32[26]{0:T(128)S(1)}, u32[]{:S(2)}, u32[]{:S(2)}) collective-permute-start(f32[26]{0:T(128)S(1)} %fusion.53), channel_id=1, source_target_pairs={{64,0},{80,16},{96,32},{112,48},{128,64},{144,80},{160,96},{176,11... | collective-permute-start | bytes 320 | tf_op jit(solution)/shard_map/ppermute | solution.py:180
  117.2 0.7 copy-start.4
  117.2 0.7 copy-start.7
  118.0 0.7 copy-start.6

commit v12 on v11

--- a/solution.py
+++ b/solution.py
@@ -5,6 +5,7 @@
 import numpy as np
 from jax import lax
 from jax.experimental import pallas as pl
+from jax.experimental.pallas import tpu as pltpu
 from jax.sharding import PartitionSpec as P
 
 NXI = 24
@@ -290,12 +291,19 @@
     )
 
 
-def sweep_kernel(rate_ref, drive_ref, sign_ref, out_ref):
-    positions = rate_ref.shape[0]
-    start = jnp.zeros(rate_ref.shape[1:], jnp.float32)
+def sweep_kernel(dist_ref, target_ref, thick_ref, speed_ref, sign_ref, out_ref, rate_ref, drive_ref):
+    positions = dist_ref.shape[0]
+    start = jnp.zeros(dist_ref.shape[1:], jnp.float32)
+    reach = speed_ref[...] * (positions * 1.0)
 
     def forward(p, carried):
-        value = rate_ref[p] * carried + drive_ref[p]
+        thick = thick_ref[p]
+        denominator = reach + thick + pseudo_rate
+        rate = reach / denominator
+        drive = (thick * target_ref[p] + pseudo_rate * dist_ref[p]) / denominator
+        rate_ref[p] = rate
+        drive_ref[p] = drive
+        value = rate * carried + drive
         out_ref[p] = value
         return value
 
@@ -311,11 +319,13 @@
     lax.fori_loop(0, positions, backward, start)
 
 
-def line_sweep(carry_rate, drive_term, node_signed):
+def line_sweep(dist_t, target, thickness, node_signed):
+    shape = dist_t.shape
     return pl.pallas_call(
         sweep_kernel,
-        out_shape=jax.ShapeDtypeStruct(drive_term.shape, jnp.float32),
-    )(carry_rate, drive_term, node_signed.reshape(1, -1))
+        out_shape=jax.ShapeDtypeStruct(shape, jnp.float32),
+        scratch_shapes=[pltpu.VMEM(shape, jnp.float32), pltpu.VMEM(shape, jnp.float32)],
+    )(dist_t, target, thickness, jnp.abs(node_signed).reshape(1, -1), node_signed.reshape(1, -1))
 
 
 def line_block(matrices, vector):
@@ -357,12 +367,7 @@
         jnp.dot(dist_t.reshape(cells, node_count), weighted.T, precision=HIGH), ("vel",)
     )
     target = jnp.dot(old_moments, rebuild, precision=HIGH).reshape(total_length, share, node_count)
-    node_speed = jnp.abs(node_signed)
-    denominator = node_speed * total_length + thickness + pseudo_rate
-    carry_rate = node_speed * total_length / denominator
-    drive_term = (thickness * target + pseudo_rate * dist_t) / denominator
-    carry_rate = jnp.broadcast_to(carry_rate, drive_term.shape)
-    half_field = line_sweep(carry_rate, drive_term, node_signed)
+    half_field = line_sweep(dist_t, target, thickness, node_signed)
     half_moments = tree_sum(
         jnp.dot(half_field.reshape(cells, node_count), weighted.T, precision=HIGH), ("vel",)
     )

time: 125 us -> 127 us (1.016)
  Pallas kernels: 2.94 us -> 5.44 us
  local copies, waits for them, and re-layouts: 12.3 us -> 13.8 us
    pallas_call x1, Pallas kernels: 2.94 us -> 5.44 us  [line_sweep(): pl.pallas_call(sweep_kernel, out_shape=jax.ShapeDtypeStruct(shape, jnp.fl...]
    unnamed x20 -> x18, local copies, waits for them, and re-layouts: 5.78 us -> 5.78 us
  transfers between devices with their start and end apart: 23 -> 23, of which waited for: 17 -> 16; matrix products, arithmetic and copies ran while one was open for 6% -> 6% of each run, Pallas kernels for 0% -> 0%
where the time goes in v12:
time: 127 us; the launch traced here: 126 us
  starting transfers between devices  52.8 us (42%)
  waiting for transfers between devices  38.5 us (30%)
  local copies, waits for them, and re-layouts  13.8 us (11%)
  matrix products  8.32 us (7%)
  other arithmetic  6.24 us (5%)
  Pallas kernels  5.44 us (4%)
    ppermute x15, starting transfers between devices, group_sum(): shifted.append(lax.ppermute(block, axis, pairs))  25.4 us
    all_to_all x1, waiting for transfers between devices, body(): lines = lax.all_to_all(packed, 'sec', 1, 0, tiled=True)  17.7 us
    ppermute x6, starting transfers between devices, group_sum(): return block + lax.ppermute(block, axis, pairs)  16.8 us
    ppermute x15, waiting for transfers between devices, group_sum(): shifted.append(lax.ppermute(block, axis, pairs))  15 us
    all_to_all x1, starting transfers between devices, body(): lines = lax.all_to_all(packed, 'sec', 1, 0, tiled=True)  7.03 us
    unnamed x18, local copies, waits for them, and re-layouts  5.78 us
    ppermute x6, waiting for transfers between devices, group_sum(): return block + lax.ppermute(block, axis, pairs)  5.75 us
    pallas_call x1, Pallas kernels, line_sweep(): pl.pallas_call(sweep_kernel, out_shape=jax.ShapeDtypeStruct(shape, jnp.fl...  5.44 us
  transfers between devices with their start and end apart: 23, of which 16 were waited for; matrix products, arithmetic and copies ran while one was open for 6% of the time, Pallas kernels for 0%

profile of v12, /device:TPU:32, one launch (start us, length us, event | category | flops | bytes accessed | tf_op | source)
XLA Modules:
  0.0 126.2 jit_solution(17120834789810069823)
XLA Ops:
  0.6 0.7 copy-done.7
  3.7 1.5 %copy.80 = f32[864,256]{0,1:T(8,128)S(1)} copy(f32[864,256]{1,0:T(8,128)} %param.10) | data formatting | bytes 1769472 | tf_op args[0]
  5.6 1.8 %copy.85 = f32[2,128,940]{2,0,1:T(2,128)} copy(f32[2,128,940]{2,1,0:T(8,128)S(1)} %bitcast.149) | data formatting | bytes 1925120 | tf_op jit(solution)/shard_map/transpose | solution.py:358
  7.4 7.0 %all-to-all-start = ((f32[2,128,940]{2,0,1:T(2,128)}), f32[2,128,940]{2,0,1:T(2,128)S(1)}, u32[]{:S(2)}, u32[]{:S(2)}) async-start(f32[2,128,940]{2,0,1:T(2,128)} %copy.85), calls=%async_computation | async-start | bytes 2097152 | tf_op jit(solution)/shard_map/all_to_all | solution.py:359
  14.5 17.7 %all-to-all-done = f32[2,128,940]{2,0,1:T(2,128)S(1)} async-done(((f32[2,128,940]{2,0,1:T(2,128)}), f32[2,128,940]{2,0,1:T(2,128)S(1)}, u32[]{:S(2)}, u32[]{:S(2)}) %all-to-all-start) | async-done | bytes 962592 | tf_op jit(solution)/shard_map/all_to_all | solution.py:359
  32.6 1.6 %fusion.2 = f32[256,5]{0,1:T(8,128)S(1)} fusion(f32[5,13824]{1,0:T(8,128)} %constant.172.clone, s32[]{:T(128)S(6)} %select_n.134, f32[32,8,940]{2,1,0:T(8,128)S(1)} %bitcast.143), kind=kOutput, calls=%fused_computation.6 | convolution fusion | flops 13271040 | bytes 951300 | tf_op jit(solution)/shard_map/dot_general | solution.py:367
  34.2 1.2 collective-permute-done
  35.4 1.9 %collective-permute-start.3 = (f32[256,5]{0,1:T(8,128)S(1)}, f32[256,5]{0,1:T(8,128)S(1)}, u32[]{:S(2)}, u32[]{:S(2)}) collective-permute-start(f32[256,5]{0,1:T(8,128)S(1)} %add.233), channel_id=1, source_target_pairs={{6,0},{7,1},{0,2},{1,3},{2,4},{3,5},{4,6},{5,7},{14,8},{15,9},{8,1... | collective-permute-start | bytes 15368 | tf_op jit(solution)/shard_map/ppermute | solution.py:181
  37.4 1.4 %collective-permute-start.2 = (f32[256,5]{0,1:T(8,128)S(1)}, f32[256,5]{0,1:T(8,128)S(1)}, u32[]{:S(2)}, u32[]{:S(2)}) collective-permute-start(f32[256,5]{0,1:T(8,128)S(1)} %add.233), channel_id=1, source_target_pairs={{4,0},{5,1},{6,2},{7,3},{0,4},{1,5},{2,6},{3,7},{12,8},{13,9},{14,... | collective-permute-start | bytes 15368 | tf_op jit(solution)/shard_map/ppermute | solution.py:181
  38.7 2.0 %collective-permute-start.1 = (f32[256,5]{0,1:T(8,128)S(1)}, f32[256,5]{0,1:T(8,128)S(1)}, u32[]{:S(2)}, u32[]{:S(2)}) collective-permute-start(f32[256,5]{0,1:T(8,128)S(1)} %add.233), channel_id=1, source_target_pairs={{2,0},{3,1},{4,2},{5,3},{6,4},{7,5},{0,6},{1,7},{10,8},{11,9},{12,... | collective-permute-start | bytes 15368 | tf_op jit(solution)/shard_map/ppermute | solution.py:181
  40.7 1.2 collective-permute-done.2
  42.4 6.5 %collective-permute-start.4 = (f32[256,5]{0,1:T(8,128)S(1)}, f32[256,5]{0,1:T(8,128)S(1)}, u32[]{:S(2)}, u32[]{:S(2)}) collective-permute-start(f32[256,5]{0,1:T(8,128)S(1)} %add_bitcast_fusion.1), channel_id=1, source_target_pairs={{0,8},{1,9},{2,10},{3,11},{4,12},{5,13},{6,14},{7,15},{8,0},{9,1},... | collective-permute-start | bytes 15368 | tf_op jit(solution)/shard_map/ppermute | solution.py:172
  48.9 0.8 slice.138.thick_ref
  49.6 1.0 slice.137.dist_ref
  50.6 2.8 %convolution_bitcast_fusion.target_ref = f32[32,8,864]{2,1,0:T(8,128)} fusion(f32[256,5]{0,1:T(8,128)S(1)} %fusion.52, f32[5,13824]{1,0:T(8,128)} %constant.173.clone, s32[]{:T(128)S(6)} %select_n.134), kind=kOutput, calls=%fused_computation.1 | convolution fusion | flops 13271040 | bytes 918532 | tf_op jit(solution)/shard_map/dot_general | solution.py:369
  53.4 5.4 %shard_map.113 = f32[32,8,864]{2,1,0:T(8,128)} custom-call(f32[32,8,864]{2,1,0:T(8,128)} %slice.137.dist_ref, f32[32,8,864]{2,1,0:T(8,128)} %convolution_bitcast_fusion.target_ref, f32[32,8,1]{2,1,0:T(8,128)} %slice.138.thick_ref, f32[1,864]{1,0:T(1,128)} %constant.194.speed_ref, f32[1,864]{1,0:T(1,128)} %constant.195.sign_ref), custom_call_target="tpu_custom_call" | custom-call | tf_op jit(solution)/shard_map/pallas_call | solution.py:324
  58.9 2.0 %fusion = f32[256,5]{0,1:T(8,128)S(1)} fusion(f32[32,8,864]{2,1,0:T(8,128)} %shard_map.113, f32[5,13824]{1,0:T(8,128)} %constant.172.clone, s32[]{:T(128)S(6)} %select_n.134), kind=kOutput, calls=%fused_computation.4 | convolution fusion | flops 13271040 | bytes 951300 | tf_op jit(solution)/shard_map/dot_general | solution.py:372
  61.0 1.1 collective-permute-done.5
  62.1 0.9 collective-permute-start.8
  63.0 2.9 %collective-permute-start.7 = (f32[256,5]{0,1:T(8,128)S(1)}, f32[256,5]{0,1:T(8,128)S(1)}, u32[]{:S(2)}, u32[]{:S(2)}) collective-permute-start(f32[256,5]{0,1:T(8,128)S(1)} %add.248), channel_id=1, source_target_pairs={{4,0},{5,1},{6,2},{7,3},{0,4},{1,5},{2,6},{3,7},{12,8},{13,9},{14,... | collective-permute-start | bytes 15368 | tf_op jit(solution)/shard_map/ppermute | solution.py:181
  65.9 1.0 collective-permute-start.6
  66.9 0.7 collective-permute-done.7
  67.6 1.9 %collective-permute-done.6 = f32[256,5]{0,1:T(8,128)S(1)} collective-permute-done((f32[256,5]{0,1:T(8,128)S(1)}, f32[256,5]{0,1:T(8,128)S(1)}, u32[]{:S(2)}, u32[]{:S(2)}) %collective-permute-start.6) | collective-permute-done | bytes 5152 | tf_op jit(solution)/shard_map/ppermute | solution.py:181
  69.5 4.8 %collective-permute-start.9 = (f32[256,5]{0,1:T(8,128)S(1)}, f32[256,5]{0,1:T(8,128)S(1)}, u32[]{:S(2)}, u32[]{:S(2)}) collective-permute-start(f32[256,5]{0,1:T(8,128)S(1)} %add_bitcast_fusion), channel_id=1, source_target_pairs={{0,8},{1,9},{2,10},{3,11},{4,12},{5,13},{6,14},{7,15},{8,0},{9,1},... | collective-permute-start | bytes 15368 | tf_op jit(solution)/shard_map/ppermute | solution.py:172
  74.9 2.5 %collective-permute-done.9 = f32[256,5]{0,1:T(8,128)S(1)} collective-permute-done((f32[256,5]{0,1:T(8,128)S(1)}, f32[256,5]{0,1:T(8,128)S(1)}, u32[]{:S(2)}, u32[]{:S(2)}) %collective-permute-start.9) | collective-permute-done | bytes 5152 | tf_op jit(solution)/shard_map/ppermute | solution.py:172
  79.2 1.7 %abs_reduce_fusion = (f32[864]{0:T(1024)S(1)}, f32[32,8,864]{2,1,0:T(8,128)S(1)}) fusion(f32[32,8,864]{2,1,0:T(8,128)S(1)} %copy-done, f32[32,8,5]{2,1,0:T(8,128)S(1)} %copy.97, f32[5,13824]{1,0:T(8,128)} %constant.173.clone, s32[]{:T(128)S(6)} %select_n.134), kind=kOutput, calls=%fused_computation.9 | convolution fusion | flops 13933728 | bytes 1806724 | tf_op jit(solution)/shard_map/dot_general | solution.py:386
  80.9 0.8 dynamic-slice_multiply_fusion
  82.2 1.0 collective-permute-done.10
  83.7 2.9 %collective-permute-start.12 = (f32[26]{0:T(128)S(1)}, f32[26]{0:T(128)S(1)}, u32[]{:S(2)}, u32[]{:S(2)}) collective-permute-start(f32[26]{0:T(128)S(1)} %fusion.51), channel_id=1, source_target_pairs={{4,0},{5,1},{6,2},{7,3},{0,4},{1,5},{2,6},{3,7},{12,8},{13,9},{14,... | collective-permute-start | bytes 320 | tf_op jit(solution)/shard_map/ppermute | solution.py:181
  87.1 1.1 collective-permute-done.12
  88.2 2.0 %collective-permute-done.11 = f32[26]{0:T(128)S(1)} collective-permute-done((f32[26]{0:T(128)S(1)}, f32[26]{0:T(128)S(1)}, u32[]{:S(2)}, u32[]{:S(2)}) %collective-permute-start.11) | collective-permute-done | bytes 136 | tf_op jit(solution)/shard_map/ppermute | solution.py:181
  90.2 5.5 %collective-permute-start.14 = (f32[26]{0:T(128)S(1)}, f32[26]{0:T(128)S(1)}, u32[]{:S(2)}, u32[]{:S(2)}) collective-permute-start(f32[26]{0:T(128)S(1)} %fusion.29), channel_id=1, source_target_pairs={{0,8},{1,9},{2,10},{3,11},{4,12},{5,13},{6,14},{7,15},{8,0},{9,1},... | collective-permute-start | bytes 320 | tf_op jit(solution)/shard_map/ppermute | solution.py:172
  95.7 1.0 pad_maximum_fusion
  96.7 3.6 %all-to-all-start.1 = ((f32[32,8,869]{2,1,0:T(8,128)}), f32[32,8,869]{2,1,0:T(8,128)S(1)}, u32[]{:S(2)}, u32[]{:S(2)}) async-start(f32[32,8,869]{2,1,0:T(8,128)} %pad_maximum_fusion), calls=%async_computation.1 | async-start | bytes 1835008 | tf_op jit(solution)/shard_map/all_to_all | solution.py:394
  100.4 1.9 %collective-permute-start.17 = (f32[26]{0:T(128)S(1)}, f32[26]{0:T(128)S(1)}, u32[]{:S(2)}, u32[]{:S(2)}) collective-permute-start(f32[26]{0:T(128)S(1)} %fusion.50), channel_id=1, source_target_pairs={{48,0},{0,16},{16,32},{32,48},{112,64},{64,80},{80,96},{96,112},{1... | collective-permute-start | bytes 320 | tf_op jit(solution)/shard_map/ppermute | solution.py:181
  102.3 2.7 %collective-permute-start.16 = (f32[26]{0:T(128)S(1)}, f32[26]{0:T(128)S(1)}, u32[]{:S(2)}, u32[]{:S(2)}) collective-permute-start(f32[26]{0:T(128)S(1)} %fusion.50), channel_id=1, source_target_pairs={{32,0},{48,16},{0,32},{16,48},{96,64},{112,80},{64,96},{80,112},{1... | collective-permute-start | bytes 320 | tf_op jit(solution)/shard_map/ppermute | solution.py:181
  104.9 1.5 %collective-permute-start.15 = (f32[26]{0:T(128)S(1)}, f32[26]{0:T(128)S(1)}, u32[]{:S(2)}, u32[]{:S(2)}) collective-permute-start(f32[26]{0:T(128)S(1)} %fusion.50), channel_id=1, source_target_pairs={{16,0},{32,16},{48,32},{0,48},{80,64},{96,80},{112,96},{64,112},{1... | collective-permute-start | bytes 320 | tf_op jit(solution)/shard_map/ppermute | solution.py:181
  106.4 1.6 %collective-permute-done.17 = f32[26]{0:T(128)S(1)} collective-permute-done((f32[26]{0:T(128)S(1)}, f32[26]{0:T(128)S(1)}, u32[]{:S(2)}, u32[]{:S(2)}) %collective-permute-start.17) | collective-permute-done | bytes 136 | tf_op jit(solution)/shard_map/ppermute | solution.py:181
  108.4 2.4 %collective-permute-done.15 = f32[26]{0:T(128)S(1)} collective-permute-done((f32[26]{0:T(128)S(1)}, f32[26]{0:T(128)S(1)}, u32[]{:S(2)}, u32[]{:S(2)}) %collective-permute-start.15) | collective-permute-done | bytes 136 | tf_op jit(solution)/shard_map/ppermute | solution.py:181
  110.8 2.1 %collective-permute-start.20 = (f32[26]{0:T(128)S(1)}, f32[26]{0:T(128)S(1)}, u32[]{:S(2)}, u32[]{:S(2)}) collective-permute-start(f32[26]{0:T(128)S(1)} %fusion.49), channel_id=1, source_target_pairs={{192,0},{208,16},{224,32},{240,48},{0,64},{16,80},{32,96},{48,112}... | collective-permute-start | bytes 320 | tf_op jit(solution)/shard_map/ppermute | solution.py:181
  112.9 3.2 %collective-permute-start.19 = (f32[26]{0:T(128)S(1)}, f32[26]{0:T(128)S(1)}, u32[]{:S(2)}, u32[]{:S(2)}) collective-permute-start(f32[26]{0:T(128)S(1)} %fusion.49), channel_id=1, source_target_pairs={{128,0},{144,16},{160,32},{176,48},{192,64},{208,80},{224,96},{240... | collective-permute-start | bytes 320 | tf_op jit(solution)/shard_map/ppermute | solution.py:181
  116.2 1.7 %collective-permute-done.19 = f32[26]{0:T(128)S(1)} collective-permute-done((f32[26]{0:T(128)S(1)}, f32[26]{0:T(128)S(1)}, u32[]{:S(2)}, u32[]{:S(2)}) %collective-permute-start.19) | collective-permute-done | bytes 136 | tf_op jit(solution)/shard_map/ppermute | solution.py:181
  117.9 1.6 %collective-permute-done.18 = f32[26]{0:T(128)S(1)} collective-permute-done((f32[26]{0:T(128)S(1)}, f32[26]{0:T(128)S(1)}, u32[]{:S(2)}, u32[]{:S(2)}) %collective-permute-start.18) | collective-permute-done | bytes 136 | tf_op jit(solution)/shard_map/ppermute | solution.py:181
  120.4 0.7 copy-done.5
  121.1 1.3 %multiply_bitcast_fusion.1 = (f32[1,24]{1,0:T(1,128)S(1)}, f32[1,24]{1,0:T(1,128)S(1)}, f32[1,24]{1,0:T(1,128)S(1)}, f32[1,24]{1,0:T(1,128)S(1)}) fusion(f32[24]{0:T(128)S(1)} %copy-done.4, f32[1,26]{1,0:T(1,128)S(1)} %fusion.15, f32[1,24]{1,0:T(1,128)S(1)} %copy-done.5, f32[5,24]{1,0:T(8,128)S(1)} %fusion.9, f32[]{:T(128)} %bitcast.50, f32[]{:T(128)} %bitcast.51), kind=kLoop, calls=%fused_computation.82 | loop fusion | flops 480 | bytes 1160 | tf_op jit(solution)/shard_map/stack | solution.py:409
  122.6 1.3 %add_bitcast_fusion.2 = f32[24]{0:T(128)S(1)} fusion(f32[1,24]{1,0:T(1,128)S(1)} %copy-done.5, f32[1,24]{1,0:T(1,128)S(1)} %get-tuple-element.13, f32[1,24]{1,0:T(1,128)S(1)} %get-tuple-element.12, f32[5,24]{1,0:T(8,128)S(1)} %fusion.7, f32[]{:T(128)} %bitcast.51, f32[]{:T(128)} %bitcast.50), kind=kLoop, calls=%fused_computation.79 | loop fusion | flops 432 | bytes 872 | tf_op jit(solution)/shard_map/sub | solution.py:416
  124.2 0.7 copy.103
  125.2 1.1 multiply_add_fusion
  (108 shorter events, 9.7 us)
Async XLA Ops:
  0.6 0.7 copy-start.7
  1.3 0.8 copy-start.1
  2.1 0.8 copy-start.2
  2.8 0.8 copy-start.3
  7.4 24.7 %all-to-all-start = ((f32[2,128,940]{2,0,1:T(2,128)}), f32[2,128,940]{2,0,1:T(2,128)S(1)}, u32[]{:S(2)}, u32[]{:S(2)}) async-start(f32[2,128,940]{2,0,1:T(2,128)} %copy.85), calls=%async_computation | async-start | bytes 2097152 | tf_op jit(solution)/shard_map/all_to_all | solution.py:359
  34.2 1.2 collective-permute-start
  35.4 5.3 %collective-permute-start.3 = (f32[256,5]{0,1:T(8,128)S(1)}, f32[256,5]{0,1:T(8,128)S(1)}, u32[]{:S(2)}, u32[]{:S(2)}) collective-permute-start(f32[256,5]{0,1:T(8,128)S(1)} %add.233), channel_id=1, source_target_pairs={{6,0},{7,1},{0,2},{1,3},{2,4},{3,5},{4,6},{5,7},{14,8},{15,9},{8,1... | collective-permute-start | bytes 15368 | tf_op jit(solution)/shard_map/ppermute | solution.py:181
  37.4 4.5 %collective-permute-start.2 = (f32[256,5]{0,1:T(8,128)S(1)}, f32[256,5]{0,1:T(8,128)S(1)}, u32[]{:S(2)}, u32[]{:S(2)}) collective-permute-start(f32[256,5]{0,1:T(8,128)S(1)} %add.233), channel_id=1, source_target_pairs={{4,0},{5,1},{6,2},{7,3},{0,4},{1,5},{2,6},{3,7},{12,8},{13,9},{14,... | collective-permute-start | bytes 15368 | tf_op jit(solution)/shard_map/ppermute | solution.py:181
  38.7 3.7 %collective-permute-start.1 = (f32[256,5]{0,1:T(8,128)S(1)}, f32[256,5]{0,1:T(8,128)S(1)}, u32[]{:S(2)}, u32[]{:S(2)}) collective-permute-start(f32[256,5]{0,1:T(8,128)S(1)} %add.233), channel_id=1, source_target_pairs={{2,0},{3,1},{4,2},{5,3},{6,4},{7,5},{0,6},{1,7},{10,8},{11,9},{12,... | collective-permute-start | bytes 15368 | tf_op jit(solution)/shard_map/ppermute | solution.py:181
  42.4 8.2 %collective-permute-start.4 = (f32[256,5]{0,1:T(8,128)S(1)}, f32[256,5]{0,1:T(8,128)S(1)}, u32[]{:S(2)}, u32[]{:S(2)}) collective-permute-start(f32[256,5]{0,1:T(8,128)S(1)} %add_bitcast_fusion.1), channel_id=1, source_target_pairs={{0,8},{1,9},{2,10},{3,11},{4,12},{5,13},{6,14},{7,15},{8,0},{9,1},... | collective-permute-start | bytes 15368 | tf_op jit(solution)/shard_map/ppermute | solution.py:172
  60.9 1.2 collective-permute-start.5
  62.1 4.8 %collective-permute-start.8 = (f32[256,5]{0,1:T(8,128)S(1)}, f32[256,5]{0,1:T(8,128)S(1)}, u32[]{:S(2)}, u32[]{:S(2)}) collective-permute-start(f32[256,5]{0,1:T(8,128)S(1)} %add.248), channel_id=1, source_target_pairs={{6,0},{7,1},{0,2},{1,3},{2,4},{3,5},{4,6},{5,7},{14,8},{15,9},{8,1... | collective-permute-start | bytes 15368 | tf_op jit(solution)/shard_map/ppermute | solution.py:181
  63.0 4.6 %collective-permute-start.7 = (f32[256,5]{0,1:T(8,128)S(1)}, f32[256,5]{0,1:T(8,128)S(1)}, u32[]{:S(2)}, u32[]{:S(2)}) collective-permute-start(f32[256,5]{0,1:T(8,128)S(1)} %add.248), channel_id=1, source_target_pairs={{4,0},{5,1},{6,2},{7,3},{0,4},{1,5},{2,6},{3,7},{12,8},{13,9},{14,... | collective-permute-start | bytes 15368 | tf_op jit(solution)/shard_map/ppermute | solution.py:181
  65.9 3.7 %collective-permute-start.6 = (f32[256,5]{0,1:T(8,128)S(1)}, f32[256,5]{0,1:T(8,128)S(1)}, u32[]{:S(2)}, u32[]{:S(2)}) collective-permute-start(f32[256,5]{0,1:T(8,128)S(1)} %add.248), channel_id=1, source_target_pairs={{2,0},{3,1},{4,2},{5,3},{6,4},{7,5},{0,6},{1,7},{10,8},{11,9},{12,... | collective-permute-start | bytes 15368 | tf_op jit(solution)/shard_map/ppermute | solution.py:181
  69.5 7.8 %collective-permute-start.9 = (f32[256,5]{0,1:T(8,128)S(1)}, f32[256,5]{0,1:T(8,128)S(1)}, u32[]{:S(2)}, u32[]{:S(2)}) collective-permute-start(f32[256,5]{0,1:T(8,128)S(1)} %add_bitcast_fusion), channel_id=1, source_target_pairs={{0,8},{1,9},{2,10},{3,11},{4,12},{5,13},{6,14},{7,15},{8,0},{9,1},... | collective-permute-start | bytes 15368 | tf_op jit(solution)/shard_map/ppermute | solution.py:172
  78.0 1.2 copy-start
  82.0 1.1 collective-permute-start.10
  83.2 3.9 %collective-permute-start.13 = (f32[26]{0:T(128)S(1)}, f32[26]{0:T(128)S(1)}, u32[]{:S(2)}, u32[]{:S(2)}) collective-permute-start(f32[26]{0:T(128)S(1)} %fusion.51), channel_id=1, source_target_pairs={{6,0},{7,1},{0,2},{1,3},{2,4},{3,5},{4,6},{5,7},{14,8},{15,9},{8,1... | collective-permute-start | bytes 320 | tf_op jit(solution)/shard_map/ppermute | solution.py:181
  83.7 4.4 %collective-permute-start.12 = (f32[26]{0:T(128)S(1)}, f32[26]{0:T(128)S(1)}, u32[]{:S(2)}, u32[]{:S(2)}) collective-permute-start(f32[26]{0:T(128)S(1)} %fusion.51), channel_id=1, source_target_pairs={{4,0},{5,1},{6,2},{7,3},{0,4},{1,5},{2,6},{3,7},{12,8},{13,9},{14,... | collective-permute-start | bytes 320 | tf_op jit(solution)/shard_map/ppermute | solution.py:181
  86.6 3.5 %collective-permute-start.11 = (f32[26]{0:T(128)S(1)}, f32[26]{0:T(128)S(1)}, u32[]{:S(2)}, u32[]{:S(2)}) collective-permute-start(f32[26]{0:T(128)S(1)} %fusion.51), channel_id=1, source_target_pairs={{2,0},{3,1},{4,2},{5,3},{6,4},{7,5},{0,6},{1,7},{10,8},{11,9},{12,... | collective-permute-start | bytes 320 | tf_op jit(solution)/shard_map/ppermute | solution.py:181
  90.2 10.2 %collective-permute-start.14 = (f32[26]{0:T(128)S(1)}, f32[26]{0:T(128)S(1)}, u32[]{:S(2)}, u32[]{:S(2)}) collective-permute-start(f32[26]{0:T(128)S(1)} %fusion.29), channel_id=1, source_target_pairs={{0,8},{1,9},{2,10},{3,11},{4,12},{5,13},{6,14},{7,15},{8,0},{9,1},... | collective-permute-start | bytes 320 | tf_op jit(solution)/shard_map/ppermute | solution.py:172
  96.7 27.3 %all-to-all-start.1 = ((f32[32,8,869]{2,1,0:T(8,128)}), f32[32,8,869]{2,1,0:T(8,128)S(1)}, u32[]{:S(2)}, u32[]{:S(2)}) async-start(f32[32,8,869]{2,1,0:T(8,128)} %pad_maximum_fusion), calls=%async_computation.1 | async-start | bytes 1835008 | tf_op jit(solution)/shard_map/all_to_all | solution.py:394
  100.4 7.6 %collective-permute-start.17 = (f32[26]{0:T(128)S(1)}, f32[26]{0:T(128)S(1)}, u32[]{:S(2)}, u32[]{:S(2)}) collective-permute-start(f32[26]{0:T(128)S(1)} %fusion.50), channel_id=1, source_target_pairs={{48,0},{0,16},{16,32},{32,48},{112,64},{64,80},{80,96},{96,112},{1... | collective-permute-start | bytes 320 | tf_op jit(solution)/shard_map/ppermute | solution.py:181
  102.3 6.1 %collective-permute-start.16 = (f32[26]{0:T(128)S(1)}, f32[26]{0:T(128)S(1)}, u32[]{:S(2)}, u32[]{:S(2)}) collective-permute-start(f32[26]{0:T(128)S(1)} %fusion.50), channel_id=1, source_target_pairs={{32,0},{48,16},{0,32},{16,48},{96,64},{112,80},{64,96},{80,112},{1... | collective-permute-start | bytes 320 | tf_op jit(solution)/shard_map/ppermute | solution.py:181
  104.9 5.8 %collective-permute-start.15 = (f32[26]{0:T(128)S(1)}, f32[26]{0:T(128)S(1)}, u32[]{:S(2)}, u32[]{:S(2)}) collective-permute-start(f32[26]{0:T(128)S(1)} %fusion.50), channel_id=1, source_target_pairs={{16,0},{32,16},{48,32},{0,48},{80,64},{96,80},{112,96},{64,112},{1... | collective-permute-start | bytes 320 | tf_op jit(solution)/shard_map/ppermute | solution.py:181
  110.8 5.4 %collective-permute-start.20 = (f32[26]{0:T(128)S(1)}, f32[26]{0:T(128)S(1)}, u32[]{:S(2)}, u32[]{:S(2)}) collective-permute-start(f32[26]{0:T(128)S(1)} %fusion.49), channel_id=1, source_target_pairs={{192,0},{208,16},{224,32},{240,48},{0,64},{16,80},{32,96},{48,112}... | collective-permute-start | bytes 320 | tf_op jit(solution)/shard_map/ppermute | solution.py:181
  112.9 5.0 %collective-permute-start.19 = (f32[26]{0:T(128)S(1)}, f32[26]{0:T(128)S(1)}, u32[]{:S(2)}, u32[]{:S(2)}) collective-permute-start(f32[26]{0:T(128)S(1)} %fusion.49), channel_id=1, source_target_pairs={{128,0},{144,16},{160,32},{176,48},{192,64},{208,80},{224,96},{240... | collective-permute-start | bytes 320 | tf_op jit(solution)/shard_map/ppermute | solution.py:181
  116.0 3.5 %collective-permute-start.18 = (f32[26]{0:T(128)S(1)}, f32[26]{0:T(128)S(1)}, u32[]{:S(2)}, u32[]{:S(2)}) collective-permute-start(f32[26]{0:T(128)S(1)} %fusion.49), channel_id=1, source_target_pairs={{64,0},{80,16},{96,32},{112,48},{128,64},{144,80},{160,96},{176,11... | collective-permute-start | bytes 320 | tf_op jit(solution)/shard_map/ppermute | solution.py:181
  119.6 0.7 copy-start.4
  119.6 0.7 copy-start.6
  120.4 0.7 copy-start.5

commit v13 on v11

--- a/solution.py
+++ b/solution.py
@@ -356,13 +356,27 @@
     old_moments = tree_sum(
         jnp.dot(dist_t.reshape(cells, node_count), weighted.T, precision=HIGH), ("vel",)
     )
-    target = jnp.dot(old_moments, rebuild, precision=HIGH).reshape(total_length, share, node_count)
     node_speed = jnp.abs(node_signed)
     denominator = node_speed * total_length + thickness + pseudo_rate
     carry_rate = node_speed * total_length / denominator
-    drive_term = (thickness * target + pseudo_rate * dist_t) / denominator
-    carry_rate = jnp.broadcast_to(carry_rate, drive_term.shape)
-    half_field = line_sweep(carry_rate, drive_term, node_signed)
+    own_drive = pseudo_rate * dist_t / denominator
+    carry_rate = jnp.broadcast_to(carry_rate, own_drive.shape)
+    own_field = line_sweep(carry_rate, own_drive, node_signed)
+    moment_signed = jnp.asarray(np.tile(along_x[:NXI], 5), jnp.float32)
+    moment_speed = jnp.abs(moment_signed)
+    moment_den = moment_speed * total_length + thickness + pseudo_rate
+    moment_rate = moment_speed * total_length / moment_den
+    moment_drive = thickness * jnp.repeat(
+        old_moments.reshape(total_length, share, 5), NXI, axis=2
+    ) / moment_den
+    moment_field = line_sweep(moment_rate, moment_drive, moment_signed)
+    chosen = jnp.asarray(
+        (np.arange(node_count)[None, :] % NXI) == np.arange(NXI)[:, None], jnp.float32
+    )
+    spread_basis = (rebuild[:, None, :] * chosen[None]).reshape(5 * NXI, node_count)
+    half_field = own_field + jnp.dot(
+        moment_field.reshape(cells, 5 * NXI), spread_basis, precision=HIGH
+    ).reshape(total_length, share, node_count)
     half_moments = tree_sum(
         jnp.dot(half_field.reshape(cells, node_count), weighted.T, precision=HIGH), ("vel",)
     )

time: 125 us -> 124 us (level)
  starting transfers between devices: 53 us -> 49.3 us
  Pallas kernels: 2.94 us -> 4.91 us
  local copies, waits for them, and re-layouts: 12.3 us -> 13.8 us
  matrix products: 8.41 us -> 6.92 us
    ppermute x6, starting transfers between devices: 16.8 us -> 13.1 us  [group_sum(): return block + lax.ppermute(block, axis, pairs)]
    pallas_call x1 -> x2, Pallas kernels: 2.94 us -> 4.91 us  [line_sweep(): pl.pallas_call(sweep_kernel, out_shape=jax.ShapeDtypeStruct(drive_term.sh...]
    unnamed x20 -> x24, local copies, waits for them, and re-layouts: 5.78 us -> 6.02 us
  transfers between devices with their start and end apart: 23 -> 23, of which waited for: 17 -> 16; matrix products, arithmetic and copies ran while one was open for 6% -> 7% of each run, Pallas kernels for 0% -> 2%
where the time goes in v13:
time: 124 us; the launch traced here: 123 us
  starting transfers between devices  49.3 us (40%)
  waiting for transfers between devices  38 us (31%)
  local copies, waits for them, and re-layouts  13.8 us (11%)
  other arithmetic  8.59 us (7%)
  matrix products  6.92 us (6%)
  Pallas kernels  4.91 us (4%)
  between operations  1.31 us (1%)
    ppermute x15, starting transfers between devices, group_sum(): shifted.append(lax.ppermute(block, axis, pairs))  25.5 us
    all_to_all x1, waiting for transfers between devices, body(): lines = lax.all_to_all(packed, 'sec', 1, 0, tiled=True)  17.7 us
    ppermute x15, waiting for transfers between devices, group_sum(): shifted.append(lax.ppermute(block, axis, pairs))  14 us
    ppermute x6, starting transfers between devices, group_sum(): return block + lax.ppermute(block, axis, pairs)  13.1 us
    all_to_all x1, starting transfers between devices, body(): lines = lax.all_to_all(packed, 'sec', 1, 0, tiled=True)  7.03 us
    ppermute x6, waiting for transfers between devices, group_sum(): return block + lax.ppermute(block, axis, pairs)  6.29 us
    unnamed x24, local copies, waits for them, and re-layouts  6.02 us
    pallas_call x2, Pallas kernels, line_sweep(): pl.pallas_call(sweep_kernel, out_shape=jax.ShapeDtypeStruct(drive_term.sh...  4.91 us
  transfers between devices with their start and end apart: 23, of which 16 were waited for; matrix products, arithmetic and copies ran while one was open for 7% of the time, Pallas kernels for 2%

profile of v13, /device:TPU:32, one launch (start us, length us, event | category | flops | bytes accessed | tf_op | source)
XLA Modules:
  0.0 122.9 jit_solution(12799778439889610862)
XLA Ops:
  0.6 0.7 copy-done.9
  3.7 1.5 %copy.94 = f32[864,256]{0,1:T(8,128)S(1)} copy(f32[864,256]{1,0:T(8,128)} %param.12) | data formatting | bytes 1769472 | tf_op args[0]
  5.6 1.8 %copy.99 = f32[2,128,940]{2,0,1:T(2,128)} copy(f32[2,128,940]{2,1,0:T(8,128)S(1)} %bitcast.157) | data formatting | bytes 1925120 | tf_op jit(solution)/shard_map/transpose | solution.py:348
  7.4 7.0 %all-to-all-start = ((f32[2,128,940]{2,0,1:T(2,128)}), f32[2,128,940]{2,0,1:T(2,128)S(1)}, u32[]{:S(2)}, u32[]{:S(2)}) async-start(f32[2,128,940]{2,0,1:T(2,128)} %copy.99), calls=%async_computation | async-start | bytes 2097152 | tf_op jit(solution)/shard_map/all_to_all | solution.py:349
  14.4 17.7 %all-to-all-done = f32[2,128,940]{2,0,1:T(2,128)S(1)} async-done(((f32[2,128,940]{2,0,1:T(2,128)}), f32[2,128,940]{2,0,1:T(2,128)S(1)}, u32[]{:S(2)}, u32[]{:S(2)}) %all-to-all-start) | async-done | bytes 962592 | tf_op jit(solution)/shard_map/all_to_all | solution.py:349
  32.6 1.6 %fusion.2 = f32[256,5]{0,1:T(8,128)S(1)} fusion(f32[32,8,940]{2,1,0:T(8,128)S(1)} %bitcast.151, f32[5,13824]{1,0:T(8,128)} %constant.181.clone, s32[]{:T(128)S(6)} %select_n.134), kind=kOutput, calls=%fused_computation.6 | convolution fusion | flops 13271040 | bytes 951300 | tf_op jit(solution)/shard_map/dot_general | solution.py:357
  34.2 0.9 constant_dynamic-slice_fusion.12
  35.4 1.9 %collective-permute-start.3 = (f32[256,5]{0,1:T(8,128)S(1)}, f32[256,5]{0,1:T(8,128)S(1)}, u32[]{:S(2)}, u32[]{:S(2)}) collective-permute-start(f32[256,5]{0,1:T(8,128)S(1)} %add.281), channel_id=1, source_target_pairs={{6,0},{7,1},{0,2},{1,3},{2,4},{3,5},{4,6},{5,7},{14,8},{15,9},{8,1... | collective-permute-start | bytes 15368 | tf_op jit(solution)/shard_map/ppermute | solution.py:180
  37.3 1.4 %collective-permute-start.2 = (f32[256,5]{0,1:T(8,128)S(1)}, f32[256,5]{0,1:T(8,128)S(1)}, u32[]{:S(2)}, u32[]{:S(2)}) collective-permute-start(f32[256,5]{0,1:T(8,128)S(1)} %add.281), channel_id=1, source_target_pairs={{4,0},{5,1},{6,2},{7,3},{0,4},{1,5},{2,6},{3,7},{12,8},{13,9},{14,... | collective-permute-start | bytes 15368 | tf_op jit(solution)/shard_map/ppermute | solution.py:180
  38.7 2.0 %collective-permute-start.1 = (f32[256,5]{0,1:T(8,128)S(1)}, f32[256,5]{0,1:T(8,128)S(1)}, u32[]{:S(2)}, u32[]{:S(2)}) collective-permute-start(f32[256,5]{0,1:T(8,128)S(1)} %add.281), channel_id=1, source_target_pairs={{2,0},{3,1},{4,2},{5,3},{6,4},{7,5},{0,6},{1,7},{10,8},{11,9},{12,... | collective-permute-start | bytes 15368 | tf_op jit(solution)/shard_map/ppermute | solution.py:180
  41.2 0.7 collective-permute-done.2
  42.4 6.5 %collective-permute-start.4 = (f32[256,5]{0,1:T(8,128)S(1)}, f32[256,5]{0,1:T(8,128)S(1)}, u32[]{:S(2)}, u32[]{:S(2)}) collective-permute-start(f32[256,5]{0,1:T(8,128)S(1)} %add_bitcast_fusion.1), channel_id=1, source_target_pairs={{0,8},{1,9},{2,10},{3,11},{4,12},{5,13},{6,14},{7,15},{8,0},{9,1},... | collective-permute-start | bytes 15368 | tf_op jit(solution)/shard_map/ppermute | solution.py:171
  48.9 1.5 %fusion.4 = (f32[32,8,864]{2,1,0:T(8,128)}, f32[32,8,864]{2,1,0:T(8,128)}) fusion(f32[32,8,940]{2,1,0:T(8,128)S(1)} %bitcast.153, f32[32,8]{1,0:T(8,128)S(1)} %bitcast.181, f32[864]{0:T(1024)S(1)} %copy-done.6), kind=kLoop, calls=%fused_computation.11 | loop fusion | flops 884736 | bytes 2658688 | tf_op jit(solution)/shard_map/div | solution.py:362
  50.4 2.9 %shard_map.131 = f32[32,8,864]{2,1,0:T(8,128)} custom-call(f32[32,8,864]{2,1,0:T(8,128)} %get-tuple-element.30.rate_ref, f32[32,8,864]{2,1,0:T(8,128)} %get-tuple-element.29.drive_ref, f32[1,864]{1,0:T(1,128)} %constant.206.sign_ref), custom_call_target="tpu_custom_call" | custom-call | tf_op jit(solution)/shard_map/pallas_call | solution.py:315
  54.3 0.8 multiply_divide_fusion
  55.1 2.0 %shard_map.132 = f32[32,8,120]{2,1,0:T(8,128)} custom-call(f32[32,8,120]{2,1,0:T(8,128)} %get-tuple-element.32.rate_ref, f32[32,8,120]{2,1,0:T(8,128)} %get-tuple-element.31.drive_ref, f32[1,120]{1,0:T(1,128)} %constant.209.sign_ref), custom_call_target="tpu_custom_call" | custom-call | tf_op jit(solution)/shard_map/pallas_call | solution.py:315
  57.1 1.8 %convolution_add_fusion.1 = f32[32,8,864]{2,1,0:T(8,128)S(1)} fusion(f32[32,8,864]{2,1,0:T(8,128)S(1)} %copy-done, f32[32,8,120]{2,1,0:T(8,128)} %shard_map.132, f32[120,864,1]{1,0,2:T(8,128)S(1)} %bitcast.175), kind=kOutput, calls=%fused_computation.1 | convolution fusion | flops 318726144 | bytes 2307072 | tf_op jit(solution)/shard_map/dot_general | solution.py:377
  58.9 1.6 %fusion = f32[256,5]{0,1:T(8,128)S(1)} fusion(f32[32,8,864]{2,1,0:T(8,128)S(1)} %convolution_add_fusion.1, f32[5,13824]{1,0:T(8,128)} %constant.181.clone, s32[]{:T(128)S(6)} %select_n.134), kind=kOutput, calls=%fused_computation.4 | convolution fusion | flops 13271040 | bytes 918532 | tf_op jit(solution)/shard_map/dot_general | solution.py:381
  60.5 1.1 collective-permute-done.5
  61.8 2.4 %collective-permute-start.7 = (f32[256,5]{0,1:T(8,128)S(1)}, f32[256,5]{0,1:T(8,128)S(1)}, u32[]{:S(2)}, u32[]{:S(2)}) collective-permute-start(f32[256,5]{0,1:T(8,128)S(1)} %add.297), channel_id=1, source_target_pairs={{4,0},{5,1},{6,2},{7,3},{0,4},{1,5},{2,6},{3,7},{12,8},{13,9},{14,... | collective-permute-start | bytes 15368 | tf_op jit(solution)/shard_map/ppermute | solution.py:180
  64.2 1.9 %collective-permute-start.6 = (f32[256,5]{0,1:T(8,128)S(1)}, f32[256,5]{0,1:T(8,128)S(1)}, u32[]{:S(2)}, u32[]{:S(2)}) collective-permute-start(f32[256,5]{0,1:T(8,128)S(1)} %add.297), channel_id=1, source_target_pairs={{2,0},{3,1},{4,2},{5,3},{6,4},{7,5},{0,6},{1,7},{10,8},{11,9},{12,... | collective-permute-start | bytes 15368 | tf_op jit(solution)/shard_map/ppermute | solution.py:180
  66.4 1.5 %collective-permute-done.6 = f32[256,5]{0,1:T(8,128)S(1)} collective-permute-done((f32[256,5]{0,1:T(8,128)S(1)}, f32[256,5]{0,1:T(8,128)S(1)}, u32[]{:S(2)}, u32[]{:S(2)}) %collective-permute-start.6) | collective-permute-done | bytes 5152 | tf_op jit(solution)/shard_map/ppermute | solution.py:180
  67.8 3.4 %collective-permute-start.9 = (f32[256,5]{0,1:T(8,128)S(1)}, f32[256,5]{0,1:T(8,128)S(1)}, u32[]{:S(2)}, u32[]{:S(2)}) collective-permute-start(f32[256,5]{0,1:T(8,128)S(1)} %add_bitcast_fusion), channel_id=1, source_target_pairs={{0,8},{1,9},{2,10},{3,11},{4,12},{5,13},{6,14},{7,15},{8,0},{9,1},... | collective-permute-start | bytes 15368 | tf_op jit(solution)/shard_map/ppermute | solution.py:171
  71.8 3.9 %collective-permute-done.9 = f32[256,5]{0,1:T(8,128)S(1)} collective-permute-done((f32[256,5]{0,1:T(8,128)S(1)}, f32[256,5]{0,1:T(8,128)S(1)}, u32[]{:S(2)}, u32[]{:S(2)}) %collective-permute-start.9) | collective-permute-done | bytes 5152 | tf_op jit(solution)/shard_map/ppermute | solution.py:171
  77.2 1.7 %abs_reduce_fusion = (f32[864]{0:T(1024)S(1)}, f32[32,8,864]{2,1,0:T(8,128)S(1)}) fusion(f32[32,8,864]{2,1,0:T(8,128)S(1)} %convolution_add_fusion.1, f32[32,8,5]{2,1,0:T(8,128)S(1)} %copy.115, f32[5,13824]{1,0:T(8,128)} %constant.182.clone, s32[]{:T(128)S(6)} %select_n.134), kind=kOutput, calls=%fused_computation.9 | convolution fusion | flops 13933728 | bytes 1806724 | tf_op jit(solution)/shard_map/dot_general | solution.py:395
  78.9 0.8 dynamic-slice_multiply_fusion
  80.2 1.0 collective-permute-done.10
  81.2 1.4 %collective-permute-start.13 = (f32[26]{0:T(128)S(1)}, f32[26]{0:T(128)S(1)}, u32[]{:S(2)}, u32[]{:S(2)}) collective-permute-start(f32[26]{0:T(128)S(1)} %fusion.55), channel_id=1, source_target_pairs={{6,0},{7,1},{0,2},{1,3},{2,4},{3,5},{4,6},{5,7},{14,8},{15,9},{8,1... | collective-permute-start | bytes 320 | tf_op jit(solution)/shard_map/ppermute | solution.py:180
  82.6 2.9 %collective-permute-start.12 = (f32[26]{0:T(128)S(1)}, f32[26]{0:T(128)S(1)}, u32[]{:S(2)}, u32[]{:S(2)}) collective-permute-start(f32[26]{0:T(128)S(1)} %fusion.55), channel_id=1, source_target_pairs={{4,0},{5,1},{6,2},{7,3},{0,4},{1,5},{2,6},{3,7},{12,8},{13,9},{14,... | collective-permute-start | bytes 320 | tf_op jit(solution)/shard_map/ppermute | solution.py:180
  85.6 1.4 %collective-permute-done.12 = f32[26]{0:T(128)S(1)} collective-permute-done((f32[26]{0:T(128)S(1)}, f32[26]{0:T(128)S(1)}, u32[]{:S(2)}, u32[]{:S(2)}) %collective-permute-start.12) | collective-permute-done | bytes 136 | tf_op jit(solution)/shard_map/ppermute | solution.py:180
  87.0 2.0 %collective-permute-done.11 = f32[26]{0:T(128)S(1)} collective-permute-done((f32[26]{0:T(128)S(1)}, f32[26]{0:T(128)S(1)}, u32[]{:S(2)}, u32[]{:S(2)}) %collective-permute-start.11) | collective-permute-done | bytes 136 | tf_op jit(solution)/shard_map/ppermute | solution.py:180
  89.1 3.2 %collective-permute-start.14 = (f32[26]{0:T(128)S(1)}, f32[26]{0:T(128)S(1)}, u32[]{:S(2)}, u32[]{:S(2)}) collective-permute-start(f32[26]{0:T(128)S(1)} %fusion.33), channel_id=1, source_target_pairs={{0,8},{1,9},{2,10},{3,11},{4,12},{5,13},{6,14},{7,15},{8,0},{9,1},... | collective-permute-start | bytes 320 | tf_op jit(solution)/shard_map/ppermute | solution.py:171
  92.3 1.0 pad_maximum_fusion
  93.3 3.6 %all-to-all-start.1 = ((f32[32,8,869]{2,1,0:T(8,128)}), f32[32,8,869]{2,1,0:T(8,128)S(1)}, u32[]{:S(2)}, u32[]{:S(2)}) async-start(f32[32,8,869]{2,1,0:T(8,128)} %pad_maximum_fusion), calls=%async_computation.1 | async-start | bytes 1835008 | tf_op jit(solution)/shard_map/all_to_all | solution.py:403
  97.0 1.9 %collective-permute-start.17 = (f32[26]{0:T(128)S(1)}, f32[26]{0:T(128)S(1)}, u32[]{:S(2)}, u32[]{:S(2)}) collective-permute-start(f32[26]{0:T(128)S(1)} %fusion.54), channel_id=1, source_target_pairs={{48,0},{0,16},{16,32},{32,48},{112,64},{64,80},{80,96},{96,112},{1... | collective-permute-start | bytes 320 | tf_op jit(solution)/shard_map/ppermute | solution.py:180
  98.9 2.7 %collective-permute-start.16 = (f32[26]{0:T(128)S(1)}, f32[26]{0:T(128)S(1)}, u32[]{:S(2)}, u32[]{:S(2)}) collective-permute-start(f32[26]{0:T(128)S(1)} %fusion.54), channel_id=1, source_target_pairs={{32,0},{48,16},{0,32},{16,48},{96,64},{112,80},{64,96},{80,112},{1... | collective-permute-start | bytes 320 | tf_op jit(solution)/shard_map/ppermute | solution.py:180
  101.6 1.5 %collective-permute-start.15 = (f32[26]{0:T(128)S(1)}, f32[26]{0:T(128)S(1)}, u32[]{:S(2)}, u32[]{:S(2)}) collective-permute-start(f32[26]{0:T(128)S(1)} %fusion.54), channel_id=1, source_target_pairs={{16,0},{32,16},{48,32},{0,48},{80,64},{96,80},{112,96},{64,112},{1... | collective-permute-start | bytes 320 | tf_op jit(solution)/shard_map/ppermute | solution.py:180
  103.0 1.6 %collective-permute-done.17 = f32[26]{0:T(128)S(1)} collective-permute-done((f32[26]{0:T(128)S(1)}, f32[26]{0:T(128)S(1)}, u32[]{:S(2)}, u32[]{:S(2)}) %collective-permute-start.17) | collective-permute-done | bytes 136 | tf_op jit(solution)/shard_map/ppermute | solution.py:180
  105.0 2.4 %collective-permute-done.15 = f32[26]{0:T(128)S(1)} collective-permute-done((f32[26]{0:T(128)S(1)}, f32[26]{0:T(128)S(1)}, u32[]{:S(2)}, u32[]{:S(2)}) %collective-permute-start.15) | collective-permute-done | bytes 136 | tf_op jit(solution)/shard_map/ppermute | solution.py:180
  107.4 2.1 %collective-permute-start.20 = (f32[26]{0:T(128)S(1)}, f32[26]{0:T(128)S(1)}, u32[]{:S(2)}, u32[]{:S(2)}) collective-permute-start(f32[26]{0:T(128)S(1)} %fusion.53), channel_id=1, source_target_pairs={{192,0},{208,16},{224,32},{240,48},{0,64},{16,80},{32,96},{48,112}... | collective-permute-start | bytes 320 | tf_op jit(solution)/shard_map/ppermute | solution.py:180
  109.5 3.2 %collective-permute-start.19 = (f32[26]{0:T(128)S(1)}, f32[26]{0:T(128)S(1)}, u32[]{:S(2)}, u32[]{:S(2)}) collective-permute-start(f32[26]{0:T(128)S(1)} %fusion.53), channel_id=1, source_target_pairs={{128,0},{144,16},{160,32},{176,48},{192,64},{208,80},{224,96},{240... | collective-permute-start | bytes 320 | tf_op jit(solution)/shard_map/ppermute | solution.py:180
  112.8 1.7 %collective-permute-done.19 = f32[26]{0:T(128)S(1)} collective-permute-done((f32[26]{0:T(128)S(1)}, f32[26]{0:T(128)S(1)}, u32[]{:S(2)}, u32[]{:S(2)}) %collective-permute-start.19) | collective-permute-done | bytes 136 | tf_op jit(solution)/shard_map/ppermute | solution.py:180
  114.5 1.6 %collective-permute-done.18 = f32[26]{0:T(128)S(1)} collective-permute-done((f32[26]{0:T(128)S(1)}, f32[26]{0:T(128)S(1)}, u32[]{:S(2)}, u32[]{:S(2)}) %collective-permute-start.18) | collective-permute-done | bytes 136 | tf_op jit(solution)/shard_map/ppermute | solution.py:180
  117.0 0.7 copy-done.7
  117.7 1.3 %multiply_bitcast_fusion.1 = (f32[1,24]{1,0:T(1,128)S(1)}, f32[1,24]{1,0:T(1,128)S(1)}, f32[1,24]{1,0:T(1,128)S(1)}, f32[1,24]{1,0:T(1,128)S(1)}) fusion(f32[24]{0:T(128)S(1)} %copy-done.5, f32[1,26]{1,0:T(1,128)S(1)} %fusion.19, f32[1,24]{1,0:T(1,128)S(1)} %copy-done.7, f32[5,24]{1,0:T(8,128)S(1)} %fusion.14, f32[]{:T(128)} %bitcast.55, f32[]{:T(128)} %bitcast.56), kind=kLoop, calls=%fused_computation.90 | loop fusion | flops 480 | bytes 1160 | tf_op jit(solution)/shard_map/stack | solution.py:418
  119.2 1.3 %add_bitcast_fusion.2 = f32[24]{0:T(128)S(1)} fusion(f32[1,24]{1,0:T(1,128)S(1)} %copy-done.7, f32[1,24]{1,0:T(1,128)S(1)} %get-tuple-element.13, f32[1,24]{1,0:T(1,128)S(1)} %get-tuple-element.12, f32[5,24]{1,0:T(8,128)S(1)} %fusion.12, f32[]{:T(128)} %bitcast.56, f32[]{:T(128)} %bitcast.55), kind=kLoop, calls=%fused_computation.87 | loop fusion | flops 432 | bytes 872 | tf_op jit(solution)/shard_map/sub | solution.py:425
  120.8 0.7 copy.121
  121.8 1.1 multiply_add_fusion
  (123 shorter events, 10.6 us)
Async XLA Ops:
  0.6 0.7 copy-start.9
  1.3 0.8 copy-start.2
  2.1 0.8 copy-start.3
  2.8 0.8 copy-start.4
  7.4 24.7 %all-to-all-start = ((f32[2,128,940]{2,0,1:T(2,128)}), f32[2,128,940]{2,0,1:T(2,128)S(1)}, u32[]{:S(2)}, u32[]{:S(2)}) async-start(f32[2,128,940]{2,0,1:T(2,128)} %copy.99), calls=%async_computation | async-start | bytes 2097152 | tf_op jit(solution)/shard_map/all_to_all | solution.py:349
  32.6 8.2 %copy-start.1 = (f32[24,864]{1,0:T(8,128)S(1)}, f32[24,864]{1,0:T(8,128)}, u32[]{:S(2)}) copy-start(f32[24,864]{1,0:T(8,128)} %constant.187.clone) | copy-start | bytes 248836
  34.2 1.2 %collective-permute-start = (f32[256,5]{0,1:T(8,128)S(1)}, f32[256,5]{0,1:T(8,128)S(1)}, u32[]{:S(2)}, u32[]{:S(2)}) collective-permute-start(f32[256,5]{0,1:T(8,128)S(1)} %fusion.2), channel_id=1, source_target_pairs={{0,1},{1,0},{2,3},{3,2},{4,5},{5,4},{6,7},{7,6},{8,9},{9,8},{10,11... | collective-permute-start | bytes 15368 | tf_op jit(solution)/shard_map/ppermute | solution.py:171
  35.4 5.8 %collective-permute-start.3 = (f32[256,5]{0,1:T(8,128)S(1)}, f32[256,5]{0,1:T(8,128)S(1)}, u32[]{:S(2)}, u32[]{:S(2)}) collective-permute-start(f32[256,5]{0,1:T(8,128)S(1)} %add.281), channel_id=1, source_target_pairs={{6,0},{7,1},{0,2},{1,3},{2,4},{3,5},{4,6},{5,7},{14,8},{15,9},{8,1... | collective-permute-start | bytes 15368 | tf_op jit(solution)/shard_map/ppermute | solution.py:180
  37.3 4.5 %collective-permute-start.2 = (f32[256,5]{0,1:T(8,128)S(1)}, f32[256,5]{0,1:T(8,128)S(1)}, u32[]{:S(2)}, u32[]{:S(2)}) collective-permute-start(f32[256,5]{0,1:T(8,128)S(1)} %add.281), channel_id=1, source_target_pairs={{4,0},{5,1},{6,2},{7,3},{0,4},{1,5},{2,6},{3,7},{12,8},{13,9},{14,... | collective-permute-start | bytes 15368 | tf_op jit(solution)/shard_map/ppermute | solution.py:180
  38.7 3.7 %collective-permute-start.1 = (f32[256,5]{0,1:T(8,128)S(1)}, f32[256,5]{0,1:T(8,128)S(1)}, u32[]{:S(2)}, u32[]{:S(2)}) collective-permute-start(f32[256,5]{0,1:T(8,128)S(1)} %add.281), channel_id=1, source_target_pairs={{2,0},{3,1},{4,2},{5,3},{6,4},{7,5},{0,6},{1,7},{10,8},{11,9},{12,... | collective-permute-start | bytes 15368 | tf_op jit(solution)/shard_map/ppermute | solution.py:180
  42.4 6.5 %copy-start.6 = (f32[864]{0:T(1024)S(1)}, f32[864]{0:T(1024)}, u32[]{:S(2)}) copy-start(f32[864]{0:T(1024)} %constant.205) | copy-start | bytes 10372
  42.4 10.9 %collective-permute-start.4 = (f32[256,5]{0,1:T(8,128)S(1)}, f32[256,5]{0,1:T(8,128)S(1)}, u32[]{:S(2)}, u32[]{:S(2)}) collective-permute-start(f32[256,5]{0,1:T(8,128)S(1)} %add_bitcast_fusion.1), channel_id=1, source_target_pairs={{0,8},{1,9},{2,10},{3,11},{4,12},{5,13},{6,14},{7,15},{8,0},{9,1},... | collective-permute-start | bytes 15368 | tf_op jit(solution)/shard_map/ppermute | solution.py:171
  53.5 3.6 %copy-start = (f32[32,8,864]{2,1,0:T(8,128)S(1)}, f32[32,8,864]{2,1,0:T(8,128)}, u32[]{:S(2)}) copy-start(f32[32,8,864]{2,1,0:T(8,128)} %shard_map.131) | copy-start | bytes 2654212
  53.6 0.7 copy-start.10
  60.4 1.2 %collective-permute-start.5 = (f32[256,5]{0,1:T(8,128)S(1)}, f32[256,5]{0,1:T(8,128)S(1)}, u32[]{:S(2)}, u32[]{:S(2)}) collective-permute-start(f32[256,5]{0,1:T(8,128)S(1)} %fusion), channel_id=1, source_target_pairs={{0,1},{1,0},{2,3},{3,2},{4,5},{5,4},{6,7},{7,6},{8,9},{9,8},{10,11... | collective-permute-start | bytes 15368 | tf_op jit(solution)/shard_map/ppermute | solution.py:171
  61.7 4.4 %collective-permute-start.8 = (f32[256,5]{0,1:T(8,128)S(1)}, f32[256,5]{0,1:T(8,128)S(1)}, u32[]{:S(2)}, u32[]{:S(2)}) collective-permute-start(f32[256,5]{0,1:T(8,128)S(1)} %add.297), channel_id=1, source_target_pairs={{6,0},{7,1},{0,2},{1,3},{2,4},{3,5},{4,6},{5,7},{14,8},{15,9},{8,1... | collective-permute-start | bytes 15368 | tf_op jit(solution)/shard_map/ppermute | solution.py:180
  61.8 4.5 %collective-permute-start.7 = (f32[256,5]{0,1:T(8,128)S(1)}, f32[256,5]{0,1:T(8,128)S(1)}, u32[]{:S(2)}, u32[]{:S(2)}) collective-permute-start(f32[256,5]{0,1:T(8,128)S(1)} %add.297), channel_id=1, source_target_pairs={{4,0},{5,1},{6,2},{7,3},{0,4},{1,5},{2,6},{3,7},{12,8},{13,9},{14,... | collective-permute-start | bytes 15368 | tf_op jit(solution)/shard_map/ppermute | solution.py:180
  64.2 3.7 %collective-permute-start.6 = (f32[256,5]{0,1:T(8,128)S(1)}, f32[256,5]{0,1:T(8,128)S(1)}, u32[]{:S(2)}, u32[]{:S(2)}) collective-permute-start(f32[256,5]{0,1:T(8,128)S(1)} %add.297), channel_id=1, source_target_pairs={{2,0},{3,1},{4,2},{5,3},{6,4},{7,5},{0,6},{1,7},{10,8},{11,9},{12,... | collective-permute-start | bytes 15368 | tf_op jit(solution)/shard_map/ppermute | solution.py:180
  67.8 7.8 %collective-permute-start.9 = (f32[256,5]{0,1:T(8,128)S(1)}, f32[256,5]{0,1:T(8,128)S(1)}, u32[]{:S(2)}, u32[]{:S(2)}) collective-permute-start(f32[256,5]{0,1:T(8,128)S(1)} %add_bitcast_fusion), channel_id=1, source_target_pairs={{0,8},{1,9},{2,10},{3,11},{4,12},{5,13},{6,14},{7,15},{8,0},{9,1},... | collective-permute-start | bytes 15368 | tf_op jit(solution)/shard_map/ppermute | solution.py:171
  80.0 1.1 collective-permute-start.10
  81.2 4.4 %collective-permute-start.13 = (f32[26]{0:T(128)S(1)}, f32[26]{0:T(128)S(1)}, u32[]{:S(2)}, u32[]{:S(2)}) collective-permute-start(f32[26]{0:T(128)S(1)} %fusion.55), channel_id=1, source_target_pairs={{6,0},{7,1},{0,2},{1,3},{2,4},{3,5},{4,6},{5,7},{14,8},{15,9},{8,1... | collective-permute-start | bytes 320 | tf_op jit(solution)/shard_map/ppermute | solution.py:180
  82.6 4.4 %collective-permute-start.12 = (f32[26]{0:T(128)S(1)}, f32[26]{0:T(128)S(1)}, u32[]{:S(2)}, u32[]{:S(2)}) collective-permute-start(f32[26]{0:T(128)S(1)} %fusion.55), channel_id=1, source_target_pairs={{4,0},{5,1},{6,2},{7,3},{0,4},{1,5},{2,6},{3,7},{12,8},{13,9},{14,... | collective-permute-start | bytes 320 | tf_op jit(solution)/shard_map/ppermute | solution.py:180
  85.5 3.5 %collective-permute-start.11 = (f32[26]{0:T(128)S(1)}, f32[26]{0:T(128)S(1)}, u32[]{:S(2)}, u32[]{:S(2)}) collective-permute-start(f32[26]{0:T(128)S(1)} %fusion.55), channel_id=1, source_target_pairs={{2,0},{3,1},{4,2},{5,3},{6,4},{7,5},{0,6},{1,7},{10,8},{11,9},{12,... | collective-permute-start | bytes 320 | tf_op jit(solution)/shard_map/ppermute | solution.py:180
  89.1 7.9 %collective-permute-start.14 = (f32[26]{0:T(128)S(1)}, f32[26]{0:T(128)S(1)}, u32[]{:S(2)}, u32[]{:S(2)}) collective-permute-start(f32[26]{0:T(128)S(1)} %fusion.33), channel_id=1, source_target_pairs={{0,8},{1,9},{2,10},{3,11},{4,12},{5,13},{6,14},{7,15},{8,0},{9,1},... | collective-permute-start | bytes 320 | tf_op jit(solution)/shard_map/ppermute | solution.py:171
  93.3 27.3 %all-to-all-start.1 = ((f32[32,8,869]{2,1,0:T(8,128)}), f32[32,8,869]{2,1,0:T(8,128)S(1)}, u32[]{:S(2)}, u32[]{:S(2)}) async-start(f32[32,8,869]{2,1,0:T(8,128)} %pad_maximum_fusion), calls=%async_computation.1 | async-start | bytes 1835008 | tf_op jit(solution)/shard_map/all_to_all | solution.py:403
  97.0 7.6 %collective-permute-start.17 = (f32[26]{0:T(128)S(1)}, f32[26]{0:T(128)S(1)}, u32[]{:S(2)}, u32[]{:S(2)}) collective-permute-start(f32[26]{0:T(128)S(1)} %fusion.54), channel_id=1, source_target_pairs={{48,0},{0,16},{16,32},{32,48},{112,64},{64,80},{80,96},{96,112},{1... | collective-permute-start | bytes 320 | tf_op jit(solution)/shard_map/ppermute | solution.py:180
  98.9 6.1 %collective-permute-start.16 = (f32[26]{0:T(128)S(1)}, f32[26]{0:T(128)S(1)}, u32[]{:S(2)}, u32[]{:S(2)}) collective-permute-start(f32[26]{0:T(128)S(1)} %fusion.54), channel_id=1, source_target_pairs={{32,0},{48,16},{0,32},{16,48},{96,64},{112,80},{64,96},{80,112},{1... | collective-permute-start | bytes 320 | tf_op jit(solution)/shard_map/ppermute | solution.py:180
  101.6 5.8 %collective-permute-start.15 = (f32[26]{0:T(128)S(1)}, f32[26]{0:T(128)S(1)}, u32[]{:S(2)}, u32[]{:S(2)}) collective-permute-start(f32[26]{0:T(128)S(1)} %fusion.54), channel_id=1, source_target_pairs={{16,0},{32,16},{48,32},{0,48},{80,64},{96,80},{112,96},{64,112},{1... | collective-permute-start | bytes 320 | tf_op jit(solution)/shard_map/ppermute | solution.py:180
  107.4 5.4 %collective-permute-start.20 = (f32[26]{0:T(128)S(1)}, f32[26]{0:T(128)S(1)}, u32[]{:S(2)}, u32[]{:S(2)}) collective-permute-start(f32[26]{0:T(128)S(1)} %fusion.53), channel_id=1, source_target_pairs={{192,0},{208,16},{224,32},{240,48},{0,64},{16,80},{32,96},{48,112}... | collective-permute-start | bytes 320 | tf_op jit(solution)/shard_map/ppermute | solution.py:180
  109.5 5.0 %collective-permute-start.19 = (f32[26]{0:T(128)S(1)}, f32[26]{0:T(128)S(1)}, u32[]{:S(2)}, u32[]{:S(2)}) collective-permute-start(f32[26]{0:T(128)S(1)} %fusion.53), channel_id=1, source_target_pairs={{128,0},{144,16},{160,32},{176,48},{192,64},{208,80},{224,96},{240... | collective-permute-start | bytes 320 | tf_op jit(solution)/shard_map/ppermute | solution.py:180
  112.6 3.5 %collective-permute-start.18 = (f32[26]{0:T(128)S(1)}, f32[26]{0:T(128)S(1)}, u32[]{:S(2)}, u32[]{:S(2)}) collective-permute-start(f32[26]{0:T(128)S(1)} %fusion.53), channel_id=1, source_target_pairs={{64,0},{80,16},{96,32},{112,48},{128,64},{144,80},{160,96},{176,11... | collective-permute-start | bytes 320 | tf_op jit(solution)/shard_map/ppermute | solution.py:180
  116.2 0.7 copy-start.5
  116.2 0.7 copy-start.8
  117.0 0.7 copy-start.7

commit v14 on v13

--- a/solution.py
+++ b/solution.py
@@ -190,12 +190,10 @@
     bits = count.bit_length() - 1
     plan = []
     bit = 0
-    if axis == "vel" and bits % 2 == 1:
+    if axis == "vel" and bits >= 2:
         plan.append((0, 2))
-        bit = 1
-    elif axis == "vel" and bits >= 2:
-        plan.append((0, 2))
-        bit = 1
+        plan.append((1, 1 << (bits - 1)))
+        return plan
     while bit + 1 < bits:
         plan.append((bit, 4))
         bit += 2

time: 124 us -> 145 us (1.17)
  starting transfers between devices: 49.3 us -> 70.4 us
  waiting for transfers between devices: 38 us -> 34.2 us
  local copies, waits for them, and re-layouts: 13.8 us -> 16.1 us
    ppermute x15 -> x27, starting transfers between devices: 25.5 us -> 59.6 us  [group_sum(): shifted.append(lax.ppermute(block, axis, pairs))]
    ppermute x6 -> x3, starting transfers between devices: 13.1 us -> 0.11 us  [group_sum(): return block + lax.ppermute(block, axis, pairs)]
    ppermute x6 -> x3, waiting for transfers between devices: 6.29 us -> 1.73 us  [group_sum(): return block + lax.ppermute(block, axis, pairs)]
    ppermute x15 -> x27, waiting for transfers between devices: 14 us -> 15.7 us  [group_sum(): shifted.append(lax.ppermute(block, axis, pairs))]
    unnamed x24 -> x36, local copies, waits for them, and re-layouts: 6.02 us -> 6.62 us
  transfers between devices with their start and end apart: 23 -> 32, of which waited for: 16 -> 13; matrix products, arithmetic and copies ran while one was open for 7% -> 6% of each run, Pallas kernels for 2% -> 2%
where the time goes in v14:
time: 145 us; the launch traced here: 143 us
  starting transfers between devices  70.4 us (49%)
  waiting for transfers between devices  34.2 us (24%)
  local copies, waits for them, and re-layouts  16.1 us (11%)
  other arithmetic  8.74 us (6%)
  matrix products  6.9 us (5%)
  Pallas kernels  4.9 us (3%)
  between operations  1.65 us (1%)
    ppermute x27, starting transfers between devices, group_sum(): shifted.append(lax.ppermute(block, axis, pairs))  59.6 us
    all_to_all x1, waiting for transfers between devices, body(): lines = lax.all_to_all(packed, 'sec', 1, 0, tiled=True)  16.7 us
    ppermute x27, waiting for transfers between devices, group_sum(): shifted.append(lax.ppermute(block, axis, pairs))  15.7 us
    all_to_all x1, starting transfers between devices, body(): lines = lax.all_to_all(packed, 'sec', 1, 0, tiled=True)  7.03 us
    unnamed x36, local copies, waits for them, and re-layouts  6.62 us
    pallas_call x2, Pallas kernels, line_sweep(): pl.pallas_call(sweep_kernel, out_shape=jax.ShapeDtypeStruct(drive_term.sh...  4.9 us
    all_to_all x1, starting transfers between devices, body(): back = lax.all_to_all(back, 'sec', 0, 1, tiled=True)  3.63 us
  transfers between devices with their start and end apart: 32, of which 13 were waited for; matrix products, arithmetic and copies ran while one was open for 6% of the time, Pallas kernels for 2%

profile of v14, /device:TPU:32, one launch (start us, length us, event | category | flops | bytes accessed | tf_op | source)
XLA Modules:
  0.0 142.9 jit_solution(5178936106850567487)
XLA Ops:
  3.7 1.5 %copy.139 = f32[864,256]{0,1:T(8,128)S(1)} copy(f32[864,256]{1,0:T(8,128)} %param.12) | data formatting | bytes 1769472 | tf_op args[0]
  5.6 1.8 %copy.144 = f32[2,128,940]{2,0,1:T(2,128)} copy(f32[2,128,940]{2,1,0:T(8,128)S(1)} %bitcast.199) | data formatting | bytes 1925120 | tf_op jit(solution)/shard_map/transpose | solution.py:346
  7.4 7.0 %all-to-all-start = ((f32[2,128,940]{2,0,1:T(2,128)}), f32[2,128,940]{2,0,1:T(2,128)S(1)}, u32[]{:S(2)}, u32[]{:S(2)}) async-start(f32[2,128,940]{2,0,1:T(2,128)} %copy.144), calls=%async_computation | async-start | bytes 2097152 | tf_op jit(solution)/shard_map/all_to_all | solution.py:347
  15.4 16.7 %all-to-all-done = f32[2,128,940]{2,0,1:T(2,128)S(1)} async-done(((f32[2,128,940]{2,0,1:T(2,128)}), f32[2,128,940]{2,0,1:T(2,128)S(1)}, u32[]{:S(2)}, u32[]{:S(2)}) %all-to-all-start) | async-done | bytes 962592 | tf_op jit(solution)/shard_map/all_to_all | solution.py:347
  32.6 1.6 %fusion.2 = f32[256,5]{0,1:T(8,128)S(1)} fusion(f32[32,8,940]{2,1,0:T(8,128)S(1)} %bitcast.192, f32[5,13824]{1,0:T(8,128)} %constant.250.clone, s32[]{:T(128)S(6)} %select_n.187), kind=kOutput, calls=%fused_computation.6 | convolution fusion | flops 13271040 | bytes 951300 | tf_op jit(solution)/shard_map/dot_general | solution.py:355
  36.1 1.5 %fusion.4 = (f32[32,8,864]{2,1,0:T(8,128)}, f32[32,8,864]{2,1,0:T(8,128)}) fusion(f32[32,8,940]{2,1,0:T(8,128)S(1)} %bitcast.194, f32[32,8]{1,0:T(8,128)S(1)} %bitcast.222, f32[864]{0:T(1024)S(1)} %copy-done.6), kind=kLoop, calls=%fused_computation.11 | loop fusion | flops 884736 | bytes 2658688 | tf_op jit(solution)/shard_map/div | solution.py:360
  37.6 2.9 %shard_map.131 = f32[32,8,864]{2,1,0:T(8,128)} custom-call(f32[32,8,864]{2,1,0:T(8,128)} %get-tuple-element.32.rate_ref, f32[32,8,864]{2,1,0:T(8,128)} %get-tuple-element.31.drive_ref, f32[1,864]{1,0:T(1,128)} %constant.275.sign_ref), custom_call_target="tpu_custom_call" | custom-call | tf_op jit(solution)/shard_map/pallas_call | solution.py:313
  40.5 3.3 %collective-permute-start.6 = (f32[256,5]{0,1:T(8,128)S(1)}, f32[256,5]{0,1:T(8,128)S(1)}, u32[]{:S(2)}, u32[]{:S(2)}) collective-permute-start(f32[256,5]{0,1:T(8,128)S(1)} %get-tuple-element.19), channel_id=1, source_target_pairs={{12,0},{13,1},{14,2},{15,3},{0,4},{1,5},{2,6},{3,7},{4,8},{5,9},{6... | collective-permute-start | bytes 15368 | tf_op jit(solution)/shard_map/ppermute | solution.py:180
  43.8 4.4 %collective-permute-start.5 = (f32[256,5]{0,1:T(8,128)S(1)}, f32[256,5]{0,1:T(8,128)S(1)}, u32[]{:S(2)}, u32[]{:S(2)}) collective-permute-start(f32[256,5]{0,1:T(8,128)S(1)} %get-tuple-element.19), channel_id=1, source_target_pairs={{10,0},{11,1},{12,2},{13,3},{14,4},{15,5},{0,6},{1,7},{2,8},{3,9},... | collective-permute-start | bytes 15368 | tf_op jit(solution)/shard_map/ppermute | solution.py:180
  48.1 2.1 %collective-permute-start.4 = (f32[256,5]{0,1:T(8,128)S(1)}, f32[256,5]{0,1:T(8,128)S(1)}, u32[]{:S(2)}, u32[]{:S(2)}) collective-permute-start(f32[256,5]{0,1:T(8,128)S(1)} %get-tuple-element.19), channel_id=1, source_target_pairs={{8,0},{9,1},{10,2},{11,3},{12,4},{13,5},{14,6},{15,7},{0,8},{1,9},... | collective-permute-start | bytes 15368 | tf_op jit(solution)/shard_map/ppermute | solution.py:180
  50.3 3.4 %collective-permute-start.3 = (f32[256,5]{0,1:T(8,128)S(1)}, f32[256,5]{0,1:T(8,128)S(1)}, u32[]{:S(2)}, u32[]{:S(2)}) collective-permute-start(f32[256,5]{0,1:T(8,128)S(1)} %get-tuple-element.19), channel_id=1, source_target_pairs={{6,0},{7,1},{8,2},{9,3},{10,4},{11,5},{12,6},{13,7},{14,8},{15,9},... | collective-permute-start | bytes 15368 | tf_op jit(solution)/shard_map/ppermute | solution.py:180
  53.6 1.5 %collective-permute-start.2 = (f32[256,5]{0,1:T(8,128)S(1)}, f32[256,5]{0,1:T(8,128)S(1)}, u32[]{:S(2)}, u32[]{:S(2)}) collective-permute-start(f32[256,5]{0,1:T(8,128)S(1)} %get-tuple-element.19), channel_id=1, source_target_pairs={{4,0},{5,1},{6,2},{7,3},{8,4},{9,5},{10,6},{11,7},{12,8},{13,9},{1... | collective-permute-start | bytes 15368 | tf_op jit(solution)/shard_map/ppermute | solution.py:180
  55.1 3.1 %collective-permute-done.2 = f32[256,5]{0,1:T(8,128)S(1)} collective-permute-done((f32[256,5]{0,1:T(8,128)S(1)}, f32[256,5]{0,1:T(8,128)S(1)}, u32[]{:S(2)}, u32[]{:S(2)}) %collective-permute-start.2) | collective-permute-done | bytes 5152 | tf_op jit(solution)/shard_map/ppermute | solution.py:180
  58.2 3.4 %collective-permute-start.7 = (f32[256,5]{0,1:T(8,128)S(1)}, f32[256,5]{0,1:T(8,128)S(1)}, u32[]{:S(2)}, u32[]{:S(2)}) collective-permute-start(f32[256,5]{0,1:T(8,128)S(1)} %get-tuple-element.19), channel_id=1, source_target_pairs={{14,0},{15,1},{0,2},{1,3},{2,4},{3,5},{4,6},{5,7},{6,8},{7,9},{8,1... | collective-permute-start | bytes 15368 | tf_op jit(solution)/shard_map/ppermute | solution.py:180
  61.7 1.3 collective-permute-done.7
  64.9 2.0 %shard_map.132 = f32[32,8,120]{2,1,0:T(8,128)} custom-call(f32[32,8,120]{2,1,0:T(8,128)} %get-tuple-element.34.rate_ref, f32[32,8,120]{2,1,0:T(8,128)} %get-tuple-element.33.drive_ref, f32[1,120]{1,0:T(1,128)} %constant.278.sign_ref), custom_call_target="tpu_custom_call" | custom-call | tf_op jit(solution)/shard_map/pallas_call | solution.py:313
  66.8 1.8 %convolution_add_fusion.1 = f32[32,8,864]{2,1,0:T(8,128)S(1)} fusion(f32[32,8,864]{2,1,0:T(8,128)S(1)} %copy-done, f32[32,8,120]{2,1,0:T(8,128)} %shard_map.132, f32[120,864,1]{1,0,2:T(8,128)S(1)} %bitcast.217), kind=kOutput, calls=%fused_computation.1 | convolution fusion | flops 318726144 | bytes 2307072 | tf_op jit(solution)/shard_map/dot_general | solution.py:375
  68.6 1.6 %fusion = f32[256,5]{0,1:T(8,128)S(1)} fusion(f32[32,8,864]{2,1,0:T(8,128)S(1)} %convolution_add_fusion.1, f32[5,13824]{1,0:T(8,128)} %constant.250.clone, s32[]{:T(128)S(6)} %select_n.187), kind=kOutput, calls=%fused_computation.4 | convolution fusion | flops 13271040 | bytes 918532 | tf_op jit(solution)/shard_map/dot_general | solution.py:379
  71.4 1.1 collective-permute-start.9
  73.1 2.8 %collective-permute-start.14 = (f32[256,5]{0,1:T(8,128)S(1)}, f32[256,5]{0,1:T(8,128)S(1)}, u32[]{:S(2)}, u32[]{:S(2)}) collective-permute-start(f32[256,5]{0,1:T(8,128)S(1)} %get-tuple-element.17), channel_id=1, source_target_pairs={{12,0},{13,1},{14,2},{15,3},{0,4},{1,5},{2,6},{3,7},{4,8},{5,9},{6... | collective-permute-start | bytes 15368 | tf_op jit(solution)/shard_map/ppermute | solution.py:180
  76.6 3.7 %collective-permute-start.12 = (f32[256,5]{0,1:T(8,128)S(1)}, f32[256,5]{0,1:T(8,128)S(1)}, u32[]{:S(2)}, u32[]{:S(2)}) collective-permute-start(f32[256,5]{0,1:T(8,128)S(1)} %get-tuple-element.17), channel_id=1, source_target_pairs={{8,0},{9,1},{10,2},{11,3},{12,4},{13,5},{14,6},{15,7},{0,8},{1,9},... | collective-permute-start | bytes 15368 | tf_op jit(solution)/shard_map/ppermute | solution.py:180
  80.3 2.6 %collective-permute-start.11 = (f32[256,5]{0,1:T(8,128)S(1)}, f32[256,5]{0,1:T(8,128)S(1)}, u32[]{:S(2)}, u32[]{:S(2)}) collective-permute-start(f32[256,5]{0,1:T(8,128)S(1)} %get-tuple-element.17), channel_id=1, source_target_pairs={{6,0},{7,1},{8,2},{9,3},{10,4},{11,5},{12,6},{13,7},{14,8},{15,9},... | collective-permute-start | bytes 15368 | tf_op jit(solution)/shard_map/ppermute | solution.py:180
  82.9 1.3 collective-permute-start.10
  84.2 3.2 %collective-permute-done.10 = f32[256,5]{0,1:T(8,128)S(1)} collective-permute-done((f32[256,5]{0,1:T(8,128)S(1)}, f32[256,5]{0,1:T(8,128)S(1)}, u32[]{:S(2)}, u32[]{:S(2)}) %collective-permute-start.10) | collective-permute-done | bytes 5152 | tf_op jit(solution)/shard_map/ppermute | solution.py:180
  87.5 2.6 %collective-permute-start.15 = (f32[256,5]{0,1:T(8,128)S(1)}, f32[256,5]{0,1:T(8,128)S(1)}, u32[]{:S(2)}, u32[]{:S(2)}) collective-permute-start(f32[256,5]{0,1:T(8,128)S(1)} %get-tuple-element.17), channel_id=1, source_target_pairs={{14,0},{15,1},{0,2},{1,3},{2,4},{3,5},{4,6},{5,7},{6,8},{7,9},{8,1... | collective-permute-start | bytes 15368 | tf_op jit(solution)/shard_map/ppermute | solution.py:180
  90.1 1.3 collective-permute-done.15
  94.8 1.7 %abs_reduce_fusion = (f32[864]{0:T(1024)S(1)}, f32[32,8,864]{2,1,0:T(8,128)S(1)}) fusion(f32[32,8,864]{2,1,0:T(8,128)S(1)} %convolution_add_fusion.1, f32[32,8,5]{2,1,0:T(8,128)S(1)} %copy.170, f32[5,13824]{1,0:T(8,128)} %constant.251.clone, s32[]{:T(128)S(6)} %select_n.187), kind=kOutput, calls=%fused_computation.9 | convolution fusion | flops 13933728 | bytes 1806724 | tf_op jit(solution)/shard_map/dot_general | solution.py:393
  97.8 1.0 pad_maximum_fusion
  98.8 3.6 %all-to-all-start.1 = ((f32[32,8,869]{2,1,0:T(8,128)}), f32[32,8,869]{2,1,0:T(8,128)S(1)}, u32[]{:S(2)}, u32[]{:S(2)}) async-start(f32[32,8,869]{2,1,0:T(8,128)} %pad_maximum_fusion), calls=%async_computation.1 | async-start | bytes 1835008 | tf_op jit(solution)/shard_map/all_to_all | solution.py:401
  102.5 2.3 %collective-permute-start.23 = (f32[26]{0:T(128)S(1)}, f32[26]{0:T(128)S(1)}, u32[]{:S(2)}, u32[]{:S(2)}) collective-permute-start(f32[26]{0:T(128)S(1)} %fusion.73), channel_id=1, source_target_pairs={{14,0},{15,1},{0,2},{1,3},{2,4},{3,5},{4,6},{5,7},{6,8},{7,9},{8,1... | collective-permute-start | bytes 320 | tf_op jit(solution)/shard_map/ppermute | solution.py:180
  104.8 1.7 %collective-permute-start.22 = (f32[26]{0:T(128)S(1)}, f32[26]{0:T(128)S(1)}, u32[]{:S(2)}, u32[]{:S(2)}) collective-permute-start(f32[26]{0:T(128)S(1)} %fusion.73), channel_id=1, source_target_pairs={{12,0},{13,1},{14,2},{15,3},{0,4},{1,5},{2,6},{3,7},{4,8},{5,9},{6... | collective-permute-start | bytes 320 | tf_op jit(solution)/shard_map/ppermute | solution.py:180
  106.5 2.2 %collective-permute-start.21 = (f32[26]{0:T(128)S(1)}, f32[26]{0:T(128)S(1)}, u32[]{:S(2)}, u32[]{:S(2)}) collective-permute-start(f32[26]{0:T(128)S(1)} %fusion.73), channel_id=1, source_target_pairs={{10,0},{11,1},{12,2},{13,3},{14,4},{15,5},{0,6},{1,7},{2,8},{3,9},... | collective-permute-start | bytes 320 | tf_op jit(solution)/shard_map/ppermute | solution.py:180
  108.7 2.1 %collective-permute-start.20 = (f32[26]{0:T(128)S(1)}, f32[26]{0:T(128)S(1)}, u32[]{:S(2)}, u32[]{:S(2)}) collective-permute-start(f32[26]{0:T(128)S(1)} %fusion.73), channel_id=1, source_target_pairs={{8,0},{9,1},{10,2},{11,3},{12,4},{13,5},{14,6},{15,7},{0,8},{1,9},... | collective-permute-start | bytes 320 | tf_op jit(solution)/shard_map/ppermute | solution.py:180
  110.8 3.8 %collective-permute-start.19 = (f32[26]{0:T(128)S(1)}, f32[26]{0:T(128)S(1)}, u32[]{:S(2)}, u32[]{:S(2)}) collective-permute-start(f32[26]{0:T(128)S(1)} %fusion.73), channel_id=1, source_target_pairs={{6,0},{7,1},{8,2},{9,3},{10,4},{11,5},{12,6},{13,7},{14,8},{15,9},... | collective-permute-start | bytes 320 | tf_op jit(solution)/shard_map/ppermute | solution.py:180
  114.6 2.0 %collective-permute-start.18 = (f32[26]{0:T(128)S(1)}, f32[26]{0:T(128)S(1)}, u32[]{:S(2)}, u32[]{:S(2)}) collective-permute-start(f32[26]{0:T(128)S(1)} %fusion.73), channel_id=1, source_target_pairs={{4,0},{5,1},{6,2},{7,3},{8,4},{9,5},{10,6},{11,7},{12,8},{13,9},{1... | collective-permute-start | bytes 320 | tf_op jit(solution)/shard_map/ppermute | solution.py:180
  117.5 1.5 %collective-permute-done.18 = f32[26]{0:T(128)S(1)} collective-permute-done((f32[26]{0:T(128)S(1)}, f32[26]{0:T(128)S(1)}, u32[]{:S(2)}, u32[]{:S(2)}) %collective-permute-start.18) | collective-permute-done | bytes 136 | tf_op jit(solution)/shard_map/ppermute | solution.py:180
  119.0 1.1 collective-permute-done.17
  120.2 1.9 %collective-permute-start.26 = (f32[26]{0:T(128)S(1)}, f32[26]{0:T(128)S(1)}, u32[]{:S(2)}, u32[]{:S(2)}) collective-permute-start(f32[26]{0:T(128)S(1)} %fusion.72), channel_id=1, source_target_pairs={{48,0},{0,16},{16,32},{32,48},{112,64},{64,80},{80,96},{96,112},{1... | collective-permute-start | bytes 320 | tf_op jit(solution)/shard_map/ppermute | solution.py:180
  122.1 2.7 %collective-permute-start.25 = (f32[26]{0:T(128)S(1)}, f32[26]{0:T(128)S(1)}, u32[]{:S(2)}, u32[]{:S(2)}) collective-permute-start(f32[26]{0:T(128)S(1)} %fusion.72), channel_id=1, source_target_pairs={{32,0},{48,16},{0,32},{16,48},{96,64},{112,80},{64,96},{80,112},{1... | collective-permute-start | bytes 320 | tf_op jit(solution)/shard_map/ppermute | solution.py:180
  124.8 1.5 %collective-permute-start.24 = (f32[26]{0:T(128)S(1)}, f32[26]{0:T(128)S(1)}, u32[]{:S(2)}, u32[]{:S(2)}) collective-permute-start(f32[26]{0:T(128)S(1)} %fusion.72), channel_id=1, source_target_pairs={{16,0},{32,16},{48,32},{0,48},{80,64},{96,80},{112,96},{64,112},{1... | collective-permute-start | bytes 320 | tf_op jit(solution)/shard_map/ppermute | solution.py:180
  127.1 1.2 collective-permute-done.24
  128.4 1.6 %collective-permute-start.29 = (f32[26]{0:T(128)S(1)}, f32[26]{0:T(128)S(1)}, u32[]{:S(2)}, u32[]{:S(2)}) collective-permute-start(f32[26]{0:T(128)S(1)} %fusion.71), channel_id=1, source_target_pairs={{192,0},{208,16},{224,32},{240,48},{0,64},{16,80},{32,96},{48,112}... | collective-permute-start | bytes 320 | tf_op jit(solution)/shard_map/ppermute | solution.py:180
  129.9 2.7 %collective-permute-start.28 = (f32[26]{0:T(128)S(1)}, f32[26]{0:T(128)S(1)}, u32[]{:S(2)}, u32[]{:S(2)}) collective-permute-start(f32[26]{0:T(128)S(1)} %fusion.71), channel_id=1, source_target_pairs={{128,0},{144,16},{160,32},{176,48},{192,64},{208,80},{224,96},{240... | collective-permute-start | bytes 320 | tf_op jit(solution)/shard_map/ppermute | solution.py:180
  132.7 1.4 %collective-permute-start.27 = (f32[26]{0:T(128)S(1)}, f32[26]{0:T(128)S(1)}, u32[]{:S(2)}, u32[]{:S(2)}) collective-permute-start(f32[26]{0:T(128)S(1)} %fusion.71), channel_id=1, source_target_pairs={{64,0},{80,16},{96,32},{112,48},{128,64},{144,80},{160,96},{176,11... | collective-permute-start | bytes 320 | tf_op jit(solution)/shard_map/ppermute | solution.py:180
  135.0 1.2 collective-permute-done.27
  137.7 1.3 multiply_bitcast_fusion.1
  139.2 1.3 add_bitcast_fusion
  141.8 1.1 multiply_add_fusion
  (165 shorter events, 21.1 us)
Async XLA Ops:
  0.6 0.7 copy-start.9
  1.3 0.8 copy-start.2
  2.1 0.8 copy-start.3
  2.8 0.8 copy-start.4
  7.4 24.7 %all-to-all-start = ((f32[2,128,940]{2,0,1:T(2,128)}), f32[2,128,940]{2,0,1:T(2,128)S(1)}, u32[]{:S(2)}, u32[]{:S(2)}) async-start(f32[2,128,940]{2,0,1:T(2,128)} %copy.144), calls=%async_computation | async-start | bytes 2097152 | tf_op jit(solution)/shard_map/all_to_all | solution.py:347
  14.5 0.9 copy-start.1
  34.2 1.2 collective-permute-start
  35.4 0.7 copy-start.6
  35.4 18.2 %collective-permute-start.1 = (f32[256,5]{0,1:T(8,128)S(1)}, f32[256,5]{0,1:T(8,128)S(1)}, u32[]{:S(2)}, u32[]{:S(2)}) collective-permute-start(f32[256,5]{0,1:T(8,128)S(1)} %get-tuple-element.19), channel_id=1, source_target_pairs={{2,0},{3,1},{4,2},{5,3},{6,4},{7,5},{8,6},{9,7},{10,8},{11,9},{12,... | collective-permute-start | bytes 15368 | tf_op jit(solution)/shard_map/ppermute | solution.py:180
  40.5 21.2 %collective-permute-start.6 = (f32[256,5]{0,1:T(8,128)S(1)}, f32[256,5]{0,1:T(8,128)S(1)}, u32[]{:S(2)}, u32[]{:S(2)}) collective-permute-start(f32[256,5]{0,1:T(8,128)S(1)} %get-tuple-element.19), channel_id=1, source_target_pairs={{12,0},{13,1},{14,2},{15,3},{0,4},{1,5},{2,6},{3,7},{4,8},{5,9},{6... | collective-permute-start | bytes 15368 | tf_op jit(solution)/shard_map/ppermute | solution.py:180
  43.8 17.9 %collective-permute-start.5 = (f32[256,5]{0,1:T(8,128)S(1)}, f32[256,5]{0,1:T(8,128)S(1)}, u32[]{:S(2)}, u32[]{:S(2)}) collective-permute-start(f32[256,5]{0,1:T(8,128)S(1)} %get-tuple-element.19), channel_id=1, source_target_pairs={{10,0},{11,1},{12,2},{13,3},{14,4},{15,5},{0,6},{1,7},{2,8},{3,9},... | collective-permute-start | bytes 15368 | tf_op jit(solution)/shard_map/ppermute | solution.py:180
  48.1 13.5 %collective-permute-start.4 = (f32[256,5]{0,1:T(8,128)S(1)}, f32[256,5]{0,1:T(8,128)S(1)}, u32[]{:S(2)}, u32[]{:S(2)}) collective-permute-start(f32[256,5]{0,1:T(8,128)S(1)} %get-tuple-element.19), channel_id=1, source_target_pairs={{8,0},{9,1},{10,2},{11,3},{12,4},{13,5},{14,6},{15,7},{0,8},{1,9},... | collective-permute-start | bytes 15368 | tf_op jit(solution)/shard_map/ppermute | solution.py:180
  50.3 11.4 %collective-permute-start.3 = (f32[256,5]{0,1:T(8,128)S(1)}, f32[256,5]{0,1:T(8,128)S(1)}, u32[]{:S(2)}, u32[]{:S(2)}) collective-permute-start(f32[256,5]{0,1:T(8,128)S(1)} %get-tuple-element.19), channel_id=1, source_target_pairs={{6,0},{7,1},{8,2},{9,3},{10,4},{11,5},{12,6},{13,7},{14,8},{15,9},... | collective-permute-start | bytes 15368 | tf_op jit(solution)/shard_map/ppermute | solution.py:180
  53.6 4.6 %collective-permute-start.2 = (f32[256,5]{0,1:T(8,128)S(1)}, f32[256,5]{0,1:T(8,128)S(1)}, u32[]{:S(2)}, u32[]{:S(2)}) collective-permute-start(f32[256,5]{0,1:T(8,128)S(1)} %get-tuple-element.19), channel_id=1, source_target_pairs={{4,0},{5,1},{6,2},{7,3},{8,4},{9,5},{10,6},{11,7},{12,8},{13,9},{1... | collective-permute-start | bytes 15368 | tf_op jit(solution)/shard_map/ppermute | solution.py:180
  58.2 4.8 %collective-permute-start.7 = (f32[256,5]{0,1:T(8,128)S(1)}, f32[256,5]{0,1:T(8,128)S(1)}, u32[]{:S(2)}, u32[]{:S(2)}) collective-permute-start(f32[256,5]{0,1:T(8,128)S(1)} %get-tuple-element.19), channel_id=1, source_target_pairs={{14,0},{15,1},{0,2},{1,3},{2,4},{3,5},{4,6},{5,7},{6,8},{7,9},{8,1... | collective-permute-start | bytes 15368 | tf_op jit(solution)/shard_map/ppermute | solution.py:180
  63.3 3.5 %copy-start = (f32[32,8,864]{2,1,0:T(8,128)S(1)}, f32[32,8,864]{2,1,0:T(8,128)}, u32[]{:S(2)}) copy-start(f32[32,8,864]{2,1,0:T(8,128)} %shard_map.131) | copy-start | bytes 2654212
  63.3 0.7 copy-start.10
  70.2 1.2 collective-permute-start.8
  71.4 11.5 %collective-permute-start.9 = (f32[256,5]{0,1:T(8,128)S(1)}, f32[256,5]{0,1:T(8,128)S(1)}, u32[]{:S(2)}, u32[]{:S(2)}) collective-permute-start(f32[256,5]{0,1:T(8,128)S(1)} %get-tuple-element.17), channel_id=1, source_target_pairs={{2,0},{3,1},{4,2},{5,3},{6,4},{7,5},{8,6},{9,7},{10,8},{11,9},{12,... | collective-permute-start | bytes 15368 | tf_op jit(solution)/shard_map/ppermute | solution.py:180
  73.1 17.0 %collective-permute-start.14 = (f32[256,5]{0,1:T(8,128)S(1)}, f32[256,5]{0,1:T(8,128)S(1)}, u32[]{:S(2)}, u32[]{:S(2)}) collective-permute-start(f32[256,5]{0,1:T(8,128)S(1)} %get-tuple-element.17), channel_id=1, source_target_pairs={{12,0},{13,1},{14,2},{15,3},{0,4},{1,5},{2,6},{3,7},{4,8},{5,9},{6... | collective-permute-start | bytes 15368 | tf_op jit(solution)/shard_map/ppermute | solution.py:180
  75.9 14.2 %collective-permute-start.13 = (f32[256,5]{0,1:T(8,128)S(1)}, f32[256,5]{0,1:T(8,128)S(1)}, u32[]{:S(2)}, u32[]{:S(2)}) collective-permute-start(f32[256,5]{0,1:T(8,128)S(1)} %get-tuple-element.17), channel_id=1, source_target_pairs={{10,0},{11,1},{12,2},{13,3},{14,4},{15,5},{0,6},{1,7},{2,8},{3,9},... | collective-permute-start | bytes 15368 | tf_op jit(solution)/shard_map/ppermute | solution.py:180
  76.6 13.4 %collective-permute-start.12 = (f32[256,5]{0,1:T(8,128)S(1)}, f32[256,5]{0,1:T(8,128)S(1)}, u32[]{:S(2)}, u32[]{:S(2)}) collective-permute-start(f32[256,5]{0,1:T(8,128)S(1)} %get-tuple-element.17), channel_id=1, source_target_pairs={{8,0},{9,1},{10,2},{11,3},{12,4},{13,5},{14,6},{15,7},{0,8},{1,9},... | collective-permute-start | bytes 15368 | tf_op jit(solution)/shard_map/ppermute | solution.py:180
  80.3 9.7 %collective-permute-start.11 = (f32[256,5]{0,1:T(8,128)S(1)}, f32[256,5]{0,1:T(8,128)S(1)}, u32[]{:S(2)}, u32[]{:S(2)}) collective-permute-start(f32[256,5]{0,1:T(8,128)S(1)} %get-tuple-element.17), channel_id=1, source_target_pairs={{6,0},{7,1},{8,2},{9,3},{10,4},{11,5},{12,6},{13,7},{14,8},{15,9},... | collective-permute-start | bytes 15368 | tf_op jit(solution)/shard_map/ppermute | solution.py:180
  82.9 4.6 %collective-permute-start.10 = (f32[256,5]{0,1:T(8,128)S(1)}, f32[256,5]{0,1:T(8,128)S(1)}, u32[]{:S(2)}, u32[]{:S(2)}) collective-permute-start(f32[256,5]{0,1:T(8,128)S(1)} %get-tuple-element.17), channel_id=1, source_target_pairs={{4,0},{5,1},{6,2},{7,3},{8,4},{9,5},{10,6},{11,7},{12,8},{13,9},{1... | collective-permute-start | bytes 15368 | tf_op jit(solution)/shard_map/ppermute | solution.py:180
  87.5 3.9 %collective-permute-start.15 = (f32[256,5]{0,1:T(8,128)S(1)}, f32[256,5]{0,1:T(8,128)S(1)}, u32[]{:S(2)}, u32[]{:S(2)}) collective-permute-start(f32[256,5]{0,1:T(8,128)S(1)} %get-tuple-element.17), channel_id=1, source_target_pairs={{14,0},{15,1},{0,2},{1,3},{2,4},{3,5},{4,6},{5,7},{6,8},{7,9},{8,1... | collective-permute-start | bytes 15368 | tf_op jit(solution)/shard_map/ppermute | solution.py:180
  97.7 4.7 %collective-permute-start.16 = (f32[26]{0:T(128)S(1)}, f32[26]{0:T(128)S(1)}, u32[]{:S(2)}, u32[]{:S(2)}) collective-permute-start(f32[26]{0:T(128)S(1)} %pad_maximum_fusion.3), channel_id=1, source_target_pairs={{0,1},{1,0},{2,3},{3,2},{4,5},{5,4},{6,7},{7,6},{8,9},{9,8},{10,11... | collective-permute-start | bytes 320 | tf_op jit(solution)/shard_map/ppermute | solution.py:171
  98.8 41.8 %all-to-all-start.1 = ((f32[32,8,869]{2,1,0:T(8,128)}), f32[32,8,869]{2,1,0:T(8,128)S(1)}, u32[]{:S(2)}, u32[]{:S(2)}) async-start(f32[32,8,869]{2,1,0:T(8,128)} %pad_maximum_fusion), calls=%async_computation.1 | async-start | bytes 1835008 | tf_op jit(solution)/shard_map/all_to_all | solution.py:401
  102.5 12.1 %collective-permute-start.23 = (f32[26]{0:T(128)S(1)}, f32[26]{0:T(128)S(1)}, u32[]{:S(2)}, u32[]{:S(2)}) collective-permute-start(f32[26]{0:T(128)S(1)} %fusion.73), channel_id=1, source_target_pairs={{14,0},{15,1},{0,2},{1,3},{2,4},{3,5},{4,6},{5,7},{6,8},{7,9},{8,1... | collective-permute-start | bytes 320 | tf_op jit(solution)/shard_map/ppermute | solution.py:180
  104.8 11.8 %collective-permute-start.22 = (f32[26]{0:T(128)S(1)}, f32[26]{0:T(128)S(1)}, u32[]{:S(2)}, u32[]{:S(2)}) collective-permute-start(f32[26]{0:T(128)S(1)} %fusion.73), channel_id=1, source_target_pairs={{12,0},{13,1},{14,2},{15,3},{0,4},{1,5},{2,6},{3,7},{4,8},{5,9},{6... | collective-permute-start | bytes 320 | tf_op jit(solution)/shard_map/ppermute | solution.py:180
  106.5 11.0 %collective-permute-start.21 = (f32[26]{0:T(128)S(1)}, f32[26]{0:T(128)S(1)}, u32[]{:S(2)}, u32[]{:S(2)}) collective-permute-start(f32[26]{0:T(128)S(1)} %fusion.73), channel_id=1, source_target_pairs={{10,0},{11,1},{12,2},{13,3},{14,4},{15,5},{0,6},{1,7},{2,8},{3,9},... | collective-permute-start | bytes 320 | tf_op jit(solution)/shard_map/ppermute | solution.py:180
  108.7 8.8 %collective-permute-start.20 = (f32[26]{0:T(128)S(1)}, f32[26]{0:T(128)S(1)}, u32[]{:S(2)}, u32[]{:S(2)}) collective-permute-start(f32[26]{0:T(128)S(1)} %fusion.73), channel_id=1, source_target_pairs={{8,0},{9,1},{10,2},{11,3},{12,4},{13,5},{14,6},{15,7},{0,8},{1,9},... | collective-permute-start | bytes 320 | tf_op jit(solution)/shard_map/ppermute | solution.py:180
  110.8 6.7 %collective-permute-start.19 = (f32[26]{0:T(128)S(1)}, f32[26]{0:T(128)S(1)}, u32[]{:S(2)}, u32[]{:S(2)}) collective-permute-start(f32[26]{0:T(128)S(1)} %fusion.73), channel_id=1, source_target_pairs={{6,0},{7,1},{8,2},{9,3},{10,4},{11,5},{12,6},{13,7},{14,8},{15,9},... | collective-permute-start | bytes 320 | tf_op jit(solution)/shard_map/ppermute | solution.py:180
  114.6 4.4 %collective-permute-start.18 = (f32[26]{0:T(128)S(1)}, f32[26]{0:T(128)S(1)}, u32[]{:S(2)}, u32[]{:S(2)}) collective-permute-start(f32[26]{0:T(128)S(1)} %fusion.73), channel_id=1, source_target_pairs={{4,0},{5,1},{6,2},{7,3},{8,4},{9,5},{10,6},{11,7},{12,8},{13,9},{1... | collective-permute-start | bytes 320 | tf_op jit(solution)/shard_map/ppermute | solution.py:180
  116.6 3.5 %collective-permute-start.17 = (f32[26]{0:T(128)S(1)}, f32[26]{0:T(128)S(1)}, u32[]{:S(2)}, u32[]{:S(2)}) collective-permute-start(f32[26]{0:T(128)S(1)} %fusion.73), channel_id=1, source_target_pairs={{2,0},{3,1},{4,2},{5,3},{6,4},{7,5},{8,6},{9,7},{10,8},{11,9},{12,... | collective-permute-start | bytes 320 | tf_op jit(solution)/shard_map/ppermute | solution.py:180
  120.2 6.0 %collective-permute-start.26 = (f32[26]{0:T(128)S(1)}, f32[26]{0:T(128)S(1)}, u32[]{:S(2)}, u32[]{:S(2)}) collective-permute-start(f32[26]{0:T(128)S(1)} %fusion.72), channel_id=1, source_target_pairs={{48,0},{0,16},{16,32},{32,48},{112,64},{64,80},{80,96},{96,112},{1... | collective-permute-start | bytes 320 | tf_op jit(solution)/shard_map/ppermute | solution.py:180
  122.1 5.0 %collective-permute-start.25 = (f32[26]{0:T(128)S(1)}, f32[26]{0:T(128)S(1)}, u32[]{:S(2)}, u32[]{:S(2)}) collective-permute-start(f32[26]{0:T(128)S(1)} %fusion.72), channel_id=1, source_target_pairs={{32,0},{48,16},{0,32},{16,48},{96,64},{112,80},{64,96},{80,112},{1... | collective-permute-start | bytes 320 | tf_op jit(solution)/shard_map/ppermute | solution.py:180
  124.8 3.5 %collective-permute-start.24 = (f32[26]{0:T(128)S(1)}, f32[26]{0:T(128)S(1)}, u32[]{:S(2)}, u32[]{:S(2)}) collective-permute-start(f32[26]{0:T(128)S(1)} %fusion.72), channel_id=1, source_target_pairs={{16,0},{32,16},{48,32},{0,48},{80,64},{96,80},{112,96},{64,112},{1... | collective-permute-start | bytes 320 | tf_op jit(solution)/shard_map/ppermute | solution.py:180
  128.4 5.7 %collective-permute-start.29 = (f32[26]{0:T(128)S(1)}, f32[26]{0:T(128)S(1)}, u32[]{:S(2)}, u32[]{:S(2)}) collective-permute-start(f32[26]{0:T(128)S(1)} %fusion.71), channel_id=1, source_target_pairs={{192,0},{208,16},{224,32},{240,48},{0,64},{16,80},{32,96},{48,112}... | collective-permute-start | bytes 320 | tf_op jit(solution)/shard_map/ppermute | solution.py:180
  129.9 5.0 %collective-permute-start.28 = (f32[26]{0:T(128)S(1)}, f32[26]{0:T(128)S(1)}, u32[]{:S(2)}, u32[]{:S(2)}) collective-permute-start(f32[26]{0:T(128)S(1)} %fusion.71), channel_id=1, source_target_pairs={{128,0},{144,16},{160,32},{176,48},{192,64},{208,80},{224,96},{240... | collective-permute-start | bytes 320 | tf_op jit(solution)/shard_map/ppermute | solution.py:180
  132.7 3.5 %collective-permute-start.27 = (f32[26]{0:T(128)S(1)}, f32[26]{0:T(128)S(1)}, u32[]{:S(2)}, u32[]{:S(2)}) collective-permute-start(f32[26]{0:T(128)S(1)} %fusion.71), channel_id=1, source_target_pairs={{64,0},{80,16},{96,32},{112,48},{128,64},{144,80},{160,96},{176,11... | collective-permute-start | bytes 320 | tf_op jit(solution)/shard_map/ppermute | solution.py:180
  136.2 0.7 copy-start.5
  136.2 0.7 copy-start.8
  137.1 0.7 copy-start.7

commit v15 on v13

--- a/solution.py
+++ b/solution.py
@@ -340,12 +340,10 @@
     node_mass = lax.dynamic_slice_in_dim(jnp.asarray(node_weight, jnp.float32), offset, node_count, 0)
     line_signed = jnp.asarray(along_x[:NXI], jnp.float32)
     node_signed = jnp.asarray(np.tile(along_x[:NXI], node_rows), jnp.float32)
+    pieces = [distribution, collision.reshape(1, cell_count), lower_blocks, upper_blocks, diag_inverse]
     packed = jnp.concatenate(
-        [distribution, collision.reshape(1, cell_count), lower_blocks, upper_blocks, diag_inverse],
-        axis=0,
-    )
-    rows = packed.shape[0]
-    packed = packed.reshape(rows, length, TUBES).transpose(1, 2, 0)
+        [piece.reshape(-1, length, TUBES).transpose(1, 2, 0) for piece in pieces], axis=2
+    )
     lines = lax.all_to_all(packed, "sec", 1, 0, tiled=True)
     dist_t = lines[:, :, :node_count]
     thickness = lines[:, :, node_count : node_count + 1]

time: 124 us -> 124 us (level)
    transpose x1 -> x0, local copies, waits for them, and re-layouts: 1.78 us -> none  [body(): packed = packed.reshape(rows, length, TUBES).transpose(1, 2, 0)]
    concatenate x5 -> x2, local copies, waits for them, and re-layouts: 0.91 us -> 2.22 us  [body(): jnp.concatenate([piece.reshape(-1, length, TUBES).transpose(1, 2, 0) for...]
where the time goes in v15:
time: 124 us; the launch traced here: 123 us
  starting transfers between devices  49.3 us (40%)
  waiting for transfers between devices  38 us (31%)
  local copies, waits for them, and re-layouts  13.8 us (11%)
  other arithmetic  8.59 us (7%)
  matrix products  6.92 us (6%)
  Pallas kernels  4.91 us (4%)
  between operations  1.31 us (1%)
    ppermute x15, starting transfers between devices, group_sum(): shifted.append(lax.ppermute(block, axis, pairs))  25.5 us
    all_to_all x1, waiting for transfers between devices, body(): lines = lax.all_to_all(packed, 'sec', 1, 0, tiled=True)  17.7 us
    ppermute x15, waiting for transfers between devices, group_sum(): shifted.append(lax.ppermute(block, axis, pairs))  14 us
    ppermute x6, starting transfers between devices, group_sum(): return block + lax.ppermute(block, axis, pairs)  13.1 us
    all_to_all x1, starting transfers between devices, body(): lines = lax.all_to_all(packed, 'sec', 1, 0, tiled=True)  7.03 us
    ppermute x6, waiting for transfers between devices, group_sum(): return block + lax.ppermute(block, axis, pairs)  6.29 us
    unnamed x24, local copies, waits for them, and re-layouts  6.02 us
    pallas_call x2, Pallas kernels, line_sweep(): pl.pallas_call(sweep_kernel, out_shape=jax.ShapeDtypeStruct(drive_term.sh...  4.91 us
  transfers between devices with their start and end apart: 23, of which 16 were waited for; matrix products, arithmetic and copies ran while one was open for 7% of the time, Pallas kernels for 2%

profile of v15, /device:TPU:32, one launch (start us, length us, event | category | flops | bytes accessed | tf_op | source)
XLA Modules:
  0.0 122.9 jit_solution(12799778439889610862)
XLA Ops:
  0.6 0.7 copy-done.9
  3.7 1.5 %copy.94 = f32[864,256]{0,1:T(8,128)S(1)} copy(f32[864,256]{1,0:T(8,128)} %param.12) | data formatting | bytes 1769472 | tf_op args[0]
  5.6 1.8 %copy.99 = f32[2,128,940]{2,0,1:T(2,128)} copy(f32[2,128,940]{2,1,0:T(8,128)S(1)} %concatenate.33) | data formatting | bytes 1925120 | tf_op jit(solution)/shard_map/concatenate | solution.py:344
  7.4 7.0 %all-to-all-start = ((f32[2,128,940]{2,0,1:T(2,128)}), f32[2,128,940]{2,0,1:T(2,128)S(1)}, u32[]{:S(2)}, u32[]{:S(2)}) async-start(f32[2,128,940]{2,0,1:T(2,128)} %copy.99), calls=%async_computation | async-start | bytes 2097152 | tf_op jit(solution)/shard_map/all_to_all | solution.py:347
  14.4 17.7 %all-to-all-done = f32[2,128,940]{2,0,1:T(2,128)S(1)} async-done(((f32[2,128,940]{2,0,1:T(2,128)}), f32[2,128,940]{2,0,1:T(2,128)S(1)}, u32[]{:S(2)}, u32[]{:S(2)}) %all-to-all-start) | async-done | bytes 962592 | tf_op jit(solution)/shard_map/all_to_all | solution.py:347
  32.6 1.6 %fusion.2 = f32[256,5]{0,1:T(8,128)S(1)} fusion(f32[32,8,940]{2,1,0:T(8,128)S(1)} %bitcast.158, f32[5,13824]{1,0:T(8,128)} %constant.181.clone, s32[]{:T(128)S(6)} %select_n.134), kind=kOutput, calls=%fused_computation.6 | convolution fusion | flops 13271040 | bytes 951300 | tf_op jit(solution)/shard_map/dot_general | solution.py:355
  34.2 0.9 constant_dynamic-slice_fusion.12
  35.4 1.9 %collective-permute-start.3 = (f32[256,5]{0,1:T(8,128)S(1)}, f32[256,5]{0,1:T(8,128)S(1)}, u32[]{:S(2)}, u32[]{:S(2)}) collective-permute-start(f32[256,5]{0,1:T(8,128)S(1)} %add.281), channel_id=1, source_target_pairs={{6,0},{7,1},{0,2},{1,3},{2,4},{3,5},{4,6},{5,7},{14,8},{15,9},{8,1... | collective-permute-start | bytes 15368 | tf_op jit(solution)/shard_map/ppermute | solution.py:180
  37.3 1.4 %collective-permute-start.2 = (f32[256,5]{0,1:T(8,128)S(1)}, f32[256,5]{0,1:T(8,128)S(1)}, u32[]{:S(2)}, u32[]{:S(2)}) collective-permute-start(f32[256,5]{0,1:T(8,128)S(1)} %add.281), channel_id=1, source_target_pairs={{4,0},{5,1},{6,2},{7,3},{0,4},{1,5},{2,6},{3,7},{12,8},{13,9},{14,... | collective-permute-start | bytes 15368 | tf_op jit(solution)/shard_map/ppermute | solution.py:180
  38.7 2.0 %collective-permute-start.1 = (f32[256,5]{0,1:T(8,128)S(1)}, f32[256,5]{0,1:T(8,128)S(1)}, u32[]{:S(2)}, u32[]{:S(2)}) collective-permute-start(f32[256,5]{0,1:T(8,128)S(1)} %add.281), channel_id=1, source_target_pairs={{2,0},{3,1},{4,2},{5,3},{6,4},{7,5},{0,6},{1,7},{10,8},{11,9},{12,... | collective-permute-start | bytes 15368 | tf_op jit(solution)/shard_map/ppermute | solution.py:180
  41.2 0.7 collective-permute-done.2
  42.4 6.5 %collective-permute-start.4 = (f32[256,5]{0,1:T(8,128)S(1)}, f32[256,5]{0,1:T(8,128)S(1)}, u32[]{:S(2)}, u32[]{:S(2)}) collective-permute-start(f32[256,5]{0,1:T(8,128)S(1)} %add_bitcast_fusion.1), channel_id=1, source_target_pairs={{0,8},{1,9},{2,10},{3,11},{4,12},{5,13},{6,14},{7,15},{8,0},{9,1},... | collective-permute-start | bytes 15368 | tf_op jit(solution)/shard_map/ppermute | solution.py:171
  48.9 1.5 %fusion.4 = (f32[32,8,864]{2,1,0:T(8,128)}, f32[32,8,864]{2,1,0:T(8,128)}) fusion(f32[32,8,940]{2,1,0:T(8,128)S(1)} %bitcast.160, f32[32,8]{1,0:T(8,128)S(1)} %bitcast.187, f32[864]{0:T(1024)S(1)} %copy-done.6), kind=kLoop, calls=%fused_computation.11 | loop fusion | flops 884736 | bytes 2658688 | tf_op jit(solution)/shard_map/div | solution.py:360
  50.4 2.9 %shard_map.131 = f32[32,8,864]{2,1,0:T(8,128)} custom-call(f32[32,8,864]{2,1,0:T(8,128)} %get-tuple-element.30.rate_ref, f32[32,8,864]{2,1,0:T(8,128)} %get-tuple-element.29.drive_ref, f32[1,864]{1,0:T(1,128)} %constant.206.sign_ref), custom_call_target="tpu_custom_call" | custom-call | tf_op jit(solution)/shard_map/pallas_call | solution.py:315
  54.3 0.8 multiply_divide_fusion
  55.1 2.0 %shard_map.132 = f32[32,8,120]{2,1,0:T(8,128)} custom-call(f32[32,8,120]{2,1,0:T(8,128)} %get-tuple-element.32.rate_ref, f32[32,8,120]{2,1,0:T(8,128)} %get-tuple-element.31.drive_ref, f32[1,120]{1,0:T(1,128)} %constant.209.sign_ref), custom_call_target="tpu_custom_call" | custom-call | tf_op jit(solution)/shard_map/pallas_call | solution.py:315
  57.1 1.8 %convolution_add_fusion.1 = f32[32,8,864]{2,1,0:T(8,128)S(1)} fusion(f32[32,8,864]{2,1,0:T(8,128)S(1)} %copy-done, f32[32,8,120]{2,1,0:T(8,128)} %shard_map.132, f32[120,864,1]{1,0,2:T(8,128)S(1)} %bitcast.181), kind=kOutput, calls=%fused_computation.1 | convolution fusion | flops 318726144 | bytes 2307072 | tf_op jit(solution)/shard_map/dot_general | solution.py:375
  58.9 1.6 %fusion = f32[256,5]{0,1:T(8,128)S(1)} fusion(f32[32,8,864]{2,1,0:T(8,128)S(1)} %convolution_add_fusion.1, f32[5,13824]{1,0:T(8,128)} %constant.181.clone, s32[]{:T(128)S(6)} %select_n.134), kind=kOutput, calls=%fused_computation.4 | convolution fusion | flops 13271040 | bytes 918532 | tf_op jit(solution)/shard_map/dot_general | solution.py:379
  60.5 1.1 collective-permute-done.5
  61.8 2.4 %collective-permute-start.7 = (f32[256,5]{0,1:T(8,128)S(1)}, f32[256,5]{0,1:T(8,128)S(1)}, u32[]{:S(2)}, u32[]{:S(2)}) collective-permute-start(f32[256,5]{0,1:T(8,128)S(1)} %add.297), channel_id=1, source_target_pairs={{4,0},{5,1},{6,2},{7,3},{0,4},{1,5},{2,6},{3,7},{12,8},{13,9},{14,... | collective-permute-start | bytes 15368 | tf_op jit(solution)/shard_map/ppermute | solution.py:180
  64.2 1.9 %collective-permute-start.6 = (f32[256,5]{0,1:T(8,128)S(1)}, f32[256,5]{0,1:T(8,128)S(1)}, u32[]{:S(2)}, u32[]{:S(2)}) collective-permute-start(f32[256,5]{0,1:T(8,128)S(1)} %add.297), channel_id=1, source_target_pairs={{2,0},{3,1},{4,2},{5,3},{6,4},{7,5},{0,6},{1,7},{10,8},{11,9},{12,... | collective-permute-start | bytes 15368 | tf_op jit(solution)/shard_map/ppermute | solution.py:180
  66.4 1.5 %collective-permute-done.6 = f32[256,5]{0,1:T(8,128)S(1)} collective-permute-done((f32[256,5]{0,1:T(8,128)S(1)}, f32[256,5]{0,1:T(8,128)S(1)}, u32[]{:S(2)}, u32[]{:S(2)}) %collective-permute-start.6) | collective-permute-done | bytes 5152 | tf_op jit(solution)/shard_map/ppermute | solution.py:180
  67.8 3.4 %collective-permute-start.9 = (f32[256,5]{0,1:T(8,128)S(1)}, f32[256,5]{0,1:T(8,128)S(1)}, u32[]{:S(2)}, u32[]{:S(2)}) collective-permute-start(f32[256,5]{0,1:T(8,128)S(1)} %add_bitcast_fusion), channel_id=1, source_target_pairs={{0,8},{1,9},{2,10},{3,11},{4,12},{5,13},{6,14},{7,15},{8,0},{9,1},... | collective-permute-start | bytes 15368 | tf_op jit(solution)/shard_map/ppermute | solution.py:171
  71.8 3.9 %collective-permute-done.9 = f32[256,5]{0,1:T(8,128)S(1)} collective-permute-done((f32[256,5]{0,1:T(8,128)S(1)}, f32[256,5]{0,1:T(8,128)S(1)}, u32[]{:S(2)}, u32[]{:S(2)}) %collective-permute-start.9) | collective-permute-done | bytes 5152 | tf_op jit(solution)/shard_map/ppermute | solution.py:171
  77.2 1.7 %abs_reduce_fusion = (f32[864]{0:T(1024)S(1)}, f32[32,8,864]{2,1,0:T(8,128)S(1)}) fusion(f32[32,8,864]{2,1,0:T(8,128)S(1)} %convolution_add_fusion.1, f32[32,8,5]{2,1,0:T(8,128)S(1)} %copy.115, f32[5,13824]{1,0:T(8,128)} %constant.182.clone, s32[]{:T(128)S(6)} %select_n.134), kind=kOutput, calls=%fused_computation.9 | convolution fusion | flops 13933728 | bytes 1806724 | tf_op jit(solution)/shard_map/dot_general | solution.py:393
  78.9 0.8 dynamic-slice_multiply_fusion
  80.2 1.0 collective-permute-done.10
  81.2 1.4 %collective-permute-start.13 = (f32[26]{0:T(128)S(1)}, f32[26]{0:T(128)S(1)}, u32[]{:S(2)}, u32[]{:S(2)}) collective-permute-start(f32[26]{0:T(128)S(1)} %fusion.55), channel_id=1, source_target_pairs={{6,0},{7,1},{0,2},{1,3},{2,4},{3,5},{4,6},{5,7},{14,8},{15,9},{8,1... | collective-permute-start | bytes 320 | tf_op jit(solution)/shard_map/ppermute | solution.py:180
  82.6 2.9 %collective-permute-start.12 = (f32[26]{0:T(128)S(1)}, f32[26]{0:T(128)S(1)}, u32[]{:S(2)}, u32[]{:S(2)}) collective-permute-start(f32[26]{0:T(128)S(1)} %fusion.55), channel_id=1, source_target_pairs={{4,0},{5,1},{6,2},{7,3},{0,4},{1,5},{2,6},{3,7},{12,8},{13,9},{14,... | collective-permute-start | bytes 320 | tf_op jit(solution)/shard_map/ppermute | solution.py:180
  85.6 1.4 %collective-permute-done.12 = f32[26]{0:T(128)S(1)} collective-permute-done((f32[26]{0:T(128)S(1)}, f32[26]{0:T(128)S(1)}, u32[]{:S(2)}, u32[]{:S(2)}) %collective-permute-start.12) | collective-permute-done | bytes 136 | tf_op jit(solution)/shard_map/ppermute | solution.py:180
  87.0 2.0 %collective-permute-done.11 = f32[26]{0:T(128)S(1)} collective-permute-done((f32[26]{0:T(128)S(1)}, f32[26]{0:T(128)S(1)}, u32[]{:S(2)}, u32[]{:S(2)}) %collective-permute-start.11) | collective-permute-done | bytes 136 | tf_op jit(solution)/shard_map/ppermute | solution.py:180
  89.1 3.2 %collective-permute-start.14 = (f32[26]{0:T(128)S(1)}, f32[26]{0:T(128)S(1)}, u32[]{:S(2)}, u32[]{:S(2)}) collective-permute-start(f32[26]{0:T(128)S(1)} %fusion.33), channel_id=1, source_target_pairs={{0,8},{1,9},{2,10},{3,11},{4,12},{5,13},{6,14},{7,15},{8,0},{9,1},... | collective-permute-start | bytes 320 | tf_op jit(solution)/shard_map/ppermute | solution.py:171
  92.3 1.0 pad_maximum_fusion
  93.3 3.6 %all-to-all-start.1 = ((f32[32,8,869]{2,1,0:T(8,128)}), f32[32,8,869]{2,1,0:T(8,128)S(1)}, u32[]{:S(2)}, u32[]{:S(2)}) async-start(f32[32,8,869]{2,1,0:T(8,128)} %pad_maximum_fusion), calls=%async_computation.1 | async-start | bytes 1835008 | tf_op jit(solution)/shard_map/all_to_all | solution.py:401
  97.0 1.9 %collective-permute-start.17 = (f32[26]{0:T(128)S(1)}, f32[26]{0:T(128)S(1)}, u32[]{:S(2)}, u32[]{:S(2)}) collective-permute-start(f32[26]{0:T(128)S(1)} %fusion.54), channel_id=1, source_target_pairs={{48,0},{0,16},{16,32},{32,48},{112,64},{64,80},{80,96},{96,112},{1... | collective-permute-start | bytes 320 | tf_op jit(solution)/shard_map/ppermute | solution.py:180
  98.9 2.7 %collective-permute-start.16 = (f32[26]{0:T(128)S(1)}, f32[26]{0:T(128)S(1)}, u32[]{:S(2)}, u32[]{:S(2)}) collective-permute-start(f32[26]{0:T(128)S(1)} %fusion.54), channel_id=1, source_target_pairs={{32,0},{48,16},{0,32},{16,48},{96,64},{112,80},{64,96},{80,112},{1... | collective-permute-start | bytes 320 | tf_op jit(solution)/shard_map/ppermute | solution.py:180
  101.6 1.5 %collective-permute-start.15 = (f32[26]{0:T(128)S(1)}, f32[26]{0:T(128)S(1)}, u32[]{:S(2)}, u32[]{:S(2)}) collective-permute-start(f32[26]{0:T(128)S(1)} %fusion.54), channel_id=1, source_target_pairs={{16,0},{32,16},{48,32},{0,48},{80,64},{96,80},{112,96},{64,112},{1... | collective-permute-start | bytes 320 | tf_op jit(solution)/shard_map/ppermute | solution.py:180
  103.0 1.6 %collective-permute-done.17 = f32[26]{0:T(128)S(1)} collective-permute-done((f32[26]{0:T(128)S(1)}, f32[26]{0:T(128)S(1)}, u32[]{:S(2)}, u32[]{:S(2)}) %collective-permute-start.17) | collective-permute-done | bytes 136 | tf_op jit(solution)/shard_map/ppermute | solution.py:180
  105.0 2.4 %collective-permute-done.15 = f32[26]{0:T(128)S(1)} collective-permute-done((f32[26]{0:T(128)S(1)}, f32[26]{0:T(128)S(1)}, u32[]{:S(2)}, u32[]{:S(2)}) %collective-permute-start.15) | collective-permute-done | bytes 136 | tf_op jit(solution)/shard_map/ppermute | solution.py:180
  107.4 2.1 %collective-permute-start.20 = (f32[26]{0:T(128)S(1)}, f32[26]{0:T(128)S(1)}, u32[]{:S(2)}, u32[]{:S(2)}) collective-permute-start(f32[26]{0:T(128)S(1)} %fusion.53), channel_id=1, source_target_pairs={{192,0},{208,16},{224,32},{240,48},{0,64},{16,80},{32,96},{48,112}... | collective-permute-start | bytes 320 | tf_op jit(solution)/shard_map/ppermute | solution.py:180
  109.5 3.2 %collective-permute-start.19 = (f32[26]{0:T(128)S(1)}, f32[26]{0:T(128)S(1)}, u32[]{:S(2)}, u32[]{:S(2)}) collective-permute-start(f32[26]{0:T(128)S(1)} %fusion.53), channel_id=1, source_target_pairs={{128,0},{144,16},{160,32},{176,48},{192,64},{208,80},{224,96},{240... | collective-permute-start | bytes 320 | tf_op jit(solution)/shard_map/ppermute | solution.py:180
  112.8 1.7 %collective-permute-done.19 = f32[26]{0:T(128)S(1)} collective-permute-done((f32[26]{0:T(128)S(1)}, f32[26]{0:T(128)S(1)}, u32[]{:S(2)}, u32[]{:S(2)}) %collective-permute-start.19) | collective-permute-done | bytes 136 | tf_op jit(solution)/shard_map/ppermute | solution.py:180
  114.5 1.6 %collective-permute-done.18 = f32[26]{0:T(128)S(1)} collective-permute-done((f32[26]{0:T(128)S(1)}, f32[26]{0:T(128)S(1)}, u32[]{:S(2)}, u32[]{:S(2)}) %collective-permute-start.18) | collective-permute-done | bytes 136 | tf_op jit(solution)/shard_map/ppermute | solution.py:180
  117.0 0.7 copy-done.7
  117.7 1.3 %multiply_bitcast_fusion.1 = (f32[1,24]{1,0:T(1,128)S(1)}, f32[1,24]{1,0:T(1,128)S(1)}, f32[1,24]{1,0:T(1,128)S(1)}, f32[1,24]{1,0:T(1,128)S(1)}) fusion(f32[24]{0:T(128)S(1)} %copy-done.5, f32[1,26]{1,0:T(1,128)S(1)} %fusion.19, f32[1,24]{1,0:T(1,128)S(1)} %copy-done.7, f32[5,24]{1,0:T(8,128)S(1)} %fusion.14, f32[]{:T(128)} %bitcast.58, f32[]{:T(128)} %bitcast.59), kind=kLoop, calls=%fused_computation.90 | loop fusion | flops 480 | bytes 1160 | tf_op jit(solution)/shard_map/stack | solution.py:416
  119.2 1.3 %add_bitcast_fusion.2 = f32[24]{0:T(128)S(1)} fusion(f32[1,24]{1,0:T(1,128)S(1)} %copy-done.7, f32[1,24]{1,0:T(1,128)S(1)} %get-tuple-element.13, f32[1,24]{1,0:T(1,128)S(1)} %get-tuple-element.12, f32[5,24]{1,0:T(8,128)S(1)} %fusion.12, f32[]{:T(128)} %bitcast.59, f32[]{:T(128)} %bitcast.58), kind=kLoop, calls=%fused_computation.87 | loop fusion | flops 432 | bytes 872 | tf_op jit(solution)/shard_map/sub | solution.py:423
  120.8 0.7 copy.121
  121.8 1.1 multiply_add_fusion
  (123 shorter events, 10.6 us)
Async XLA Ops:
  0.6 0.7 copy-start.9
  1.3 0.8 copy-start.2
  2.1 0.8 copy-start.3
  2.8 0.8 copy-start.4
  7.4 24.7 %all-to-all-start = ((f32[2,128,940]{2,0,1:T(2,128)}), f32[2,128,940]{2,0,1:T(2,128)S(1)}, u32[]{:S(2)}, u32[]{:S(2)}) async-start(f32[2,128,940]{2,0,1:T(2,128)} %copy.99), calls=%async_computation | async-start | bytes 2097152 | tf_op jit(solution)/shard_map/all_to_all | solution.py:347
  32.6 8.2 %copy-start.1 = (f32[24,864]{1,0:T(8,128)S(1)}, f32[24,864]{1,0:T(8,128)}, u32[]{:S(2)}) copy-start(f32[24,864]{1,0:T(8,128)} %constant.187.clone) | copy-start | bytes 248836
  34.2 1.2 %collective-permute-start = (f32[256,5]{0,1:T(8,128)S(1)}, f32[256,5]{0,1:T(8,128)S(1)}, u32[]{:S(2)}, u32[]{:S(2)}) collective-permute-start(f32[256,5]{0,1:T(8,128)S(1)} %fusion.2), channel_id=1, source_target_pairs={{0,1},{1,0},{2,3},{3,2},{4,5},{5,4},{6,7},{7,6},{8,9},{9,8},{10,11... | collective-permute-start | bytes 15368 | tf_op jit(solution)/shard_map/ppermute | solution.py:171
  35.4 5.8 %collective-permute-start.3 = (f32[256,5]{0,1:T(8,128)S(1)}, f32[256,5]{0,1:T(8,128)S(1)}, u32[]{:S(2)}, u32[]{:S(2)}) collective-permute-start(f32[256,5]{0,1:T(8,128)S(1)} %add.281), channel_id=1, source_target_pairs={{6,0},{7,1},{0,2},{1,3},{2,4},{3,5},{4,6},{5,7},{14,8},{15,9},{8,1... | collective-permute-start | bytes 15368 | tf_op jit(solution)/shard_map/ppermute | solution.py:180
  37.3 4.5 %collective-permute-start.2 = (f32[256,5]{0,1:T(8,128)S(1)}, f32[256,5]{0,1:T(8,128)S(1)}, u32[]{:S(2)}, u32[]{:S(2)}) collective-permute-start(f32[256,5]{0,1:T(8,128)S(1)} %add.281), channel_id=1, source_target_pairs={{4,0},{5,1},{6,2},{7,3},{0,4},{1,5},{2,6},{3,7},{12,8},{13,9},{14,... | collective-permute-start | bytes 15368 | tf_op jit(solution)/shard_map/ppermute | solution.py:180
  38.7 3.7 %collective-permute-start.1 = (f32[256,5]{0,1:T(8,128)S(1)}, f32[256,5]{0,1:T(8,128)S(1)}, u32[]{:S(2)}, u32[]{:S(2)}) collective-permute-start(f32[256,5]{0,1:T(8,128)S(1)} %add.281), channel_id=1, source_target_pairs={{2,0},{3,1},{4,2},{5,3},{6,4},{7,5},{0,6},{1,7},{10,8},{11,9},{12,... | collective-permute-start | bytes 15368 | tf_op jit(solution)/shard_map/ppermute | solution.py:180
  42.4 6.5 %copy-start.6 = (f32[864]{0:T(1024)S(1)}, f32[864]{0:T(1024)}, u32[]{:S(2)}) copy-start(f32[864]{0:T(1024)} %constant.205) | copy-start | bytes 10372
  42.4 10.9 %collective-permute-start.4 = (f32[256,5]{0,1:T(8,128)S(1)}, f32[256,5]{0,1:T(8,128)S(1)}, u32[]{:S(2)}, u32[]{:S(2)}) collective-permute-start(f32[256,5]{0,1:T(8,128)S(1)} %add_bitcast_fusion.1), channel_id=1, source_target_pairs={{0,8},{1,9},{2,10},{3,11},{4,12},{5,13},{6,14},{7,15},{8,0},{9,1},... | collective-permute-start | bytes 15368 | tf_op jit(solution)/shard_map/ppermute | solution.py:171
  53.5 3.6 %copy-start = (f32[32,8,864]{2,1,0:T(8,128)S(1)}, f32[32,8,864]{2,1,0:T(8,128)}, u32[]{:S(2)}) copy-start(f32[32,8,864]{2,1,0:T(8,128)} %shard_map.131) | copy-start | bytes 2654212
  53.6 0.7 copy-start.10
  60.4 1.2 %collective-permute-start.5 = (f32[256,5]{0,1:T(8,128)S(1)}, f32[256,5]{0,1:T(8,128)S(1)}, u32[]{:S(2)}, u32[]{:S(2)}) collective-permute-start(f32[256,5]{0,1:T(8,128)S(1)} %fusion), channel_id=1, source_target_pairs={{0,1},{1,0},{2,3},{3,2},{4,5},{5,4},{6,7},{7,6},{8,9},{9,8},{10,11... | collective-permute-start | bytes 15368 | tf_op jit(solution)/shard_map/ppermute | solution.py:171
  61.7 4.4 %collective-permute-start.8 = (f32[256,5]{0,1:T(8,128)S(1)}, f32[256,5]{0,1:T(8,128)S(1)}, u32[]{:S(2)}, u32[]{:S(2)}) collective-permute-start(f32[256,5]{0,1:T(8,128)S(1)} %add.297), channel_id=1, source_target_pairs={{6,0},{7,1},{0,2},{1,3},{2,4},{3,5},{4,6},{5,7},{14,8},{15,9},{8,1... | collective-permute-start | bytes 15368 | tf_op jit(solution)/shard_map/ppermute | solution.py:180
  61.8 4.5 %collective-permute-start.7 = (f32[256,5]{0,1:T(8,128)S(1)}, f32[256,5]{0,1:T(8,128)S(1)}, u32[]{:S(2)}, u32[]{:S(2)}) collective-permute-start(f32[256,5]{0,1:T(8,128)S(1)} %add.297), channel_id=1, source_target_pairs={{4,0},{5,1},{6,2},{7,3},{0,4},{1,5},{2,6},{3,7},{12,8},{13,9},{14,... | collective-permute-start | bytes 15368 | tf_op jit(solution)/shard_map/ppermute | solution.py:180
  64.2 3.7 %collective-permute-start.6 = (f32[256,5]{0,1:T(8,128)S(1)}, f32[256,5]{0,1:T(8,128)S(1)}, u32[]{:S(2)}, u32[]{:S(2)}) collective-permute-start(f32[256,5]{0,1:T(8,128)S(1)} %add.297), channel_id=1, source_target_pairs={{2,0},{3,1},{4,2},{5,3},{6,4},{7,5},{0,6},{1,7},{10,8},{11,9},{12,... | collective-permute-start | bytes 15368 | tf_op jit(solution)/shard_map/ppermute | solution.py:180
  67.8 7.8 %collective-permute-start.9 = (f32[256,5]{0,1:T(8,128)S(1)}, f32[256,5]{0,1:T(8,128)S(1)}, u32[]{:S(2)}, u32[]{:S(2)}) collective-permute-start(f32[256,5]{0,1:T(8,128)S(1)} %add_bitcast_fusion), channel_id=1, source_target_pairs={{0,8},{1,9},{2,10},{3,11},{4,12},{5,13},{6,14},{7,15},{8,0},{9,1},... | collective-permute-start | bytes 15368 | tf_op jit(solution)/shard_map/ppermute | solution.py:171
  80.0 1.1 collective-permute-start.10
  81.2 4.4 %collective-permute-start.13 = (f32[26]{0:T(128)S(1)}, f32[26]{0:T(128)S(1)}, u32[]{:S(2)}, u32[]{:S(2)}) collective-permute-start(f32[26]{0:T(128)S(1)} %fusion.55), channel_id=1, source_target_pairs={{6,0},{7,1},{0,2},{1,3},{2,4},{3,5},{4,6},{5,7},{14,8},{15,9},{8,1... | collective-permute-start | bytes 320 | tf_op jit(solution)/shard_map/ppermute | solution.py:180
  82.6 4.4 %collective-permute-start.12 = (f32[26]{0:T(128)S(1)}, f32[26]{0:T(128)S(1)}, u32[]{:S(2)}, u32[]{:S(2)}) collective-permute-start(f32[26]{0:T(128)S(1)} %fusion.55), channel_id=1, source_target_pairs={{4,0},{5,1},{6,2},{7,3},{0,4},{1,5},{2,6},{3,7},{12,8},{13,9},{14,... | collective-permute-start | bytes 320 | tf_op jit(solution)/shard_map/ppermute | solution.py:180
  85.5 3.5 %collective-permute-start.11 = (f32[26]{0:T(128)S(1)}, f32[26]{0:T(128)S(1)}, u32[]{:S(2)}, u32[]{:S(2)}) collective-permute-start(f32[26]{0:T(128)S(1)} %fusion.55), channel_id=1, source_target_pairs={{2,0},{3,1},{4,2},{5,3},{6,4},{7,5},{0,6},{1,7},{10,8},{11,9},{12,... | collective-permute-start | bytes 320 | tf_op jit(solution)/shard_map/ppermute | solution.py:180
  89.1 7.9 %collective-permute-start.14 = (f32[26]{0:T(128)S(1)}, f32[26]{0:T(128)S(1)}, u32[]{:S(2)}, u32[]{:S(2)}) collective-permute-start(f32[26]{0:T(128)S(1)} %fusion.33), channel_id=1, source_target_pairs={{0,8},{1,9},{2,10},{3,11},{4,12},{5,13},{6,14},{7,15},{8,0},{9,1},... | collective-permute-start | bytes 320 | tf_op jit(solution)/shard_map/ppermute | solution.py:171
  93.3 27.3 %all-to-all-start.1 = ((f32[32,8,869]{2,1,0:T(8,128)}), f32[32,8,869]{2,1,0:T(8,128)S(1)}, u32[]{:S(2)}, u32[]{:S(2)}) async-start(f32[32,8,869]{2,1,0:T(8,128)} %pad_maximum_fusion), calls=%async_computation.1 | async-start | bytes 1835008 | tf_op jit(solution)/shard_map/all_to_all | solution.py:401
  97.0 7.6 %collective-permute-start.17 = (f32[26]{0:T(128)S(1)}, f32[26]{0:T(128)S(1)}, u32[]{:S(2)}, u32[]{:S(2)}) collective-permute-start(f32[26]{0:T(128)S(1)} %fusion.54), channel_id=1, source_target_pairs={{48,0},{0,16},{16,32},{32,48},{112,64},{64,80},{80,96},{96,112},{1... | collective-permute-start | bytes 320 | tf_op jit(solution)/shard_map/ppermute | solution.py:180
  98.9 6.1 %collective-permute-start.16 = (f32[26]{0:T(128)S(1)}, f32[26]{0:T(128)S(1)}, u32[]{:S(2)}, u32[]{:S(2)}) collective-permute-start(f32[26]{0:T(128)S(1)} %fusion.54), channel_id=1, source_target_pairs={{32,0},{48,16},{0,32},{16,48},{96,64},{112,80},{64,96},{80,112},{1... | collective-permute-start | bytes 320 | tf_op jit(solution)/shard_map/ppermute | solution.py:180
  101.6 5.8 %collective-permute-start.15 = (f32[26]{0:T(128)S(1)}, f32[26]{0:T(128)S(1)}, u32[]{:S(2)}, u32[]{:S(2)}) collective-permute-start(f32[26]{0:T(128)S(1)} %fusion.54), channel_id=1, source_target_pairs={{16,0},{32,16},{48,32},{0,48},{80,64},{96,80},{112,96},{64,112},{1... | collective-permute-start | bytes 320 | tf_op jit(solution)/shard_map/ppermute | solution.py:180
  107.4 5.4 %collective-permute-start.20 = (f32[26]{0:T(128)S(1)}, f32[26]{0:T(128)S(1)}, u32[]{:S(2)}, u32[]{:S(2)}) collective-permute-start(f32[26]{0:T(128)S(1)} %fusion.53), channel_id=1, source_target_pairs={{192,0},{208,16},{224,32},{240,48},{0,64},{16,80},{32,96},{48,112}... | collective-permute-start | bytes 320 | tf_op jit(solution)/shard_map/ppermute | solution.py:180
  109.5 5.0 %collective-permute-start.19 = (f32[26]{0:T(128)S(1)}, f32[26]{0:T(128)S(1)}, u32[]{:S(2)}, u32[]{:S(2)}) collective-permute-start(f32[26]{0:T(128)S(1)} %fusion.53), channel_id=1, source_target_pairs={{128,0},{144,16},{160,32},{176,48},{192,64},{208,80},{224,96},{240... | collective-permute-start | bytes 320 | tf_op jit(solution)/shard_map/ppermute | solution.py:180
  112.6 3.5 %collective-permute-start.18 = (f32[26]{0:T(128)S(1)}, f32[26]{0:T(128)S(1)}, u32[]{:S(2)}, u32[]{:S(2)}) collective-permute-start(f32[26]{0:T(128)S(1)} %fusion.53), channel_id=1, source_target_pairs={{64,0},{80,16},{96,32},{112,48},{128,64},{144,80},{160,96},{176,11... | collective-permute-start | bytes 320 | tf_op jit(solution)/shard_map/ppermute | solution.py:180
  116.2 0.7 copy-start.5
  116.2 0.7 copy-start.8
  117.0 0.7 copy-start.7

commit v16 on v15

--- a/solution.py
+++ b/solution.py
@@ -351,9 +351,7 @@
     upper_t = lines[:, :, node_count + 26 : node_count + 51]
     inverse_t = lines[:, :, node_count + 51 : node_count + 76]
     cells = total_length * share
-    old_moments = tree_sum(
-        jnp.dot(dist_t.reshape(cells, node_count), weighted.T, precision=HIGH), ("vel",)
-    )
+    old_part = jnp.dot(dist_t.reshape(cells, node_count), weighted.T, precision=HIGH)
     node_speed = jnp.abs(node_signed)
     denominator = node_speed * total_length + thickness + pseudo_rate
     carry_rate = node_speed * total_length / denominator
@@ -365,18 +363,27 @@
     moment_den = moment_speed * total_length + thickness + pseudo_rate
     moment_rate = moment_speed * total_length / moment_den
     moment_drive = thickness * jnp.repeat(
-        old_moments.reshape(total_length, share, 5), NXI, axis=2
+        old_part.reshape(total_length, share, 5), NXI, axis=2
     ) / moment_den
-    moment_field = line_sweep(moment_rate, moment_drive, moment_signed)
+    moment_part = line_sweep(moment_rate, moment_drive, moment_signed).reshape(cells, 5 * NXI)
+    coupling = jnp.asarray(np.einsum(
+        "irx,jrx->jxi",
+        weighted_np.reshape(5, -1, NXI),
+        rebuild_np.reshape(5, -1, NXI),
+    ).reshape(5 * NXI, 5), jnp.float32)
+    half_part = jnp.dot(
+        own_field.reshape(cells, node_count), weighted.T, precision=HIGH
+    ) + jnp.dot(moment_part, coupling, precision=HIGH)
+    summed = tree_sum(jnp.concatenate([half_part, old_part, moment_part], axis=1), ("vel",))
+    half_moments = summed[:, :5]
+    old_moments = summed[:, 5:10]
+    moment_field = summed[:, 10:]
     chosen = jnp.asarray(
         (np.arange(node_count)[None, :] % NXI) == np.arange(NXI)[:, None], jnp.float32
     )
     spread_basis = (rebuild[:, None, :] * chosen[None]).reshape(5 * NXI, node_count)
-    half_field = own_field + jnp.dot(
-        moment_field.reshape(cells, 5 * NXI), spread_basis, precision=HIGH
-    ).reshape(total_length, share, node_count)
-    half_moments = tree_sum(
-        jnp.dot(half_field.reshape(cells, node_count), weighted.T, precision=HIGH), ("vel",)
+    half_field = own_field + jnp.dot(moment_field, spread_basis, precision=HIGH).reshape(
+        total_length, share, node_count
     )
     residual = (half_moments - old_moments).reshape(total_length, share, 5)
     correction = line_block(inverse_t, residual)

time: 124 us -> 127 us (1.024)
  waiting for transfers between devices: 38 us -> 44.3 us
  starting transfers between devices: 49.3 us -> 43.5 us
  local copies, waits for them, and re-layouts: 13.8 us -> 15.5 us
    ppermute x15 -> x12, waiting for transfers between devices: 14 us -> 19.5 us  [group_sum(): shifted.append(lax.ppermute(block, axis, pairs))]
    ppermute x15 -> x12, starting transfers between devices: 25.5 us -> 21.1 us  [group_sum(): shifted.append(lax.ppermute(block, axis, pairs))]
    ppermute x6 -> x4, starting transfers between devices: 13.1 us -> 11.7 us  [group_sum(): return block + lax.ppermute(block, axis, pairs)]
    ppermute x6 -> x4, waiting for transfers between devices: 6.29 us -> 7.11 us  [group_sum(): return block + lax.ppermute(block, axis, pairs)]
    unnamed x24 -> x28, local copies, waits for them, and re-layouts: 6.02 us -> 6.45 us
    dot_general x2 -> x3, matrix products: 3.36 us -> 3.12 us  [the longest x1 2.03 us: body(): jnp.dot(own_field.reshape(cells, node_count), weighted.T, precision=HIGH)]
  transfers between devices with their start and end apart: 23 -> 18, of which waited for: 16 -> 16; matrix products, arithmetic and copies ran while one was open for 7% -> 5% of each run, Pallas kernels for 2% -> 0%
where the time goes in v16:
time: 127 us; the launch traced here: 125 us
  waiting for transfers between devices  44.3 us (35%)
  starting transfers between devices  43.5 us (34%)
  local copies, waits for them, and re-layouts  15.5 us (12%)
  other arithmetic  8.76 us (7%)
  matrix products  6.67 us (5%)
  Pallas kernels  4.91 us (4%)
  between operations  1.52 us (1%)
    ppermute x12, starting transfers between devices, group_sum(): shifted.append(lax.ppermute(block, axis, pairs))  21.1 us
    ppermute x12, waiting for transfers between devices, group_sum(): shifted.append(lax.ppermute(block, axis, pairs))  19.5 us
    all_to_all x1, waiting for transfers between devices, body(): lines = lax.all_to_all(packed, 'sec', 1, 0, tiled=True)  17.7 us
    ppermute x4, starting transfers between devices, group_sum(): return block + lax.ppermute(block, axis, pairs)  11.7 us
    ppermute x4, waiting for transfers between devices, group_sum(): return block + lax.ppermute(block, axis, pairs)  7.11 us
    all_to_all x1, starting transfers between devices, body(): lines = lax.all_to_all(packed, 'sec', 1, 0, tiled=True)  7.03 us
    unnamed x28, local copies, waits for them, and re-layouts  6.45 us
    pallas_call x2, Pallas kernels, line_sweep(): pl.pallas_call(sweep_kernel, out_shape=jax.ShapeDtypeStruct(drive_term.sh...  4.91 us
  transfers between devices with their start and end apart: 18, of which 16 were waited for; matrix products, arithmetic and copies ran while one was open for 5% of the time, Pallas kernels for 0%

profile of v16, /device:TPU:32, one launch (start us, length us, event | category | flops | bytes accessed | tf_op | source)
XLA Modules:
  0.0 125.2 jit_solution(15542295996751831580)
XLA Ops:
  0.6 0.7 copy-done.11
  1.5 0.6 copy-done.4
  2.2 0.6 copy-done.5
  2.9 0.6 copy-done.6
  3.7 1.5 %copy.150 = f32[864,256]{0,1:T(8,128)S(1)} copy(f32[864,256]{1,0:T(8,128)} %param.13) | data formatting | bytes 1769472 | tf_op args[0]
  5.6 1.8 %copy.155 = f32[2,128,940]{2,0,1:T(2,128)} copy(f32[2,128,940]{2,1,0:T(8,128)S(1)} %concatenate.36) | data formatting | bytes 1925120 | tf_op jit(solution)/shard_map/concatenate | solution.py:344
  7.4 7.0 %all-to-all-start = ((f32[2,128,940]{2,0,1:T(2,128)}), f32[2,128,940]{2,0,1:T(2,128)S(1)}, u32[]{:S(2)}, u32[]{:S(2)}) async-start(f32[2,128,940]{2,0,1:T(2,128)} %copy.155), calls=%async_computation | async-start | bytes 2097152 | tf_op jit(solution)/shard_map/all_to_all | solution.py:347
  14.5 17.7 %all-to-all-done = f32[2,128,940]{2,0,1:T(2,128)S(1)} async-done(((f32[2,128,940]{2,0,1:T(2,128)}), f32[2,128,940]{2,0,1:T(2,128)S(1)}, u32[]{:S(2)}, u32[]{:S(2)}) %all-to-all-start) | async-done | bytes 962592 | tf_op jit(solution)/shard_map/all_to_all | solution.py:347
  32.7 1.6 %fusion = f32[256,5]{0,1:T(8,128)S(1)} fusion(f32[32,8,940]{2,1,0:T(8,128)S(1)} %bitcast.157, f32[5,13824]{1,0:T(8,128)} %constant.165.clone, s32[]{:T(128)S(6)} %select_n.120), kind=kOutput, calls=%fused_computation.5 | convolution fusion | flops 13271040 | bytes 951300 | tf_op jit(solution)/shard_map/dot_general | solution.py:354
  35.1 0.6 copy-done.12
  35.7 0.8 multiply_divide_fusion
  36.5 2.0 %shard_map.141 = f32[32,8,120]{2,1,0:T(8,128)} custom-call(f32[32,8,120]{2,1,0:T(8,128)} %get-tuple-element.34.rate_ref, f32[32,8,120]{2,1,0:T(8,128)} %get-tuple-element.33.drive_ref, f32[1,120]{1,0:T(1,128)} %constant.194.sign_ref), custom_call_target="tpu_custom_call" | custom-call | tf_op jit(solution)/shard_map/pallas_call | solution.py:315
  38.5 1.0 copy.163
  39.5 1.5 %fusion.4 = (f32[32,8,864]{2,1,0:T(8,128)}, f32[32,8,864]{2,1,0:T(8,128)}) fusion(f32[32,8,940]{2,1,0:T(8,128)S(1)} %bitcast.158, f32[32,8]{1,0:T(8,128)S(1)} %bitcast.188, f32[864]{0:T(1024)S(1)} %copy-done.8), kind=kLoop, calls=%fused_computation.12 | loop fusion | flops 884736 | bytes 2658688 | tf_op jit(solution)/shard_map/div | solution.py:358
  41.0 2.9 %shard_map.140 = f32[32,8,864]{2,1,0:T(8,128)} custom-call(f32[32,8,864]{2,1,0:T(8,128)} %get-tuple-element.32.rate_ref, f32[32,8,864]{2,1,0:T(8,128)} %get-tuple-element.31.drive_ref, f32[1,864]{1,0:T(1,128)} %constant.191.sign_ref), custom_call_target="tpu_custom_call" | custom-call | tf_op jit(solution)/shard_map/pallas_call | solution.py:315
  44.0 2.0 %fusion.2 = f32[256,5]{0,1:T(8,128)S(1)} fusion(f32[32,8,864]{2,1,0:T(8,128)} %shard_map.140, f32[5,13824]{1,0:T(8,128)} %constant.165.clone, s32[]{:T(128)S(6)} %select_n.120), kind=kOutput, calls=%fused_computation.7 | convolution fusion | flops 13271040 | bytes 951300 | tf_op jit(solution)/shard_map/dot_general | solution.py:374
  46.7 0.8 constant_dynamic-slice_fusion.11
  47.8 2.0 %collective-permute-start.3 = (f32[256,130]{0,1:T(8,128)S(1)}, f32[256,130]{0,1:T(8,128)S(1)}, u32[]{:S(2)}, u32[]{:S(2)}) collective-permute-start(f32[256,130]{0,1:T(8,128)S(1)} %fusion.41), channel_id=1, source_target_pairs={{6,0},{7,1},{0,2},{1,3},{2,4},{3,5},{4,6},{5,7},{14,8},{15,9},{8,1... | collective-permute-start | bytes 399368 | tf_op jit(solution)/shard_map/ppermute | solution.py:180
  49.8 1.5 %collective-permute-start.2 = (f32[256,130]{0,1:T(8,128)S(1)}, f32[256,130]{0,1:T(8,128)S(1)}, u32[]{:S(2)}, u32[]{:S(2)}) collective-permute-start(f32[256,130]{0,1:T(8,128)S(1)} %fusion.41), channel_id=1, source_target_pairs={{4,0},{5,1},{6,2},{7,3},{0,4},{1,5},{2,6},{3,7},{12,8},{13,9},{14,... | collective-permute-start | bytes 399368 | tf_op jit(solution)/shard_map/ppermute | solution.py:180
  51.3 1.9 %collective-permute-start.1 = (f32[256,130]{0,1:T(8,128)S(1)}, f32[256,130]{0,1:T(8,128)S(1)}, u32[]{:S(2)}, u32[]{:S(2)}) collective-permute-start(f32[256,130]{0,1:T(8,128)S(1)} %fusion.41), channel_id=1, source_target_pairs={{2,0},{3,1},{4,2},{5,3},{6,4},{7,5},{0,6},{1,7},{10,8},{11,9},{12,... | collective-permute-start | bytes 399368 | tf_op jit(solution)/shard_map/ppermute | solution.py:180
  53.2 6.6 %collective-permute-done.3 = f32[256,130]{0,1:T(8,128)S(1)} collective-permute-done((f32[256,130]{0,1:T(8,128)S(1)}, f32[256,130]{0,1:T(8,128)S(1)}, u32[]{:S(2)}, u32[]{:S(2)}) %collective-permute-start.3) | collective-permute-done | bytes 133152 | tf_op jit(solution)/shard_map/ppermute | solution.py:180
  59.8 2.2 %collective-permute-done.2 = f32[256,130]{0,1:T(8,128)S(1)} collective-permute-done((f32[256,130]{0,1:T(8,128)S(1)}, f32[256,130]{0,1:T(8,128)S(1)}, u32[]{:S(2)}, u32[]{:S(2)}) %collective-permute-start.2) | collective-permute-done | bytes 133152 | tf_op jit(solution)/shard_map/ppermute | solution.py:180
  62.0 2.1 %collective-permute-done.1 = f32[256,130]{0,1:T(8,128)S(1)} collective-permute-done((f32[256,130]{0,1:T(8,128)S(1)}, f32[256,130]{0,1:T(8,128)S(1)}, u32[]{:S(2)}, u32[]{:S(2)}) %collective-permute-start.1) | collective-permute-done | bytes 133152 | tf_op jit(solution)/shard_map/ppermute | solution.py:180
  64.2 6.1 %collective-permute-start.4 = (f32[256,130]{0,1:T(8,128)S(1)}, f32[256,130]{0,1:T(8,128)S(1)}, u32[]{:S(2)}, u32[]{:S(2)}) collective-permute-start(f32[256,130]{0,1:T(8,128)S(1)} %add_bitcast_fusion), channel_id=1, source_target_pairs={{0,8},{1,9},{2,10},{3,11},{4,12},{5,13},{6,14},{7,15},{8,0},{9,1},... | collective-permute-start | bytes 399368 | tf_op jit(solution)/shard_map/ppermute | solution.py:171
  70.9 5.9 %collective-permute-done.4 = f32[256,130]{0,1:T(8,128)S(1)} collective-permute-done((f32[256,130]{0,1:T(8,128)S(1)}, f32[256,130]{0,1:T(8,128)S(1)}, u32[]{:S(2)}, u32[]{:S(2)}) %collective-permute-start.4) | collective-permute-done | bytes 133152 | tf_op jit(solution)/shard_map/ppermute | solution.py:171
  78.9 0.9 convolution_add_fusion.1
  79.8 1.7 %abs_reduce_fusion = (f32[864]{0:T(1024)S(1)}, f32[32,8,864]{2,1,0:T(8,128)S(1)}) fusion(f32[32,8,864]{2,1,0:T(8,128)S(1)} %convolution_add_fusion.1, f32[32,8,5]{2,1,0:T(8,128)S(1)} %copy.173, f32[5,13824]{1,0:T(8,128)} %constant.166.clone, s32[]{:T(128)S(6)} %select_n.120), kind=kOutput, calls=%fused_computation.10 | convolution fusion | flops 13933728 | bytes 1806724 | tf_op jit(solution)/shard_map/dot_general | solution.py:400
  81.6 0.8 dynamic-slice_multiply_fusion
  82.7 0.9 collective-permute-done.5
  84.1 1.7 %collective-permute-start.6 = (f32[26]{0:T(128)S(1)}, f32[26]{0:T(128)S(1)}, u32[]{:S(2)}, u32[]{:S(2)}) collective-permute-start(f32[26]{0:T(128)S(1)} %fusion.57), channel_id=1, source_target_pairs={{2,0},{3,1},{4,2},{5,3},{6,4},{7,5},{0,6},{1,7},{10,8},{11,9},{12,... | collective-permute-start | bytes 320 | tf_op jit(solution)/shard_map/ppermute | solution.py:180
  85.8 1.5 %collective-permute-done.8 = f32[26]{0:T(128)S(1)} collective-permute-done((f32[26]{0:T(128)S(1)}, f32[26]{0:T(128)S(1)}, u32[]{:S(2)}, u32[]{:S(2)}) %collective-permute-start.8) | collective-permute-done | bytes 136 | tf_op jit(solution)/shard_map/ppermute | solution.py:180
  87.3 1.2 collective-permute-done.7
  88.8 5.5 %collective-permute-start.9 = (f32[26]{0:T(128)S(1)}, f32[26]{0:T(128)S(1)}, u32[]{:S(2)}, u32[]{:S(2)}) collective-permute-start(f32[26]{0:T(128)S(1)} %fusion.34), channel_id=1, source_target_pairs={{0,8},{1,9},{2,10},{3,11},{4,12},{5,13},{6,14},{7,15},{8,0},{9,1},... | collective-permute-start | bytes 320 | tf_op jit(solution)/shard_map/ppermute | solution.py:171
  94.3 1.0 pad_maximum_fusion
  95.3 3.6 %all-to-all-start.1 = ((f32[32,8,869]{2,1,0:T(8,128)}), f32[32,8,869]{2,1,0:T(8,128)S(1)}, u32[]{:S(2)}, u32[]{:S(2)}) async-start(f32[32,8,869]{2,1,0:T(8,128)} %pad_maximum_fusion), calls=%async_computation.1 | async-start | bytes 1835008 | tf_op jit(solution)/shard_map/all_to_all | solution.py:408
  99.0 1.9 %collective-permute-start.12 = (f32[26]{0:T(128)S(1)}, f32[26]{0:T(128)S(1)}, u32[]{:S(2)}, u32[]{:S(2)}) collective-permute-start(f32[26]{0:T(128)S(1)} %fusion.56), channel_id=1, source_target_pairs={{48,0},{0,16},{16,32},{32,48},{112,64},{64,80},{80,96},{96,112},{1... | collective-permute-start | bytes 320 | tf_op jit(solution)/shard_map/ppermute | solution.py:180
  100.9 2.7 %collective-permute-start.11 = (f32[26]{0:T(128)S(1)}, f32[26]{0:T(128)S(1)}, u32[]{:S(2)}, u32[]{:S(2)}) collective-permute-start(f32[26]{0:T(128)S(1)} %fusion.56), channel_id=1, source_target_pairs={{32,0},{48,16},{0,32},{16,48},{96,64},{112,80},{64,96},{80,112},{1... | collective-permute-start | bytes 320 | tf_op jit(solution)/shard_map/ppermute | solution.py:180
  103.6 1.5 %collective-permute-start.10 = (f32[26]{0:T(128)S(1)}, f32[26]{0:T(128)S(1)}, u32[]{:S(2)}, u32[]{:S(2)}) collective-permute-start(f32[26]{0:T(128)S(1)} %fusion.56), channel_id=1, source_target_pairs={{16,0},{32,16},{48,32},{0,48},{80,64},{96,80},{112,96},{64,112},{1... | collective-permute-start | bytes 320 | tf_op jit(solution)/shard_map/ppermute | solution.py:180
  105.0 1.9 %collective-permute-done.12 = f32[26]{0:T(128)S(1)} collective-permute-done((f32[26]{0:T(128)S(1)}, f32[26]{0:T(128)S(1)}, u32[]{:S(2)}, u32[]{:S(2)}) %collective-permute-start.12) | collective-permute-done | bytes 136 | tf_op jit(solution)/shard_map/ppermute | solution.py:180
  107.2 4.6 %collective-permute-start.15 = (f32[26]{0:T(128)S(1)}, f32[26]{0:T(128)S(1)}, u32[]{:S(2)}, u32[]{:S(2)}) collective-permute-start(f32[26]{0:T(128)S(1)} %fusion.55), channel_id=1, source_target_pairs={{192,0},{208,16},{224,32},{240,48},{0,64},{16,80},{32,96},{48,112}... | collective-permute-start | bytes 320 | tf_op jit(solution)/shard_map/ppermute | solution.py:180
  111.8 3.1 %collective-permute-start.14 = (f32[26]{0:T(128)S(1)}, f32[26]{0:T(128)S(1)}, u32[]{:S(2)}, u32[]{:S(2)}) collective-permute-start(f32[26]{0:T(128)S(1)} %fusion.55), channel_id=1, source_target_pairs={{128,0},{144,16},{160,32},{176,48},{192,64},{208,80},{224,96},{240... | collective-permute-start | bytes 320 | tf_op jit(solution)/shard_map/ppermute | solution.py:180
  115.0 1.9 %collective-permute-done.14 = f32[26]{0:T(128)S(1)} collective-permute-done((f32[26]{0:T(128)S(1)}, f32[26]{0:T(128)S(1)}, u32[]{:S(2)}, u32[]{:S(2)}) %collective-permute-start.14) | collective-permute-done | bytes 136 | tf_op jit(solution)/shard_map/ppermute | solution.py:180
  116.8 1.6 %collective-permute-done.13 = f32[26]{0:T(128)S(1)} collective-permute-done((f32[26]{0:T(128)S(1)}, f32[26]{0:T(128)S(1)}, u32[]{:S(2)}, u32[]{:S(2)}) %collective-permute-start.13) | collective-permute-done | bytes 136 | tf_op jit(solution)/shard_map/ppermute | solution.py:180
  119.3 0.7 copy-done.9
  120.0 1.3 %multiply_bitcast_fusion.1 = (f32[1,24]{1,0:T(1,128)S(1)}, f32[1,24]{1,0:T(1,128)S(1)}, f32[1,24]{1,0:T(1,128)S(1)}, f32[1,24]{1,0:T(1,128)S(1)}) fusion(f32[24]{0:T(128)S(1)} %copy-done.7, f32[1,26]{1,0:T(1,128)S(1)} %fusion.20, f32[1,24]{1,0:T(1,128)S(1)} %copy-done.9, f32[5,24]{1,0:T(8,128)S(1)} %fusion.15, f32[]{:T(128)} %bitcast.55, f32[]{:T(128)} %bitcast.56), kind=kLoop, calls=%fused_computation.93 | loop fusion | flops 480 | bytes 1160 | tf_op jit(solution)/shard_map/stack | solution.py:423
  121.5 1.3 %add_bitcast_fusion.1 = f32[24]{0:T(128)S(1)} fusion(f32[1,24]{1,0:T(1,128)S(1)} %copy-done.9, f32[1,24]{1,0:T(1,128)S(1)} %get-tuple-element.17, f32[1,24]{1,0:T(1,128)S(1)} %get-tuple-element.16, f32[5,24]{1,0:T(8,128)S(1)} %fusion.13, f32[]{:T(128)} %bitcast.56, f32[]{:T(128)} %bitcast.55), kind=kLoop, calls=%fused_computation.90 | loop fusion | flops 432 | bytes 872 | tf_op jit(solution)/shard_map/sub | solution.py:430
  123.1 0.7 copy.179
  124.1 1.1 multiply_add_fusion
  (119 shorter events, 8.4 us)
Async XLA Ops:
  0.6 0.7 copy-start.11
  1.3 0.8 copy-start.4
  2.1 0.8 copy-start.5
  2.8 0.8 copy-start.6
  7.4 24.7 %all-to-all-start = ((f32[2,128,940]{2,0,1:T(2,128)}), f32[2,128,940]{2,0,1:T(2,128)S(1)}, u32[]{:S(2)}, u32[]{:S(2)}) async-start(f32[2,128,940]{2,0,1:T(2,128)} %copy.155), calls=%async_computation | async-start | bytes 2097152 | tf_op jit(solution)/shard_map/all_to_all | solution.py:347
  35.1 0.7 copy-start.12
  38.5 1.0 copy-start.8
  44.0 2.0 %copy-start.1 = (f32[32,8,120]{2,1,0:T(8,128)S(1)}, f32[32,8,120]{2,1,0:T(8,128)}, u32[]{:S(2)}) copy-start(f32[32,8,120]{2,1,0:T(8,128)} %shard_map.141) | copy-start | bytes 368644
  44.0 2.1 %copy-start.3 = (f32[120,5]{1,0:T(8,128)S(1)}, f32[120,5]{1,0:T(8,128)}, u32[]{:S(2)}) copy-start(f32[120,5]{1,0:T(8,128)} %constant.171.clone) | copy-start | bytes 7204
  46.3 1.4 %collective-permute-start = (f32[256,130]{0,1:T(8,128)S(1)}, f32[256,130]{0,1:T(8,128)S(1)}, u32[]{:S(2)}, u32[]{:S(2)}) collective-permute-start(f32[256,130]{0,1:T(8,128)S(1)} %pad_maximum_fusion.2), channel_id=1, source_target_pairs={{0,1},{1,0},{2,3},{3,2},{4,5},{5,4},{6,7},{7,6},{8,9},{9,8},{10,11... | collective-permute-start | bytes 399368 | tf_op jit(solution)/shard_map/ppermute | solution.py:171
  47.6 5.6 %copy-start.2 = (f32[24,864]{1,0:T(8,128)S(1)}, f32[24,864]{1,0:T(8,128)}, u32[]{:S(2)}) copy-start(f32[24,864]{1,0:T(8,128)} %constant.172.clone) | copy-start | bytes 248836
  47.8 12.0 %collective-permute-start.3 = (f32[256,130]{0,1:T(8,128)S(1)}, f32[256,130]{0,1:T(8,128)S(1)}, u32[]{:S(2)}, u32[]{:S(2)}) collective-permute-start(f32[256,130]{0,1:T(8,128)S(1)} %fusion.41), channel_id=1, source_target_pairs={{6,0},{7,1},{0,2},{1,3},{2,4},{3,5},{4,6},{5,7},{14,8},{15,9},{8,1... | collective-permute-start | bytes 399368 | tf_op jit(solution)/shard_map/ppermute | solution.py:180
  49.8 12.2 %collective-permute-start.2 = (f32[256,130]{0,1:T(8,128)S(1)}, f32[256,130]{0,1:T(8,128)S(1)}, u32[]{:S(2)}, u32[]{:S(2)}) collective-permute-start(f32[256,130]{0,1:T(8,128)S(1)} %fusion.41), channel_id=1, source_target_pairs={{4,0},{5,1},{6,2},{7,3},{0,4},{1,5},{2,6},{3,7},{12,8},{13,9},{14,... | collective-permute-start | bytes 399368 | tf_op jit(solution)/shard_map/ppermute | solution.py:180
  51.3 12.8 %collective-permute-start.1 = (f32[256,130]{0,1:T(8,128)S(1)}, f32[256,130]{0,1:T(8,128)S(1)}, u32[]{:S(2)}, u32[]{:S(2)}) collective-permute-start(f32[256,130]{0,1:T(8,128)S(1)} %fusion.41), channel_id=1, source_target_pairs={{2,0},{3,1},{4,2},{5,3},{6,4},{7,5},{0,6},{1,7},{10,8},{11,9},{12,... | collective-permute-start | bytes 399368 | tf_op jit(solution)/shard_map/ppermute | solution.py:180
  64.2 12.6 %collective-permute-start.4 = (f32[256,130]{0,1:T(8,128)S(1)}, f32[256,130]{0,1:T(8,128)S(1)}, u32[]{:S(2)}, u32[]{:S(2)}) collective-permute-start(f32[256,130]{0,1:T(8,128)S(1)} %add_bitcast_fusion), channel_id=1, source_target_pairs={{0,8},{1,9},{2,10},{3,11},{4,12},{5,13},{6,14},{7,15},{8,0},{9,1},... | collective-permute-start | bytes 399368 | tf_op jit(solution)/shard_map/ppermute | solution.py:171
  77.8 1.2 copy-start
  82.5 1.1 collective-permute-start.5
  83.8 3.6 %collective-permute-start.8 = (f32[26]{0:T(128)S(1)}, f32[26]{0:T(128)S(1)}, u32[]{:S(2)}, u32[]{:S(2)}) collective-permute-start(f32[26]{0:T(128)S(1)} %fusion.57), channel_id=1, source_target_pairs={{6,0},{7,1},{0,2},{1,3},{2,4},{3,5},{4,6},{5,7},{14,8},{15,9},{8,1... | collective-permute-start | bytes 320 | tf_op jit(solution)/shard_map/ppermute | solution.py:180
  83.8 4.7 %collective-permute-start.7 = (f32[26]{0:T(128)S(1)}, f32[26]{0:T(128)S(1)}, u32[]{:S(2)}, u32[]{:S(2)}) collective-permute-start(f32[26]{0:T(128)S(1)} %fusion.57), channel_id=1, source_target_pairs={{4,0},{5,1},{6,2},{7,3},{0,4},{1,5},{2,6},{3,7},{12,8},{13,9},{14,... | collective-permute-start | bytes 320 | tf_op jit(solution)/shard_map/ppermute | solution.py:180
  84.1 4.7 %collective-permute-start.6 = (f32[26]{0:T(128)S(1)}, f32[26]{0:T(128)S(1)}, u32[]{:S(2)}, u32[]{:S(2)}) collective-permute-start(f32[26]{0:T(128)S(1)} %fusion.57), channel_id=1, source_target_pairs={{2,0},{3,1},{4,2},{5,3},{6,4},{7,5},{0,6},{1,7},{10,8},{11,9},{12,... | collective-permute-start | bytes 320 | tf_op jit(solution)/shard_map/ppermute | solution.py:180
  88.8 10.2 %collective-permute-start.9 = (f32[26]{0:T(128)S(1)}, f32[26]{0:T(128)S(1)}, u32[]{:S(2)}, u32[]{:S(2)}) collective-permute-start(f32[26]{0:T(128)S(1)} %fusion.34), channel_id=1, source_target_pairs={{0,8},{1,9},{2,10},{3,11},{4,12},{5,13},{6,14},{7,15},{8,0},{9,1},... | collective-permute-start | bytes 320 | tf_op jit(solution)/shard_map/ppermute | solution.py:171
  95.3 27.6 %all-to-all-start.1 = ((f32[32,8,869]{2,1,0:T(8,128)}), f32[32,8,869]{2,1,0:T(8,128)S(1)}, u32[]{:S(2)}, u32[]{:S(2)}) async-start(f32[32,8,869]{2,1,0:T(8,128)} %pad_maximum_fusion), calls=%async_computation.1 | async-start | bytes 1835008 | tf_op jit(solution)/shard_map/all_to_all | solution.py:408
  99.0 7.9 %collective-permute-start.12 = (f32[26]{0:T(128)S(1)}, f32[26]{0:T(128)S(1)}, u32[]{:S(2)}, u32[]{:S(2)}) collective-permute-start(f32[26]{0:T(128)S(1)} %fusion.56), channel_id=1, source_target_pairs={{48,0},{0,16},{16,32},{32,48},{112,64},{64,80},{80,96},{96,112},{1... | collective-permute-start | bytes 320 | tf_op jit(solution)/shard_map/ppermute | solution.py:180
  100.9 6.1 %collective-permute-start.11 = (f32[26]{0:T(128)S(1)}, f32[26]{0:T(128)S(1)}, u32[]{:S(2)}, u32[]{:S(2)}) collective-permute-start(f32[26]{0:T(128)S(1)} %fusion.56), channel_id=1, source_target_pairs={{32,0},{48,16},{0,32},{16,48},{96,64},{112,80},{64,96},{80,112},{1... | collective-permute-start | bytes 320 | tf_op jit(solution)/shard_map/ppermute | solution.py:180
  103.6 3.6 %collective-permute-start.10 = (f32[26]{0:T(128)S(1)}, f32[26]{0:T(128)S(1)}, u32[]{:S(2)}, u32[]{:S(2)}) collective-permute-start(f32[26]{0:T(128)S(1)} %fusion.56), channel_id=1, source_target_pairs={{16,0},{32,16},{48,32},{0,48},{80,64},{96,80},{112,96},{64,112},{1... | collective-permute-start | bytes 320 | tf_op jit(solution)/shard_map/ppermute | solution.py:180
  107.2 7.8 %collective-permute-start.15 = (f32[26]{0:T(128)S(1)}, f32[26]{0:T(128)S(1)}, u32[]{:S(2)}, u32[]{:S(2)}) collective-permute-start(f32[26]{0:T(128)S(1)} %fusion.55), channel_id=1, source_target_pairs={{192,0},{208,16},{224,32},{240,48},{0,64},{16,80},{32,96},{48,112}... | collective-permute-start | bytes 320 | tf_op jit(solution)/shard_map/ppermute | solution.py:180
  111.8 5.0 %collective-permute-start.14 = (f32[26]{0:T(128)S(1)}, f32[26]{0:T(128)S(1)}, u32[]{:S(2)}, u32[]{:S(2)}) collective-permute-start(f32[26]{0:T(128)S(1)} %fusion.55), channel_id=1, source_target_pairs={{128,0},{144,16},{160,32},{176,48},{192,64},{208,80},{224,96},{240... | collective-permute-start | bytes 320 | tf_op jit(solution)/shard_map/ppermute | solution.py:180
  114.9 3.5 %collective-permute-start.13 = (f32[26]{0:T(128)S(1)}, f32[26]{0:T(128)S(1)}, u32[]{:S(2)}, u32[]{:S(2)}) collective-permute-start(f32[26]{0:T(128)S(1)} %fusion.55), channel_id=1, source_target_pairs={{64,0},{80,16},{96,32},{112,48},{128,64},{144,80},{160,96},{176,11... | collective-permute-start | bytes 320 | tf_op jit(solution)/shard_map/ppermute | solution.py:180
  118.5 0.7 copy-start.7
  118.5 0.7 copy-start.10
  119.3 0.7 copy-start.9

commit v17 on v13

--- a/solution.py
+++ b/solution.py
@@ -344,9 +344,8 @@
         [distribution, collision.reshape(1, cell_count), lower_blocks, upper_blocks, diag_inverse],
         axis=0,
     )
-    rows = packed.shape[0]
-    packed = packed.reshape(rows, length, TUBES).transpose(1, 2, 0)
-    lines = lax.all_to_all(packed, "sec", 1, 0, tiled=True)
+    packed = packed.reshape(packed.shape[0], length, TUBES)
+    lines = lax.all_to_all(packed, "sec", 2, 1, tiled=True).transpose(1, 2, 0)
     dist_t = lines[:, :, :node_count]
     thickness = lines[:, :, node_count : node_count + 1]
     lower_t = lines[:, :, node_count + 1 : node_count + 26]

time: 124 us -> 124 us (level)
    concatenate x5 -> x6, local copies, waits for them, and re-layouts: 0.91 us -> 2.69 us  [body(): jnp.concatenate([distribution, collision.reshape(1, cell_count), lower_bl...]
    transpose x1 -> x0, local copies, waits for them, and re-layouts: 1.78 us -> none  [body(): packed = packed.reshape(rows, length, TUBES).transpose(1, 2, 0)]
where the time goes in v17:
time: 124 us; the launch traced here: 123 us
  starting transfers between devices  49.3 us (40%)
  waiting for transfers between devices  38 us (31%)
  local copies, waits for them, and re-layouts  13.8 us (11%)
  other arithmetic  8.59 us (7%)
  matrix products  6.92 us (6%)
  Pallas kernels  4.91 us (4%)
  between operations  1.31 us (1%)
    ppermute x15, starting transfers between devices, group_sum(): shifted.append(lax.ppermute(block, axis, pairs))  25.5 us
    all_to_all x1, waiting for transfers between devices, body(): lines = lax.all_to_all(packed, 'sec', 2, 1, tiled=True).transpose(1, 2, 0)  17.7 us
    ppermute x15, waiting for transfers between devices, group_sum(): shifted.append(lax.ppermute(block, axis, pairs))  14 us
    ppermute x6, starting transfers between devices, group_sum(): return block + lax.ppermute(block, axis, pairs)  13.1 us
    all_to_all x1, starting transfers between devices, body(): lines = lax.all_to_all(packed, 'sec', 2, 1, tiled=True).transpose(1, 2, 0)  7.03 us
    ppermute x6, waiting for transfers between devices, group_sum(): return block + lax.ppermute(block, axis, pairs)  6.29 us
    unnamed x24, local copies, waits for them, and re-layouts  6.02 us
    pallas_call x2, Pallas kernels, line_sweep(): pl.pallas_call(sweep_kernel, out_shape=jax.ShapeDtypeStruct(drive_term.sh...  4.91 us
  transfers between devices with their start and end apart: 23, of which 16 were waited for; matrix products, arithmetic and copies ran while one was open for 7% of the time, Pallas kernels for 2%

profile of v17, /device:TPU:32, one launch (start us, length us, event | category | flops | bytes accessed | tf_op | source)
XLA Modules:
  0.0 122.9 jit_solution(12799778439889610862)
XLA Ops:
  0.6 0.7 copy-done.9
  3.7 1.5 %copy.94 = f32[864,256]{0,1:T(8,128)S(1)} copy(f32[864,256]{1,0:T(8,128)} %param.12) | data formatting | bytes 1769472 | tf_op args[0]
  5.6 1.8 %copy.99 = f32[940,2,128]{0,1,2:T(2,128)} copy(f32[940,2,128]{0,2,1:T(8,128)S(1)} %concatenate.49) | data formatting | bytes 1925120 | tf_op jit(solution)/shard_map/concatenate | solution.py:343
  7.4 7.0 %all-to-all-start = ((f32[940,2,128]{0,1,2:T(2,128)}), f32[940,2,128]{0,1,2:T(2,128)S(1)}, u32[]{:S(2)}, u32[]{:S(2)}) async-start(f32[940,2,128]{0,1,2:T(2,128)} %copy.99), calls=%async_computation | async-start | bytes 2097152 | tf_op jit(solution)/shard_map/all_to_all | solution.py:348
  14.4 17.7 %all-to-all-done = f32[940,2,128]{0,1,2:T(2,128)S(1)} async-done(((f32[940,2,128]{0,1,2:T(2,128)}), f32[940,2,128]{0,1,2:T(2,128)S(1)}, u32[]{:S(2)}, u32[]{:S(2)}) %all-to-all-start) | async-done | bytes 962592 | tf_op jit(solution)/shard_map/all_to_all | solution.py:348
  32.6 1.6 %fusion.2 = f32[256,5]{0,1:T(8,128)S(1)} fusion(f32[32,8,940]{2,1,0:T(8,128)S(1)} %bitcast.152, f32[5,13824]{1,0:T(8,128)} %constant.181.clone, s32[]{:T(128)S(6)} %select_n.134), kind=kOutput, calls=%fused_computation.6 | convolution fusion | flops 13271040 | bytes 951300 | tf_op jit(solution)/shard_map/dot_general | solution.py:356
  34.2 0.9 constant_dynamic-slice_fusion.12
  35.4 1.9 %collective-permute-start.3 = (f32[256,5]{0,1:T(8,128)S(1)}, f32[256,5]{0,1:T(8,128)S(1)}, u32[]{:S(2)}, u32[]{:S(2)}) collective-permute-start(f32[256,5]{0,1:T(8,128)S(1)} %add.281), channel_id=1, source_target_pairs={{6,0},{7,1},{0,2},{1,3},{2,4},{3,5},{4,6},{5,7},{14,8},{15,9},{8,1... | collective-permute-start | bytes 15368 | tf_op jit(solution)/shard_map/ppermute | solution.py:180
  37.3 1.4 %collective-permute-start.2 = (f32[256,5]{0,1:T(8,128)S(1)}, f32[256,5]{0,1:T(8,128)S(1)}, u32[]{:S(2)}, u32[]{:S(2)}) collective-permute-start(f32[256,5]{0,1:T(8,128)S(1)} %add.281), channel_id=1, source_target_pairs={{4,0},{5,1},{6,2},{7,3},{0,4},{1,5},{2,6},{3,7},{12,8},{13,9},{14,... | collective-permute-start | bytes 15368 | tf_op jit(solution)/shard_map/ppermute | solution.py:180
  38.7 2.0 %collective-permute-start.1 = (f32[256,5]{0,1:T(8,128)S(1)}, f32[256,5]{0,1:T(8,128)S(1)}, u32[]{:S(2)}, u32[]{:S(2)}) collective-permute-start(f32[256,5]{0,1:T(8,128)S(1)} %add.281), channel_id=1, source_target_pairs={{2,0},{3,1},{4,2},{5,3},{6,4},{7,5},{0,6},{1,7},{10,8},{11,9},{12,... | collective-permute-start | bytes 15368 | tf_op jit(solution)/shard_map/ppermute | solution.py:180
  41.2 0.7 collective-permute-done.2
  42.4 6.5 %collective-permute-start.4 = (f32[256,5]{0,1:T(8,128)S(1)}, f32[256,5]{0,1:T(8,128)S(1)}, u32[]{:S(2)}, u32[]{:S(2)}) collective-permute-start(f32[256,5]{0,1:T(8,128)S(1)} %add_bitcast_fusion.1), channel_id=1, source_target_pairs={{0,8},{1,9},{2,10},{3,11},{4,12},{5,13},{6,14},{7,15},{8,0},{9,1},... | collective-permute-start | bytes 15368 | tf_op jit(solution)/shard_map/ppermute | solution.py:171
  48.9 1.5 %fusion.4 = (f32[32,8,864]{2,1,0:T(8,128)}, f32[32,8,864]{2,1,0:T(8,128)}) fusion(f32[32,8,940]{2,1,0:T(8,128)S(1)} %bitcast.154, f32[32,8]{1,0:T(8,128)S(1)} %bitcast.181, f32[864]{0:T(1024)S(1)} %copy-done.6), kind=kLoop, calls=%fused_computation.11 | loop fusion | flops 884736 | bytes 2658688 | tf_op jit(solution)/shard_map/div | solution.py:361
  50.4 2.9 %shard_map.131 = f32[32,8,864]{2,1,0:T(8,128)} custom-call(f32[32,8,864]{2,1,0:T(8,128)} %get-tuple-element.30.rate_ref, f32[32,8,864]{2,1,0:T(8,128)} %get-tuple-element.29.drive_ref, f32[1,864]{1,0:T(1,128)} %constant.206.sign_ref), custom_call_target="tpu_custom_call" | custom-call | tf_op jit(solution)/shard_map/pallas_call | solution.py:315
  54.3 0.8 multiply_divide_fusion
  55.1 2.0 %shard_map.132 = f32[32,8,120]{2,1,0:T(8,128)} custom-call(f32[32,8,120]{2,1,0:T(8,128)} %get-tuple-element.32.rate_ref, f32[32,8,120]{2,1,0:T(8,128)} %get-tuple-element.31.drive_ref, f32[1,120]{1,0:T(1,128)} %constant.209.sign_ref), custom_call_target="tpu_custom_call" | custom-call | tf_op jit(solution)/shard_map/pallas_call | solution.py:315
  57.1 1.8 %convolution_add_fusion.1 = f32[32,8,864]{2,1,0:T(8,128)S(1)} fusion(f32[32,8,864]{2,1,0:T(8,128)S(1)} %copy-done, f32[32,8,120]{2,1,0:T(8,128)} %shard_map.132, f32[120,864,1]{1,0,2:T(8,128)S(1)} %bitcast.175), kind=kOutput, calls=%fused_computation.1 | convolution fusion | flops 318726144 | bytes 2307072 | tf_op jit(solution)/shard_map/dot_general | solution.py:376
  58.9 1.6 %fusion = f32[256,5]{0,1:T(8,128)S(1)} fusion(f32[32,8,864]{2,1,0:T(8,128)S(1)} %convolution_add_fusion.1, f32[5,13824]{1,0:T(8,128)} %constant.181.clone, s32[]{:T(128)S(6)} %select_n.134), kind=kOutput, calls=%fused_computation.4 | convolution fusion | flops 13271040 | bytes 918532 | tf_op jit(solution)/shard_map/dot_general | solution.py:380
  60.5 1.1 collective-permute-done.5
  61.8 2.4 %collective-permute-start.7 = (f32[256,5]{0,1:T(8,128)S(1)}, f32[256,5]{0,1:T(8,128)S(1)}, u32[]{:S(2)}, u32[]{:S(2)}) collective-permute-start(f32[256,5]{0,1:T(8,128)S(1)} %add.297), channel_id=1, source_target_pairs={{4,0},{5,1},{6,2},{7,3},{0,4},{1,5},{2,6},{3,7},{12,8},{13,9},{14,... | collective-permute-start | bytes 15368 | tf_op jit(solution)/shard_map/ppermute | solution.py:180
  64.2 1.9 %collective-permute-start.6 = (f32[256,5]{0,1:T(8,128)S(1)}, f32[256,5]{0,1:T(8,128)S(1)}, u32[]{:S(2)}, u32[]{:S(2)}) collective-permute-start(f32[256,5]{0,1:T(8,128)S(1)} %add.297), channel_id=1, source_target_pairs={{2,0},{3,1},{4,2},{5,3},{6,4},{7,5},{0,6},{1,7},{10,8},{11,9},{12,... | collective-permute-start | bytes 15368 | tf_op jit(solution)/shard_map/ppermute | solution.py:180
  66.4 1.5 %collective-permute-done.6 = f32[256,5]{0,1:T(8,128)S(1)} collective-permute-done((f32[256,5]{0,1:T(8,128)S(1)}, f32[256,5]{0,1:T(8,128)S(1)}, u32[]{:S(2)}, u32[]{:S(2)}) %collective-permute-start.6) | collective-permute-done | bytes 5152 | tf_op jit(solution)/shard_map/ppermute | solution.py:180
  67.8 3.4 %collective-permute-start.9 = (f32[256,5]{0,1:T(8,128)S(1)}, f32[256,5]{0,1:T(8,128)S(1)}, u32[]{:S(2)}, u32[]{:S(2)}) collective-permute-start(f32[256,5]{0,1:T(8,128)S(1)} %add_bitcast_fusion), channel_id=1, source_target_pairs={{0,8},{1,9},{2,10},{3,11},{4,12},{5,13},{6,14},{7,15},{8,0},{9,1},... | collective-permute-start | bytes 15368 | tf_op jit(solution)/shard_map/ppermute | solution.py:171
  71.8 3.9 %collective-permute-done.9 = f32[256,5]{0,1:T(8,128)S(1)} collective-permute-done((f32[256,5]{0,1:T(8,128)S(1)}, f32[256,5]{0,1:T(8,128)S(1)}, u32[]{:S(2)}, u32[]{:S(2)}) %collective-permute-start.9) | collective-permute-done | bytes 5152 | tf_op jit(solution)/shard_map/ppermute | solution.py:171
  77.2 1.7 %abs_reduce_fusion = (f32[864]{0:T(1024)S(1)}, f32[32,8,864]{2,1,0:T(8,128)S(1)}) fusion(f32[32,8,864]{2,1,0:T(8,128)S(1)} %convolution_add_fusion.1, f32[32,8,5]{2,1,0:T(8,128)S(1)} %copy.115, f32[5,13824]{1,0:T(8,128)} %constant.182.clone, s32[]{:T(128)S(6)} %select_n.134), kind=kOutput, calls=%fused_computation.9 | convolution fusion | flops 13933728 | bytes 1806724 | tf_op jit(solution)/shard_map/dot_general | solution.py:394
  78.9 0.8 dynamic-slice_multiply_fusion
  80.2 1.0 collective-permute-done.10
  81.2 1.4 %collective-permute-start.13 = (f32[26]{0:T(128)S(1)}, f32[26]{0:T(128)S(1)}, u32[]{:S(2)}, u32[]{:S(2)}) collective-permute-start(f32[26]{0:T(128)S(1)} %fusion.55), channel_id=1, source_target_pairs={{6,0},{7,1},{0,2},{1,3},{2,4},{3,5},{4,6},{5,7},{14,8},{15,9},{8,1... | collective-permute-start | bytes 320 | tf_op jit(solution)/shard_map/ppermute | solution.py:180
  82.6 2.9 %collective-permute-start.12 = (f32[26]{0:T(128)S(1)}, f32[26]{0:T(128)S(1)}, u32[]{:S(2)}, u32[]{:S(2)}) collective-permute-start(f32[26]{0:T(128)S(1)} %fusion.55), channel_id=1, source_target_pairs={{4,0},{5,1},{6,2},{7,3},{0,4},{1,5},{2,6},{3,7},{12,8},{13,9},{14,... | collective-permute-start | bytes 320 | tf_op jit(solution)/shard_map/ppermute | solution.py:180
  85.6 1.4 %collective-permute-done.12 = f32[26]{0:T(128)S(1)} collective-permute-done((f32[26]{0:T(128)S(1)}, f32[26]{0:T(128)S(1)}, u32[]{:S(2)}, u32[]{:S(2)}) %collective-permute-start.12) | collective-permute-done | bytes 136 | tf_op jit(solution)/shard_map/ppermute | solution.py:180
  87.0 2.0 %collective-permute-done.11 = f32[26]{0:T(128)S(1)} collective-permute-done((f32[26]{0:T(128)S(1)}, f32[26]{0:T(128)S(1)}, u32[]{:S(2)}, u32[]{:S(2)}) %collective-permute-start.11) | collective-permute-done | bytes 136 | tf_op jit(solution)/shard_map/ppermute | solution.py:180
  89.1 3.2 %collective-permute-start.14 = (f32[26]{0:T(128)S(1)}, f32[26]{0:T(128)S(1)}, u32[]{:S(2)}, u32[]{:S(2)}) collective-permute-start(f32[26]{0:T(128)S(1)} %fusion.33), channel_id=1, source_target_pairs={{0,8},{1,9},{2,10},{3,11},{4,12},{5,13},{6,14},{7,15},{8,0},{9,1},... | collective-permute-start | bytes 320 | tf_op jit(solution)/shard_map/ppermute | solution.py:171
  92.3 1.0 pad_maximum_fusion
  93.3 3.6 %all-to-all-start.1 = ((f32[32,8,869]{2,1,0:T(8,128)}), f32[32,8,869]{2,1,0:T(8,128)S(1)}, u32[]{:S(2)}, u32[]{:S(2)}) async-start(f32[32,8,869]{2,1,0:T(8,128)} %pad_maximum_fusion), calls=%async_computation.1 | async-start | bytes 1835008 | tf_op jit(solution)/shard_map/all_to_all | solution.py:402
  97.0 1.9 %collective-permute-start.17 = (f32[26]{0:T(128)S(1)}, f32[26]{0:T(128)S(1)}, u32[]{:S(2)}, u32[]{:S(2)}) collective-permute-start(f32[26]{0:T(128)S(1)} %fusion.54), channel_id=1, source_target_pairs={{48,0},{0,16},{16,32},{32,48},{112,64},{64,80},{80,96},{96,112},{1... | collective-permute-start | bytes 320 | tf_op jit(solution)/shard_map/ppermute | solution.py:180
  98.9 2.7 %collective-permute-start.16 = (f32[26]{0:T(128)S(1)}, f32[26]{0:T(128)S(1)}, u32[]{:S(2)}, u32[]{:S(2)}) collective-permute-start(f32[26]{0:T(128)S(1)} %fusion.54), channel_id=1, source_target_pairs={{32,0},{48,16},{0,32},{16,48},{96,64},{112,80},{64,96},{80,112},{1... | collective-permute-start | bytes 320 | tf_op jit(solution)/shard_map/ppermute | solution.py:180
  101.6 1.5 %collective-permute-start.15 = (f32[26]{0:T(128)S(1)}, f32[26]{0:T(128)S(1)}, u32[]{:S(2)}, u32[]{:S(2)}) collective-permute-start(f32[26]{0:T(128)S(1)} %fusion.54), channel_id=1, source_target_pairs={{16,0},{32,16},{48,32},{0,48},{80,64},{96,80},{112,96},{64,112},{1... | collective-permute-start | bytes 320 | tf_op jit(solution)/shard_map/ppermute | solution.py:180
  103.0 1.6 %collective-permute-done.17 = f32[26]{0:T(128)S(1)} collective-permute-done((f32[26]{0:T(128)S(1)}, f32[26]{0:T(128)S(1)}, u32[]{:S(2)}, u32[]{:S(2)}) %collective-permute-start.17) | collective-permute-done | bytes 136 | tf_op jit(solution)/shard_map/ppermute | solution.py:180
  105.0 2.4 %collective-permute-done.15 = f32[26]{0:T(128)S(1)} collective-permute-done((f32[26]{0:T(128)S(1)}, f32[26]{0:T(128)S(1)}, u32[]{:S(2)}, u32[]{:S(2)}) %collective-permute-start.15) | collective-permute-done | bytes 136 | tf_op jit(solution)/shard_map/ppermute | solution.py:180
  107.4 2.1 %collective-permute-start.20 = (f32[26]{0:T(128)S(1)}, f32[26]{0:T(128)S(1)}, u32[]{:S(2)}, u32[]{:S(2)}) collective-permute-start(f32[26]{0:T(128)S(1)} %fusion.53), channel_id=1, source_target_pairs={{192,0},{208,16},{224,32},{240,48},{0,64},{16,80},{32,96},{48,112}... | collective-permute-start | bytes 320 | tf_op jit(solution)/shard_map/ppermute | solution.py:180
  109.5 3.2 %collective-permute-start.19 = (f32[26]{0:T(128)S(1)}, f32[26]{0:T(128)S(1)}, u32[]{:S(2)}, u32[]{:S(2)}) collective-permute-start(f32[26]{0:T(128)S(1)} %fusion.53), channel_id=1, source_target_pairs={{128,0},{144,16},{160,32},{176,48},{192,64},{208,80},{224,96},{240... | collective-permute-start | bytes 320 | tf_op jit(solution)/shard_map/ppermute | solution.py:180
  112.8 1.7 %collective-permute-done.19 = f32[26]{0:T(128)S(1)} collective-permute-done((f32[26]{0:T(128)S(1)}, f32[26]{0:T(128)S(1)}, u32[]{:S(2)}, u32[]{:S(2)}) %collective-permute-start.19) | collective-permute-done | bytes 136 | tf_op jit(solution)/shard_map/ppermute | solution.py:180
  114.5 1.6 %collective-permute-done.18 = f32[26]{0:T(128)S(1)} collective-permute-done((f32[26]{0:T(128)S(1)}, f32[26]{0:T(128)S(1)}, u32[]{:S(2)}, u32[]{:S(2)}) %collective-permute-start.18) | collective-permute-done | bytes 136 | tf_op jit(solution)/shard_map/ppermute | solution.py:180
  117.0 0.7 copy-done.7
  117.7 1.3 %multiply_bitcast_fusion.1 = (f32[1,24]{1,0:T(1,128)S(1)}, f32[1,24]{1,0:T(1,128)S(1)}, f32[1,24]{1,0:T(1,128)S(1)}, f32[1,24]{1,0:T(1,128)S(1)}) fusion(f32[24]{0:T(128)S(1)} %copy-done.5, f32[1,26]{1,0:T(1,128)S(1)} %fusion.19, f32[1,24]{1,0:T(1,128)S(1)} %copy-done.7, f32[5,24]{1,0:T(8,128)S(1)} %fusion.14, f32[]{:T(128)} %bitcast.56, f32[]{:T(128)} %bitcast.57), kind=kLoop, calls=%fused_computation.90 | loop fusion | flops 480 | bytes 1160 | tf_op jit(solution)/shard_map/stack | solution.py:417
  119.2 1.3 %add_bitcast_fusion.2 = f32[24]{0:T(128)S(1)} fusion(f32[1,24]{1,0:T(1,128)S(1)} %copy-done.7, f32[1,24]{1,0:T(1,128)S(1)} %get-tuple-element.13, f32[1,24]{1,0:T(1,128)S(1)} %get-tuple-element.12, f32[5,24]{1,0:T(8,128)S(1)} %fusion.12, f32[]{:T(128)} %bitcast.57, f32[]{:T(128)} %bitcast.56), kind=kLoop, calls=%fused_computation.87 | loop fusion | flops 432 | bytes 872 | tf_op jit(solution)/shard_map/sub | solution.py:424
  120.8 0.7 copy.121
  121.8 1.1 multiply_add_fusion
  (123 shorter events, 10.6 us)
Async XLA Ops:
  0.6 0.7 copy-start.9
  1.3 0.8 copy-start.2
  2.1 0.8 copy-start.3
  2.8 0.8 copy-start.4
  7.4 24.7 %all-to-all-start = ((f32[940,2,128]{0,1,2:T(2,128)}), f32[940,2,128]{0,1,2:T(2,128)S(1)}, u32[]{:S(2)}, u32[]{:S(2)}) async-start(f32[940,2,128]{0,1,2:T(2,128)} %copy.99), calls=%async_computation | async-start | bytes 2097152 | tf_op jit(solution)/shard_map/all_to_all | solution.py:348
  32.6 8.2 %copy-start.1 = (f32[24,864]{1,0:T(8,128)S(1)}, f32[24,864]{1,0:T(8,128)}, u32[]{:S(2)}) copy-start(f32[24,864]{1,0:T(8,128)} %constant.187.clone) | copy-start | bytes 248836
  34.2 1.2 %collective-permute-start = (f32[256,5]{0,1:T(8,128)S(1)}, f32[256,5]{0,1:T(8,128)S(1)}, u32[]{:S(2)}, u32[]{:S(2)}) collective-permute-start(f32[256,5]{0,1:T(8,128)S(1)} %fusion.2), channel_id=1, source_target_pairs={{0,1},{1,0},{2,3},{3,2},{4,5},{5,4},{6,7},{7,6},{8,9},{9,8},{10,11... | collective-permute-start | bytes 15368 | tf_op jit(solution)/shard_map/ppermute | solution.py:171
  35.4 5.8 %collective-permute-start.3 = (f32[256,5]{0,1:T(8,128)S(1)}, f32[256,5]{0,1:T(8,128)S(1)}, u32[]{:S(2)}, u32[]{:S(2)}) collective-permute-start(f32[256,5]{0,1:T(8,128)S(1)} %add.281), channel_id=1, source_target_pairs={{6,0},{7,1},{0,2},{1,3},{2,4},{3,5},{4,6},{5,7},{14,8},{15,9},{8,1... | collective-permute-start | bytes 15368 | tf_op jit(solution)/shard_map/ppermute | solution.py:180
  37.3 4.5 %collective-permute-start.2 = (f32[256,5]{0,1:T(8,128)S(1)}, f32[256,5]{0,1:T(8,128)S(1)}, u32[]{:S(2)}, u32[]{:S(2)}) collective-permute-start(f32[256,5]{0,1:T(8,128)S(1)} %add.281), channel_id=1, source_target_pairs={{4,0},{5,1},{6,2},{7,3},{0,4},{1,5},{2,6},{3,7},{12,8},{13,9},{14,... | collective-permute-start | bytes 15368 | tf_op jit(solution)/shard_map/ppermute | solution.py:180
  38.7 3.7 %collective-permute-start.1 = (f32[256,5]{0,1:T(8,128)S(1)}, f32[256,5]{0,1:T(8,128)S(1)}, u32[]{:S(2)}, u32[]{:S(2)}) collective-permute-start(f32[256,5]{0,1:T(8,128)S(1)} %add.281), channel_id=1, source_target_pairs={{2,0},{3,1},{4,2},{5,3},{6,4},{7,5},{0,6},{1,7},{10,8},{11,9},{12,... | collective-permute-start | bytes 15368 | tf_op jit(solution)/shard_map/ppermute | solution.py:180
  42.4 6.5 %copy-start.6 = (f32[864]{0:T(1024)S(1)}, f32[864]{0:T(1024)}, u32[]{:S(2)}) copy-start(f32[864]{0:T(1024)} %constant.205) | copy-start | bytes 10372
  42.4 10.9 %collective-permute-start.4 = (f32[256,5]{0,1:T(8,128)S(1)}, f32[256,5]{0,1:T(8,128)S(1)}, u32[]{:S(2)}, u32[]{:S(2)}) collective-permute-start(f32[256,5]{0,1:T(8,128)S(1)} %add_bitcast_fusion.1), channel_id=1, source_target_pairs={{0,8},{1,9},{2,10},{3,11},{4,12},{5,13},{6,14},{7,15},{8,0},{9,1},... | collective-permute-start | bytes 15368 | tf_op jit(solution)/shard_map/ppermute | solution.py:171
  53.5 3.6 %copy-start = (f32[32,8,864]{2,1,0:T(8,128)S(1)}, f32[32,8,864]{2,1,0:T(8,128)}, u32[]{:S(2)}) copy-start(f32[32,8,864]{2,1,0:T(8,128)} %shard_map.131) | copy-start | bytes 2654212
  53.6 0.7 copy-start.10
  60.4 1.2 %collective-permute-start.5 = (f32[256,5]{0,1:T(8,128)S(1)}, f32[256,5]{0,1:T(8,128)S(1)}, u32[]{:S(2)}, u32[]{:S(2)}) collective-permute-start(f32[256,5]{0,1:T(8,128)S(1)} %fusion), channel_id=1, source_target_pairs={{0,1},{1,0},{2,3},{3,2},{4,5},{5,4},{6,7},{7,6},{8,9},{9,8},{10,11... | collective-permute-start | bytes 15368 | tf_op jit(solution)/shard_map/ppermute | solution.py:171
  61.7 4.4 %collective-permute-start.8 = (f32[256,5]{0,1:T(8,128)S(1)}, f32[256,5]{0,1:T(8,128)S(1)}, u32[]{:S(2)}, u32[]{:S(2)}) collective-permute-start(f32[256,5]{0,1:T(8,128)S(1)} %add.297), channel_id=1, source_target_pairs={{6,0},{7,1},{0,2},{1,3},{2,4},{3,5},{4,6},{5,7},{14,8},{15,9},{8,1... | collective-permute-start | bytes 15368 | tf_op jit(solution)/shard_map/ppermute | solution.py:180
  61.8 4.5 %collective-permute-start.7 = (f32[256,5]{0,1:T(8,128)S(1)}, f32[256,5]{0,1:T(8,128)S(1)}, u32[]{:S(2)}, u32[]{:S(2)}) collective-permute-start(f32[256,5]{0,1:T(8,128)S(1)} %add.297), channel_id=1, source_target_pairs={{4,0},{5,1},{6,2},{7,3},{0,4},{1,5},{2,6},{3,7},{12,8},{13,9},{14,... | collective-permute-start | bytes 15368 | tf_op jit(solution)/shard_map/ppermute | solution.py:180
  64.2 3.7 %collective-permute-start.6 = (f32[256,5]{0,1:T(8,128)S(1)}, f32[256,5]{0,1:T(8,128)S(1)}, u32[]{:S(2)}, u32[]{:S(2)}) collective-permute-start(f32[256,5]{0,1:T(8,128)S(1)} %add.297), channel_id=1, source_target_pairs={{2,0},{3,1},{4,2},{5,3},{6,4},{7,5},{0,6},{1,7},{10,8},{11,9},{12,... | collective-permute-start | bytes 15368 | tf_op jit(solution)/shard_map/ppermute | solution.py:180
  67.8 7.8 %collective-permute-start.9 = (f32[256,5]{0,1:T(8,128)S(1)}, f32[256,5]{0,1:T(8,128)S(1)}, u32[]{:S(2)}, u32[]{:S(2)}) collective-permute-start(f32[256,5]{0,1:T(8,128)S(1)} %add_bitcast_fusion), channel_id=1, source_target_pairs={{0,8},{1,9},{2,10},{3,11},{4,12},{5,13},{6,14},{7,15},{8,0},{9,1},... | collective-permute-start | bytes 15368 | tf_op jit(solution)/shard_map/ppermute | solution.py:171
  80.0 1.1 collective-permute-start.10
  81.2 4.4 %collective-permute-start.13 = (f32[26]{0:T(128)S(1)}, f32[26]{0:T(128)S(1)}, u32[]{:S(2)}, u32[]{:S(2)}) collective-permute-start(f32[26]{0:T(128)S(1)} %fusion.55), channel_id=1, source_target_pairs={{6,0},{7,1},{0,2},{1,3},{2,4},{3,5},{4,6},{5,7},{14,8},{15,9},{8,1... | collective-permute-start | bytes 320 | tf_op jit(solution)/shard_map/ppermute | solution.py:180
  82.6 4.4 %collective-permute-start.12 = (f32[26]{0:T(128)S(1)}, f32[26]{0:T(128)S(1)}, u32[]{:S(2)}, u32[]{:S(2)}) collective-permute-start(f32[26]{0:T(128)S(1)} %fusion.55), channel_id=1, source_target_pairs={{4,0},{5,1},{6,2},{7,3},{0,4},{1,5},{2,6},{3,7},{12,8},{13,9},{14,... | collective-permute-start | bytes 320 | tf_op jit(solution)/shard_map/ppermute | solution.py:180
  85.5 3.5 %collective-permute-start.11 = (f32[26]{0:T(128)S(1)}, f32[26]{0:T(128)S(1)}, u32[]{:S(2)}, u32[]{:S(2)}) collective-permute-start(f32[26]{0:T(128)S(1)} %fusion.55), channel_id=1, source_target_pairs={{2,0},{3,1},{4,2},{5,3},{6,4},{7,5},{0,6},{1,7},{10,8},{11,9},{12,... | collective-permute-start | bytes 320 | tf_op jit(solution)/shard_map/ppermute | solution.py:180
  89.1 7.9 %collective-permute-start.14 = (f32[26]{0:T(128)S(1)}, f32[26]{0:T(128)S(1)}, u32[]{:S(2)}, u32[]{:S(2)}) collective-permute-start(f32[26]{0:T(128)S(1)} %fusion.33), channel_id=1, source_target_pairs={{0,8},{1,9},{2,10},{3,11},{4,12},{5,13},{6,14},{7,15},{8,0},{9,1},... | collective-permute-start | bytes 320 | tf_op jit(solution)/shard_map/ppermute | solution.py:171
  93.3 27.3 %all-to-all-start.1 = ((f32[32,8,869]{2,1,0:T(8,128)}), f32[32,8,869]{2,1,0:T(8,128)S(1)}, u32[]{:S(2)}, u32[]{:S(2)}) async-start(f32[32,8,869]{2,1,0:T(8,128)} %pad_maximum_fusion), calls=%async_computation.1 | async-start | bytes 1835008 | tf_op jit(solution)/shard_map/all_to_all | solution.py:402
  97.0 7.6 %collective-permute-start.17 = (f32[26]{0:T(128)S(1)}, f32[26]{0:T(128)S(1)}, u32[]{:S(2)}, u32[]{:S(2)}) collective-permute-start(f32[26]{0:T(128)S(1)} %fusion.54), channel_id=1, source_target_pairs={{48,0},{0,16},{16,32},{32,48},{112,64},{64,80},{80,96},{96,112},{1... | collective-permute-start | bytes 320 | tf_op jit(solution)/shard_map/ppermute | solution.py:180
  98.9 6.1 %collective-permute-start.16 = (f32[26]{0:T(128)S(1)}, f32[26]{0:T(128)S(1)}, u32[]{:S(2)}, u32[]{:S(2)}) collective-permute-start(f32[26]{0:T(128)S(1)} %fusion.54), channel_id=1, source_target_pairs={{32,0},{48,16},{0,32},{16,48},{96,64},{112,80},{64,96},{80,112},{1... | collective-permute-start | bytes 320 | tf_op jit(solution)/shard_map/ppermute | solution.py:180
  101.6 5.8 %collective-permute-start.15 = (f32[26]{0:T(128)S(1)}, f32[26]{0:T(128)S(1)}, u32[]{:S(2)}, u32[]{:S(2)}) collective-permute-start(f32[26]{0:T(128)S(1)} %fusion.54), channel_id=1, source_target_pairs={{16,0},{32,16},{48,32},{0,48},{80,64},{96,80},{112,96},{64,112},{1... | collective-permute-start | bytes 320 | tf_op jit(solution)/shard_map/ppermute | solution.py:180
  107.4 5.4 %collective-permute-start.20 = (f32[26]{0:T(128)S(1)}, f32[26]{0:T(128)S(1)}, u32[]{:S(2)}, u32[]{:S(2)}) collective-permute-start(f32[26]{0:T(128)S(1)} %fusion.53), channel_id=1, source_target_pairs={{192,0},{208,16},{224,32},{240,48},{0,64},{16,80},{32,96},{48,112}... | collective-permute-start | bytes 320 | tf_op jit(solution)/shard_map/ppermute | solution.py:180
  109.5 5.0 %collective-permute-start.19 = (f32[26]{0:T(128)S(1)}, f32[26]{0:T(128)S(1)}, u32[]{:S(2)}, u32[]{:S(2)}) collective-permute-start(f32[26]{0:T(128)S(1)} %fusion.53), channel_id=1, source_target_pairs={{128,0},{144,16},{160,32},{176,48},{192,64},{208,80},{224,96},{240... | collective-permute-start | bytes 320 | tf_op jit(solution)/shard_map/ppermute | solution.py:180
  112.6 3.5 %collective-permute-start.18 = (f32[26]{0:T(128)S(1)}, f32[26]{0:T(128)S(1)}, u32[]{:S(2)}, u32[]{:S(2)}) collective-permute-start(f32[26]{0:T(128)S(1)} %fusion.53), channel_id=1, source_target_pairs={{64,0},{80,16},{96,32},{112,48},{128,64},{144,80},{160,96},{176,11... | collective-permute-start | bytes 320 | tf_op jit(solution)/shard_map/ppermute | solution.py:180
  116.2 0.7 copy-start.5
  116.2 0.7 copy-start.8
  117.0 0.7 copy-start.7

commit v18 on v17

--- a/solution.py
+++ b/solution.py
@@ -186,14 +186,11 @@
     return total
 
 
-def sum_plan(axis, count):
+def sum_plan(axis, count, pair_first=False):
     bits = count.bit_length() - 1
     plan = []
     bit = 0
-    if axis == "vel" and bits % 2 == 1:
-        plan.append((0, 2))
-        bit = 1
-    elif axis == "vel" and bits >= 2:
+    if axis == "vel" and (bits % 2 == 1 or pair_first):
         plan.append((0, 2))
         bit = 1
     while bit + 1 < bits:
@@ -204,13 +201,13 @@
     return plan
 
 
-def tree_sum(block, axes):
+def tree_sum(block, axes, pair_first=False):
     for axis in axes:
         count = lax.axis_size(axis)
         if count & (count - 1):
             block = lax.psum(block, axis)
             continue
-        for low_bit, members in sum_plan(axis, count):
+        for low_bit, members in sum_plan(axis, count, pair_first):
             block = group_sum(block, axis, low_bit, members)
     return block
 
@@ -402,7 +399,7 @@
     back = lax.all_to_all(back, "sec", 0, 1, tiled=True)
     back = back.transpose(2, 0, 1).reshape(node_count + 5, cell_count)
     gathered = tree_sum(
-        jnp.concatenate([line_loaded, local_totals * first_copy]), ("vel", "sec")
+        jnp.concatenate([line_loaded, local_totals * first_copy]), ("vel", "sec"), True
     )
     loaded = gathered[:NXI]
     goal_mass = jnp.broadcast_to(gathered[NXI], (NXI,))

time: 124 us -> 125 us (level)
  waiting for transfers between devices: 38 us -> 34.8 us
  starting transfers between devices: 49.3 us -> 51.6 us
  local copies, waits for them, and re-layouts: 13.8 us -> 15.8 us
    ppermute x15 -> x21, starting transfers between devices: 25.5 us -> 37.8 us  [group_sum(): shifted.append(lax.ppermute(block, axis, pairs))]
    ppermute x6 -> x2, starting transfers between devices: 13.1 us -> 3.13 us  [group_sum(): return block + lax.ppermute(block, axis, pairs)]
    ppermute x6 -> x2, waiting for transfers between devices: 6.29 us -> 1.09 us  [group_sum(): return block + lax.ppermute(block, axis, pairs)]
    ppermute x15 -> x21, waiting for transfers between devices: 14 us -> 17.4 us  [group_sum(): shifted.append(lax.ppermute(block, axis, pairs))]
    all_to_all x1, waiting for transfers between devices: 17.7 us -> 16.3 us  [body(): lines = lax.all_to_all(packed, 'sec', 2, 1, tiled=True).transpose(1, 2, 0)]
  transfers between devices with their start and end apart: 23 -> 25, of which waited for: 16 -> 14; matrix products, arithmetic and copies ran while one was open for 7% -> 6% of each run, Pallas kernels for 2% -> 2%
where the time goes in v18:
time: 125 us; the launch traced here: 124 us
  starting transfers between devices  51.6 us (41%)
  waiting for transfers between devices  34.8 us (28%)
  local copies, waits for them, and re-layouts  15.8 us (13%)
  other arithmetic  8.81 us (7%)
  matrix products  6.9 us (6%)
  Pallas kernels  4.91 us (4%)
  between operations  1.68 us (1%)
    ppermute x21, starting transfers between devices, group_sum(): shifted.append(lax.ppermute(block, axis, pairs))  37.8 us
    ppermute x21, waiting for transfers between devices, group_sum(): shifted.append(lax.ppermute(block, axis, pairs))  17.4 us
    all_to_all x1, waiting for transfers between devices, body(): lines = lax.all_to_all(packed, 'sec', 2, 1, tiled=True).transpose(1, 2, 0)  16.3 us
    all_to_all x1, starting transfers between devices, body(): lines = lax.all_to_all(packed, 'sec', 2, 1, tiled=True).transpose(1, 2, 0)  7.03 us
    unnamed x24, local copies, waits for them, and re-layouts  6.36 us
    pallas_call x2, Pallas kernels, line_sweep(): pl.pallas_call(sweep_kernel, out_shape=jax.ShapeDtypeStruct(drive_term.sh...  4.91 us
    all_to_all x1, starting transfers between devices, body(): back = lax.all_to_all(back, 'sec', 0, 1, tiled=True)  3.63 us
    ppermute x2, starting transfers between devices, group_sum(): return block + lax.ppermute(block, axis, pairs)  3.13 us
  transfers between devices with their start and end apart: 25, of which 14 were waited for; matrix products, arithmetic and copies ran while one was open for 6% of the time, Pallas kernels for 2%

profile of v18, /device:TPU:32, one launch (start us, length us, event | category | flops | bytes accessed | tf_op | source)
XLA Modules:
  0.0 124.4 jit_solution(5165206547899391947)
XLA Ops:
  0.6 0.7 copy-done.9
  3.7 1.5 %copy.139 = f32[864,256]{0,1:T(8,128)S(1)} copy(f32[864,256]{1,0:T(8,128)} %param.12) | data formatting | bytes 1769472 | tf_op args[0]
  5.6 1.8 %copy.144 = f32[940,2,128]{0,1,2:T(2,128)} copy(f32[940,2,128]{0,2,1:T(8,128)S(1)} %concatenate.49) | data formatting | bytes 1925120 | tf_op jit(solution)/shard_map/concatenate | solution.py:340
  7.4 7.0 %all-to-all-start = ((f32[940,2,128]{0,1,2:T(2,128)}), f32[940,2,128]{0,1,2:T(2,128)S(1)}, u32[]{:S(2)}, u32[]{:S(2)}) async-start(f32[940,2,128]{0,1,2:T(2,128)} %copy.144), calls=%async_computation | async-start | bytes 2097152 | tf_op jit(solution)/shard_map/all_to_all | solution.py:345
  15.0 0.8 constant_dynamic-slice_fusion.11
  15.8 16.3 %all-to-all-done = f32[940,2,128]{0,1,2:T(2,128)S(1)} async-done(((f32[940,2,128]{0,1,2:T(2,128)}), f32[940,2,128]{0,1,2:T(2,128)S(1)}, u32[]{:S(2)}, u32[]{:S(2)}) %all-to-all-start) | async-done | bytes 962592 | tf_op jit(solution)/shard_map/all_to_all | solution.py:345
  32.6 1.6 %fusion.2 = f32[256,5]{0,1:T(8,128)S(1)} fusion(f32[32,8,940]{2,1,0:T(8,128)S(1)} %bitcast.178, f32[5,13824]{1,0:T(8,128)} %constant.237.clone, s32[]{:T(128)S(6)} %select_n.198), kind=kOutput, calls=%fused_computation.6 | convolution fusion | flops 13271040 | bytes 951300 | tf_op jit(solution)/shard_map/dot_general | solution.py:353
  34.4 1.6 %collective-permute-start = (f32[256,5]{0,1:T(8,128)S(1)}, f32[256,5]{0,1:T(8,128)S(1)}, u32[]{:S(2)}, u32[]{:S(2)}) collective-permute-start(f32[256,5]{0,1:T(8,128)S(1)} %fusion.2), channel_id=1, source_target_pairs={{1,0},{2,1},{3,2},{0,3},{5,4},{6,5},{7,6},{4,7},{9,8},{10,9},{11,1... | collective-permute-start | bytes 15368 | tf_op jit(solution)/shard_map/ppermute | solution.py:180
  36.7 1.5 %fusion.4 = (f32[32,8,864]{2,1,0:T(8,128)}, f32[32,8,864]{2,1,0:T(8,128)}) fusion(f32[32,8,940]{2,1,0:T(8,128)S(1)} %bitcast.180, f32[32,8]{1,0:T(8,128)S(1)} %bitcast.207, f32[864]{0:T(1024)S(1)} %copy-done.6), kind=kLoop, calls=%fused_computation.11 | loop fusion | flops 884736 | bytes 2658688 | tf_op jit(solution)/shard_map/div | solution.py:358
  38.2 2.9 %shard_map.131 = f32[32,8,864]{2,1,0:T(8,128)} custom-call(f32[32,8,864]{2,1,0:T(8,128)} %get-tuple-element.28.rate_ref, f32[32,8,864]{2,1,0:T(8,128)} %get-tuple-element.27.drive_ref, f32[1,864]{1,0:T(1,128)} %constant.262.sign_ref), custom_call_target="tpu_custom_call" | custom-call | tf_op jit(solution)/shard_map/pallas_call | solution.py:312
  41.2 3.3 %collective-permute-start.5 = (f32[256,5]{0,1:T(8,128)S(1)}, f32[256,5]{0,1:T(8,128)S(1)}, u32[]{:S(2)}, u32[]{:S(2)}) collective-permute-start(f32[256,5]{0,1:T(8,128)S(1)} %fusion.58), channel_id=1, source_target_pairs={{12,0},{13,1},{14,2},{15,3},{0,4},{1,5},{2,6},{3,7},{4,8},{5,9},{6... | collective-permute-start | bytes 15368 | tf_op jit(solution)/shard_map/ppermute | solution.py:180
  44.5 5.2 %collective-permute-start.4 = (f32[256,5]{0,1:T(8,128)S(1)}, f32[256,5]{0,1:T(8,128)S(1)}, u32[]{:S(2)}, u32[]{:S(2)}) collective-permute-start(f32[256,5]{0,1:T(8,128)S(1)} %fusion.58), channel_id=1, source_target_pairs={{8,0},{9,1},{10,2},{11,3},{12,4},{13,5},{14,6},{15,7},{0,8},{1,9},... | collective-permute-start | bytes 15368 | tf_op jit(solution)/shard_map/ppermute | solution.py:180
  49.7 2.7 %collective-permute-start.3 = (f32[256,5]{0,1:T(8,128)S(1)}, f32[256,5]{0,1:T(8,128)S(1)}, u32[]{:S(2)}, u32[]{:S(2)}) collective-permute-start(f32[256,5]{0,1:T(8,128)S(1)} %fusion.58), channel_id=1, source_target_pairs={{4,0},{5,1},{6,2},{7,3},{8,4},{9,5},{10,6},{11,7},{12,8},{13,9},{1... | collective-permute-start | bytes 15368 | tf_op jit(solution)/shard_map/ppermute | solution.py:180
  52.4 1.9 %collective-permute-done.3 = f32[256,5]{0,1:T(8,128)S(1)} collective-permute-done((f32[256,5]{0,1:T(8,128)S(1)}, f32[256,5]{0,1:T(8,128)S(1)}, u32[]{:S(2)}, u32[]{:S(2)}) %collective-permute-start.3) | collective-permute-done | bytes 5152 | tf_op jit(solution)/shard_map/ppermute | solution.py:180
  55.3 0.8 multiply_divide_fusion
  56.1 2.0 %shard_map.132 = f32[32,8,120]{2,1,0:T(8,128)} custom-call(f32[32,8,120]{2,1,0:T(8,128)} %get-tuple-element.30.rate_ref, f32[32,8,120]{2,1,0:T(8,128)} %get-tuple-element.29.drive_ref, f32[1,120]{1,0:T(1,128)} %constant.265.sign_ref), custom_call_target="tpu_custom_call" | custom-call | tf_op jit(solution)/shard_map/pallas_call | solution.py:312
  58.1 1.8 %convolution_add_fusion.1 = f32[32,8,864]{2,1,0:T(8,128)S(1)} fusion(f32[32,8,864]{2,1,0:T(8,128)S(1)} %copy-done, f32[32,8,120]{2,1,0:T(8,128)} %shard_map.132, f32[120,864,1]{1,0,2:T(8,128)S(1)} %bitcast.202), kind=kOutput, calls=%fused_computation.1 | convolution fusion | flops 318726144 | bytes 2307072 | tf_op jit(solution)/shard_map/dot_general | solution.py:373
  59.9 1.6 %fusion = f32[256,5]{0,1:T(8,128)S(1)} fusion(f32[32,8,864]{2,1,0:T(8,128)S(1)} %convolution_add_fusion.1, f32[5,13824]{1,0:T(8,128)} %constant.237.clone, s32[]{:T(128)S(6)} %select_n.198), kind=kOutput, calls=%fused_computation.4 | convolution fusion | flops 13271040 | bytes 918532 | tf_op jit(solution)/shard_map/dot_general | solution.py:377
  61.5 1.1 collective-permute-start.7
  62.6 1.4 %collective-permute-start.6 = (f32[256,5]{0,1:T(8,128)S(1)}, f32[256,5]{0,1:T(8,128)S(1)}, u32[]{:S(2)}, u32[]{:S(2)}) collective-permute-start(f32[256,5]{0,1:T(8,128)S(1)} %fusion), channel_id=1, source_target_pairs={{1,0},{2,1},{3,2},{0,3},{5,4},{6,5},{7,6},{4,7},{9,8},{10,9},{11,1... | collective-permute-start | bytes 15368 | tf_op jit(solution)/shard_map/ppermute | solution.py:180
  65.4 2.2 %collective-permute-start.11 = (f32[256,5]{0,1:T(8,128)S(1)}, f32[256,5]{0,1:T(8,128)S(1)}, u32[]{:S(2)}, u32[]{:S(2)}) collective-permute-start(f32[256,5]{0,1:T(8,128)S(1)} %fusion.57), channel_id=1, source_target_pairs={{12,0},{13,1},{14,2},{15,3},{0,4},{1,5},{2,6},{3,7},{4,8},{5,9},{6... | collective-permute-start | bytes 15368 | tf_op jit(solution)/shard_map/ppermute | solution.py:180
  67.6 4.1 %collective-permute-start.10 = (f32[256,5]{0,1:T(8,128)S(1)}, f32[256,5]{0,1:T(8,128)S(1)}, u32[]{:S(2)}, u32[]{:S(2)}) collective-permute-start(f32[256,5]{0,1:T(8,128)S(1)} %fusion.57), channel_id=1, source_target_pairs={{8,0},{9,1},{10,2},{11,3},{12,4},{13,5},{14,6},{15,7},{0,8},{1,9},... | collective-permute-start | bytes 15368 | tf_op jit(solution)/shard_map/ppermute | solution.py:180
  71.7 0.9 collective-permute-start.9
  72.7 2.5 %collective-permute-done.10 = f32[256,5]{0,1:T(8,128)S(1)} collective-permute-done((f32[256,5]{0,1:T(8,128)S(1)}, f32[256,5]{0,1:T(8,128)S(1)}, u32[]{:S(2)}, u32[]{:S(2)}) %collective-permute-start.10) | collective-permute-done | bytes 5152 | tf_op jit(solution)/shard_map/ppermute | solution.py:180
  75.2 1.1 collective-permute-done.9
  79.9 1.7 %abs_reduce_fusion = (f32[864]{0:T(1024)S(1)}, f32[32,8,864]{2,1,0:T(8,128)S(1)}) fusion(f32[32,8,864]{2,1,0:T(8,128)S(1)} %convolution_add_fusion.1, f32[32,8,5]{2,1,0:T(8,128)S(1)} %copy.170, f32[5,13824]{1,0:T(8,128)} %constant.238.clone, s32[]{:T(128)S(6)} %select_n.198), kind=kOutput, calls=%fused_computation.9 | convolution fusion | flops 13933728 | bytes 1806724 | tf_op jit(solution)/shard_map/dot_general | solution.py:391
  81.6 0.8 dynamic-slice_multiply_fusion
  82.6 1.1 collective-permute-done.12
  83.8 1.0 collective-permute-start.15
  84.8 2.4 %collective-permute-start.14 = (f32[26]{0:T(128)S(1)}, f32[26]{0:T(128)S(1)}, u32[]{:S(2)}, u32[]{:S(2)}) collective-permute-start(f32[26]{0:T(128)S(1)} %fusion.56), channel_id=1, source_target_pairs={{4,0},{5,1},{6,2},{7,3},{0,4},{1,5},{2,6},{3,7},{12,8},{13,9},{14,... | collective-permute-start | bytes 320 | tf_op jit(solution)/shard_map/ppermute | solution.py:180
  87.4 1.9 %collective-permute-done.14 = f32[26]{0:T(128)S(1)} collective-permute-done((f32[26]{0:T(128)S(1)}, f32[26]{0:T(128)S(1)}, u32[]{:S(2)}, u32[]{:S(2)}) %collective-permute-start.14) | collective-permute-done | bytes 136 | tf_op jit(solution)/shard_map/ppermute | solution.py:180
  89.3 1.5 %collective-permute-done.13 = f32[26]{0:T(128)S(1)} collective-permute-done((f32[26]{0:T(128)S(1)}, f32[26]{0:T(128)S(1)}, u32[]{:S(2)}, u32[]{:S(2)}) %collective-permute-start.13) | collective-permute-done | bytes 136 | tf_op jit(solution)/shard_map/ppermute | solution.py:180
  90.8 3.1 %collective-permute-start.16 = (f32[26]{0:T(128)S(1)}, f32[26]{0:T(128)S(1)}, u32[]{:S(2)}, u32[]{:S(2)}) collective-permute-start(f32[26]{0:T(128)S(1)} %fusion.35), channel_id=1, source_target_pairs={{0,8},{1,9},{2,10},{3,11},{4,12},{5,13},{6,14},{7,15},{8,0},{9,1},... | collective-permute-start | bytes 320 | tf_op jit(solution)/shard_map/ppermute | solution.py:171
  93.9 1.0 pad_maximum_fusion
  94.9 3.6 %all-to-all-start.1 = ((f32[32,8,869]{2,1,0:T(8,128)}), f32[32,8,869]{2,1,0:T(8,128)S(1)}, u32[]{:S(2)}, u32[]{:S(2)}) async-start(f32[32,8,869]{2,1,0:T(8,128)} %pad_maximum_fusion), calls=%async_computation.1 | async-start | bytes 1835008 | tf_op jit(solution)/shard_map/all_to_all | solution.py:399
  98.6 1.9 %collective-permute-start.19 = (f32[26]{0:T(128)S(1)}, f32[26]{0:T(128)S(1)}, u32[]{:S(2)}, u32[]{:S(2)}) collective-permute-start(f32[26]{0:T(128)S(1)} %fusion.55), channel_id=1, source_target_pairs={{48,0},{0,16},{16,32},{32,48},{112,64},{64,80},{80,96},{96,112},{1... | collective-permute-start | bytes 320 | tf_op jit(solution)/shard_map/ppermute | solution.py:180
  100.4 2.7 %collective-permute-start.18 = (f32[26]{0:T(128)S(1)}, f32[26]{0:T(128)S(1)}, u32[]{:S(2)}, u32[]{:S(2)}) collective-permute-start(f32[26]{0:T(128)S(1)} %fusion.55), channel_id=1, source_target_pairs={{32,0},{48,16},{0,32},{16,48},{96,64},{112,80},{64,96},{80,112},{1... | collective-permute-start | bytes 320 | tf_op jit(solution)/shard_map/ppermute | solution.py:180
  103.1 1.5 %collective-permute-start.17 = (f32[26]{0:T(128)S(1)}, f32[26]{0:T(128)S(1)}, u32[]{:S(2)}, u32[]{:S(2)}) collective-permute-start(f32[26]{0:T(128)S(1)} %fusion.55), channel_id=1, source_target_pairs={{16,0},{32,16},{48,32},{0,48},{80,64},{96,80},{112,96},{64,112},{1... | collective-permute-start | bytes 320 | tf_op jit(solution)/shard_map/ppermute | solution.py:180
  104.6 1.6 %collective-permute-done.19 = f32[26]{0:T(128)S(1)} collective-permute-done((f32[26]{0:T(128)S(1)}, f32[26]{0:T(128)S(1)}, u32[]{:S(2)}, u32[]{:S(2)}) %collective-permute-start.19) | collective-permute-done | bytes 136 | tf_op jit(solution)/shard_map/ppermute | solution.py:180
  106.5 2.4 %collective-permute-done.17 = f32[26]{0:T(128)S(1)} collective-permute-done((f32[26]{0:T(128)S(1)}, f32[26]{0:T(128)S(1)}, u32[]{:S(2)}, u32[]{:S(2)}) %collective-permute-start.17) | collective-permute-done | bytes 136 | tf_op jit(solution)/shard_map/ppermute | solution.py:180
  109.0 2.1 %collective-permute-start.22 = (f32[26]{0:T(128)S(1)}, f32[26]{0:T(128)S(1)}, u32[]{:S(2)}, u32[]{:S(2)}) collective-permute-start(f32[26]{0:T(128)S(1)} %fusion.54), channel_id=1, source_target_pairs={{192,0},{208,16},{224,32},{240,48},{0,64},{16,80},{32,96},{48,112}... | collective-permute-start | bytes 320 | tf_op jit(solution)/shard_map/ppermute | solution.py:180
  111.1 3.2 %collective-permute-start.21 = (f32[26]{0:T(128)S(1)}, f32[26]{0:T(128)S(1)}, u32[]{:S(2)}, u32[]{:S(2)}) collective-permute-start(f32[26]{0:T(128)S(1)} %fusion.54), channel_id=1, source_target_pairs={{128,0},{144,16},{160,32},{176,48},{192,64},{208,80},{224,96},{240... | collective-permute-start | bytes 320 | tf_op jit(solution)/shard_map/ppermute | solution.py:180
  114.4 1.7 %collective-permute-done.21 = f32[26]{0:T(128)S(1)} collective-permute-done((f32[26]{0:T(128)S(1)}, f32[26]{0:T(128)S(1)}, u32[]{:S(2)}, u32[]{:S(2)}) %collective-permute-start.21) | collective-permute-done | bytes 136 | tf_op jit(solution)/shard_map/ppermute | solution.py:180
  116.1 1.6 %collective-permute-done.20 = f32[26]{0:T(128)S(1)} collective-permute-done((f32[26]{0:T(128)S(1)}, f32[26]{0:T(128)S(1)}, u32[]{:S(2)}, u32[]{:S(2)}) %collective-permute-start.20) | collective-permute-done | bytes 136 | tf_op jit(solution)/shard_map/ppermute | solution.py:180
  119.3 1.3 %multiply_bitcast_fusion.1 = (f32[1,24]{1,0:T(1,128)S(1)}, f32[1,24]{1,0:T(1,128)S(1)}, f32[1,24]{1,0:T(1,128)S(1)}, f32[1,24]{1,0:T(1,128)S(1)}) fusion(f32[24]{0:T(128)S(1)} %copy-done.5, f32[1,26]{1,0:T(1,128)S(1)} %fusion.22, f32[1,24]{1,0:T(1,128)S(1)} %copy-done.7, f32[5,24]{1,0:T(8,128)S(1)} %fusion.19, f32[]{:T(128)} %bitcast.65, f32[]{:T(128)} %bitcast.66), kind=kLoop, calls=%fused_computation.98 | loop fusion | flops 480 | bytes 1160 | tf_op jit(solution)/shard_map/stack | solution.py:414
  120.8 1.3 %add_bitcast_fusion = f32[24]{0:T(128)S(1)} fusion(f32[1,24]{1,0:T(1,128)S(1)} %copy-done.7, f32[1,24]{1,0:T(1,128)S(1)} %get-tuple-element.15, f32[1,24]{1,0:T(1,128)S(1)} %get-tuple-element.14, f32[5,24]{1,0:T(8,128)S(1)} %fusion.17, f32[]{:T(128)} %bitcast.66, f32[]{:T(128)} %bitcast.65), kind=kLoop, calls=%fused_computation.95 | loop fusion | flops 432 | bytes 872 | tf_op jit(solution)/shard_map/sub | solution.py:421
  122.4 0.7 copy.176
  123.3 1.1 multiply_add_fusion
  (143 shorter events, 13.4 us)
Async XLA Ops:
  0.6 0.7 copy-start.9
  1.3 0.8 copy-start.2
  2.1 0.8 copy-start.3
  2.8 0.8 copy-start.4
  7.4 24.7 %all-to-all-start = ((f32[940,2,128]{0,1,2:T(2,128)}), f32[940,2,128]{0,1,2:T(2,128)S(1)}, u32[]{:S(2)}, u32[]{:S(2)}) async-start(f32[940,2,128]{0,1,2:T(2,128)} %copy.144), calls=%async_computation | async-start | bytes 2097152 | tf_op jit(solution)/shard_map/all_to_all | solution.py:345
  14.8 1.0 copy-start.1
  34.1 7.0 %collective-permute-start.2 = (f32[256,5]{0,1:T(8,128)S(1)}, f32[256,5]{0,1:T(8,128)S(1)}, u32[]{:S(2)}, u32[]{:S(2)}) collective-permute-start(f32[256,5]{0,1:T(8,128)S(1)} %fusion.2), channel_id=1, source_target_pairs={{3,0},{0,1},{1,2},{2,3},{7,4},{4,5},{5,6},{6,7},{11,8},{8,9},{9,10... | collective-permute-start | bytes 15368 | tf_op jit(solution)/shard_map/ppermute | solution.py:180
  34.2 6.9 %collective-permute-start.1 = (f32[256,5]{0,1:T(8,128)S(1)}, f32[256,5]{0,1:T(8,128)S(1)}, u32[]{:S(2)}, u32[]{:S(2)}) collective-permute-start(f32[256,5]{0,1:T(8,128)S(1)} %fusion.2), channel_id=1, source_target_pairs={{2,0},{3,1},{0,2},{1,3},{6,4},{7,5},{4,6},{5,7},{10,8},{11,9},{8,1... | collective-permute-start | bytes 15368 | tf_op jit(solution)/shard_map/ppermute | solution.py:180
  34.4 6.7 %collective-permute-start = (f32[256,5]{0,1:T(8,128)S(1)}, f32[256,5]{0,1:T(8,128)S(1)}, u32[]{:S(2)}, u32[]{:S(2)}) collective-permute-start(f32[256,5]{0,1:T(8,128)S(1)} %fusion.2), channel_id=1, source_target_pairs={{1,0},{2,1},{3,2},{0,3},{5,4},{6,5},{7,6},{4,7},{9,8},{10,9},{11,1... | collective-permute-start | bytes 15368 | tf_op jit(solution)/shard_map/ppermute | solution.py:180
  36.0 0.7 copy-start.6
  41.2 11.2 %collective-permute-start.5 = (f32[256,5]{0,1:T(8,128)S(1)}, f32[256,5]{0,1:T(8,128)S(1)}, u32[]{:S(2)}, u32[]{:S(2)}) collective-permute-start(f32[256,5]{0,1:T(8,128)S(1)} %fusion.58), channel_id=1, source_target_pairs={{12,0},{13,1},{14,2},{15,3},{0,4},{1,5},{2,6},{3,7},{4,8},{5,9},{6... | collective-permute-start | bytes 15368 | tf_op jit(solution)/shard_map/ppermute | solution.py:180
  44.5 7.9 %collective-permute-start.4 = (f32[256,5]{0,1:T(8,128)S(1)}, f32[256,5]{0,1:T(8,128)S(1)}, u32[]{:S(2)}, u32[]{:S(2)}) collective-permute-start(f32[256,5]{0,1:T(8,128)S(1)} %fusion.58), channel_id=1, source_target_pairs={{8,0},{9,1},{10,2},{11,3},{12,4},{13,5},{14,6},{15,7},{0,8},{1,9},... | collective-permute-start | bytes 15368 | tf_op jit(solution)/shard_map/ppermute | solution.py:180
  49.7 4.5 %collective-permute-start.3 = (f32[256,5]{0,1:T(8,128)S(1)}, f32[256,5]{0,1:T(8,128)S(1)}, u32[]{:S(2)}, u32[]{:S(2)}) collective-permute-start(f32[256,5]{0,1:T(8,128)S(1)} %fusion.58), channel_id=1, source_target_pairs={{4,0},{5,1},{6,2},{7,3},{8,4},{9,5},{10,6},{11,7},{12,8},{13,9},{1... | collective-permute-start | bytes 15368 | tf_op jit(solution)/shard_map/ppermute | solution.py:180
  54.5 3.6 %copy-start = (f32[32,8,864]{2,1,0:T(8,128)S(1)}, f32[32,8,864]{2,1,0:T(8,128)}, u32[]{:S(2)}) copy-start(f32[32,8,864]{2,1,0:T(8,128)} %shard_map.131) | copy-start | bytes 2654212
  54.6 0.7 copy-start.10
  61.5 3.2 %collective-permute-start.8 = (f32[256,5]{0,1:T(8,128)S(1)}, f32[256,5]{0,1:T(8,128)S(1)}, u32[]{:S(2)}, u32[]{:S(2)}) collective-permute-start(f32[256,5]{0,1:T(8,128)S(1)} %fusion), channel_id=1, source_target_pairs={{3,0},{0,1},{1,2},{2,3},{7,4},{4,5},{5,6},{6,7},{11,8},{8,9},{9,10... | collective-permute-start | bytes 15368 | tf_op jit(solution)/shard_map/ppermute | solution.py:180
  61.5 3.7 %collective-permute-start.7 = (f32[256,5]{0,1:T(8,128)S(1)}, f32[256,5]{0,1:T(8,128)S(1)}, u32[]{:S(2)}, u32[]{:S(2)}) collective-permute-start(f32[256,5]{0,1:T(8,128)S(1)} %fusion), channel_id=1, source_target_pairs={{2,0},{3,1},{0,2},{1,3},{6,4},{7,5},{4,6},{5,7},{10,8},{11,9},{8,1... | collective-permute-start | bytes 15368 | tf_op jit(solution)/shard_map/ppermute | solution.py:180
  62.6 2.8 %collective-permute-start.6 = (f32[256,5]{0,1:T(8,128)S(1)}, f32[256,5]{0,1:T(8,128)S(1)}, u32[]{:S(2)}, u32[]{:S(2)}) collective-permute-start(f32[256,5]{0,1:T(8,128)S(1)} %fusion), channel_id=1, source_target_pairs={{1,0},{2,1},{3,2},{0,3},{5,4},{6,5},{7,6},{4,7},{9,8},{10,9},{11,1... | collective-permute-start | bytes 15368 | tf_op jit(solution)/shard_map/ppermute | solution.py:180
  65.4 7.2 %collective-permute-start.11 = (f32[256,5]{0,1:T(8,128)S(1)}, f32[256,5]{0,1:T(8,128)S(1)}, u32[]{:S(2)}, u32[]{:S(2)}) collective-permute-start(f32[256,5]{0,1:T(8,128)S(1)} %fusion.57), channel_id=1, source_target_pairs={{12,0},{13,1},{14,2},{15,3},{0,4},{1,5},{2,6},{3,7},{4,8},{5,9},{6... | collective-permute-start | bytes 15368 | tf_op jit(solution)/shard_map/ppermute | solution.py:180
  67.6 7.6 %collective-permute-start.10 = (f32[256,5]{0,1:T(8,128)S(1)}, f32[256,5]{0,1:T(8,128)S(1)}, u32[]{:S(2)}, u32[]{:S(2)}) collective-permute-start(f32[256,5]{0,1:T(8,128)S(1)} %fusion.57), channel_id=1, source_target_pairs={{8,0},{9,1},{10,2},{11,3},{12,4},{13,5},{14,6},{15,7},{0,8},{1,9},... | collective-permute-start | bytes 15368 | tf_op jit(solution)/shard_map/ppermute | solution.py:180
  71.7 4.5 %collective-permute-start.9 = (f32[256,5]{0,1:T(8,128)S(1)}, f32[256,5]{0,1:T(8,128)S(1)}, u32[]{:S(2)}, u32[]{:S(2)}) collective-permute-start(f32[256,5]{0,1:T(8,128)S(1)} %fusion.57), channel_id=1, source_target_pairs={{4,0},{5,1},{6,2},{7,3},{8,4},{9,5},{10,6},{11,7},{12,8},{13,9},{1... | collective-permute-start | bytes 15368 | tf_op jit(solution)/shard_map/ppermute | solution.py:180
  82.6 1.1 collective-permute-start.12
  83.8 3.6 %collective-permute-start.15 = (f32[26]{0:T(128)S(1)}, f32[26]{0:T(128)S(1)}, u32[]{:S(2)}, u32[]{:S(2)}) collective-permute-start(f32[26]{0:T(128)S(1)} %fusion.56), channel_id=1, source_target_pairs={{6,0},{7,1},{0,2},{1,3},{2,4},{3,5},{4,6},{5,7},{14,8},{15,9},{8,1... | collective-permute-start | bytes 320 | tf_op jit(solution)/shard_map/ppermute | solution.py:180
  84.8 4.4 %collective-permute-start.14 = (f32[26]{0:T(128)S(1)}, f32[26]{0:T(128)S(1)}, u32[]{:S(2)}, u32[]{:S(2)}) collective-permute-start(f32[26]{0:T(128)S(1)} %fusion.56), channel_id=1, source_target_pairs={{4,0},{5,1},{6,2},{7,3},{0,4},{1,5},{2,6},{3,7},{12,8},{13,9},{14,... | collective-permute-start | bytes 320 | tf_op jit(solution)/shard_map/ppermute | solution.py:180
  87.2 3.5 %collective-permute-start.13 = (f32[26]{0:T(128)S(1)}, f32[26]{0:T(128)S(1)}, u32[]{:S(2)}, u32[]{:S(2)}) collective-permute-start(f32[26]{0:T(128)S(1)} %fusion.56), channel_id=1, source_target_pairs={{2,0},{3,1},{4,2},{5,3},{6,4},{7,5},{0,6},{1,7},{10,8},{11,9},{12,... | collective-permute-start | bytes 320 | tf_op jit(solution)/shard_map/ppermute | solution.py:180
  90.8 7.8 %collective-permute-start.16 = (f32[26]{0:T(128)S(1)}, f32[26]{0:T(128)S(1)}, u32[]{:S(2)}, u32[]{:S(2)}) collective-permute-start(f32[26]{0:T(128)S(1)} %fusion.35), channel_id=1, source_target_pairs={{0,8},{1,9},{2,10},{3,11},{4,12},{5,13},{6,14},{7,15},{8,0},{9,1},... | collective-permute-start | bytes 320 | tf_op jit(solution)/shard_map/ppermute | solution.py:171
  94.9 27.3 %all-to-all-start.1 = ((f32[32,8,869]{2,1,0:T(8,128)}), f32[32,8,869]{2,1,0:T(8,128)S(1)}, u32[]{:S(2)}, u32[]{:S(2)}) async-start(f32[32,8,869]{2,1,0:T(8,128)} %pad_maximum_fusion), calls=%async_computation.1 | async-start | bytes 1835008 | tf_op jit(solution)/shard_map/all_to_all | solution.py:399
  98.6 7.6 %collective-permute-start.19 = (f32[26]{0:T(128)S(1)}, f32[26]{0:T(128)S(1)}, u32[]{:S(2)}, u32[]{:S(2)}) collective-permute-start(f32[26]{0:T(128)S(1)} %fusion.55), channel_id=1, source_target_pairs={{48,0},{0,16},{16,32},{32,48},{112,64},{64,80},{80,96},{96,112},{1... | collective-permute-start | bytes 320 | tf_op jit(solution)/shard_map/ppermute | solution.py:180
  100.4 6.1 %collective-permute-start.18 = (f32[26]{0:T(128)S(1)}, f32[26]{0:T(128)S(1)}, u32[]{:S(2)}, u32[]{:S(2)}) collective-permute-start(f32[26]{0:T(128)S(1)} %fusion.55), channel_id=1, source_target_pairs={{32,0},{48,16},{0,32},{16,48},{96,64},{112,80},{64,96},{80,112},{1... | collective-permute-start | bytes 320 | tf_op jit(solution)/shard_map/ppermute | solution.py:180
  103.1 5.8 %collective-permute-start.17 = (f32[26]{0:T(128)S(1)}, f32[26]{0:T(128)S(1)}, u32[]{:S(2)}, u32[]{:S(2)}) collective-permute-start(f32[26]{0:T(128)S(1)} %fusion.55), channel_id=1, source_target_pairs={{16,0},{32,16},{48,32},{0,48},{80,64},{96,80},{112,96},{64,112},{1... | collective-permute-start | bytes 320 | tf_op jit(solution)/shard_map/ppermute | solution.py:180
  109.0 5.4 %collective-permute-start.22 = (f32[26]{0:T(128)S(1)}, f32[26]{0:T(128)S(1)}, u32[]{:S(2)}, u32[]{:S(2)}) collective-permute-start(f32[26]{0:T(128)S(1)} %fusion.54), channel_id=1, source_target_pairs={{192,0},{208,16},{224,32},{240,48},{0,64},{16,80},{32,96},{48,112}... | collective-permute-start | bytes 320 | tf_op jit(solution)/shard_map/ppermute | solution.py:180
  111.1 5.0 %collective-permute-start.21 = (f32[26]{0:T(128)S(1)}, f32[26]{0:T(128)S(1)}, u32[]{:S(2)}, u32[]{:S(2)}) collective-permute-start(f32[26]{0:T(128)S(1)} %fusion.54), channel_id=1, source_target_pairs={{128,0},{144,16},{160,32},{176,48},{192,64},{208,80},{224,96},{240... | collective-permute-start | bytes 320 | tf_op jit(solution)/shard_map/ppermute | solution.py:180
  114.2 3.5 %collective-permute-start.20 = (f32[26]{0:T(128)S(1)}, f32[26]{0:T(128)S(1)}, u32[]{:S(2)}, u32[]{:S(2)}) collective-permute-start(f32[26]{0:T(128)S(1)} %fusion.54), channel_id=1, source_target_pairs={{64,0},{80,16},{96,32},{112,48},{128,64},{144,80},{160,96},{176,11... | collective-permute-start | bytes 320 | tf_op jit(solution)/shard_map/ppermute | solution.py:180
  117.8 0.7 copy-start.5
  117.8 0.7 copy-start.8
  118.6 0.7 copy-start.7
